TPU v7x, 256 devices: a whole 4x4x8 slice. The times are simulated.
256 devices in a mesh: tile: 128 (over z, x, y), chan: 2 (over core).
Axes of the slice: x: 4, y: 4, z: 8, core: 2. Of those that a mesh axis runs over, the one named last changes fastest.
Arguments:
- jacobian: bfloat16 [1024, 616, 411], P('tile', 'chan'), may hold values from -0.3125 to 0.3125
- r_inverse: bfloat16 [616, 616], P('chan'), as said below
- innovation: bfloat16 [1024, 616], P('tile', 'chan'), may hold values from -6 to 6
- increments: bfloat16 [2048, 128, 411], P('tile'), may hold values from -6 to 6
- owner_offset: int32 [1024, 1], P('tile'), may hold values from 0 to 3; in each aligned block of 8 rows (0 to 7, 8 to 15, ...) at most 3 rows name the same one
- column_slot: int32 [1024], P('tile'), may hold values from 0 to 15
- foot_counts: int32 [128], P('tile'), may hold values from 1 to 8, as said below
Outputs:
- gradient: bfloat16 [2048, 128, 411], P('tile')
Inputs may be any that keep to these rules, and one draw needn't show every extreme that they name: r_inverse is symmetric. `owner_offset`: the 8 footprints of one tile name each value at most 3 times, and some tile names some value exactly 3 times. `foot_counts`: each count is 8 divided by 1, 2, 4 or 8; some tile has 8.
All inputs are finite; a program needn't handle non-finite values.
Results may differ from a plain program's by a relative error of at most 0.0052.
Values may be sent and summed in bfloat16 or wider, within the bound.
No kernel may reach another device: no remote copies, remote signals or barrier semaphores. Data moves between devices by JAX's collectives and lax.ppermute only.
A program may use at most 64 MiB of HBM per device.

v0:
```python
import jax
import jax.numpy as jnp
from jax import lax
from jax.sharding import PartitionSpec as P

SPAN = 4
CAP = 3


group_rows = 8


def passed_along(value, axis, by):
    count = lax.axis_size(axis)
    return lax.ppermute(value, axis, [(i, (i + by) % count) for i in range(count)])


def on_device(jacobian, r_inverse, innovation, increments, owner_offset, column_slot, foot_counts):
    foot = jacobian.shape[0]
    state = jacobian.shape[2]
    columns = increments.shape[0]
    members = increments.shape[1]
    capacity = CAP
    slots_total = SPAN * capacity
    offset = owner_offset[:, 0]
    order = jnp.arange(foot, dtype=jnp.int32)
    earlier = (offset[:, None] == offset[None, :]) & (order[None, :] < order[:, None])
    rank = jnp.sum(earlier.astype(jnp.int32), axis=1)
    place = offset * capacity + rank
    select = place[None, :] == jnp.arange(slots_total, dtype=jnp.int32)[:, None]
    request = jnp.sum(jnp.where(select, column_slot[None, :], 0), axis=1)
    jac_all, innov_all, r_all = (jacobian, innovation, r_inverse)
    fetched_parts = []
    for neighbor_rank in range(SPAN):
        wanted = request[neighbor_rank * capacity : (neighbor_rank + 1) * capacity]
        if neighbor_rank == 1:
            fetched_parts.append(jnp.take(increments, wanted, axis=0))
        else:
            asked = passed_along(wanted, "tile", neighbor_rank - 1)
            picked = jnp.take(increments, asked, axis=0)
            fetched_parts.append(passed_along(picked, "tile", 1 - neighbor_rank))
    fetched = jnp.concatenate(fetched_parts, axis=0)
    column_state = jnp.take(fetched, place, axis=0)
    count = foot_counts[0]
    block_total = (count + group_rows - 1) // group_rows
    adjoint_buf = jnp.zeros((foot, members, state), jnp.bfloat16)

    def one_block(block_index, buf):
        start = block_index * group_rows
        evolved = jnp.einsum(
            "fks,fms->fmk", jac_all, column_state, preferred_element_type=jnp.float32
        )
        departure = (evolved - innov_all.astype(jnp.float32)[:, None, :]).astype(jnp.bfloat16)
        all_channels = lax.all_gather(departure, "chan", axis=2, tiled=True)
        weighted = jnp.einsum(
            "fmk,ik->fmi", all_channels, r_all, preferred_element_type=jnp.float32
        )
        weighted = weighted.astype(jnp.bfloat16)
        partial_adj = jnp.einsum(
            "fks,fmk->fms", jac_all, weighted, preferred_element_type=jnp.float32
        )
        summed = lax.psum(partial_adj, "chan")
        live = start + jnp.arange(group_rows, dtype=jnp.int32) < count
        summed = jnp.where(live[:, None, None], summed, jnp.zeros_like(summed)).astype(jnp.bfloat16)
        return summed

    adjoint_buf = lax.fori_loop(0, block_total, one_block, adjoint_buf)
    flat = adjoint_buf.reshape(foot, members * state)
    packed = jnp.dot(select.astype(jnp.bfloat16), flat, preferred_element_type=jnp.float32).astype(
        jnp.bfloat16
    )
    received_parts = []
    slot_parts = []
    for neighbor_rank in range(SPAN):
        piece = packed[neighbor_rank * capacity : (neighbor_rank + 1) * capacity]
        wanted = request[neighbor_rank * capacity : (neighbor_rank + 1) * capacity]
        if neighbor_rank == 1:
            received_parts.append(piece)
            slot_parts.append(wanted)
        else:
            moved, moved_slots = passed_along((piece, wanted), "tile", neighbor_rank - 1)
            received_parts.append(moved)
            slot_parts.append(moved_slots)
    received = jnp.concatenate(received_parts, axis=0)
    got_slots = jnp.concatenate(slot_parts, axis=0)
    assign = (got_slots[None, :] == jnp.arange(columns, dtype=jnp.int32)[:, None]).astype(
        jnp.bfloat16
    )
    gradient = jnp.dot(assign, received, preferred_element_type=jnp.float32).astype(jnp.bfloat16)
    gradient = gradient.reshape(columns, members, state)
    return gradient


def solution(mesh):
    in_specs = (
        P("tile", "chan", None),
        P("chan", None),
        P("tile", "chan"),
        P("tile", None, None),
        P("tile", None),
        P("tile"),
        P("tile"),
    )
    out_specs = P("tile", None, None)
    return jax.shard_map(
        on_device, mesh=mesh, in_specs=in_specs, out_specs=out_specs, check_vma=False
    )
```

profile of v0, /device:TPU:8, one launch (start us, length us, event | category | flops | bytes accessed | tf_op | source)
XLA Modules:
  0.0 157.7 jit_solution(7195260682323156579)
XLA Ops:
  6.5 1.0 convert_reduce_fusion
  7.5 0.7 multiply_add_fusion
  8.2 0.7 select_reduce_fusion
  8.9 0.1 fusion.22
  9.0 2.2 %collective-permute-start = (s32[3]{0:T(128)S(1)}, s32[3]{0:T(128)S(1)}, u32[]{:S(2)}, u32[]{:S(2)}) collective-permute-start(s32[3]{0:T(128)S(1)} %get-tuple-element.221), channel_id=1, source_target_pairs={{0,254},{2,0},{4,2},{6,4},{8,6},{10,8},{12,10},{14,12},{16,14},{18... | collective-permute-start | bytes 44 | tf_op jit(solution)/shard_map/ppermute | solution.py:15
  11.2 4.3 %collective-permute-start.2 = (s32[3]{0:T(128)S(1)}, s32[3]{0:T(128)S(1)}, u32[]{:S(2)}, u32[]{:S(2)}) collective-permute-start(s32[3]{0:T(128)S(1)} %get-tuple-element.219), channel_id=1, source_target_pairs={{0,4},{2,6},{4,8},{6,10},{8,12},{10,14},{12,16},{14,18},{16,20},{1... | collective-permute-start | bytes 44 | tf_op jit(solution)/shard_map/ppermute | solution.py:15
  15.4 0.1 compare_and_fusion.2
  15.5 0.7 and_bitcast_fusion
  16.2 4.5 %copy.26 = bf16[8,308,411]{1,2,0:T(8,128)(2,1)} copy(bf16[8,308,411]{2,0,1:T(8,128)(2,1)} %param.11) | data formatting | bytes 4050816 | tf_op args[0]
  20.8 2.5 %gather_fusion.2 = bf16[3,128,411]{1,0,2:T(4,128)(2,1)S(1)} fusion(bf16[16,128,411]{1,0,2:T(8,128)(2,1)S(1)} %copy-done, s32[1024]{0:T(1024)S(1)} %pad_clamp_fusion.3), kind=kCustom, calls=%fused_computation.1.clone | custom fusion | bytes 631308 | tf_op jit(solution)/shard_map/jit(_take)/gather | solution.py:37
  23.3 2.5 %gather_fusion.1 = bf16[3,128,411]{1,0,2:T(4,128)(2,1)S(1)} fusion(bf16[16,128,411]{1,0,2:T(8,128)(2,1)S(1)} %copy-done, s32[1024]{0:T(1024)S(1)} %pad_clamp_fusion.4), kind=kCustom, calls=%fused_computation.clone | custom fusion | bytes 631308 | tf_op jit(solution)/shard_map/jit(_take)/gather | solution.py:40
  25.7 1.0 broadcast_select_fusion.3
  26.8 2.5 %gather_fusion.3 = bf16[3,128,411]{1,0,2:T(4,128)(2,1)S(1)} fusion(bf16[16,128,411]{1,0,2:T(8,128)(2,1)S(1)} %copy-done, s32[1024]{0:T(1024)S(1)} %pad_clamp_fusion.2), kind=kCustom, calls=%fused_computation.2.clone | custom fusion | bytes 631308 | tf_op jit(solution)/shard_map/jit(_take)/gather | solution.py:40
  29.3 1.0 broadcast_select_fusion.1
  30.3 4.5 %collective-permute-start.4 = (bf16[3,128,411]{1,0,2:T(4,128)(2,1)}, bf16[3,128,411]{1,0,2:T(4,128)(2,1)S(1)}, u32[]{:S(2)}, u32[]{:S(2)}) collective-permute-start(bf16[3,128,411]{1,0,2:T(4,128)(2,1)} %broadcast_select_fusion.1), channel_id=1, source_target_pairs={{0,254},{2,0},{4,2},{6,4},{8,6},{10,8},{12,10},{14,12},{16,14},{18... | collective-permute-start | bytes 946952 | tf_op jit(solution)/shard_map/ppermute | solution.py:15
  34.8 2.5 %gather_fusion.4 = bf16[3,128,411]{1,0,2:T(4,128)(2,1)S(1)} fusion(bf16[16,128,411]{1,0,2:T(8,128)(2,1)S(1)} %copy-done, s32[1024]{0:T(1024)S(1)} %pad_clamp_fusion.1), kind=kCustom, calls=%fused_computation.3.clone | custom fusion | bytes 631308 | tf_op jit(solution)/shard_map/jit(_take)/gather | solution.py:40
  37.3 0.2 broadcast_select_fusion
  37.5 8.4 %collective-permute-start.5 = (bf16[3,128,411]{1,0,2:T(4,128)(2,1)S(1)}, bf16[3,128,411]{1,0,2:T(4,128)(2,1)S(1)}, u32[]{:S(2)}, u32[]{:S(2)}) collective-permute-start(bf16[3,128,411]{1,0,2:T(4,128)(2,1)S(1)} %broadcast_select_fusion), channel_id=1, source_target_pairs={{0,252},{2,254},{4,0},{6,2},{8,4},{10,6},{12,8},{14,10},{16,12},{1... | collective-permute-start | bytes 946952 | tf_op jit(solution)/shard_map/ppermute | solution.py:15
  45.9 0.2 broadcast_select_fusion.2
  46.1 6.7 %collective-permute-done.4 = bf16[3,128,411]{1,0,2:T(4,128)(2,1)S(1)} collective-permute-done((bf16[3,128,411]{1,0,2:T(4,128)(2,1)}, bf16[3,128,411]{1,0,2:T(4,128)(2,1)S(1)}, u32[]{:S(2)}, u32[]{:S(2)}) %collective-permute-start.4) | collective-permute-done | bytes 315680 | tf_op jit(solution)/shard_map/ppermute | solution.py:15
  52.8 4.7 %collective-permute-done.5 = bf16[3,128,411]{1,0,2:T(4,128)(2,1)S(1)} collective-permute-done((bf16[3,128,411]{1,0,2:T(4,128)(2,1)S(1)}, bf16[3,128,411]{1,0,2:T(4,128)(2,1)S(1)}, u32[]{:S(2)}, u32[]{:S(2)}) %collective-permute-start.5) | collective-permute-done | bytes 315680 | tf_op jit(solution)/shard_map/ppermute | solution.py:15
  57.5 1.4 pad_maximum_fusion
  58.8 0.3 copy.22
  59.2 1.6 gather_fusion
  60.7 3.3 %fusion.7 = bf16[8,128,308]{1,2,0:T(8,128)(2,1)S(1)} fusion(bf16[8,308,411]{1,2,0:T(8,128)(2,1)} %copy.26, bf16[8,128,411]{1,2,0:T(8,128)(2,1)} %gather_fusion, pred[8]{0:T(512)(128)(4,1)S(1)} %get-tuple-element.210, f32[8,308]{1,0:T(8,128)S(1)} %convert_element_type.46), kind=kOutput, calls=%fused_computation.18 | convolution fusion | flops 260303872 | bytes 3507784 | tf_op jit(solution)/shard_map/while/body/fks,fms->fmk/dot_general | solution.py:50
  64.0 0.9 copy.24
  64.9 0.0 all-gather.2.cloned.1.call-update
  65.6 15.6 %all-gather.2.cloned.1.call-done = bf16[8,128,616]{1,0,2:T(8,128)(2,1)} async-done(((bf16[8,128,308]{1,0,2:T(8,128)(2,1)}), bf16[8,128,616]{1,0,2:T(8,128)(2,1)}) %all-gather.2.cloned.1.call-update) | async-done | bytes 1261584 | tf_op jit(solution)/shard_map/while/body/all_gather | solution.py:54
  81.2 3.6 %fusion.8 = f32[8,128,411]{1,2,0:T(8,128)S(1)} fusion(bf16[8,308,411]{1,2,0:T(8,128)(2,1)} %copy.26, bf16[8,128,616]{1,0,2:T(8,128)(2,1)} %all-gather.2.cloned.1.call-done, bf16[308,616]{1,0:T(8,128)(2,1)} %param.12), kind=kOutput, calls=%fused_computation.20 | convolution fusion | flops 648130560 | bytes 5349888 | tf_op jit(solution)/shard_map/while/body/fks,fmk->fms/dot_general | solution.py:59
  84.8 8.4 %all-reduce.1 = bf16[8,128,411]{1,2,0:T(8,128)(2,1)} all-reduce(f32[8,128,411]{1,2,0:T(8,128)S(1)} %fusion.8), channel_id=1, replica_groups=mesh['tile'=128,'chan'=2] {'chan'}, use_global_device_ids=true, to_apply=%region_2.4 | all-reduce | flops 420864 | bytes 2525184 | tf_op jit(solution)/shard_map/while/body/psum | solution.py:62
  93.3 1.4 copy.27
  94.7 1.1 broadcast_in_dim.60
  95.8 2.0 %while.16 = (s32[]{:T(128)}, bf16[8,128,411]{2,1,0:T(8,128)(2,1)}, s32[]{:T(128)}, s32[]{:T(128)}, bf16[8,128,411]{2,1,0:T(8,128)(2,1)S(1)}, /*index=5*/s32[]{:T(128)}, s32[]{:T(128)}) while((s32[]{:T(128)}, bf16[8,128,411]{2,1,0:T(8,128)(2,1)}, s32[]{:T(128)}, s32[]{:T(128)}, bf16[8,128,411]{2,1,0:T(8,128)(2,1)S(1)}, /*index=5*/s32[]{:T(128)}, ...), condition=%wide.region_4.6_spmd, body=%wide.region_3.5_spmd.sunk | while | flops 420883 | bytes 1683569 | solution.py:67
  95.8 0.7 add_compare_fusion.2
  96.4 1.3 select_convert_fusion.2
  97.8 2.6 %reshape.37 = bf16[8,52608]{1,0:T(8,128)(2,1)S(1)} reshape(bf16[8,128,411]{2,1,0:T(8,128)(2,1)} %get-tuple-element.179) | data formatting | bytes 1683456 | tf_op jit(solution)/shard_map/reshape | solution.py:68
  100.4 0.7 convolution_convert_fusion.1
  101.1 0.7 fusion.21
  101.8 1.1 collective-permute-start.6
  102.9 1.2 collective-permute-start.7
  104.1 4.2 %collective-permute-start.8 = (bf16[3,52608]{1,0:T(4,128)(2,1)S(1)}, bf16[3,52608]{1,0:T(4,128)(2,1)S(1)}, u32[]{:S(2)}, u32[]{:S(2)}) collective-permute-start(bf16[3,52608]{1,0:T(4,128)(2,1)S(1)} %get-tuple-element.215), channel_id=1, source_target_pairs={{0,4},{2,6},{4,8},{6,10},{8,12},{10,14},{12,16},{14,18},{16,20},{1... | collective-permute-start | bytes 946952 | tf_op jit(solution)/shard_map/ppermute | solution.py:15
  108.3 0.1 pad_add_fusion
  108.4 5.5 %collective-permute-done.6 = bf16[3,52608]{1,0:T(4,128)(2,1)S(1)} collective-permute-done((bf16[3,52608]{1,0:T(4,128)(2,1)S(1)}, bf16[3,52608]{1,0:T(4,128)(2,1)S(1)}, u32[]{:S(2)}, u32[]{:S(2)}) %collective-permute-start.6) | collective-permute-done | bytes 315680 | tf_op jit(solution)/shard_map/ppermute | solution.py:15
  113.9 6.9 %collective-permute-done.7 = bf16[3,52608]{1,0:T(4,128)(2,1)S(1)} collective-permute-done((bf16[3,52608]{1,0:T(4,128)(2,1)S(1)}, bf16[3,52608]{1,0:T(4,128)(2,1)S(1)}, u32[]{:S(2)}, u32[]{:S(2)}) %collective-permute-start.7) | collective-permute-done | bytes 315680 | tf_op jit(solution)/shard_map/ppermute | solution.py:15
  120.8 19.4 %collective-permute-done.8 = bf16[3,52608]{1,0:T(4,128)(2,1)S(1)} collective-permute-done((bf16[3,52608]{1,0:T(4,128)(2,1)S(1)}, bf16[3,52608]{1,0:T(4,128)(2,1)S(1)}, u32[]{:S(2)}, u32[]{:S(2)}) %collective-permute-start.8) | collective-permute-done | bytes 315680 | tf_op jit(solution)/shard_map/ppermute | solution.py:15
  140.1 1.4 convolution_convert_fusion
  141.6 5.0 %reshape.38 = bf16[16,128,411]{2,1,0:T(8,128)(2,1)} reshape(bf16[16,52608]{1,0:T(8,128)(2,1)S(1)} %convolution_convert_fusion) | data formatting | bytes 3366912 | tf_op jit(solution)/shard_map/reshape | solution.py:90
  146.5 4.3 %copy.28 = bf16[16,128,411]{1,0,2:T(8,128)(2,1)} copy(bf16[16,128,411]{2,1,0:T(8,128)(2,1)} %reshape.38) | data formatting | bytes 3366912 | tf_op jit(solution)/shard_map/reshape | solution.py:90
  (23 shorter events, 0.1 us)
Async XLA Ops:
  6.5 14.2 %copy-start = (bf16[16,128,411]{1,0,2:T(8,128)(2,1)S(1)}, bf16[16,128,411]{1,0,2:T(8,128)(2,1)}, u32[]{:S(2)}) copy-start(bf16[16,128,411]{1,0,2:T(8,128)(2,1)} %param.14) | copy-start | bytes 5050372
  6.5 74.7 %all-gather.2.cloned.1.call-start = ((), (), s32[]{:S(2)}) async-start(), calls=%async_computation | async-start | bytes 1892352 | tf_op jit(solution)/shard_map/while/body/all_gather | solution.py:54
  9.0 14.2 %collective-permute-start = (s32[3]{0:T(128)S(1)}, s32[3]{0:T(128)S(1)}, u32[]{:S(2)}, u32[]{:S(2)}) collective-permute-start(s32[3]{0:T(128)S(1)} %get-tuple-element.221), channel_id=1, source_target_pairs={{0,254},{2,0},{4,2},{6,4},{8,6},{10,8},{12,10},{14,12},{16,14},{18... | collective-permute-start | bytes 44 | tf_op jit(solution)/shard_map/ppermute | solution.py:15
  11.2 15.6 %collective-permute-start.1 = (s32[3]{0:T(128)S(1)}, s32[3]{0:T(128)S(1)}, u32[]{:S(2)}, u32[]{:S(2)}) collective-permute-start(s32[3]{0:T(128)S(1)} %get-tuple-element.220), channel_id=1, source_target_pairs={{0,2},{2,4},{4,6},{6,8},{8,10},{10,12},{12,14},{14,16},{16,18},{18... | collective-permute-start | bytes 44 | tf_op jit(solution)/shard_map/ppermute | solution.py:15
  11.2 23.6 %collective-permute-start.2 = (s32[3]{0:T(128)S(1)}, s32[3]{0:T(128)S(1)}, u32[]{:S(2)}, u32[]{:S(2)}) collective-permute-start(s32[3]{0:T(128)S(1)} %get-tuple-element.219), channel_id=1, source_target_pairs={{0,4},{2,6},{4,8},{6,10},{8,12},{10,14},{12,16},{14,18},{16,20},{1... | collective-permute-start | bytes 44 | tf_op jit(solution)/shard_map/ppermute | solution.py:15
  16.2 4.6 %copy-start.1 = (bf16[8,308]{1,0:T(8,128)(2,1)S(1)}, bf16[8,308]{1,0:T(8,128)(2,1)}, u32[]{:S(2)}) copy-start(bf16[8,308]{1,0:T(8,128)(2,1)} %param.13) | copy-start | bytes 14788
  26.8 19.4 %collective-permute-start.3 = (bf16[3,128,411]{1,0,2:T(4,128)(2,1)}, bf16[3,128,411]{1,0,2:T(4,128)(2,1)S(1)}, u32[]{:S(2)}, u32[]{:S(2)}) collective-permute-start(bf16[3,128,411]{1,0,2:T(4,128)(2,1)} %broadcast_select_fusion.3), channel_id=1, source_target_pairs={{0,2},{2,4},{4,6},{6,8},{8,10},{10,12},{12,14},{14,16},{16,18},{18... | collective-permute-start | bytes 946952 | tf_op jit(solution)/shard_map/ppermute | solution.py:15
  30.3 22.5 %collective-permute-start.4 = (bf16[3,128,411]{1,0,2:T(4,128)(2,1)}, bf16[3,128,411]{1,0,2:T(4,128)(2,1)S(1)}, u32[]{:S(2)}, u32[]{:S(2)}) collective-permute-start(bf16[3,128,411]{1,0,2:T(4,128)(2,1)} %broadcast_select_fusion.1), channel_id=1, source_target_pairs={{0,254},{2,0},{4,2},{6,4},{8,6},{10,8},{12,10},{14,12},{16,14},{18... | collective-permute-start | bytes 946952 | tf_op jit(solution)/shard_map/ppermute | solution.py:15
  37.5 19.9 %collective-permute-start.5 = (bf16[3,128,411]{1,0,2:T(4,128)(2,1)S(1)}, bf16[3,128,411]{1,0,2:T(4,128)(2,1)S(1)}, u32[]{:S(2)}, u32[]{:S(2)}) collective-permute-start(bf16[3,128,411]{1,0,2:T(4,128)(2,1)S(1)} %broadcast_select_fusion), channel_id=1, source_target_pairs={{0,252},{2,254},{4,0},{6,2},{8,4},{10,6},{12,8},{14,10},{16,12},{1... | collective-permute-start | bytes 946952 | tf_op jit(solution)/shard_map/ppermute | solution.py:15
  101.8 12.1 %collective-permute-start.6 = (bf16[3,52608]{1,0:T(4,128)(2,1)S(1)}, bf16[3,52608]{1,0:T(4,128)(2,1)S(1)}, u32[]{:S(2)}, u32[]{:S(2)}) collective-permute-start(bf16[3,52608]{1,0:T(4,128)(2,1)S(1)} %get-tuple-element.214), channel_id=1, source_target_pairs={{0,254},{2,0},{4,2},{6,4},{8,6},{10,8},{12,10},{14,12},{16,14},{18... | collective-permute-start | bytes 946952 | tf_op jit(solution)/shard_map/ppermute | solution.py:15
  102.9 17.9 %collective-permute-start.7 = (bf16[3,52608]{1,0:T(4,128)(2,1)S(1)}, bf16[3,52608]{1,0:T(4,128)(2,1)S(1)}, u32[]{:S(2)}, u32[]{:S(2)}) collective-permute-start(bf16[3,52608]{1,0:T(4,128)(2,1)S(1)} %get-tuple-element.216), channel_id=1, source_target_pairs={{0,2},{2,4},{4,6},{6,8},{8,10},{10,12},{12,14},{14,16},{16,18},{18... | collective-permute-start | bytes 946952 | tf_op jit(solution)/shard_map/ppermute | solution.py:15
  104.1 36.0 %collective-permute-start.8 = (bf16[3,52608]{1,0:T(4,128)(2,1)S(1)}, bf16[3,52608]{1,0:T(4,128)(2,1)S(1)}, u32[]{:S(2)}, u32[]{:S(2)}) collective-permute-start(bf16[3,52608]{1,0:T(4,128)(2,1)S(1)} %get-tuple-element.215), channel_id=1, source_target_pairs={{0,4},{2,6},{4,8},{6,10},{8,12},{10,14},{12,16},{14,18},{16,20},{1... | collective-permute-start | bytes 946952 | tf_op jit(solution)/shard_map/ppermute | solution.py:15
Sparse Core Ops, SparseCore 0:
  65.1 16.1 all-gather.1
where the time goes:
time: 158 us
  waiting for transfers between devices  58.7 us (37%)
  local copies, waits for them, and re-layouts  32.4 us (21%)
  starting transfers between devices  25.9 us (16%)
  between operations  14.2 us (9%)
  other arithmetic  9.06 us (6%)
  matrix products  9.01 us (6%)
  blocking collectives  8.43 us (5%)
    ppermute x9, waiting for transfers between devices, passed_along(): lax.ppermute(value, axis, [(i, (i + by) % count) for i in range(count)])  43.1 us
    ppermute x9, starting transfers between devices, passed_along(): lax.ppermute(value, axis, [(i, (i + by) % count) for i in range(count)])  25.9 us
    all_gather x1, waiting for transfers between devices, one_block(): all_channels = lax.all_gather(departure, 'chan', axis=2, tiled=True)  15.6 us
    reshape x2, local copies, waits for them, and re-layouts, on_device(): gradient = gradient.reshape(columns, members, state)  9.34 us
    psum x1, blocking collectives, one_block(): summed = lax.psum(partial_adj, 'chan')  8.43 us
    gather x3, local copies, waits for them, and re-layouts, on_device(): picked = jnp.take(increments, asked, axis=0)  7.38 us
    unnamed x5, local copies, waits for them, and re-layouts  4.56 us
    dot_general x1, matrix products, one_block(): jnp.einsum('fks,fmk->fms', jac_all, weighted, preferred_element_type=jnp....  3.6 us
  transfers between devices with their start and end apart: 10, of which 6 were waited for; matrix products, arithmetic and copies ran while one was open for 11% of the time, Pallas kernels for 0%

commit v1 on v0

v1 whole, which is shorter than its diff:
```python
import jax
import jax.numpy as jnp
from jax import lax
from jax.sharding import PartitionSpec as P

SPAN = 4
CAP = 3


def passed_along(value, axis, by):
    count = lax.axis_size(axis)
    return lax.ppermute(value, axis, [(i, (i + by) % count) for i in range(count)])


def passed_across(value, by):
    tiles = lax.axis_size("tile")
    cores = lax.axis_size("chan")
    pairs = []
    for t in range(tiles):
        for c in range(cores):
            pairs.append((t * cores + c, ((t + by) % tiles) * cores + (cores - 1 - c)))
    return lax.ppermute(value, ("tile", "chan"), pairs)


def swapped(value):
    return lax.ppermute(value, "chan", [(0, 1), (1, 0)])


def one_hot_rows(index, size):
    return (index[:, None] == jnp.arange(size, dtype=jnp.int32)[None, :]).astype(jnp.bfloat16)


def on_device(jacobian, r_inverse, innovation, increments, owner_offset, column_slot, foot_counts):
    foot = jacobian.shape[0]
    half_ch = jacobian.shape[1]
    state = jacobian.shape[2]
    columns = increments.shape[0]
    members = increments.shape[1]
    cores = lax.axis_size("chan")
    half_m = members // cores
    core = lax.axis_index("chan")
    capacity = CAP
    slots_total = SPAN * capacity

    jac_full = jnp.concatenate([jacobian, swapped(jacobian)], axis=1)
    innov_full = jnp.concatenate([innovation, swapped(innovation)], axis=1).astype(jnp.float32)
    r_rows = jnp.concatenate([r_inverse, swapped(r_inverse)], axis=0)
    r_full = jnp.roll(r_rows, -core * half_ch, axis=1)

    offset = owner_offset[:, 0]
    order = jnp.arange(foot, dtype=jnp.int32)
    earlier = (offset[:, None] == offset[None, :]) & (order[None, :] < order[:, None])
    rank = jnp.sum(earlier.astype(jnp.int32), axis=1)
    place = offset * capacity + rank
    select = (place[None, :] == jnp.arange(slots_total, dtype=jnp.int32)[:, None]).astype(jnp.bfloat16)
    request = jnp.sum(jnp.where(select > 0, column_slot[None, :], 0), axis=1)

    own_inc = lax.dynamic_slice_in_dim(increments, core * half_m, half_m, axis=1)
    own_inc = own_inc.reshape(columns, half_m * state)

    def pick(index):
        return jnp.dot(one_hot_rows(index, columns), own_inc,
                       preferred_element_type=jnp.float32).astype(jnp.bfloat16)

    fetched_parts = []
    slot_parts = []
    for g in range(SPAN):
        wanted = request[g * capacity:(g + 1) * capacity]
        if g == 1:
            fetched_parts.append(pick(wanted))
            slot_parts.append(wanted)
        else:
            asked = passed_along(wanted, "tile", g - 1)
            fetched_parts.append(passed_along(pick(asked), "tile", 1 - g))
            slot_parts.append(asked)
    fetched = jnp.concatenate(fetched_parts, axis=0)
    column_state = jnp.dot(select.T, fetched, preferred_element_type=jnp.float32).astype(jnp.bfloat16)
    column_state = column_state.reshape(foot, half_m, state)

    evolved = jnp.einsum("fks,fms->fmk", jac_full, column_state, preferred_element_type=jnp.float32)
    departure = (evolved - innov_full[:, None, :]).astype(jnp.bfloat16)
    weighted = jnp.einsum("fmk,ik->fmi", departure, r_full,
                          preferred_element_type=jnp.float32).astype(jnp.bfloat16)
    adjoint = jnp.einsum("fks,fmk->fms", jac_full, weighted, preferred_element_type=jnp.float32)
    live = jnp.arange(foot, dtype=jnp.int32) < foot_counts[0]
    adjoint = jnp.where(live[:, None, None], adjoint, 0.0).astype(jnp.bfloat16)

    packed = jnp.dot(select, adjoint.reshape(foot, half_m * state),
                     preferred_element_type=jnp.float32).astype(jnp.bfloat16)
    same_parts = []
    other_parts = []
    for g in range(SPAN):
        piece = packed[g * capacity:(g + 1) * capacity]
        if g == 1:
            same_parts.append(piece)
            other_parts.append(swapped(piece))
        else:
            same_parts.append(passed_along(piece, "tile", g - 1))
            other_parts.append(passed_across(piece, g - 1))
    got_slots = jnp.concatenate(slot_parts, axis=0)
    assign = one_hot_rows(got_slots, columns).T
    grad_same = jnp.dot(assign, jnp.concatenate(same_parts, axis=0),
                        preferred_element_type=jnp.float32).astype(jnp.bfloat16)
    grad_other = jnp.dot(assign, jnp.concatenate(other_parts, axis=0),
                         preferred_element_type=jnp.float32).astype(jnp.bfloat16)
    low = jnp.where(core == 0, grad_same, grad_other).reshape(columns, half_m, state)
    high = jnp.where(core == 0, grad_other, grad_same).reshape(columns, half_m, state)
    return jnp.concatenate([low, high], axis=1)


def solution(mesh):
    in_specs = (
        P("tile", "chan", None),
        P("chan", None),
        P("tile", "chan"),
        P("tile", None, None),
        P("tile", None),
        P("tile"),
        P("tile"),
    )
    out_specs = P("tile", None, None)
    return jax.shard_map(
        on_device, mesh=mesh, in_specs=in_specs, out_specs=out_specs, check_vma=False
    )
```

time: 158 us -> 113 us (0.72)
  the two profiles are of different devices: /device:TPU:8 before, /device:TPU:9 now
where the time goes in v1:
time: 113 us
  starting transfers between devices  30.3 us (27%)
  local copies, waits for them, and re-layouts  29.7 us (26%)
  waiting for transfers between devices  28.5 us (25%)
  matrix products  17.5 us (15%)
  other arithmetic  6.01 us (5%)
    ppermute x9, starting transfers between devices, passed_along(): lax.ppermute(value, axis, [(i, (i + by) % count) for i in range(count)])  24.2 us
    ppermute x3, waiting for transfers between devices, passed_across(): return lax.ppermute(value, ('tile', 'chan'), pairs)  19 us
    ppermute x9, waiting for transfers between devices, passed_along(): lax.ppermute(value, axis, [(i, (i + by) % count) for i in range(count)])  9.48 us
    reshape x2, local copies, waits for them, and re-layouts, on_device(): jnp.where(core == 0, grad_other, grad_same).reshape(columns, half_m, state)  7.41 us
    dot_general x1, matrix products, on_device(): jnp.einsum('fks,fmk->fms', jac_full, weighted, preferred_element_type=jnp...  6.5 us
    reshape x2, local copies, waits for them, and re-layouts, on_device(): jnp.where(core == 0, grad_same, grad_other).reshape(columns, half_m, state)  5.76 us
    ppermute x1, local copies, waits for them, and re-layouts, swapped(): return lax.ppermute(value, 'chan', [(0, 1), (1, 0)])  4.56 us
    unnamed x5, local copies, waits for them, and re-layouts  4.54 us
  transfers between devices with their start and end apart: 16, of which 4 were waited for; matrix products, arithmetic and copies ran while one was open for 24% of the time, Pallas kernels for 0%

profile of v1, /device:TPU:9, one launch (start us, length us, event | category | flops | bytes accessed | tf_op | source)
XLA Modules:
  0.0 112.9 jit_solution(8875598355421510329)
XLA Ops:
  0.0 0.7 collective-permute-start.6
  0.7 0.9 convert_reduce_fusion
  1.6 0.7 multiply_add_fusion
  2.3 0.7 select_reduce_fusion
  3.0 0.1 fusion.54
  3.1 1.9 %collective-permute-start = (s32[3]{0:T(128)S(1)}, s32[3]{0:T(128)S(1)}, u32[]{:S(2)}, u32[]{:S(2)}) collective-permute-start(s32[3]{0:T(128)S(1)} %get-tuple-element.11), channel_id=1, source_target_pairs={{0,254},{2,0},{4,2},{6,4},{8,6},{10,8},{12,10},{14,12},{16,14},{18... | collective-permute-start | bytes 44 | tf_op jit(solution)/shard_map/ppermute | solution.py:12
  5.0 3.7 %collective-permute-start.2 = (s32[3]{0:T(128)S(1)}, s32[3]{0:T(128)S(1)}, u32[]{:S(2)}, u32[]{:S(2)}) collective-permute-start(s32[3]{0:T(128)S(1)} %get-tuple-element.12), channel_id=1, source_target_pairs={{0,4},{2,6},{4,8},{6,10},{8,12},{10,14},{12,16},{14,18},{16,20},{1... | collective-permute-start | bytes 44 | tf_op jit(solution)/shard_map/ppermute | solution.py:12
  8.7 0.9 collective-permute-start.7
  9.6 0.5 constant_dynamic-slice_fusion
  10.1 2.1 %copy.22 = bf16[16,64,411]{2,1,0:T(8,128)(2,1)} copy(bf16[16,64,411]{1,0,2:T(8,128)(2,1)S(1)} %constant_dynamic-slice_fusion) | data formatting | bytes 1683456 | tf_op jit(solution)/shard_map/dynamic_slice | solution.py:58
  12.2 2.7 %reshape.49 = bf16[16,26304]{1,0:T(8,128)(2,1)S(1)} reshape(bf16[16,64,411]{2,1,0:T(8,128)(2,1)} %copy.22) | data formatting | bytes 1683456 | tf_op jit(solution)/shard_map/reshape | solution.py:59
  15.6 0.3 convolution_convert_fusion.6
  15.9 0.0 collective-permute-done
  15.9 0.3 convolution_convert_fusion.7
  16.3 0.1 collective-permute-start.3
  16.4 0.3 convolution_convert_fusion.5
  16.7 5.0 %collective-permute-start.4 = (bf16[3,26304]{1,0:T(4,128)(2,1)S(1)}, bf16[3,26304]{1,0:T(4,128)(2,1)}, u32[]{:S(2)}, u32[]{:S(2)}) collective-permute-start(bf16[3,26304]{1,0:T(4,128)(2,1)S(1)} %convolution_convert_fusion.5), channel_id=1, source_target_pairs={{0,254},{2,0},{4,2},{6,4},{8,6},{10,8},{12,10},{14,12},{16,14},{18... | collective-permute-start | bytes 473480 | tf_op jit(solution)/shard_map/ppermute | solution.py:12
  21.7 0.0 collective-permute-done.2
  21.7 0.3 convolution_convert_fusion.4
  22.1 7.1 %collective-permute-start.5 = (bf16[3,26304]{1,0:T(4,128)(2,1)S(1)}, bf16[3,26304]{1,0:T(4,128)(2,1)S(1)}, u32[]{:S(2)}, u32[]{:S(2)}) collective-permute-start(bf16[3,26304]{1,0:T(4,128)(2,1)S(1)} %convolution_convert_fusion.4), channel_id=1, source_target_pairs={{0,252},{2,254},{4,0},{6,2},{8,4},{10,6},{12,8},{14,10},{16,12},{1... | collective-permute-start | bytes 473480 | tf_op jit(solution)/shard_map/ppermute | solution.py:12
  29.2 4.5 %copy.23 = bf16[8,308,411]{1,2,0:T(8,128)(2,1)} copy(bf16[8,308,411]{2,0,1:T(8,128)(2,1)} %param.7) | data formatting | bytes 4050816 | tf_op args[0]
  33.7 0.8 collective-permute-start.8
  34.6 0.1 maximum_convert_fusion
  34.6 0.0 collective-permute-done.3
  34.6 1.8 %convolution_convert_fusion.3 = bf16[8,26304]{1,0:T(8,128)(2,1)S(1)} fusion(bf16[3,26304]{1,0:T(4,128)(2,1)S(1)} %collective-permute-done.5, bf16[3,26304]{1,0:T(4,128)(2,1)} %collective-permute-done.4, bf16[3,26304]{1,0:T(4,128)(2,1)S(1)} %convolution_convert_fusion.6, bf16[3,26304]{1,0:T(4,128)(2,1)} %collective-permute-done.3, s32[8]{0:T(128)S(1)} %multiply_add_fusion), kind=kOutput, calls=%fused_computation.3 | convolution fusion | flops 7786080 | bytes 1052192 | tf_op jit(solution)/shard_map/dot_general | solution.py:77
  36.4 1.0 reshape.50
  37.5 4.6 %copy.24 = bf16[8,308,411]{1,2,0:T(8,128)(2,1)} copy(bf16[8,308,411]{2,0,1:T(8,128)(2,1)} %collective-permute-done.6) | data formatting | bytes 4050816 | tf_op jit(solution)/shard_map/ppermute | solution.py:26
  42.0 3.9 %fusion.3 = bf16[8,64,616]{2,1,0:T(8,128)(2,1)S(1)} fusion(bf16[8,64,411]{2,1,0:T(8,128)(2,1)S(1)} %reshape.50, bf16[8,308,411]{1,2,0:T(8,128)(2,1)} %copy.24, bf16[8,308,411]{1,2,0:T(8,128)(2,1)} %copy.23, f32[8,616]{1,0:T(8,128)S(1)} %maximum_convert_fusion), kind=kOutput, calls=%fused_computation.17 | convolution fusion | flops 267984640 | bytes 5122176 | tf_op jit(solution)/shard_map/fks,fms->fmk/dot_general | solution.py:80
  45.9 6.5 %fusion.5 = bf16[8,64,411]{2,1,0:T(8,128)(2,1)S(1)} fusion(bf16[8,308,411]{1,2,0:T(8,128)(2,1)} %copy.24, bf16[8,308,411]{1,2,0:T(8,128)(2,1)} %copy.23, bf16[8,64,616]{2,1,0:T(8,128)(2,1)S(1)} %fusion.3, s32[]{:T(128)S(6)} %select_n.40, bf16[308,616]{1,0:T(8,128)(2,1)} %param.8, bf16[308,616]{1,0:T(8,128)(2,1)} %collective-permute-done.8, ...), kind=kOutput, calls=%fused_computation.20 | convolution fusion | flops 659688704 | bytes 5861388 | tf_op jit(solution)/shard_map/fks,fmk->fms/dot_general | solution.py:84
  52.4 0.7 reshape.51
  53.1 0.5 convolution_convert_fusion.2
  53.6 0.3 fusion.53
  53.9 3.7 %collective-permute-start.12 = (bf16[3,26304]{1,0:T(4,128)(2,1)S(1)}, bf16[3,26304]{1,0:T(4,128)(2,1)S(1)}, u32[]{:S(2)}, u32[]{:S(2)}) collective-permute-start(bf16[3,26304]{1,0:T(4,128)(2,1)S(1)} %get-tuple-element.7), channel_id=1, source_target_pairs={{0,255},{1,254},{2,1},{3,0},{4,3},{5,2},{6,5},{7,4},{8,7},{9,6},{1... | collective-permute-start | bytes 473480 | tf_op jit(solution)/shard_map/ppermute | solution.py:22
  57.6 0.1 pad_add_fusion
  57.7 0.0 collective-permute-start.10
  57.7 4.9 %collective-permute-done.12 = bf16[3,26304]{1,0:T(4,128)(2,1)S(1)} collective-permute-done((bf16[3,26304]{1,0:T(4,128)(2,1)S(1)}, bf16[3,26304]{1,0:T(4,128)(2,1)S(1)}, u32[]{:S(2)}, u32[]{:S(2)}) %collective-permute-start.12) | collective-permute-done | bytes 157856 | tf_op jit(solution)/shard_map/ppermute | solution.py:22
  62.6 0.0 collective-permute-start.11
  62.6 6.4 %collective-permute-start.9 = (bf16[3,26304]{1,0:T(4,128)(2,1)S(1)}, bf16[3,26304]{1,0:T(4,128)(2,1)S(1)}, u32[]{:S(2)}, u32[]{:S(2)}) collective-permute-start(bf16[3,26304]{1,0:T(4,128)(2,1)S(1)} %get-tuple-element.7), channel_id=1, source_target_pairs={{0,254},{2,0},{4,2},{6,4},{8,6},{10,8},{12,10},{14,12},{16,14},{18... | collective-permute-start | bytes 473480 | tf_op jit(solution)/shard_map/ppermute | solution.py:12
  69.0 2.1 %collective-permute-done.14 = bf16[3,26304]{1,0:T(4,128)(2,1)S(1)} collective-permute-done((bf16[3,26304]{1,0:T(4,128)(2,1)S(1)}, bf16[3,26304]{1,0:T(4,128)(2,1)S(1)}, u32[]{:S(2)}, u32[]{:S(2)}) %collective-permute-start.14) | collective-permute-done | bytes 157856 | tf_op jit(solution)/shard_map/ppermute | solution.py:22
  71.1 12.0 %collective-permute-done.15 = bf16[3,26304]{1,0:T(4,128)(2,1)} collective-permute-done((bf16[3,26304]{1,0:T(4,128)(2,1)S(1)}, bf16[3,26304]{1,0:T(4,128)(2,1)}, u32[]{:S(2)}, u32[]{:S(2)}) %collective-permute-start.15) | collective-permute-done | bytes 157856 | tf_op jit(solution)/shard_map/ppermute | solution.py:22
  83.1 1.8 %convolution_convert_fusion = bf16[16,26304]{1,0:T(8,128)(2,1)S(1)} fusion(bf16[3,26304]{1,0:T(4,128)(2,1)} %collective-permute-done.15, bf16[3,26304]{1,0:T(4,128)(2,1)S(1)} %collective-permute-done.14, bf16[3,26304]{1,0:T(4,128)(2,1)S(1)} %collective-permute-done.13, bf16[3,26304]{1,0:T(4,128)(2,1)S(1)} %collective-permute-done.12, s32[12]{0:T(128)S(1)} %pad_add_fusion), kind=kOutput, calls=%fused_computation | convolution fusion | flops 13046976 | bytes 1473072 | tf_op jit(solution)/shard_map/dot_general | solution.py:104
  84.9 9.5 %collective-permute-done.11 = bf16[3,26304]{1,0:T(4,128)(2,1)S(1)} collective-permute-done((bf16[3,26304]{1,0:T(4,128)(2,1)S(1)}, bf16[3,26304]{1,0:T(4,128)(2,1)S(1)}, u32[]{:S(2)}, u32[]{:S(2)}) %collective-permute-start.11) | collective-permute-done | bytes 157856 | tf_op jit(solution)/shard_map/ppermute | solution.py:12
  94.4 1.8 %broadcast_select_fusion.1 = (bf16[16,26304]{1,0:T(8,128)(2,1)S(1)}, bf16[16,26304]{1,0:T(8,128)(2,1)}) fusion(bf16[16,26304]{1,0:T(8,128)(2,1)S(1)} %convolution_convert_fusion, pred[]{:T(512)S(6)} %eq.47, bf16[3,26304]{1,0:T(4,128)(2,1)S(1)} %collective-permute-done.11, bf16[3,26304]{1,0:T(4,128)(2,1)S(1)} %collective-permute-done.10, ...), kind=kOutput, calls=%fused_computation.43 | convolution fusion | flops 13888704 | bytes 3156529 | tf_op jit(solution)/shard_map/dot_general | solution.py:102
  96.2 3.2 %reshape.52 = bf16[16,64,411]{2,1,0:T(8,128)(2,1)} reshape(bf16[16,26304]{1,0:T(8,128)(2,1)S(1)} %get-tuple-element.5) | data formatting | bytes 1683456 | tf_op jit(solution)/shard_map/reshape | solution.py:106
  99.4 2.5 %copy.25 = bf16[16,64,411]{1,0,2:T(8,128)(2,1)S(1)} copy(bf16[16,64,411]{2,1,0:T(8,128)(2,1)} %reshape.52) | data formatting | bytes 1683456 | tf_op jit(solution)/shard_map/reshape | solution.py:106
  101.9 4.2 %reshape.53 = bf16[16,64,411]{2,1,0:T(8,128)(2,1)} reshape(bf16[16,26304]{1,0:T(8,128)(2,1)} %get-tuple-element.6) | data formatting | bytes 1683456 | tf_op jit(solution)/shard_map/reshape | solution.py:107
  106.1 3.2 %copy.26 = bf16[16,64,411]{1,0,2:T(8,128)(2,1)} copy(bf16[16,64,411]{2,1,0:T(8,128)(2,1)} %reshape.53) | data formatting | bytes 1683456 | tf_op jit(solution)/shard_map/reshape | solution.py:107
  109.4 3.5 %pad_maximum_fusion.3 = bf16[16,128,411]{1,0,2:T(8,128)(2,1)} fusion(bf16[16,64,411]{1,0,2:T(8,128)(2,1)} %copy.26, bf16[16,64,411]{1,0,2:T(8,128)(2,1)S(1)} %copy.25), kind=kLoop, calls=%fused_computation.11 | loop fusion | flops 3366912 | bytes 3366912 | tf_op jit(solution)/shard_map/concatenate | solution.py:108
  (18 shorter events, 0.0 us)
Async XLA Ops:
  0.0 9.6 %copy-start = (bf16[16,128,411]{1,0,2:T(8,128)(2,1)S(1)}, bf16[16,128,411]{1,0,2:T(8,128)(2,1)}, u32[]{:S(2)}) copy-start(bf16[16,128,411]{1,0,2:T(8,128)(2,1)} %param.10) | copy-start | bytes 5050372
  0.0 37.4 %collective-permute-start.6 = (bf16[8,308,411]{2,0,1:T(8,128)(2,1)}, bf16[8,308,411]{2,0,1:T(8,128)(2,1)}, u32[]{:S(2)}, u32[]{:S(2)}) collective-permute-start(bf16[8,308,411]{2,0,1:T(8,128)(2,1)} %param.7), channel_id=1, source_target_pairs={{0,1},{1,0},{2,3},{3,2},{4,5},{5,4},{6,7},{7,6},{8,9},{9,8},{10,11... | collective-permute-start | bytes 6076232 | tf_op jit(solution)/shard_map/ppermute | solution.py:26
  3.1 12.9 %collective-permute-start = (s32[3]{0:T(128)S(1)}, s32[3]{0:T(128)S(1)}, u32[]{:S(2)}, u32[]{:S(2)}) collective-permute-start(s32[3]{0:T(128)S(1)} %get-tuple-element.11), channel_id=1, source_target_pairs={{0,254},{2,0},{4,2},{6,4},{8,6},{10,8},{12,10},{14,12},{16,14},{18... | collective-permute-start | bytes 44 | tf_op jit(solution)/shard_map/ppermute | solution.py:12
  5.0 11.4 %collective-permute-start.1 = (s32[3]{0:T(128)S(1)}, s32[3]{0:T(128)S(1)}, u32[]{:S(2)}, u32[]{:S(2)}) collective-permute-start(s32[3]{0:T(128)S(1)} %get-tuple-element.13), channel_id=1, source_target_pairs={{0,2},{2,4},{4,6},{6,8},{8,10},{10,12},{12,14},{14,16},{16,18},{18... | collective-permute-start | bytes 44 | tf_op jit(solution)/shard_map/ppermute | solution.py:12
  5.0 16.8 %collective-permute-start.2 = (s32[3]{0:T(128)S(1)}, s32[3]{0:T(128)S(1)}, u32[]{:S(2)}, u32[]{:S(2)}) collective-permute-start(s32[3]{0:T(128)S(1)} %get-tuple-element.12), channel_id=1, source_target_pairs={{0,4},{2,6},{4,8},{6,10},{8,12},{10,14},{12,16},{14,18},{16,20},{1... | collective-permute-start | bytes 44 | tf_op jit(solution)/shard_map/ppermute | solution.py:12
  8.7 25.0 %collective-permute-start.7 = (bf16[8,308]{1,0:T(8,128)(2,1)}, bf16[8,308]{1,0:T(8,128)(2,1)S(1)}, u32[]{:S(2)}, u32[]{:S(2)}) collective-permute-start(bf16[8,308]{1,0:T(8,128)(2,1)} %param.9), channel_id=1, source_target_pairs={{0,1},{1,0},{2,3},{3,2},{4,5},{5,4},{6,7},{7,6},{8,9},{9,8},{10,11... | collective-permute-start | bytes 14792 | tf_op jit(solution)/shard_map/ppermute | solution.py:26
  16.3 18.4 %collective-permute-start.3 = (bf16[3,26304]{1,0:T(4,128)(2,1)S(1)}, bf16[3,26304]{1,0:T(4,128)(2,1)}, u32[]{:S(2)}, u32[]{:S(2)}) collective-permute-start(bf16[3,26304]{1,0:T(4,128)(2,1)S(1)} %convolution_convert_fusion.7), channel_id=1, source_target_pairs={{0,2},{2,4},{4,6},{6,8},{8,10},{10,12},{12,14},{14,16},{16,18},{18... | collective-permute-start | bytes 473480 | tf_op jit(solution)/shard_map/ppermute | solution.py:12
  16.7 17.9 %collective-permute-start.4 = (bf16[3,26304]{1,0:T(4,128)(2,1)S(1)}, bf16[3,26304]{1,0:T(4,128)(2,1)}, u32[]{:S(2)}, u32[]{:S(2)}) collective-permute-start(bf16[3,26304]{1,0:T(4,128)(2,1)S(1)} %convolution_convert_fusion.5), channel_id=1, source_target_pairs={{0,254},{2,0},{4,2},{6,4},{8,6},{10,8},{12,10},{14,12},{16,14},{18... | collective-permute-start | bytes 473480 | tf_op jit(solution)/shard_map/ppermute | solution.py:12
  22.1 12.6 %collective-permute-start.5 = (bf16[3,26304]{1,0:T(4,128)(2,1)S(1)}, bf16[3,26304]{1,0:T(4,128)(2,1)S(1)}, u32[]{:S(2)}, u32[]{:S(2)}) collective-permute-start(bf16[3,26304]{1,0:T(4,128)(2,1)S(1)} %convolution_convert_fusion.4), channel_id=1, source_target_pairs={{0,252},{2,254},{4,0},{6,2},{8,4},{10,6},{12,8},{14,10},{16,12},{1... | collective-permute-start | bytes 473480 | tf_op jit(solution)/shard_map/ppermute | solution.py:12
  29.2 5.4 %copy-start.1 = (bf16[8,308]{1,0:T(8,128)(2,1)S(1)}, bf16[8,308]{1,0:T(8,128)(2,1)}, u32[]{:S(2)}) copy-start(bf16[8,308]{1,0:T(8,128)(2,1)} %param.9) | copy-start | bytes 14788
  33.7 12.2 %collective-permute-start.8 = (bf16[308,616]{1,0:T(8,128)(2,1)}, bf16[308,616]{1,0:T(8,128)(2,1)}, u32[]{:S(2)}, u32[]{:S(2)}) collective-permute-start(bf16[308,616]{1,0:T(8,128)(2,1)} %param.8), channel_id=1, source_target_pairs={{0,1},{1,0},{2,3},{3,2},{4,5},{5,4},{6,7},{7,6},{8,9},{9,8},{10,11... | collective-permute-start | bytes 1138376 | tf_op jit(solution)/shard_map/ppermute | solution.py:26
  53.9 8.7 %collective-permute-start.12 = (bf16[3,26304]{1,0:T(4,128)(2,1)S(1)}, bf16[3,26304]{1,0:T(4,128)(2,1)S(1)}, u32[]{:S(2)}, u32[]{:S(2)}) collective-permute-start(bf16[3,26304]{1,0:T(4,128)(2,1)S(1)} %get-tuple-element.7), channel_id=1, source_target_pairs={{0,255},{1,254},{2,1},{3,0},{4,3},{5,2},{6,5},{7,4},{8,7},{9,6},{1... | collective-permute-start | bytes 473480 | tf_op jit(solution)/shard_map/ppermute | solution.py:22
  57.6 5.0 %collective-permute-start.13 = (bf16[3,26304]{1,0:T(4,128)(2,1)S(1)}, bf16[3,26304]{1,0:T(4,128)(2,1)S(1)}, u32[]{:S(2)}, u32[]{:S(2)}) collective-permute-start(bf16[3,26304]{1,0:T(4,128)(2,1)S(1)} %get-tuple-element.10), channel_id=1, source_target_pairs={{0,1},{1,0},{2,3},{3,2},{4,5},{5,4},{6,7},{7,6},{8,9},{9,8},{10,11... | collective-permute-start | bytes 473480 | tf_op jit(solution)/shard_map/ppermute | solution.py:26
  57.6 13.5 %collective-permute-start.14 = (bf16[3,26304]{1,0:T(4,128)(2,1)S(1)}, bf16[3,26304]{1,0:T(4,128)(2,1)S(1)}, u32[]{:S(2)}, u32[]{:S(2)}) collective-permute-start(bf16[3,26304]{1,0:T(4,128)(2,1)S(1)} %get-tuple-element.9), channel_id=1, source_target_pairs={{0,3},{1,2},{2,5},{3,4},{4,7},{5,6},{6,9},{7,8},{8,11},{9,10},{10,... | collective-permute-start | bytes 473480 | tf_op jit(solution)/shard_map/ppermute | solution.py:22
  57.6 25.5 %collective-permute-start.15 = (bf16[3,26304]{1,0:T(4,128)(2,1)S(1)}, bf16[3,26304]{1,0:T(4,128)(2,1)}, u32[]{:S(2)}, u32[]{:S(2)}) collective-permute-start(bf16[3,26304]{1,0:T(4,128)(2,1)S(1)} %get-tuple-element.8), channel_id=1, source_target_pairs={{0,5},{1,4},{2,7},{3,6},{4,9},{5,8},{6,11},{7,10},{8,13},{9,12},{1... | collective-permute-start | bytes 473480 | tf_op jit(solution)/shard_map/ppermute | solution.py:22
  57.7 27.2 %collective-permute-start.10 = (bf16[3,26304]{1,0:T(4,128)(2,1)S(1)}, bf16[3,26304]{1,0:T(4,128)(2,1)S(1)}, u32[]{:S(2)}, u32[]{:S(2)}) collective-permute-start(bf16[3,26304]{1,0:T(4,128)(2,1)S(1)} %get-tuple-element.9), channel_id=1, source_target_pairs={{0,2},{2,4},{4,6},{6,8},{8,10},{10,12},{12,14},{14,16},{16,18},{18... | collective-permute-start | bytes 473480 | tf_op jit(solution)/shard_map/ppermute | solution.py:12
  62.6 31.8 %collective-permute-start.11 = (bf16[3,26304]{1,0:T(4,128)(2,1)S(1)}, bf16[3,26304]{1,0:T(4,128)(2,1)S(1)}, u32[]{:S(2)}, u32[]{:S(2)}) collective-permute-start(bf16[3,26304]{1,0:T(4,128)(2,1)S(1)} %get-tuple-element.8), channel_id=1, source_target_pairs={{0,4},{2,6},{4,8},{6,10},{8,12},{10,14},{12,16},{14,18},{16,20},{1... | collective-permute-start | bytes 473480 | tf_op jit(solution)/shard_map/ppermute | solution.py:12
  62.6 31.7 %collective-permute-start.9 = (bf16[3,26304]{1,0:T(4,128)(2,1)S(1)}, bf16[3,26304]{1,0:T(4,128)(2,1)S(1)}, u32[]{:S(2)}, u32[]{:S(2)}) collective-permute-start(bf16[3,26304]{1,0:T(4,128)(2,1)S(1)} %get-tuple-element.7), channel_id=1, source_target_pairs={{0,254},{2,0},{4,2},{6,4},{8,6},{10,8},{12,10},{14,12},{16,14},{18... | collective-permute-start | bytes 473480 | tf_op jit(solution)/shard_map/ppermute | solution.py:12

commit v2 on v1

v2 whole, which is shorter than its diff:
```python
import jax
import jax.numpy as jnp
from jax import lax
from jax.experimental import pallas as pl
from jax.experimental.pallas import tpu as pltpu
from jax.sharding import PartitionSpec as P

SPAN = 4
CAP = 3

NT = (((1,), (1,)), ((), ()))


def passed_along(value, axis, by):
    count = lax.axis_size(axis)
    return lax.ppermute(value, axis, [(i, (i + by) % count) for i in range(count)])


def swapped(value):
    return lax.ppermute(value, "chan", [(0, 1), (1, 0)])


def one_hot(index, size):
    return (index[:, None] == jnp.arange(size, dtype=jnp.int32)[None, :]).astype(jnp.bfloat16)


def adjoint_kernel(place_ref, count_ref, state_ref, jc_ref, jo_ref, ic_ref, io_ref,
                   rcc_ref, rco_ref, roc_ref, roo_ref, out_ref):
    f = pl.program_id(0)
    s = state_ref[0]
    jc = jc_ref[0]
    jo = jo_ref[0]
    ev_c = lax.dot_general(s, jc, NT, preferred_element_type=jnp.float32)
    ev_o = lax.dot_general(s, jo, NT, preferred_element_type=jnp.float32)
    dep_c = (ev_c - ic_ref[pl.ds(f, 1), :]).astype(jnp.bfloat16)
    dep_o = (ev_o - io_ref[pl.ds(f, 1), :]).astype(jnp.bfloat16)
    w_c = (jnp.dot(dep_c, rcc_ref[...], preferred_element_type=jnp.float32)
           + jnp.dot(dep_o, roc_ref[...], preferred_element_type=jnp.float32)).astype(jnp.bfloat16)
    w_o = (jnp.dot(dep_c, rco_ref[...], preferred_element_type=jnp.float32)
           + jnp.dot(dep_o, roo_ref[...], preferred_element_type=jnp.float32)).astype(jnp.bfloat16)
    adj = (jnp.dot(w_c, jc, preferred_element_type=jnp.float32)
           + jnp.dot(w_o, jo, preferred_element_type=jnp.float32))
    live = f < count_ref[0]
    out_ref[0] = jnp.where(live, adj, 0.0).astype(out_ref.dtype)


def adjoints(place, count, fetched, jac_c, jac_o, innov_c, innov_o, r_blocks):
    foot, half_ch, state = jac_c.shape
    half_m = fetched.shape[1]
    full = lambda f, p, n: (0, 0)
    grid_spec = pltpu.PrefetchScalarGridSpec(
        num_scalar_prefetch=2,
        grid=(foot,),
        in_specs=[
            pl.BlockSpec((1, half_m, state), lambda f, p, n: (p[f], 0, 0)),
            pl.BlockSpec((1, half_ch, state), lambda f, p, n: (f, 0, 0)),
            pl.BlockSpec((1, half_ch, state), lambda f, p, n: (f, 0, 0)),
            pl.BlockSpec((foot, half_ch), full),
            pl.BlockSpec((foot, half_ch), full),
        ] + [pl.BlockSpec((half_ch, half_ch), full) for _ in range(4)],
        out_specs=pl.BlockSpec((1, half_m, state), lambda f, p, n: (f, 0, 0)),
    )
    return pl.pallas_call(
        adjoint_kernel,
        grid_spec=grid_spec,
        out_shape=jax.ShapeDtypeStruct((foot, half_m, state), jnp.bfloat16),
    )(place, count, fetched, jac_c, jac_o, innov_c, innov_o, *r_blocks)


def on_device(jacobian, r_inverse, innovation, increments, owner_offset, column_slot, foot_counts):
    foot = jacobian.shape[0]
    half_ch = jacobian.shape[1]
    columns = increments.shape[0]
    members = increments.shape[1]
    cores = lax.axis_size("chan")
    half_m = members // cores
    core = lax.axis_index("chan")
    capacity = CAP
    slots_total = SPAN * capacity

    jac_o = swapped(jacobian)
    innov_c = innovation.astype(jnp.float32)
    innov_o = swapped(innovation).astype(jnp.float32)
    r_o = swapped(r_inverse)
    own_cols = core * half_ch
    other_cols = (1 - core) * half_ch
    r_blocks = (
        lax.dynamic_slice_in_dim(r_inverse, own_cols, half_ch, axis=1),
        lax.dynamic_slice_in_dim(r_inverse, other_cols, half_ch, axis=1),
        lax.dynamic_slice_in_dim(r_o, own_cols, half_ch, axis=1),
        lax.dynamic_slice_in_dim(r_o, other_cols, half_ch, axis=1),
    )

    offset = owner_offset[:, 0]
    order = jnp.arange(foot, dtype=jnp.int32)
    earlier = (offset[:, None] == offset[None, :]) & (order[None, :] < order[:, None])
    rank = jnp.sum(earlier.astype(jnp.int32), axis=1)
    place = offset * capacity + rank
    hit = place[None, :] == jnp.arange(slots_total, dtype=jnp.int32)[:, None]
    request = jnp.sum(jnp.where(hit, column_slot[None, :], 0), axis=1)

    own_inc = lax.dynamic_slice_in_dim(increments, core * half_m, half_m, axis=1)

    def pick(index):
        return jnp.einsum("ac,cms->ams", one_hot(index, columns), own_inc,
                          preferred_element_type=jnp.float32).astype(jnp.bfloat16)

    fetched_parts = []
    slot_parts = []
    for g in range(SPAN):
        wanted = request[g * capacity:(g + 1) * capacity]
        if g == 1:
            fetched_parts.append(pick(wanted))
            slot_parts.append(wanted)
        else:
            asked = passed_along(wanted, "tile", g - 1)
            fetched_parts.append(passed_along(pick(asked), "tile", 1 - g))
            slot_parts.append(asked)
    fetched = jnp.concatenate(fetched_parts, axis=0)

    adjoint = adjoints(place, foot_counts, fetched, jacobian, jac_o, innov_c, innov_o, r_blocks)

    packed = jnp.einsum("af,fmd->amd", hit.astype(jnp.bfloat16), adjoint,
                        preferred_element_type=jnp.float32).astype(jnp.bfloat16)
    recv_parts = []
    for g in range(SPAN):
        piece = packed[g * capacity:(g + 1) * capacity]
        if g == 1:
            recv_parts.append(piece)
        else:
            recv_parts.append(passed_along(piece, "tile", g - 1))
    got_slots = jnp.concatenate(slot_parts, axis=0)
    mine = jnp.einsum("ac,amd->cmd", one_hot(got_slots, columns), jnp.concatenate(recv_parts, axis=0),
                      preferred_element_type=jnp.float32).astype(jnp.bfloat16)
    other = swapped(mine)
    return jnp.where(core == 0, jnp.concatenate([mine, other], axis=1),
                     jnp.concatenate([other, mine], axis=1))


def solution(mesh):
    in_specs = (
        P("tile", "chan", None),
        P("chan", None),
        P("tile", "chan"),
        P("tile", None, None),
        P("tile", None),
        P("tile"),
        P("tile"),
    )
    out_specs = P("tile", None, None)
    return jax.shard_map(
        on_device, mesh=mesh, in_specs=in_specs, out_specs=out_specs, check_vma=False
    )
```

time: 113 us -> 100 us (0.88)
  the two profiles are of different devices: /device:TPU:9 before, /device:TPU:1 now
where the time goes in v2:
time: 100 us; the launch traced here: 99.8 us
  starting transfers between devices  26.4 us (26%)
  waiting for transfers between devices  25.1 us (25%)
  local copies, waits for them, and re-layouts  23.9 us (24%)
  Pallas kernels  10.5 us (10%)
  other arithmetic  9.16 us (9%)
  matrix products  3.97 us (4%)
    ppermute x9, waiting for transfers between devices, passed_along(): lax.ppermute(value, axis, [(i, (i + by) % count) for i in range(count)])  22.7 us
    ppermute x9, starting transfers between devices, passed_along(): lax.ppermute(value, axis, [(i, (i + by) % count) for i in range(count)])  17.5 us
    pallas_call x1, Pallas kernels, adjoints(): pl.pallas_call(adjoint_kernel, grid_spec=grid_spec, out_shape=jax.ShapeDt...  10.5 us
    ppermute x4, starting transfers between devices, swapped(): return lax.ppermute(value, 'chan', [(0, 1), (1, 0)])  8.97 us
    unnamed x12, local copies, waits for them, and re-layouts  7.41 us
    select_n x1, local copies, waits for them, and re-layouts, on_device(): jnp.where(core == 0, jnp.concatenate([mine, other], axis=1), jnp.concaten...  4.94 us
    ppermute x1, local copies, waits for them, and re-layouts, swapped(): return lax.ppermute(value, 'chan', [(0, 1), (1, 0)])  4.04 us
    select_n x1, other arithmetic, on_device(): jnp.where(core == 0, jnp.concatenate([mine, other], axis=1), jnp.concaten...  3.46 us
  transfers between devices with their start and end apart: 13, of which 6 were waited for; matrix products, arithmetic and copies ran while one was open for 22% of the time, Pallas kernels for 0%

profile of v2, /device:TPU:1, one launch (start us, length us, event | category | flops | bytes accessed | tf_op | source)
XLA Modules:
  0.0 99.8 jit_solution(16564004743914809389)
XLA Ops:
  0.0 3.2 %collective-permute-start.6 = (bf16[8,308,411]{2,0,1:T(8,128)(2,1)}, bf16[8,308,411]{2,0,1:T(8,128)(2,1)}, u32[]{:S(2)}, u32[]{:S(2)}) collective-permute-start(bf16[8,308,411]{2,0,1:T(8,128)(2,1)} %param.7), channel_id=1, source_target_pairs={{0,1},{1,0},{2,3},{3,2},{4,5},{5,4},{6,7},{7,6},{8,9},{9,8},{10,11... | collective-permute-start | bytes 6076232 | tf_op jit(solution)/shard_map/ppermute | solution.py:20
  3.2 0.9 convert_reduce_fusion
  4.1 0.7 multiply_add_fusion.place_ref
  4.8 0.7 select_reduce_fusion
  5.5 0.1 fusion.33
  5.6 8.5 %collective-permute-start = (s32[3]{0:T(128)S(1)}, s32[3]{0:T(128)S(1)}, u32[]{:S(2)}, u32[]{:S(2)}) collective-permute-start(s32[3]{0:T(128)S(1)} %get-tuple-element.13), channel_id=1, source_target_pairs={{0,254},{2,0},{4,2},{6,4},{8,6},{10,8},{12,10},{14,12},{16,14},{18... | collective-permute-start | bytes 44 | tf_op jit(solution)/shard_map/ppermute | solution.py:16
  14.1 0.0 collective-permute-start.1
  14.1 0.4 collective-permute-start.7
  14.5 1.7 %constant_dynamic-slice_fusion.4 = bf16[16,64,411]{1,0,2:T(8,128)(2,1)} fusion(bf16[16,128,411]{1,0,2:T(8,128)(2,1)S(1)} %copy-done, s32[]{:T(128)S(6)} %select_n.25), kind=kLoop, calls=%fused_computation.42 | loop fusion | bytes 1683460 | tf_op jit(solution)/shard_map/dynamic_slice | solution.py:102
  16.2 3.3 %copy.25 = bf16[16,64,411]{2,0,1:T(8,128)(2,1)S(1)} copy(bf16[16,64,411]{1,0,2:T(8,128)(2,1)} %constant_dynamic-slice_fusion.4) | data formatting | bytes 1683456
  19.5 2.7 %collective-permute-done.2 = s32[3]{0:T(128)S(1)} collective-permute-done((s32[3]{0:T(128)S(1)}, s32[3]{0:T(128)S(1)}, u32[]{:S(2)}, u32[]{:S(2)}) %collective-permute-start.2) | collective-permute-done | bytes 44 | tf_op jit(solution)/shard_map/ppermute | solution.py:16
  22.3 1.5 %collective-permute-start.8 = (bf16[308,616]{1,0:T(8,128)(2,1)S(1)}, bf16[308,616]{1,0:T(8,128)(2,1)}, u32[]{:S(2)}, u32[]{:S(2)}) collective-permute-start(bf16[308,616]{1,0:T(8,128)(2,1)S(1)} %copy-done.1), channel_id=1, source_target_pairs={{0,1},{1,0},{2,3},{3,2},{4,5},{5,4},{6,7},{7,6},{8,9},{9,8},{10,11... | collective-permute-start | bytes 1138376 | tf_op jit(solution)/shard_map/ppermute | solution.py:20
  23.8 0.3 fusion.25
  24.1 0.7 copy.32
  24.8 0.0 collective-permute-done.1
  24.8 3.4 %collective-permute-start.5 = (bf16[3,64,411]{2,1,0:T(8,128)(2,1)}, bf16[3,64,411]{2,1,0:T(8,128)(2,1)}, u32[]{:S(2)}, u32[]{:S(2)}) collective-permute-start(bf16[3,64,411]{2,1,0:T(8,128)(2,1)} %copy.32), channel_id=1, source_target_pairs={{0,252},{2,254},{4,0},{6,2},{8,4},{10,6},{12,8},{14,10},{16,12},{1... | collective-permute-start | bytes 473480 | tf_op jit(solution)/shard_map/ppermute | solution.py:16
  28.2 0.3 fusion.22
  28.6 0.0 copy-start.2
  28.6 0.7 copy.33
  29.3 0.0 collective-permute-done
  29.3 2.3 %collective-permute-start.4 = (bf16[3,64,411]{2,1,0:T(8,128)(2,1)}, bf16[3,64,411]{2,1,0:T(8,128)(2,1)}, u32[]{:S(2)}, u32[]{:S(2)}) collective-permute-start(bf16[3,64,411]{2,1,0:T(8,128)(2,1)} %copy.33), channel_id=1, source_target_pairs={{0,254},{2,0},{4,2},{6,4},{8,6},{10,8},{12,10},{14,12},{16,14},{18... | collective-permute-start | bytes 473480 | tf_op jit(solution)/shard_map/ppermute | solution.py:16
  31.6 0.3 fusion.16
  32.0 0.7 copy.35
  32.7 0.0 collective-permute-start.3
  32.7 0.3 fusion.19
  33.1 0.6 convert_element_type.38.ic_ref
  33.7 4.0 %copy.21.jc_ref = bf16[8,308,411]{2,1,0:T(8,128)(2,1)} copy(bf16[8,308,411]{2,0,1:T(8,128)(2,1)} %param.7) | data formatting | bytes 4050816 | tf_op args[0]
  38.4 1.1 %constant_dynamic-slice_fusion.2 = (bf16[308,308]{1,0:T(8,128)(2,1)}, bf16[308,308]{1,0:T(8,128)(2,1)}) fusion(bf16[308,616]{1,0:T(8,128)(2,1)S(1)} %copy-done.1, s32[]{:T(128)S(6)} %select_n.27, s32[]{:T(128)S(6)} %select_n.26), kind=kLoop, calls=%fused_computation.40 | loop fusion | bytes 758920 | tf_op jit(solution)/shard_map/dynamic_slice | solution.py:89
  39.5 0.6 convert_element_type.39.io_ref
  40.1 0.0 collective-permute-done.5
  40.1 0.0 collective-permute-done.4
  40.1 3.8 %collective-permute-done.3 = bf16[3,64,411]{2,1,0:T(8,128)(2,1)} collective-permute-done((bf16[3,64,411]{2,1,0:T(8,128)(2,1)}, bf16[3,64,411]{2,1,0:T(8,128)(2,1)}, u32[]{:S(2)}, u32[]{:S(2)}) %collective-permute-start.3) | collective-permute-done | bytes 157856 | tf_op jit(solution)/shard_map/ppermute | solution.py:16
  43.9 2.1 %pad_maximum_fusion.state_ref = bf16[12,64,411]{2,1,0:T(8,128)(2,1)} fusion(bf16[3,64,411]{2,1,0:T(8,128)(2,1)} %collective-permute-done.5, bf16[3,64,411]{2,1,0:T(8,128)(2,1)} %collective-permute-done.4, bf16[3,64,411]{2,1,0:T(8,128)(2,1)S(1)} %copy.34, bf16[3,64,411]{2,1,0:T(8,128)(2,1)} %collective-permute-done.3), kind=kLoop, calls=%fused_computation.10 | loop fusion | flops 946944 | bytes 1262592 | tf_op jit(solution)/shard_map/concatenate | solution.py:119
  46.0 2.1 %constant_dynamic-slice_fusion = (bf16[308,308]{1,0:T(8,128)(2,1)}, bf16[308,308]{1,0:T(8,128)(2,1)}) fusion(bf16[308,616]{1,0:T(8,128)(2,1)} %collective-permute-done.8, s32[]{:T(128)S(6)} %select_n.27, s32[]{:T(128)S(6)} %select_n.26), kind=kLoop, calls=%fused_computation.38 | loop fusion | bytes 758920 | tf_op jit(solution)/shard_map/dynamic_slice | solution.py:91
  48.1 4.0 %copy.22.jo_ref = bf16[8,308,411]{2,1,0:T(8,128)(2,1)} copy(bf16[8,308,411]{2,0,1:T(8,128)(2,1)} %collective-permute-done.6) | data formatting | bytes 4050816 | tf_op jit(solution)/shard_map/ppermute | solution.py:20
  52.1 10.5 %shard_map.73 = bf16[8,64,411]{2,1,0:T(8,128)(2,1)} custom-call(s32[8]{0:T(128)} %copy-done.3, s32[1]{0:T(128)S(6)} %copy.36.count_ref, bf16[12,64,411]{2,1,0:T(8,128)(2,1)} %pad_maximum_fusion.state_ref, bf16[8,308,411]{2,1,0:T(8,128)(2,1)} %copy.21.jc_ref, bf16[8,308,411]{2,1,0:T(8,128)(2,1)} %copy.22.jo_ref, f32[8,308]{1,0:T(8,128)} %convert_element_type.38.ic_ref, ...), custom_call_target="tpu_custom_call" | custom-call | tf_op jit(solution)/shard_map/pallas_call | solution.py:63
  62.6 1.6 %convolution_convert_fusion.1 = bf16[12,64,411]{2,0,1:T(8,128)(2,1)S(1)} fusion(bf16[8,64,411]{2,1,0:T(8,128)(2,1)} %shard_map.73, s32[8]{0:T(128)S(1)} %copy-done.4), kind=kOutput, calls=%fused_computation.2 | convolution fusion | flops 5366112 | bytes 1052192 | tf_op jit(solution)/shard_map/af,fmd->amd/dot_general | solution.py:123
  64.3 0.4 fusion.32
  64.7 3.2 %collective-permute-start.9 = (bf16[3,64,411]{2,0,1:T(4,128)(2,1)S(1)}, bf16[3,64,411]{2,0,1:T(4,128)(2,1)S(1)}, u32[]{:S(2)}, u32[]{:S(2)}) collective-permute-start(bf16[3,64,411]{2,0,1:T(4,128)(2,1)S(1)} %get-tuple-element.5), channel_id=1, source_target_pairs={{0,254},{2,0},{4,2},{6,4},{8,6},{10,8},{12,10},{14,12},{16,14},{18... | collective-permute-start | bytes 473480 | tf_op jit(solution)/shard_map/ppermute | solution.py:16
  67.9 0.1 pad_add_fusion
  68.0 4.2 %collective-permute-done.9 = bf16[3,64,411]{2,0,1:T(4,128)(2,1)S(1)} collective-permute-done((bf16[3,64,411]{2,0,1:T(4,128)(2,1)S(1)}, bf16[3,64,411]{2,0,1:T(4,128)(2,1)S(1)}, u32[]{:S(2)}, u32[]{:S(2)}) %collective-permute-start.9) | collective-permute-done | bytes 157856 | tf_op jit(solution)/shard_map/ppermute | solution.py:16
  72.2 9.0 %collective-permute-done.11 = bf16[3,64,411]{2,0,1:T(4,128)(2,1)S(1)} collective-permute-done((bf16[3,64,411]{2,0,1:T(4,128)(2,1)S(1)}, bf16[3,64,411]{2,0,1:T(4,128)(2,1)S(1)}, u32[]{:S(2)}, u32[]{:S(2)}) %collective-permute-start.11) | collective-permute-done | bytes 157856 | tf_op jit(solution)/shard_map/ppermute | solution.py:16
  81.2 3.0 %collective-permute-done.10 = bf16[3,64,411]{2,0,1:T(4,128)(2,1)S(1)} collective-permute-done((bf16[3,64,411]{2,0,1:T(4,128)(2,1)S(1)}, bf16[3,64,411]{2,0,1:T(4,128)(2,1)S(1)}, u32[]{:S(2)}, u32[]{:S(2)}) %collective-permute-start.10) | collective-permute-done | bytes 157856 | tf_op jit(solution)/shard_map/ppermute | solution.py:16
  84.1 1.0 convolution_convert_fusion
  85.1 3.9 %collective-permute-start.12 = (bf16[16,64,411]{2,0,1:T(8,128)(2,1)S(1)}, bf16[16,64,411]{2,0,1:T(8,128)(2,1)}, u32[]{:S(2)}, u32[]{:S(2)}) collective-permute-start(bf16[16,64,411]{2,0,1:T(8,128)(2,1)S(1)} %convolution_convert_fusion), channel_id=1, source_target_pairs={{0,1},{1,0},{2,3},{3,2},{4,5},{5,4},{6,7},{7,6},{8,9},{9,8},{10,11... | collective-permute-start | bytes 2525192 | tf_op jit(solution)/shard_map/ppermute | solution.py:20
  89.0 2.4 %collective-permute-done.12 = bf16[16,64,411]{2,0,1:T(8,128)(2,1)} collective-permute-done((bf16[16,64,411]{2,0,1:T(8,128)(2,1)S(1)}, bf16[16,64,411]{2,0,1:T(8,128)(2,1)}, u32[]{:S(2)}, u32[]{:S(2)}) %collective-permute-start.12) | collective-permute-done | bytes 841760 | tf_op jit(solution)/shard_map/ppermute | solution.py:20
  91.4 3.5 %maximum_select_fusion = bf16[16,128,411]{2,0,1:T(8,128)(2,1)} fusion(bf16[16,64,411]{2,0,1:T(8,128)(2,1)} %collective-permute-done.12, bf16[16,64,411]{2,0,1:T(8,128)(2,1)S(1)} %convolution_convert_fusion, pred[]{:T(512)S(6)} %eq.44), kind=kLoop, calls=%fused_computation | loop fusion | flops 2525184 | bytes 3366913 | tf_op jit(solution)/shard_map/jit(_where)/select_n | solution.py:136
  94.9 4.9 %copy.24 = bf16[16,128,411]{1,0,2:T(8,128)(2,1)} copy(bf16[16,128,411]{2,0,1:T(8,128)(2,1)} %maximum_select_fusion) | data formatting | bytes 3366912 | tf_op jit(solution)/shard_map/jit(_where)/select_n | solution.py:136
  (16 shorter events, 0.1 us)
Async XLA Ops:
  0.0 14.5 %copy-start = (bf16[16,128,411]{1,0,2:T(8,128)(2,1)S(1)}, bf16[16,128,411]{1,0,2:T(8,128)(2,1)}, u32[]{:S(2)}) copy-start(bf16[16,128,411]{1,0,2:T(8,128)(2,1)} %param.10) | copy-start | bytes 5050372
  0.0 48.1 %collective-permute-start.6 = (bf16[8,308,411]{2,0,1:T(8,128)(2,1)}, bf16[8,308,411]{2,0,1:T(8,128)(2,1)}, u32[]{:S(2)}, u32[]{:S(2)}) collective-permute-start(bf16[8,308,411]{2,0,1:T(8,128)(2,1)} %param.7), channel_id=1, source_target_pairs={{0,1},{1,0},{2,3},{3,2},{4,5},{5,4},{6,7},{7,6},{8,9},{9,8},{10,11... | collective-permute-start | bytes 6076232 | tf_op jit(solution)/shard_map/ppermute | solution.py:20
  4.8 14.7 %copy-start.3 = (s32[8]{0:T(128)}, s32[8]{0:T(128)S(1)}, u32[]{:S(2)}) copy-start(s32[8]{0:T(128)S(1)} %multiply_add_fusion.place_ref) | copy-start | bytes 100
  5.6 23.7 %collective-permute-start = (s32[3]{0:T(128)S(1)}, s32[3]{0:T(128)S(1)}, u32[]{:S(2)}, u32[]{:S(2)}) collective-permute-start(s32[3]{0:T(128)S(1)} %get-tuple-element.13), channel_id=1, source_target_pairs={{0,254},{2,0},{4,2},{6,4},{8,6},{10,8},{12,10},{14,12},{16,14},{18... | collective-permute-start | bytes 44 | tf_op jit(solution)/shard_map/ppermute | solution.py:16
  14.1 8.1 %collective-permute-start.2 = (s32[3]{0:T(128)S(1)}, s32[3]{0:T(128)S(1)}, u32[]{:S(2)}, u32[]{:S(2)}) collective-permute-start(s32[3]{0:T(128)S(1)} %get-tuple-element.14), channel_id=1, source_target_pairs={{0,4},{2,6},{4,8},{6,10},{8,12},{10,14},{12,16},{14,18},{16,20},{1... | collective-permute-start | bytes 44 | tf_op jit(solution)/shard_map/ppermute | solution.py:16
  14.1 10.7 %collective-permute-start.1 = (s32[3]{0:T(128)S(1)}, s32[3]{0:T(128)S(1)}, u32[]{:S(2)}, u32[]{:S(2)}) collective-permute-start(s32[3]{0:T(128)S(1)} %get-tuple-element.15), channel_id=1, source_target_pairs={{0,2},{2,4},{4,6},{6,8},{8,10},{10,12},{12,14},{14,16},{16,18},{18... | collective-permute-start | bytes 44 | tf_op jit(solution)/shard_map/ppermute | solution.py:16
  14.1 18.6 %collective-permute-start.7 = (bf16[8,308]{1,0:T(8,128)(2,1)}, bf16[8,308]{1,0:T(8,128)(2,1)S(1)}, u32[]{:S(2)}, u32[]{:S(2)}) collective-permute-start(bf16[8,308]{1,0:T(8,128)(2,1)} %param.9), channel_id=1, source_target_pairs={{0,1},{1,0},{2,3},{3,2},{4,5},{5,4},{6,7},{7,6},{8,9},{9,8},{10,11... | collective-permute-start | bytes 14792 | tf_op jit(solution)/shard_map/ppermute | solution.py:20
  16.2 6.1 %copy-start.1 = (bf16[308,616]{1,0:T(8,128)(2,1)S(1)}, bf16[308,616]{1,0:T(8,128)(2,1)}, u32[]{:S(2)}) copy-start(bf16[308,616]{1,0:T(8,128)(2,1)} %param.8) | copy-start | bytes 1138372
  22.3 23.7 %collective-permute-start.8 = (bf16[308,616]{1,0:T(8,128)(2,1)S(1)}, bf16[308,616]{1,0:T(8,128)(2,1)}, u32[]{:S(2)}, u32[]{:S(2)}) collective-permute-start(bf16[308,616]{1,0:T(8,128)(2,1)S(1)} %copy-done.1), channel_id=1, source_target_pairs={{0,1},{1,0},{2,3},{3,2},{4,5},{5,4},{6,7},{7,6},{8,9},{9,8},{10,11... | collective-permute-start | bytes 1138376 | tf_op jit(solution)/shard_map/ppermute | solution.py:20
  24.8 15.2 %collective-permute-start.5 = (bf16[3,64,411]{2,1,0:T(8,128)(2,1)}, bf16[3,64,411]{2,1,0:T(8,128)(2,1)}, u32[]{:S(2)}, u32[]{:S(2)}) collective-permute-start(bf16[3,64,411]{2,1,0:T(8,128)(2,1)} %copy.32), channel_id=1, source_target_pairs={{0,252},{2,254},{4,0},{6,2},{8,4},{10,6},{12,8},{14,10},{16,12},{1... | collective-permute-start | bytes 473480 | tf_op jit(solution)/shard_map/ppermute | solution.py:16
  28.6 4.5 %copy-start.2 = (bf16[8,308]{1,0:T(8,128)(2,1)S(1)}, bf16[8,308]{1,0:T(8,128)(2,1)}, u32[]{:S(2)}) copy-start(bf16[8,308]{1,0:T(8,128)(2,1)} %param.9) | copy-start | bytes 14788
  29.3 10.8 %collective-permute-start.4 = (bf16[3,64,411]{2,1,0:T(8,128)(2,1)}, bf16[3,64,411]{2,1,0:T(8,128)(2,1)}, u32[]{:S(2)}, u32[]{:S(2)}) collective-permute-start(bf16[3,64,411]{2,1,0:T(8,128)(2,1)} %copy.33), channel_id=1, source_target_pairs={{0,254},{2,0},{4,2},{6,4},{8,6},{10,8},{12,10},{14,12},{16,14},{18... | collective-permute-start | bytes 473480 | tf_op jit(solution)/shard_map/ppermute | solution.py:16
  32.7 11.1 %collective-permute-start.3 = (bf16[3,64,411]{2,1,0:T(8,128)(2,1)}, bf16[3,64,411]{2,1,0:T(8,128)(2,1)}, u32[]{:S(2)}, u32[]{:S(2)}) collective-permute-start(bf16[3,64,411]{2,1,0:T(8,128)(2,1)} %copy.35), channel_id=1, source_target_pairs={{0,2},{2,4},{4,6},{6,8},{8,10},{10,12},{12,14},{14,16},{16,18},{18... | collective-permute-start | bytes 473480 | tf_op jit(solution)/shard_map/ppermute | solution.py:16
  52.1 10.5 %copy-start.4 = (s32[8]{0:T(128)S(1)}, s32[8]{0:T(128)}, u32[]{:S(2)}) copy-start(s32[8]{0:T(128)} %copy-done.3) | copy-start | bytes 100
  64.7 7.5 %collective-permute-start.9 = (bf16[3,64,411]{2,0,1:T(4,128)(2,1)S(1)}, bf16[3,64,411]{2,0,1:T(4,128)(2,1)S(1)}, u32[]{:S(2)}, u32[]{:S(2)}) collective-permute-start(bf16[3,64,411]{2,0,1:T(4,128)(2,1)S(1)} %get-tuple-element.5), channel_id=1, source_target_pairs={{0,254},{2,0},{4,2},{6,4},{8,6},{10,8},{12,10},{14,12},{16,14},{18... | collective-permute-start | bytes 473480 | tf_op jit(solution)/shard_map/ppermute | solution.py:16
  67.9 13.3 %collective-permute-start.11 = (bf16[3,64,411]{2,0,1:T(4,128)(2,1)S(1)}, bf16[3,64,411]{2,0,1:T(4,128)(2,1)S(1)}, u32[]{:S(2)}, u32[]{:S(2)}) collective-permute-start(bf16[3,64,411]{2,0,1:T(4,128)(2,1)S(1)} %get-tuple-element.6), channel_id=1, source_target_pairs={{0,4},{2,6},{4,8},{6,10},{8,12},{10,14},{12,16},{14,18},{16,20},{1... | collective-permute-start | bytes 473480 | tf_op jit(solution)/shard_map/ppermute | solution.py:16
  67.9 16.2 %collective-permute-start.10 = (bf16[3,64,411]{2,0,1:T(4,128)(2,1)S(1)}, bf16[3,64,411]{2,0,1:T(4,128)(2,1)S(1)}, u32[]{:S(2)}, u32[]{:S(2)}) collective-permute-start(bf16[3,64,411]{2,0,1:T(4,128)(2,1)S(1)} %get-tuple-element.7), channel_id=1, source_target_pairs={{0,2},{2,4},{4,6},{6,8},{8,10},{10,12},{12,14},{14,16},{16,18},{18... | collective-permute-start | bytes 473480 | tf_op jit(solution)/shard_map/ppermute | solution.py:16
  85.1 6.3 %collective-permute-start.12 = (bf16[16,64,411]{2,0,1:T(8,128)(2,1)S(1)}, bf16[16,64,411]{2,0,1:T(8,128)(2,1)}, u32[]{:S(2)}, u32[]{:S(2)}) collective-permute-start(bf16[16,64,411]{2,0,1:T(8,128)(2,1)S(1)} %convolution_convert_fusion), channel_id=1, source_target_pairs={{0,1},{1,0},{2,3},{3,2},{4,5},{5,4},{6,7},{7,6},{8,9},{9,8},{10,11... | collective-permute-start | bytes 2525192 | tf_op jit(solution)/shard_map/ppermute | solution.py:20

commit v3 on v2

--- a/solution.py
+++ b/solution.py
@@ -24,10 +24,12 @@
     return (index[:, None] == jnp.arange(size, dtype=jnp.int32)[None, :]).astype(jnp.bfloat16)
 
 
-def adjoint_kernel(place_ref, count_ref, state_ref, jc_ref, jo_ref, ic_ref, io_ref,
+def adjoint_kernel(place_ref, count_ref, s0_ref, s1_ref, s2_ref, s3_ref, jc_ref, jo_ref, ic_ref, io_ref,
                    rcc_ref, rco_ref, roc_ref, roo_ref, out_ref):
     f = pl.program_id(0)
-    s = state_ref[0]
+    group = place_ref[f] // CAP
+    s = jnp.where(group == 0, s0_ref[0], jnp.where(group == 1, s1_ref[0],
+                  jnp.where(group == 2, s2_ref[0], s3_ref[0])))
     jc = jc_ref[0]
     jo = jo_ref[0]
     ev_c = lax.dot_general(s, jc, NT, preferred_element_type=jnp.float32)
@@ -44,15 +46,31 @@
     out_ref[0] = jnp.where(live, adj, 0.0).astype(out_ref.dtype)
 
 
+def copy_kernel(x_ref, o_ref):
+    o_ref[...] = x_ref[...]
+
+
+def row_major(x):
+    block = (1,) + x.shape[1:]
+    spec = pl.BlockSpec(block, lambda i: (i,) + (0,) * (x.ndim - 1))
+    return pl.pallas_call(copy_kernel, grid=(x.shape[0],), in_specs=[spec], out_specs=spec,
+                          out_shape=jax.ShapeDtypeStruct(x.shape, x.dtype))(x)
+
+
 def adjoints(place, count, fetched, jac_c, jac_o, innov_c, innov_o, r_blocks):
     foot, half_ch, state = jac_c.shape
-    half_m = fetched.shape[1]
+    half_m = fetched[0].shape[1]
     full = lambda f, p, n: (0, 0)
+
+    def part(g):
+        return pl.BlockSpec((1, half_m, state),
+                            lambda f, p, n: (jnp.where(p[f] // CAP == g, p[f] % CAP, 0), 0, 0))
+
     grid_spec = pltpu.PrefetchScalarGridSpec(
         num_scalar_prefetch=2,
         grid=(foot,),
         in_specs=[
-            pl.BlockSpec((1, half_m, state), lambda f, p, n: (p[f], 0, 0)),
+            part(0), part(1), part(2), part(3),
             pl.BlockSpec((1, half_ch, state), lambda f, p, n: (f, 0, 0)),
             pl.BlockSpec((1, half_ch, state), lambda f, p, n: (f, 0, 0)),
             pl.BlockSpec((foot, half_ch), full),
@@ -64,7 +82,7 @@
         adjoint_kernel,
         grid_spec=grid_spec,
         out_shape=jax.ShapeDtypeStruct((foot, half_m, state), jnp.bfloat16),
-    )(place, count, fetched, jac_c, jac_o, innov_c, innov_o, *r_blocks)
+    )(place, count, *fetched, jac_c, jac_o, innov_c, innov_o, *r_blocks)
 
 
 def on_device(jacobian, r_inverse, innovation, increments, owner_offset, column_slot, foot_counts):
@@ -78,17 +96,21 @@
     capacity = CAP
     slots_total = SPAN * capacity
 
-    jac_o = swapped(jacobian)
+    jac_c = jacobian
+    jac_o = row_major(swapped(jacobian))
     innov_c = innovation.astype(jnp.float32)
     innov_o = swapped(innovation).astype(jnp.float32)
     r_o = swapped(r_inverse)
-    own_cols = core * half_ch
-    other_cols = (1 - core) * half_ch
+    first = core == 0
+    rows_lo = jnp.where(first, r_inverse, r_o)
+    rows_hi = jnp.where(first, r_o, r_inverse)
+    r00, r01 = rows_lo[:, :half_ch], rows_lo[:, half_ch:]
+    r10, r11 = rows_hi[:, :half_ch], rows_hi[:, half_ch:]
     r_blocks = (
-        lax.dynamic_slice_in_dim(r_inverse, own_cols, half_ch, axis=1),
-        lax.dynamic_slice_in_dim(r_inverse, other_cols, half_ch, axis=1),
-        lax.dynamic_slice_in_dim(r_o, own_cols, half_ch, axis=1),
-        lax.dynamic_slice_in_dim(r_o, other_cols, half_ch, axis=1),
+        jnp.where(first, r00, r11),
+        jnp.where(first, r01, r10),
+        jnp.where(first, r10, r01),
+        jnp.where(first, r11, r00),
     )
 
     offset = owner_offset[:, 0]
@@ -105,20 +127,16 @@
         return jnp.einsum("ac,cms->ams", one_hot(index, columns), own_inc,
                           preferred_element_type=jnp.float32).astype(jnp.bfloat16)
 
-    fetched_parts = []
     slot_parts = []
     for g in range(SPAN):
         wanted = request[g * capacity:(g + 1) * capacity]
-        if g == 1:
-            fetched_parts.append(pick(wanted))
-            slot_parts.append(wanted)
-        else:
-            asked = passed_along(wanted, "tile", g - 1)
-            fetched_parts.append(passed_along(pick(asked), "tile", 1 - g))
-            slot_parts.append(asked)
-    fetched = jnp.concatenate(fetched_parts, axis=0)
-
-    adjoint = adjoints(place, foot_counts, fetched, jacobian, jac_o, innov_c, innov_o, r_blocks)
+        slot_parts.append(wanted if g == 1 else passed_along(wanted, "tile", g - 1))
+    slot_parts, jac_o, r_blocks = lax.optimization_barrier((slot_parts, jac_o, r_blocks))
+    fetched_parts = []
+    for g in range(SPAN):
+        picked = pick(slot_parts[g])
+        fetched_parts.append(picked if g == 1 else passed_along(picked, "tile", 1 - g))
+    adjoint = adjoints(place, foot_counts, fetched_parts, jac_c, jac_o, innov_c, innov_o, r_blocks)
 
     packed = jnp.einsum("af,fmd->amd", hit.astype(jnp.bfloat16), adjoint,
                         preferred_element_type=jnp.float32).astype(jnp.bfloat16)
@@ -133,7 +151,7 @@
     mine = jnp.einsum("ac,amd->cmd", one_hot(got_slots, columns), jnp.concatenate(recv_parts, axis=0),
                       preferred_element_type=jnp.float32).astype(jnp.bfloat16)
     other = swapped(mine)
-    return jnp.where(core == 0, jnp.concatenate([mine, other], axis=1),
+    return jnp.where(first, jnp.concatenate([mine, other], axis=1),
                      jnp.concatenate([other, mine], axis=1))
 
 

time: 100 us -> 107 us (1.070)
  Pallas kernels: 10.5 us -> 16.8 us
  starting transfers between devices: 26.4 us -> 32 us
  local copies, waits for them, and re-layouts: 23.9 us -> 20.6 us
  waiting for transfers between devices: 25.1 us -> 23 us
  other arithmetic: 9.16 us -> 7.42 us
  matrix products: 3.97 us -> 5.25 us
    pallas_call x0 -> x1, Pallas kernels: none -> 5.8 us  [row_major(): pl.pallas_call(copy_kernel, grid=(x.shape[0],), in_specs=[spec], out_spec...]
    ppermute x9, starting transfers between devices: 17.5 us -> 22.2 us  [passed_along(): lax.ppermute(value, axis, [(i, (i + by) % count) for i in range(count)])]
    dynamic_slice x2 -> x0, local copies, waits for them, and re-layouts: 3.13 us -> none  [the longest x1 2.08 us: on_device(): lax.dynamic_slice_in_dim(r_o, other_cols, half_ch, axis=1)]
    concatenate x1 -> x0, other arithmetic: 2.11 us -> none  [on_device(): fetched = jnp.concatenate(fetched_parts, axis=0)]
    ppermute x9, waiting for transfers between devices: 22.7 us -> 20.7 us  [passed_along(): lax.ppermute(value, axis, [(i, (i + by) % count) for i in range(count)])]
    dot_general x4, local copies, waits for them, and re-layouts: 2.19 us -> 0.86 us  [pick(): jnp.einsum('ac,cms->ams', one_hot(index, columns), own_inc, preferred_ele...]
    dot_general x4, matrix products: 1.4 us -> 2.67 us  [pick(): jnp.einsum('ac,cms->ams', one_hot(index, columns), own_inc, preferred_ele...]
    unnamed x12 -> x20, local copies, waits for them, and re-layouts: 7.41 us -> 8.04 us
  transfers between devices with their start and end apart: 13 -> 13, of which waited for: 6 -> 6; matrix products, arithmetic and copies ran while one was open for 22% -> 21% of each run, Pallas kernels for 0% -> 5%
where the time goes in v3:
time: 107 us; the launch traced here: 106 us
  starting transfers between devices  32 us (30%)
  waiting for transfers between devices  23 us (21%)
  local copies, waits for them, and re-layouts  20.6 us (19%)
  Pallas kernels  16.8 us (16%)
  other arithmetic  7.42 us (7%)
  matrix products  5.25 us (5%)
    ppermute x9, starting transfers between devices, passed_along(): lax.ppermute(value, axis, [(i, (i + by) % count) for i in range(count)])  22.2 us
    ppermute x9, waiting for transfers between devices, passed_along(): lax.ppermute(value, axis, [(i, (i + by) % count) for i in range(count)])  20.7 us
    pallas_call x1, Pallas kernels, adjoints(): pl.pallas_call(adjoint_kernel, grid_spec=grid_spec, out_shape=jax.ShapeDt...  11 us
    ppermute x4, starting transfers between devices, swapped(): return lax.ppermute(value, 'chan', [(0, 1), (1, 0)])  9.78 us
    unnamed x20, local copies, waits for them, and re-layouts  8.04 us
    pallas_call x1, Pallas kernels, row_major(): pl.pallas_call(copy_kernel, grid=(x.shape[0],), in_specs=[spec], out_spec...  5.8 us
    select_n x1, local copies, waits for them, and re-layouts, on_device(): jnp.where(first, jnp.concatenate([mine, other], axis=1), jnp.concatenate(...  4.94 us
    ppermute x1, local copies, waits for them, and re-layouts, swapped(): return lax.ppermute(value, 'chan', [(0, 1), (1, 0)])  4 us
  transfers between devices with their start and end apart: 13, of which 6 were waited for; matrix products, arithmetic and copies ran while one was open for 21% of the time, Pallas kernels for 5%

profile of v3, /device:TPU:1, one launch (start us, length us, event | category | flops | bytes accessed | tf_op | source)
XLA Modules:
  0.0 105.9 jit_solution(9556562905063748445)
XLA Ops:
  0.0 3.2 %collective-permute-start.3 = (bf16[8,308,411]{2,0,1:T(8,128)(2,1)}, bf16[8,308,411]{2,0,1:T(8,128)(2,1)}, u32[]{:S(2)}, u32[]{:S(2)}) collective-permute-start(bf16[8,308,411]{2,0,1:T(8,128)(2,1)} %param.7), channel_id=1, source_target_pairs={{0,1},{1,0},{2,3},{3,2},{4,5},{5,4},{6,7},{7,6},{8,9},{9,8},{10,11... | collective-permute-start | bytes 6076232 | tf_op jit(solution)/shard_map/ppermute | solution.py:20
  3.2 0.0 collective-permute-start.4
  3.2 0.9 convert_reduce_fusion
  4.1 0.7 multiply_add_fusion.place_ref
  4.8 0.7 select_reduce_fusion
  5.5 0.6 fusion.33
  6.2 1.3 %collective-permute-start.2 = (s32[3]{0:T(128)}, s32[3]{0:T(128)}, u32[]{:S(2)}, u32[]{:S(2)}) collective-permute-start(s32[3]{0:T(128)} %get-tuple-element.33), channel_id=1, source_target_pairs={{0,4},{2,6},{4,8},{6,10},{8,12},{10,14},{12,16},{14,18},{16,20},{1... | collective-permute-start | bytes 44 | tf_op jit(solution)/shard_map/ppermute | solution.py:16
  7.5 0.4 collective-permute-start.1
  7.9 1.0 collective-permute-start.8
  8.9 1.7 %constant_dynamic-slice_fusion = bf16[16,64,411]{1,0,2:T(8,128)(2,1)} fusion(bf16[16,128,411]{1,0,2:T(8,128)(2,1)S(1)} %copy-done, s32[]{:T(128)S(6)} %select_n.57), kind=kLoop, calls=%fused_computation.49 | loop fusion | bytes 1683460 | tf_op jit(solution)/shard_map/dynamic_slice | solution.py:124
  10.5 0.6 convert_element_type.38.ic_ref
  11.1 4.0 %copy.22.jc_ref = bf16[8,308,411]{2,1,0:T(8,128)(2,1)} copy(bf16[8,308,411]{2,0,1:T(8,128)(2,1)} %param.7) | data formatting | bytes 4050816 | tf_op args[0]
  15.9 3.3 %copy.25 = bf16[16,64,411]{2,0,1:T(8,128)(2,1)S(1)} copy(bf16[16,64,411]{1,0,2:T(8,128)(2,1)} %constant_dynamic-slice_fusion) | data formatting | bytes 1683456
  19.2 0.0 collective-permute-done.8
  19.2 6.6 %collective-permute-start = (s32[3]{0:T(128)S(1)}, s32[3]{0:T(128)S(1)}, u32[]{:S(2)}, u32[]{:S(2)}) collective-permute-start(s32[3]{0:T(128)S(1)} %copy-done.8), channel_id=1, source_target_pairs={{0,254},{2,0},{4,2},{6,4},{8,6},{10,8},{12,10},{14,12},{16,14},{18... | collective-permute-start | bytes 44 | tf_op jit(solution)/shard_map/ppermute | solution.py:16
  25.8 0.6 convert_element_type.39.io_ref
  26.4 0.1 broadcast_select_fusion.1
  26.5 1.3 %broadcast_select_fusion.2 = (bf16[308,308]{1,0:T(8,128)(2,1)}, bf16[308,308]{1,0:T(8,128)(2,1)}, bf16[308,308]{1,0:T(8,128)(2,1)}, bf16[308,308]{1,0:T(8,128)(2,1)}) fusion(pred[]{:T(512)S(6)} %eq.44, bf16[308,616]{1,0:T(8,128)(2,1)S(1)} %get-tuple-element.32, bf16[308,616]{1,0:T(8,128)(2,1)S(1)} %get-tuple-element.31), kind=kLoop, calls=%fused_computation.17 | loop fusion | flops 379456 | bytes 1517825 | tf_op jit(solution)/shard_map/jit(_where)/select_n | solution.py:113
  27.7 0.0 collective-permute-done.3
  27.7 4.0 %copy.16.x_ref = bf16[8,308,411]{2,1,0:T(8,128)(2,1)} copy(bf16[8,308,411]{2,0,1:T(8,128)(2,1)} %collective-permute-done.3) | data formatting | bytes 4050816 | tf_op jit(solution)/shard_map/ppermute | solution.py:20
  31.7 5.8 %shard_map.73.jo_ref = bf16[8,308,411]{2,1,0:T(8,128)(2,1)} custom-call(bf16[8,308,411]{2,1,0:T(8,128)(2,1)} %copy.16.x_ref), custom_call_target="tpu_custom_call" | custom-call | tf_op jit(solution)/shard_map/pallas_call | solution.py:56
  37.5 0.0 collective-permute-done.2
  37.6 0.4 fusion.16
  38.0 0.1 collective-permute-start.5
  38.1 1.0 fusion.22
  39.1 0.9 fusion.25
  40.2 7.0 %collective-permute-start.6 = (bf16[3,64,411]{2,1,0:T(8,128)(2,1)S(1)}, bf16[3,64,411]{2,1,0:T(8,128)(2,1)S(1)}, u32[]{:S(2)}, u32[]{:S(2)}) collective-permute-start(bf16[3,64,411]{2,1,0:T(8,128)(2,1)S(1)} %copy.33), channel_id=1, source_target_pairs={{0,254},{2,0},{4,2},{6,4},{8,6},{10,8},{12,10},{14,12},{16,14},{18... | collective-permute-start | bytes 473480 | tf_op jit(solution)/shard_map/ppermute | solution.py:16
  47.1 0.0 collective-permute-start.7
  47.1 0.4 fusion.19
  47.5 0.7 copy.34.s1_ref
  48.2 1.4 %collective-permute-done.5.s0_ref = bf16[3,64,411]{2,1,0:T(8,128)(2,1)S(1)} collective-permute-done((bf16[3,64,411]{2,1,0:T(8,128)(2,1)S(1)}, bf16[3,64,411]{2,1,0:T(8,128)(2,1)S(1)}, u32[]{:S(2)}, u32[]{:S(2)}) %collective-permute-start.5) | collective-permute-done | bytes 157856 | tf_op jit(solution)/shard_map/ppermute | solution.py:16
  49.6 1.2 %collective-permute-done.6.s2_ref = bf16[3,64,411]{2,1,0:T(8,128)(2,1)S(1)} collective-permute-done((bf16[3,64,411]{2,1,0:T(8,128)(2,1)S(1)}, bf16[3,64,411]{2,1,0:T(8,128)(2,1)S(1)}, u32[]{:S(2)}, u32[]{:S(2)}) %collective-permute-start.6) | collective-permute-done | bytes 157856 | tf_op jit(solution)/shard_map/ppermute | solution.py:16
  50.8 4.5 %collective-permute-done.7.s3_ref = bf16[3,64,411]{2,1,0:T(8,128)(2,1)S(1)} collective-permute-done((bf16[3,64,411]{2,1,0:T(8,128)(2,1)S(1)}, bf16[3,64,411]{2,1,0:T(8,128)(2,1)S(1)}, u32[]{:S(2)}, u32[]{:S(2)}) %collective-permute-start.7) | collective-permute-done | bytes 157856 | tf_op jit(solution)/shard_map/ppermute | solution.py:16
  55.3 0.7 copy-done.4
  56.0 11.0 %shard_map.74 = bf16[8,64,411]{2,1,0:T(8,128)(2,1)} custom-call(s32[8]{0:T(128)} %copy-done.6, s32[1]{0:T(128)S(6)} %copy.36.count_ref, bf16[3,64,411]{2,1,0:T(8,128)(2,1)} %copy-done.2, bf16[3,64,411]{2,1,0:T(8,128)(2,1)} %copy.34.s1_ref, bf16[3,64,411]{2,1,0:T(8,128)(2,1)} %copy-done.3, bf16[3,64,411]{2,1,0:T(8,128)(2,1)} %copy-done.4, ...), custom_call_target="tpu_custom_call" | custom-call | tf_op jit(solution)/shard_map/pallas_call | solution.py:81
  66.9 1.6 %convolution_convert_fusion.1 = bf16[12,64,411]{2,0,1:T(8,128)(2,1)S(1)} fusion(bf16[8,64,411]{2,1,0:T(8,128)(2,1)} %shard_map.74, s32[8]{0:T(128)S(1)} %copy-done.7), kind=kOutput, calls=%fused_computation.2 | convolution fusion | flops 5366112 | bytes 1052192 | tf_op jit(solution)/shard_map/af,fmd->amd/dot_general | solution.py:141
  68.6 0.4 fusion.32
  69.0 6.9 %collective-permute-start.9 = (bf16[3,64,411]{2,0,1:T(4,128)(2,1)S(1)}, bf16[3,64,411]{2,0,1:T(4,128)(2,1)S(1)}, u32[]{:S(2)}, u32[]{:S(2)}) collective-permute-start(bf16[3,64,411]{2,0,1:T(4,128)(2,1)S(1)} %get-tuple-element.23), channel_id=1, source_target_pairs={{0,254},{2,0},{4,2},{6,4},{8,6},{10,8},{12,10},{14,12},{16,14},{18... | collective-permute-start | bytes 473480 | tf_op jit(solution)/shard_map/ppermute | solution.py:16
  75.9 0.0 collective-permute-start.11
  75.9 0.0 collective-permute-start.10
  75.9 0.8 pad_add_fusion
  76.6 2.9 %collective-permute-done.9 = bf16[3,64,411]{2,0,1:T(4,128)(2,1)S(1)} collective-permute-done((bf16[3,64,411]{2,0,1:T(4,128)(2,1)S(1)}, bf16[3,64,411]{2,0,1:T(4,128)(2,1)S(1)}, u32[]{:S(2)}, u32[]{:S(2)}) %collective-permute-start.9) | collective-permute-done | bytes 157856 | tf_op jit(solution)/shard_map/ppermute | solution.py:16
  79.5 10.8 %collective-permute-done.11 = bf16[3,64,411]{2,0,1:T(4,128)(2,1)S(1)} collective-permute-done((bf16[3,64,411]{2,0,1:T(4,128)(2,1)S(1)}, bf16[3,64,411]{2,0,1:T(4,128)(2,1)S(1)}, u32[]{:S(2)}, u32[]{:S(2)}) %collective-permute-start.11) | collective-permute-done | bytes 157856 | tf_op jit(solution)/shard_map/ppermute | solution.py:16
  90.3 1.0 convolution_convert_fusion
  91.2 5.6 %collective-permute-start.12 = (bf16[16,64,411]{2,0,1:T(8,128)(2,1)S(1)}, bf16[16,64,411]{2,0,1:T(8,128)(2,1)S(1)}, u32[]{:S(2)}, u32[]{:S(2)}) collective-permute-start(bf16[16,64,411]{2,0,1:T(8,128)(2,1)S(1)} %convolution_convert_fusion), channel_id=1, source_target_pairs={{0,1},{1,0},{2,3},{3,2},{4,5},{5,4},{6,7},{7,6},{8,9},{9,8},{10,11... | collective-permute-start | bytes 2525192 | tf_op jit(solution)/shard_map/ppermute | solution.py:20
  96.8 2.3 %collective-permute-done.12 = bf16[16,64,411]{2,0,1:T(8,128)(2,1)S(1)} collective-permute-done((bf16[16,64,411]{2,0,1:T(8,128)(2,1)S(1)}, bf16[16,64,411]{2,0,1:T(8,128)(2,1)S(1)}, u32[]{:S(2)}, u32[]{:S(2)}) %collective-permute-start.12) | collective-permute-done | bytes 841760 | tf_op jit(solution)/shard_map/ppermute | solution.py:20
  99.1 1.8 %maximum_select_fusion = bf16[16,128,411]{2,0,1:T(8,128)(2,1)} fusion(bf16[16,64,411]{2,0,1:T(8,128)(2,1)S(1)} %collective-permute-done.12, bf16[16,64,411]{2,0,1:T(8,128)(2,1)S(1)} %convolution_convert_fusion, pred[]{:T(512)S(6)} %eq.44), kind=kLoop, calls=%fused_computation | loop fusion | flops 2525184 | bytes 3366913 | tf_op jit(solution)/shard_map/jit(_where)/select_n | solution.py:154
  100.9 4.9 %copy.24 = bf16[16,128,411]{1,0,2:T(8,128)(2,1)} copy(bf16[16,128,411]{2,0,1:T(8,128)(2,1)} %maximum_select_fusion) | data formatting | bytes 3366912 | tf_op jit(solution)/shard_map/jit(_where)/select_n | solution.py:154
  (24 shorter events, 0.2 us)
Async XLA Ops:
  0.0 8.9 %copy-start = (bf16[16,128,411]{1,0,2:T(8,128)(2,1)S(1)}, bf16[16,128,411]{1,0,2:T(8,128)(2,1)}, u32[]{:S(2)}) copy-start(bf16[16,128,411]{1,0,2:T(8,128)(2,1)} %param.10) | copy-start | bytes 5050372
  0.0 10.5 %copy-start.5 = (bf16[8,308]{1,0:T(8,128)(2,1)S(1)}, bf16[8,308]{1,0:T(8,128)(2,1)}, u32[]{:S(2)}) copy-start(bf16[8,308]{1,0:T(8,128)(2,1)} %param.9) | copy-start | bytes 14788
  0.0 27.7 %collective-permute-start.3 = (bf16[8,308,411]{2,0,1:T(8,128)(2,1)}, bf16[8,308,411]{2,0,1:T(8,128)(2,1)}, u32[]{:S(2)}, u32[]{:S(2)}) collective-permute-start(bf16[8,308,411]{2,0,1:T(8,128)(2,1)} %param.7), channel_id=1, source_target_pairs={{0,1},{1,0},{2,3},{3,2},{4,5},{5,4},{6,7},{7,6},{8,9},{9,8},{10,11... | collective-permute-start | bytes 6076232 | tf_op jit(solution)/shard_map/ppermute | solution.py:20
  3.2 23.2 %collective-permute-start.4 = (bf16[308,616]{1,0:T(8,128)(2,1)}, bf16[308,616]{1,0:T(8,128)(2,1)S(1)}, u32[]{:S(2)}, u32[]{:S(2)}) collective-permute-start(bf16[308,616]{1,0:T(8,128)(2,1)} %param.8), channel_id=1, source_target_pairs={{0,1},{1,0},{2,3},{3,2},{4,5},{5,4},{6,7},{7,6},{8,9},{9,8},{10,11... | collective-permute-start | bytes 1138376 | tf_op jit(solution)/shard_map/ppermute | solution.py:20
  4.8 2.7 %copy-start.6 = (s32[8]{0:T(128)}, s32[8]{0:T(128)S(1)}, u32[]{:S(2)}) copy-start(s32[8]{0:T(128)S(1)} %multiply_add_fusion.place_ref) | copy-start | bytes 100
  6.2 31.4 %collective-permute-start.2 = (s32[3]{0:T(128)}, s32[3]{0:T(128)}, u32[]{:S(2)}, u32[]{:S(2)}) collective-permute-start(s32[3]{0:T(128)} %get-tuple-element.33), channel_id=1, source_target_pairs={{0,4},{2,6},{4,8},{6,10},{8,12},{10,14},{12,16},{14,18},{16,20},{1... | collective-permute-start | bytes 44 | tf_op jit(solution)/shard_map/ppermute | solution.py:16
  7.5 30.1 %collective-permute-start.1 = (s32[3]{0:T(128)}, s32[3]{0:T(128)}, u32[]{:S(2)}, u32[]{:S(2)}) collective-permute-start(s32[3]{0:T(128)} %get-tuple-element.34), channel_id=1, source_target_pairs={{0,2},{2,4},{4,6},{6,8},{8,10},{10,12},{12,14},{14,16},{16,18},{18... | collective-permute-start | bytes 44 | tf_op jit(solution)/shard_map/ppermute | solution.py:16
  7.9 11.3 %collective-permute-start.8 = (bf16[8,308]{1,0:T(8,128)(2,1)}, bf16[8,308]{1,0:T(8,128)(2,1)S(1)}, u32[]{:S(2)}, u32[]{:S(2)}) collective-permute-start(bf16[8,308]{1,0:T(8,128)(2,1)} %param.9), channel_id=1, source_target_pairs={{0,1},{1,0},{2,3},{3,2},{4,5},{5,4},{6,7},{7,6},{8,9},{9,8},{10,11... | collective-permute-start | bytes 14792 | tf_op jit(solution)/shard_map/ppermute | solution.py:20
  15.2 4.0 %copy-start.8 = (s32[3]{0:T(128)S(1)}, s32[3]{0:T(128)}, u32[]{:S(2)}) copy-start(s32[3]{0:T(128)} %get-tuple-element.36) | copy-start | bytes 40
  15.2 11.2 %copy-start.1 = (bf16[308,616]{1,0:T(8,128)(2,1)S(1)}, bf16[308,616]{1,0:T(8,128)(2,1)}, u32[]{:S(2)}) copy-start(bf16[308,616]{1,0:T(8,128)(2,1)} %param.8) | copy-start | bytes 1138372
  19.2 18.4 %collective-permute-start = (s32[3]{0:T(128)S(1)}, s32[3]{0:T(128)S(1)}, u32[]{:S(2)}, u32[]{:S(2)}) collective-permute-start(s32[3]{0:T(128)S(1)} %copy-done.8), channel_id=1, source_target_pairs={{0,254},{2,0},{4,2},{6,4},{8,6},{10,8},{12,10},{14,12},{16,14},{18... | collective-permute-start | bytes 44 | tf_op jit(solution)/shard_map/ppermute | solution.py:16
  38.0 11.6 %collective-permute-start.5 = (bf16[3,64,411]{2,1,0:T(8,128)(2,1)S(1)}, bf16[3,64,411]{2,1,0:T(8,128)(2,1)S(1)}, u32[]{:S(2)}, u32[]{:S(2)}) collective-permute-start(bf16[3,64,411]{2,1,0:T(8,128)(2,1)S(1)} %copy.35), channel_id=1, source_target_pairs={{0,2},{2,4},{4,6},{6,8},{8,10},{10,12},{12,14},{14,16},{16,18},{18... | collective-permute-start | bytes 473480 | tf_op jit(solution)/shard_map/ppermute | solution.py:16
  40.2 10.6 %collective-permute-start.6 = (bf16[3,64,411]{2,1,0:T(8,128)(2,1)S(1)}, bf16[3,64,411]{2,1,0:T(8,128)(2,1)S(1)}, u32[]{:S(2)}, u32[]{:S(2)}) collective-permute-start(bf16[3,64,411]{2,1,0:T(8,128)(2,1)S(1)} %copy.33), channel_id=1, source_target_pairs={{0,254},{2,0},{4,2},{6,4},{8,6},{10,8},{12,10},{14,12},{16,14},{18... | collective-permute-start | bytes 473480 | tf_op jit(solution)/shard_map/ppermute | solution.py:16
  47.1 8.2 %collective-permute-start.7 = (bf16[3,64,411]{2,1,0:T(8,128)(2,1)S(1)}, bf16[3,64,411]{2,1,0:T(8,128)(2,1)S(1)}, u32[]{:S(2)}, u32[]{:S(2)}) collective-permute-start(bf16[3,64,411]{2,1,0:T(8,128)(2,1)S(1)} %copy.32), channel_id=1, source_target_pairs={{0,252},{2,254},{4,0},{6,2},{8,4},{10,6},{12,8},{14,10},{16,12},{1... | collective-permute-start | bytes 473480 | tf_op jit(solution)/shard_map/ppermute | solution.py:16
  48.2 18.7 %copy-start.7 = (s32[8]{0:T(128)S(1)}, s32[8]{0:T(128)}, u32[]{:S(2)}) copy-start(s32[8]{0:T(128)} %copy-done.6) | copy-start | bytes 100
  49.6 5.7 %copy-start.2 = (bf16[3,64,411]{2,1,0:T(8,128)(2,1)}, bf16[3,64,411]{2,1,0:T(8,128)(2,1)S(1)}, u32[]{:S(2)}) copy-start(bf16[3,64,411]{2,1,0:T(8,128)(2,1)S(1)} %collective-permute-done.5.s0_ref) | copy-start | bytes 473476
  50.8 4.5 %copy-start.3 = (bf16[3,64,411]{2,1,0:T(8,128)(2,1)}, bf16[3,64,411]{2,1,0:T(8,128)(2,1)S(1)}, u32[]{:S(2)}) copy-start(bf16[3,64,411]{2,1,0:T(8,128)(2,1)S(1)} %collective-permute-done.6.s2_ref) | copy-start | bytes 473476
  55.3 0.7 copy-start.4
  69.0 10.5 %collective-permute-start.9 = (bf16[3,64,411]{2,0,1:T(4,128)(2,1)S(1)}, bf16[3,64,411]{2,0,1:T(4,128)(2,1)S(1)}, u32[]{:S(2)}, u32[]{:S(2)}) collective-permute-start(bf16[3,64,411]{2,0,1:T(4,128)(2,1)S(1)} %get-tuple-element.23), channel_id=1, source_target_pairs={{0,254},{2,0},{4,2},{6,4},{8,6},{10,8},{12,10},{14,12},{16,14},{18... | collective-permute-start | bytes 473480 | tf_op jit(solution)/shard_map/ppermute | solution.py:16
  75.9 14.4 %collective-permute-start.11 = (bf16[3,64,411]{2,0,1:T(4,128)(2,1)S(1)}, bf16[3,64,411]{2,0,1:T(4,128)(2,1)S(1)}, u32[]{:S(2)}, u32[]{:S(2)}) collective-permute-start(bf16[3,64,411]{2,0,1:T(4,128)(2,1)S(1)} %get-tuple-element.24), channel_id=1, source_target_pairs={{0,4},{2,6},{4,8},{6,10},{8,12},{10,14},{12,16},{14,18},{16,20},{1... | collective-permute-start | bytes 473480 | tf_op jit(solution)/shard_map/ppermute | solution.py:16
  75.9 14.4 %collective-permute-start.10 = (bf16[3,64,411]{2,0,1:T(4,128)(2,1)S(1)}, bf16[3,64,411]{2,0,1:T(4,128)(2,1)S(1)}, u32[]{:S(2)}, u32[]{:S(2)}) collective-permute-start(bf16[3,64,411]{2,0,1:T(4,128)(2,1)S(1)} %get-tuple-element.25), channel_id=1, source_target_pairs={{0,2},{2,4},{4,6},{6,8},{8,10},{10,12},{12,14},{14,16},{16,18},{18... | collective-permute-start | bytes 473480 | tf_op jit(solution)/shard_map/ppermute | solution.py:16
  91.2 7.9 %collective-permute-start.12 = (bf16[16,64,411]{2,0,1:T(8,128)(2,1)S(1)}, bf16[16,64,411]{2,0,1:T(8,128)(2,1)S(1)}, u32[]{:S(2)}, u32[]{:S(2)}) collective-permute-start(bf16[16,64,411]{2,0,1:T(8,128)(2,1)S(1)} %convolution_convert_fusion), channel_id=1, source_target_pairs={{0,1},{1,0},{2,3},{3,2},{4,5},{5,4},{6,7},{7,6},{8,9},{9,8},{10,11... | collective-permute-start | bytes 2525192 | tf_op jit(solution)/shard_map/ppermute | solution.py:20

commit v4 on v3

--- a/solution.py
+++ b/solution.py
@@ -26,61 +26,39 @@
 
 def adjoint_kernel(place_ref, count_ref, s0_ref, s1_ref, s2_ref, s3_ref, jc_ref, jo_ref, ic_ref, io_ref,
                    rcc_ref, rco_ref, roc_ref, roo_ref, out_ref):
-    f = pl.program_id(0)
-    group = place_ref[f] // CAP
-    s = jnp.where(group == 0, s0_ref[0], jnp.where(group == 1, s1_ref[0],
-                  jnp.where(group == 2, s2_ref[0], s3_ref[0])))
-    jc = jc_ref[0]
-    jo = jo_ref[0]
-    ev_c = lax.dot_general(s, jc, NT, preferred_element_type=jnp.float32)
-    ev_o = lax.dot_general(s, jo, NT, preferred_element_type=jnp.float32)
-    dep_c = (ev_c - ic_ref[pl.ds(f, 1), :]).astype(jnp.bfloat16)
-    dep_o = (ev_o - io_ref[pl.ds(f, 1), :]).astype(jnp.bfloat16)
-    w_c = (jnp.dot(dep_c, rcc_ref[...], preferred_element_type=jnp.float32)
-           + jnp.dot(dep_o, roc_ref[...], preferred_element_type=jnp.float32)).astype(jnp.bfloat16)
-    w_o = (jnp.dot(dep_c, rco_ref[...], preferred_element_type=jnp.float32)
-           + jnp.dot(dep_o, roo_ref[...], preferred_element_type=jnp.float32)).astype(jnp.bfloat16)
-    adj = (jnp.dot(w_c, jc, preferred_element_type=jnp.float32)
-           + jnp.dot(w_o, jo, preferred_element_type=jnp.float32))
-    live = f < count_ref[0]
-    out_ref[0] = jnp.where(live, adj, 0.0).astype(out_ref.dtype)
-
-
-def copy_kernel(x_ref, o_ref):
-    o_ref[...] = x_ref[...]
-
-
-def row_major(x):
-    block = (1,) + x.shape[1:]
-    spec = pl.BlockSpec(block, lambda i: (i,) + (0,) * (x.ndim - 1))
-    return pl.pallas_call(copy_kernel, grid=(x.shape[0],), in_specs=[spec], out_specs=spec,
-                          out_shape=jax.ShapeDtypeStruct(x.shape, x.dtype))(x)
+    parts = (s0_ref, s1_ref, s2_ref, s3_ref)
+    foot = out_ref.shape[0]
+    for f in range(foot):
+        group = place_ref[f] // CAP
+        rank = place_ref[f] % CAP
+        s = parts[3][rank]
+        for g in (2, 1, 0):
+            s = jnp.where(group == g, parts[g][rank], s)
+        jc = jc_ref[:, f, :]
+        jo = jo_ref[:, f, :]
+        ev_c = lax.dot_general(s, jc, NT, preferred_element_type=jnp.float32)
+        ev_o = lax.dot_general(s, jo, NT, preferred_element_type=jnp.float32)
+        dep_c = (ev_c - ic_ref[f:f + 1, :]).astype(jnp.bfloat16)
+        dep_o = (ev_o - io_ref[f:f + 1, :]).astype(jnp.bfloat16)
+        w_c = (jnp.dot(dep_c, rcc_ref[...], preferred_element_type=jnp.float32)
+               + jnp.dot(dep_o, roc_ref[...], preferred_element_type=jnp.float32)).astype(jnp.bfloat16)
+        w_o = (jnp.dot(dep_c, rco_ref[...], preferred_element_type=jnp.float32)
+               + jnp.dot(dep_o, roo_ref[...], preferred_element_type=jnp.float32)).astype(jnp.bfloat16)
+        adj = (jnp.dot(w_c, jc, preferred_element_type=jnp.float32)
+               + jnp.dot(w_o, jo, preferred_element_type=jnp.float32))
+        live = f < count_ref[0]
+        out_ref[f] = jnp.where(live, adj, 0.0).astype(out_ref.dtype)
 
 
 def adjoints(place, count, fetched, jac_c, jac_o, innov_c, innov_o, r_blocks):
-    foot, half_ch, state = jac_c.shape
+    half_ch, foot, state = jac_c.shape
     half_m = fetched[0].shape[1]
-    full = lambda f, p, n: (0, 0)
-
-    def part(g):
-        return pl.BlockSpec((1, half_m, state),
-                            lambda f, p, n: (jnp.where(p[f] // CAP == g, p[f] % CAP, 0), 0, 0))
-
-    grid_spec = pltpu.PrefetchScalarGridSpec(
-        num_scalar_prefetch=2,
-        grid=(foot,),
-        in_specs=[
-            part(0), part(1), part(2), part(3),
-            pl.BlockSpec((1, half_ch, state), lambda f, p, n: (f, 0, 0)),
-            pl.BlockSpec((1, half_ch, state), lambda f, p, n: (f, 0, 0)),
-            pl.BlockSpec((foot, half_ch), full),
-            pl.BlockSpec((foot, half_ch), full),
-        ] + [pl.BlockSpec((half_ch, half_ch), full) for _ in range(4)],
-        out_specs=pl.BlockSpec((1, half_m, state), lambda f, p, n: (f, 0, 0)),
-    )
+    smem = pl.BlockSpec(memory_space=pltpu.SMEM)
+    vmem = pl.BlockSpec(memory_space=pltpu.VMEM)
     return pl.pallas_call(
         adjoint_kernel,
-        grid_spec=grid_spec,
+        in_specs=[smem, smem] + [vmem] * 12,
+        out_specs=vmem,
         out_shape=jax.ShapeDtypeStruct((foot, half_m, state), jnp.bfloat16),
     )(place, count, *fetched, jac_c, jac_o, innov_c, innov_o, *r_blocks)
 
@@ -96,8 +74,8 @@
     capacity = CAP
     slots_total = SPAN * capacity
 
-    jac_c = jacobian
-    jac_o = row_major(swapped(jacobian))
+    jac_c = jnp.transpose(jacobian, (1, 0, 2))
+    jac_o = jnp.transpose(swapped(jacobian), (1, 0, 2))
     innov_c = innovation.astype(jnp.float32)
     innov_o = swapped(innovation).astype(jnp.float32)
     r_o = swapped(r_inverse)
@@ -131,7 +109,6 @@
     for g in range(SPAN):
         wanted = request[g * capacity:(g + 1) * capacity]
         slot_parts.append(wanted if g == 1 else passed_along(wanted, "tile", g - 1))
-    slot_parts, jac_o, r_blocks = lax.optimization_barrier((slot_parts, jac_o, r_blocks))
     fetched_parts = []
     for g in range(SPAN):
         picked = pick(slot_parts[g])

time: 107 us -> 89.8 us (0.84)
  starting transfers between devices: 32 us -> 22.5 us
  local copies, waits for them, and re-layouts: 20.6 us -> 12 us
  waiting for transfers between devices: 23 us -> 27.8 us
  Pallas kernels: 16.8 us -> 15.2 us
  matrix products: 5.25 us -> 3.97 us
    unnamed x20 -> x14, local copies, waits for them, and re-layouts: 8.04 us -> 0.67 us
    ppermute x9, starting transfers between devices: 22.2 us -> 15.3 us  [passed_along(): lax.ppermute(value, axis, [(i, (i + by) % count) for i in range(count)])]
    ppermute x9, waiting for transfers between devices: 20.7 us -> 25.5 us  [passed_along(): lax.ppermute(value, axis, [(i, (i + by) % count) for i in range(count)])]
    ppermute x1 -> x0, local copies, waits for them, and re-layouts: 4 us -> none  [swapped(): return lax.ppermute(value, 'chan', [(0, 1), (1, 0)])]
    dynamic_slice x1 -> x2, local copies, waits for them, and re-layouts: 1.69 us -> 5.04 us  [on_device(): lax.dynamic_slice_in_dim(increments, core * half_m, half_m, axis=1)]
    ppermute x4, starting transfers between devices: 9.78 us -> 7.15 us  [swapped(): return lax.ppermute(value, 'chan', [(0, 1), (1, 0)])]
    pallas_call x2 -> x1, Pallas kernels: 16.8 us -> 15.2 us  [adjoints(): pl.pallas_call(adjoint_kernel, in_specs=[smem, smem] + [vmem] * 12, out_s...]
    dot_general x4, matrix products: 2.67 us -> 1.4 us  [pick(): jnp.einsum('ac,cms->ams', one_hot(index, columns), own_inc, preferred_ele...]
  transfers between devices with their start and end apart: 13 -> 13, of which waited for: 6 -> 6; matrix products, arithmetic and copies ran while one was open for 21% -> 14% of each run, Pallas kernels for 5% -> 0%
where the time goes in v4:
time: 89.8 us; the launch traced here: 89.5 us
  waiting for transfers between devices  27.8 us (31%)
  starting transfers between devices  22.5 us (25%)
  Pallas kernels  15.2 us (17%)
  local copies, waits for them, and re-layouts  12 us (13%)
  other arithmetic  7.32 us (8%)
  matrix products  3.97 us (4%)
    ppermute x9, waiting for transfers between devices, passed_along(): lax.ppermute(value, axis, [(i, (i + by) % count) for i in range(count)])  25.5 us
    ppermute x9, starting transfers between devices, passed_along(): lax.ppermute(value, axis, [(i, (i + by) % count) for i in range(count)])  15.3 us
    pallas_call x1, Pallas kernels, adjoints(): pl.pallas_call(adjoint_kernel, in_specs=[smem, smem] + [vmem] * 12, out_s...  15.2 us
    ppermute x4, starting transfers between devices, swapped(): return lax.ppermute(value, 'chan', [(0, 1), (1, 0)])  7.15 us
    dynamic_slice x2, local copies, waits for them, and re-layouts, on_device(): lax.dynamic_slice_in_dim(increments, core * half_m, half_m, axis=1)  5.04 us
    select_n x1, local copies, waits for them, and re-layouts, on_device(): jnp.where(first, jnp.concatenate([mine, other], axis=1), jnp.concatenate(...  4.94 us
    ppermute x4, waiting for transfers between devices, swapped(): return lax.ppermute(value, 'chan', [(0, 1), (1, 0)])  2.29 us
    select_n x1, other arithmetic, on_device(): jnp.where(first, jnp.concatenate([mine, other], axis=1), jnp.concatenate(...  1.81 us
  transfers between devices with their start and end apart: 13, of which 6 were waited for; matrix products, arithmetic and copies ran while one was open for 14% of the time, Pallas kernels for 0%

profile of v4, /device:TPU:1, one launch (start us, length us, event | category | flops | bytes accessed | tf_op | source)
XLA Modules:
  0.0 89.5 jit_solution(6808742298383451119)
XLA Ops:
  0.0 3.2 %collective-permute-start.6 = (bf16[8,308,411]{2,0,1:T(8,128)(2,1)}, bf16[8,308,411]{2,0,1:T(8,128)(2,1)}, u32[]{:S(2)}, u32[]{:S(2)}) collective-permute-start(bf16[8,308,411]{2,0,1:T(8,128)(2,1)} %param.7), channel_id=1, source_target_pairs={{0,1},{1,0},{2,3},{3,2},{4,5},{5,4},{6,7},{7,6},{8,9},{9,8},{10,11... | collective-permute-start | bytes 6076232 | tf_op jit(solution)/shard_map/ppermute | solution.py:20
  3.2 0.9 %convert_reduce_fusion = s32[8]{0:T(128)S(1)} fusion(s32[8]{0:T(128)} %bitcast.27), kind=kLoop, calls=%fused_computation.27 | loop fusion | flops 312 | bytes 64 | tf_op jit(solution)/shard_map/reduce_sum | solution.py:97
  4.1 0.7 multiply_add_fusion.place_ref
  4.8 0.7 select_reduce_fusion
  5.5 0.1 fusion.33
  5.6 1.2 %collective-permute-start.2 = (s32[3]{0:T(128)S(1)}, s32[3]{0:T(128)S(1)}, u32[]{:S(2)}, u32[]{:S(2)}) collective-permute-start(s32[3]{0:T(128)S(1)} %get-tuple-element.15), channel_id=1, source_target_pairs={{0,4},{2,6},{4,8},{6,10},{8,12},{10,14},{12,16},{14,18},{16,20},{1... | collective-permute-start | bytes 44 | tf_op jit(solution)/shard_map/ppermute | solution.py:16
  6.8 0.4 collective-permute-start.1
  7.2 7.1 %collective-permute-start = (s32[3]{0:T(128)S(1)}, s32[3]{0:T(128)S(1)}, u32[]{:S(2)}, u32[]{:S(2)}) collective-permute-start(s32[3]{0:T(128)S(1)} %get-tuple-element.18), channel_id=1, source_target_pairs={{0,254},{2,0},{4,2},{6,4},{8,6},{10,8},{12,10},{14,12},{16,14},{18... | collective-permute-start | bytes 44 | tf_op jit(solution)/shard_map/ppermute | solution.py:16
  14.3 0.4 collective-permute-start.7
  14.6 1.3 %convert_element_type.38.ic_ref = f32[8,308]{1,0:T(8,128)} convert(bf16[8,308]{1,0:T(8,128)(2,1)} %param.9) | non-fusion elementwise | flops 2464 | bytes 14784 | tf_op jit(solution)/shard_map/convert_element_type | solution.py:79
  16.6 1.7 %constant_dynamic-slice_fusion = bf16[16,64,411]{1,0,2:T(8,128)(2,1)} fusion(bf16[16,128,411]{1,0,2:T(8,128)(2,1)S(1)} %copy-done, s32[]{:T(128)S(6)} %select_n.49), kind=kLoop, calls=%fused_computation.49 | loop fusion | bytes 1683460 | tf_op jit(solution)/shard_map/dynamic_slice | solution.py:102
  18.3 3.3 %copy.12 = bf16[16,64,411]{2,0,1:T(8,128)(2,1)S(1)} copy(bf16[16,64,411]{1,0,2:T(8,128)(2,1)} %constant_dynamic-slice_fusion) | data formatting | bytes 1683456 | tf_op jit(solution)/shard_map/dynamic_slice | solution.py:102
  21.7 0.4 fusion.19
  22.0 0.7 copy.25.s1_ref
  22.7 0.0 collective-permute-done.2
  22.8 0.2 collective-permute-start.8
  22.9 0.3 fusion.25
  23.3 2.4 %collective-permute-start.5 = (bf16[3,64,411]{2,1,0:T(8,128)(2,1)S(1)}, bf16[3,64,411]{2,1,0:T(8,128)(2,1)S(1)}, u32[]{:S(2)}, u32[]{:S(2)}) collective-permute-start(bf16[3,64,411]{2,1,0:T(8,128)(2,1)S(1)} %copy.23), channel_id=1, source_target_pairs={{0,252},{2,254},{4,0},{6,2},{8,4},{10,6},{12,8},{14,10},{16,12},{1... | collective-permute-start | bytes 473480 | tf_op jit(solution)/shard_map/ppermute | solution.py:16
  25.7 0.3 fusion.22
  26.1 0.0 collective-permute-done
  26.1 2.4 %collective-permute-start.4 = (bf16[3,64,411]{2,1,0:T(8,128)(2,1)S(1)}, bf16[3,64,411]{2,1,0:T(8,128)(2,1)S(1)}, u32[]{:S(2)}, u32[]{:S(2)}) collective-permute-start(bf16[3,64,411]{2,1,0:T(8,128)(2,1)S(1)} %copy.24), channel_id=1, source_target_pairs={{0,254},{2,0},{4,2},{6,4},{8,6},{10,8},{12,10},{14,12},{16,14},{18... | collective-permute-start | bytes 473480 | tf_op jit(solution)/shard_map/ppermute | solution.py:16
  28.6 0.3 fusion.16
  29.0 0.0 collective-permute-done.7
  29.0 0.3 collective-permute-start.3
  29.3 0.6 convert_element_type.39.io_ref
  29.9 0.0 collective-permute-done.8
  29.9 0.1 broadcast_select_fusion.1
  29.9 1.2 %broadcast_select_fusion.2 = (bf16[308,308]{1,0:T(8,128)(2,1)}, bf16[308,308]{1,0:T(8,128)(2,1)}, bf16[308,308]{1,0:T(8,128)(2,1)}, bf16[308,308]{1,0:T(8,128)(2,1)}) fusion(pred[]{:T(512)S(6)} %eq.44, bf16[308,616]{1,0:T(8,128)(2,1)S(1)} %get-tuple-element.14, bf16[308,616]{1,0:T(8,128)(2,1)S(1)} %get-tuple-element.13), kind=kLoop, calls=%fused_computation.17 | loop fusion | flops 379456 | bytes 1517825 | tf_op jit(solution)/shard_map/jit(_where)/select_n | solution.py:91
  31.1 0.0 collective-permute-done.5.s3_ref
  31.1 2.6 %collective-permute-done.4.s2_ref = bf16[3,64,411]{2,1,0:T(8,128)(2,1)S(1)} collective-permute-done((bf16[3,64,411]{2,1,0:T(8,128)(2,1)S(1)}, bf16[3,64,411]{2,1,0:T(8,128)(2,1)S(1)}, u32[]{:S(2)}, u32[]{:S(2)}) %collective-permute-start.4) | collective-permute-done | bytes 157856 | tf_op jit(solution)/shard_map/ppermute | solution.py:16
  33.7 6.4 %collective-permute-done.3.s0_ref = bf16[3,64,411]{2,1,0:T(8,128)(2,1)S(1)} collective-permute-done((bf16[3,64,411]{2,1,0:T(8,128)(2,1)S(1)}, bf16[3,64,411]{2,1,0:T(8,128)(2,1)S(1)}, u32[]{:S(2)}, u32[]{:S(2)}) %collective-permute-start.3) | collective-permute-done | bytes 157856 | tf_op jit(solution)/shard_map/ppermute | solution.py:16
  40.1 0.0 collective-permute-done.6
  40.1 0.6 copy-done.4
  40.7 15.2 %shard_map.73 = bf16[8,64,411]{2,1,0:T(8,128)(2,1)} custom-call(s32[8]{0:T(128)} %copy-done.5, s32[1]{0:T(128)S(6)} %copy.27.count_ref, bf16[3,64,411]{2,1,0:T(8,128)(2,1)} %copy-done.4, bf16[3,64,411]{2,1,0:T(8,128)(2,1)} %copy.25.s1_ref, bf16[3,64,411]{2,1,0:T(8,128)(2,1)} %copy-done.3, bf16[3,64,411]{2,1,0:T(8,128)(2,1)} %copy-done.2, ...), custom_call_target="tpu_custom_call" | custom-call | tf_op jit(solution)/shard_map/pallas_call | solution.py:58
  55.9 1.6 %convolution_convert_fusion.1 = bf16[12,64,411]{2,0,1:T(8,128)(2,1)S(1)} fusion(bf16[8,64,411]{2,1,0:T(8,128)(2,1)} %shard_map.73, s32[8]{0:T(128)S(1)} %copy-done.6), kind=kOutput, calls=%fused_computation.2 | convolution fusion | flops 5366112 | bytes 1052192 | tf_op jit(solution)/shard_map/af,fmd->amd/dot_general | solution.py:118
  57.6 0.4 fusion.32
  58.0 1.4 %collective-permute-start.9 = (bf16[3,64,411]{2,0,1:T(4,128)(2,1)S(1)}, bf16[3,64,411]{2,0,1:T(4,128)(2,1)S(1)}, u32[]{:S(2)}, u32[]{:S(2)}) collective-permute-start(bf16[3,64,411]{2,0,1:T(4,128)(2,1)S(1)} %get-tuple-element.5), channel_id=1, source_target_pairs={{0,254},{2,0},{4,2},{6,4},{8,6},{10,8},{12,10},{14,12},{16,14},{18... | collective-permute-start | bytes 473480 | tf_op jit(solution)/shard_map/ppermute | solution.py:16
  59.4 0.0 collective-permute-start.11
  59.4 0.1 collective-permute-start.10
  59.5 0.1 pad_add_fusion
  59.6 4.4 %collective-permute-done.9 = bf16[3,64,411]{2,0,1:T(4,128)(2,1)S(1)} collective-permute-done((bf16[3,64,411]{2,0,1:T(4,128)(2,1)S(1)}, bf16[3,64,411]{2,0,1:T(4,128)(2,1)S(1)}, u32[]{:S(2)}, u32[]{:S(2)}) %collective-permute-start.9) | collective-permute-done | bytes 157856 | tf_op jit(solution)/shard_map/ppermute | solution.py:16
  64.0 7.5 %collective-permute-done.11 = bf16[3,64,411]{2,0,1:T(4,128)(2,1)S(1)} collective-permute-done((bf16[3,64,411]{2,0,1:T(4,128)(2,1)S(1)}, bf16[3,64,411]{2,0,1:T(4,128)(2,1)S(1)}, u32[]{:S(2)}, u32[]{:S(2)}) %collective-permute-start.11) | collective-permute-done | bytes 157856 | tf_op jit(solution)/shard_map/ppermute | solution.py:16
  71.5 4.6 %collective-permute-done.10 = bf16[3,64,411]{2,0,1:T(4,128)(2,1)S(1)} collective-permute-done((bf16[3,64,411]{2,0,1:T(4,128)(2,1)S(1)}, bf16[3,64,411]{2,0,1:T(4,128)(2,1)S(1)}, u32[]{:S(2)}, u32[]{:S(2)}) %collective-permute-start.10) | collective-permute-done | bytes 157856 | tf_op jit(solution)/shard_map/ppermute | solution.py:16
  76.1 1.0 %convolution_convert_fusion = bf16[16,64,411]{2,0,1:T(8,128)(2,1)S(1)} fusion(bf16[3,64,411]{2,0,1:T(4,128)(2,1)S(1)} %collective-permute-done.11, bf16[3,64,411]{2,0,1:T(4,128)(2,1)S(1)} %collective-permute-done.10, bf16[3,64,411]{2,0,1:T(4,128)(2,1)S(1)} %get-tuple-element.8, bf16[3,64,411]{2,0,1:T(4,128)(2,1)S(1)} %collective-permute-done.9, ...), kind=kOutput, calls=%fused_computation.1 | convolution fusion | flops 13046976 | bytes 1473072 | tf_op jit(solution)/shard_map/ac,amd->cmd/dot_general | solution.py:128
  77.1 3.4 %collective-permute-start.12 = (bf16[16,64,411]{2,0,1:T(8,128)(2,1)S(1)}, bf16[16,64,411]{2,0,1:T(8,128)(2,1)S(1)}, u32[]{:S(2)}, u32[]{:S(2)}) collective-permute-start(bf16[16,64,411]{2,0,1:T(8,128)(2,1)S(1)} %convolution_convert_fusion), channel_id=1, source_target_pairs={{0,1},{1,0},{2,3},{3,2},{4,5},{5,4},{6,7},{7,6},{8,9},{9,8},{10,11... | collective-permute-start | bytes 2525192 | tf_op jit(solution)/shard_map/ppermute | solution.py:20
  80.5 2.3 %collective-permute-done.12 = bf16[16,64,411]{2,0,1:T(8,128)(2,1)S(1)} collective-permute-done((bf16[16,64,411]{2,0,1:T(8,128)(2,1)S(1)}, bf16[16,64,411]{2,0,1:T(8,128)(2,1)S(1)}, u32[]{:S(2)}, u32[]{:S(2)}) %collective-permute-start.12) | collective-permute-done | bytes 841760 | tf_op jit(solution)/shard_map/ppermute | solution.py:20
  82.8 1.8 %maximum_select_fusion = bf16[16,128,411]{2,0,1:T(8,128)(2,1)} fusion(bf16[16,64,411]{2,0,1:T(8,128)(2,1)S(1)} %collective-permute-done.12, bf16[16,64,411]{2,0,1:T(8,128)(2,1)S(1)} %convolution_convert_fusion, pred[]{:T(512)S(6)} %eq.44), kind=kLoop, calls=%fused_computation | loop fusion | flops 2525184 | bytes 3366913 | tf_op jit(solution)/shard_map/jit(_where)/select_n | solution.py:131
  84.6 4.9 %copy.11 = bf16[16,128,411]{1,0,2:T(8,128)(2,1)} copy(bf16[16,128,411]{2,0,1:T(8,128)(2,1)} %maximum_select_fusion) | data formatting | bytes 3366912 | tf_op jit(solution)/shard_map/jit(_where)/select_n | solution.py:131
  (17 shorter events, 0.2 us)
Async XLA Ops:
  0.0 16.6 %copy-start = (bf16[16,128,411]{1,0,2:T(8,128)(2,1)S(1)}, bf16[16,128,411]{1,0,2:T(8,128)(2,1)}, u32[]{:S(2)}) copy-start(bf16[16,128,411]{1,0,2:T(8,128)(2,1)} %param.10) | copy-start | bytes 5050372
  0.0 40.1 %collective-permute-start.6 = (bf16[8,308,411]{2,0,1:T(8,128)(2,1)}, bf16[8,308,411]{2,0,1:T(8,128)(2,1)}, u32[]{:S(2)}, u32[]{:S(2)}) collective-permute-start(bf16[8,308,411]{2,0,1:T(8,128)(2,1)} %param.7), channel_id=1, source_target_pairs={{0,1},{1,0},{2,3},{3,2},{4,5},{5,4},{6,7},{7,6},{8,9},{9,8},{10,11... | collective-permute-start | bytes 6076232 | tf_op jit(solution)/shard_map/ppermute | solution.py:20
  4.8 16.9 %copy-start.5 = (s32[8]{0:T(128)}, s32[8]{0:T(128)S(1)}, u32[]{:S(2)}) copy-start(s32[8]{0:T(128)S(1)} %multiply_add_fusion.place_ref) | copy-start | bytes 100
  5.6 17.2 %collective-permute-start.2 = (s32[3]{0:T(128)S(1)}, s32[3]{0:T(128)S(1)}, u32[]{:S(2)}, u32[]{:S(2)}) collective-permute-start(s32[3]{0:T(128)S(1)} %get-tuple-element.15), channel_id=1, source_target_pairs={{0,4},{2,6},{4,8},{6,10},{8,12},{10,14},{12,16},{14,18},{16,20},{1... | collective-permute-start | bytes 44 | tf_op jit(solution)/shard_map/ppermute | solution.py:16
  6.8 16.5 %collective-permute-start.1 = (s32[3]{0:T(128)S(1)}, s32[3]{0:T(128)S(1)}, u32[]{:S(2)}, u32[]{:S(2)}) collective-permute-start(s32[3]{0:T(128)S(1)} %get-tuple-element.16), channel_id=1, source_target_pairs={{0,2},{2,4},{4,6},{6,8},{8,10},{10,12},{12,14},{14,16},{16,18},{18... | collective-permute-start | bytes 44 | tf_op jit(solution)/shard_map/ppermute | solution.py:16
  7.2 18.9 %collective-permute-start = (s32[3]{0:T(128)S(1)}, s32[3]{0:T(128)S(1)}, u32[]{:S(2)}, u32[]{:S(2)}) collective-permute-start(s32[3]{0:T(128)S(1)} %get-tuple-element.18), channel_id=1, source_target_pairs={{0,254},{2,0},{4,2},{6,4},{8,6},{10,8},{12,10},{14,12},{16,14},{18... | collective-permute-start | bytes 44 | tf_op jit(solution)/shard_map/ppermute | solution.py:16
  14.3 14.7 %collective-permute-start.7 = (bf16[8,308]{1,0:T(8,128)(2,1)}, bf16[8,308]{1,0:T(8,128)(2,1)S(1)}, u32[]{:S(2)}, u32[]{:S(2)}) collective-permute-start(bf16[8,308]{1,0:T(8,128)(2,1)} %param.9), channel_id=1, source_target_pairs={{0,1},{1,0},{2,3},{3,2},{4,5},{5,4},{6,7},{7,6},{8,9},{9,8},{10,11... | collective-permute-start | bytes 14792 | tf_op jit(solution)/shard_map/ppermute | solution.py:20
  18.3 4.5 %copy-start.1 = (bf16[308,616]{1,0:T(8,128)(2,1)S(1)}, bf16[308,616]{1,0:T(8,128)(2,1)}, u32[]{:S(2)}) copy-start(bf16[308,616]{1,0:T(8,128)(2,1)} %param.8) | copy-start | bytes 1138372
  22.8 7.1 %collective-permute-start.8 = (bf16[308,616]{1,0:T(8,128)(2,1)S(1)}, bf16[308,616]{1,0:T(8,128)(2,1)S(1)}, u32[]{:S(2)}, u32[]{:S(2)}) collective-permute-start(bf16[308,616]{1,0:T(8,128)(2,1)S(1)} %copy-done.1), channel_id=1, source_target_pairs={{0,1},{1,0},{2,3},{3,2},{4,5},{5,4},{6,7},{7,6},{8,9},{9,8},{10,11... | collective-permute-start | bytes 1138376 | tf_op jit(solution)/shard_map/ppermute | solution.py:20
  23.3 7.8 %collective-permute-start.5 = (bf16[3,64,411]{2,1,0:T(8,128)(2,1)S(1)}, bf16[3,64,411]{2,1,0:T(8,128)(2,1)S(1)}, u32[]{:S(2)}, u32[]{:S(2)}) collective-permute-start(bf16[3,64,411]{2,1,0:T(8,128)(2,1)S(1)} %copy.23), channel_id=1, source_target_pairs={{0,252},{2,254},{4,0},{6,2},{8,4},{10,6},{12,8},{14,10},{16,12},{1... | collective-permute-start | bytes 473480 | tf_op jit(solution)/shard_map/ppermute | solution.py:16
  26.1 7.6 %collective-permute-start.4 = (bf16[3,64,411]{2,1,0:T(8,128)(2,1)S(1)}, bf16[3,64,411]{2,1,0:T(8,128)(2,1)S(1)}, u32[]{:S(2)}, u32[]{:S(2)}) collective-permute-start(bf16[3,64,411]{2,1,0:T(8,128)(2,1)S(1)} %copy.24), channel_id=1, source_target_pairs={{0,254},{2,0},{4,2},{6,4},{8,6},{10,8},{12,10},{14,12},{16,14},{18... | collective-permute-start | bytes 473480 | tf_op jit(solution)/shard_map/ppermute | solution.py:16
  29.0 11.1 %collective-permute-start.3 = (bf16[3,64,411]{2,1,0:T(8,128)(2,1)S(1)}, bf16[3,64,411]{2,1,0:T(8,128)(2,1)S(1)}, u32[]{:S(2)}, u32[]{:S(2)}) collective-permute-start(bf16[3,64,411]{2,1,0:T(8,128)(2,1)S(1)} %copy.26), channel_id=1, source_target_pairs={{0,2},{2,4},{4,6},{6,8},{8,10},{10,12},{12,14},{14,16},{16,18},{18... | collective-permute-start | bytes 473480 | tf_op jit(solution)/shard_map/ppermute | solution.py:16
  31.1 9.0 %copy-start.2 = (bf16[3,64,411]{2,1,0:T(8,128)(2,1)}, bf16[3,64,411]{2,1,0:T(8,128)(2,1)S(1)}, u32[]{:S(2)}) copy-start(bf16[3,64,411]{2,1,0:T(8,128)(2,1)S(1)} %collective-permute-done.5.s3_ref) | copy-start | bytes 473476
  33.7 6.4 %copy-start.3 = (bf16[3,64,411]{2,1,0:T(8,128)(2,1)}, bf16[3,64,411]{2,1,0:T(8,128)(2,1)S(1)}, u32[]{:S(2)}) copy-start(bf16[3,64,411]{2,1,0:T(8,128)(2,1)S(1)} %collective-permute-done.4.s2_ref) | copy-start | bytes 473476
  40.1 0.7 copy-start.4
  40.7 15.2 %copy-start.6 = (s32[8]{0:T(128)S(1)}, s32[8]{0:T(128)}, u32[]{:S(2)}) copy-start(s32[8]{0:T(128)} %copy-done.5) | copy-start | bytes 100
  58.0 6.0 %collective-permute-start.9 = (bf16[3,64,411]{2,0,1:T(4,128)(2,1)S(1)}, bf16[3,64,411]{2,0,1:T(4,128)(2,1)S(1)}, u32[]{:S(2)}, u32[]{:S(2)}) collective-permute-start(bf16[3,64,411]{2,0,1:T(4,128)(2,1)S(1)} %get-tuple-element.5), channel_id=1, source_target_pairs={{0,254},{2,0},{4,2},{6,4},{8,6},{10,8},{12,10},{14,12},{16,14},{18... | collective-permute-start | bytes 473480 | tf_op jit(solution)/shard_map/ppermute | solution.py:16
  59.4 12.1 %collective-permute-start.11 = (bf16[3,64,411]{2,0,1:T(4,128)(2,1)S(1)}, bf16[3,64,411]{2,0,1:T(4,128)(2,1)S(1)}, u32[]{:S(2)}, u32[]{:S(2)}) collective-permute-start(bf16[3,64,411]{2,0,1:T(4,128)(2,1)S(1)} %get-tuple-element.6), channel_id=1, source_target_pairs={{0,4},{2,6},{4,8},{6,10},{8,12},{10,14},{12,16},{14,18},{16,20},{1... | collective-permute-start | bytes 473480 | tf_op jit(solution)/shard_map/ppermute | solution.py:16
  59.4 16.7 %collective-permute-start.10 = (bf16[3,64,411]{2,0,1:T(4,128)(2,1)S(1)}, bf16[3,64,411]{2,0,1:T(4,128)(2,1)S(1)}, u32[]{:S(2)}, u32[]{:S(2)}) collective-permute-start(bf16[3,64,411]{2,0,1:T(4,128)(2,1)S(1)} %get-tuple-element.7), channel_id=1, source_target_pairs={{0,2},{2,4},{4,6},{6,8},{8,10},{10,12},{12,14},{14,16},{16,18},{18... | collective-permute-start | bytes 473480 | tf_op jit(solution)/shard_map/ppermute | solution.py:16
  77.1 5.7 %collective-permute-start.12 = (bf16[16,64,411]{2,0,1:T(8,128)(2,1)S(1)}, bf16[16,64,411]{2,0,1:T(8,128)(2,1)S(1)}, u32[]{:S(2)}, u32[]{:S(2)}) collective-permute-start(bf16[16,64,411]{2,0,1:T(8,128)(2,1)S(1)} %convolution_convert_fusion), channel_id=1, source_target_pairs={{0,1},{1,0},{2,3},{3,2},{4,5},{5,4},{6,7},{7,6},{8,9},{9,8},{10,11... | collective-permute-start | bytes 2525192 | tf_op jit(solution)/shard_map/ppermute | solution.py:20

commit v5 on v4

--- a/solution.py
+++ b/solution.py
@@ -28,6 +28,7 @@
                    rcc_ref, rco_ref, roc_ref, roo_ref, out_ref):
     parts = (s0_ref, s1_ref, s2_ref, s3_ref)
     foot = out_ref.shape[0]
+    jcs, jos, deps_c, deps_o = [], [], [], []
     for f in range(foot):
         group = place_ref[f] // CAP
         rank = place_ref[f] % CAP
@@ -36,16 +37,22 @@
             s = jnp.where(group == g, parts[g][rank], s)
         jc = jc_ref[:, f, :]
         jo = jo_ref[:, f, :]
+        jcs.append(jc)
+        jos.append(jo)
         ev_c = lax.dot_general(s, jc, NT, preferred_element_type=jnp.float32)
         ev_o = lax.dot_general(s, jo, NT, preferred_element_type=jnp.float32)
-        dep_c = (ev_c - ic_ref[f:f + 1, :]).astype(jnp.bfloat16)
-        dep_o = (ev_o - io_ref[f:f + 1, :]).astype(jnp.bfloat16)
-        w_c = (jnp.dot(dep_c, rcc_ref[...], preferred_element_type=jnp.float32)
-               + jnp.dot(dep_o, roc_ref[...], preferred_element_type=jnp.float32)).astype(jnp.bfloat16)
-        w_o = (jnp.dot(dep_c, rco_ref[...], preferred_element_type=jnp.float32)
-               + jnp.dot(dep_o, roo_ref[...], preferred_element_type=jnp.float32)).astype(jnp.bfloat16)
-        adj = (jnp.dot(w_c, jc, preferred_element_type=jnp.float32)
-               + jnp.dot(w_o, jo, preferred_element_type=jnp.float32))
+        deps_c.append((ev_c - ic_ref[f:f + 1, :]).astype(jnp.bfloat16))
+        deps_o.append((ev_o - io_ref[f:f + 1, :]).astype(jnp.bfloat16))
+    dep_c = jnp.concatenate(deps_c, axis=0)
+    dep_o = jnp.concatenate(deps_o, axis=0)
+    w_c = (jnp.dot(dep_c, rcc_ref[...], preferred_element_type=jnp.float32)
+           + jnp.dot(dep_o, roc_ref[...], preferred_element_type=jnp.float32)).astype(jnp.bfloat16)
+    w_o = (jnp.dot(dep_c, rco_ref[...], preferred_element_type=jnp.float32)
+           + jnp.dot(dep_o, roo_ref[...], preferred_element_type=jnp.float32)).astype(jnp.bfloat16)
+    rows = deps_c[0].shape[0]
+    for f in range(foot):
+        adj = (jnp.dot(w_c[f * rows:(f + 1) * rows], jcs[f], preferred_element_type=jnp.float32)
+               + jnp.dot(w_o[f * rows:(f + 1) * rows], jos[f], preferred_element_type=jnp.float32))
         live = f < count_ref[0]
         out_ref[f] = jnp.where(live, adj, 0.0).astype(out_ref.dtype)
 

time: 89.8 us -> 88.3 us (0.983)
  Pallas kernels: 15.2 us -> 13.7 us
    pallas_call x1, Pallas kernels: 15.2 us -> 13.7 us  [adjoints(): pl.pallas_call(adjoint_kernel, in_specs=[smem, smem] + [vmem] * 12, out_s...]
  transfers between devices with their start and end apart: 13 -> 13, of which waited for: 6 -> 6; matrix products, arithmetic and copies ran while one was open for 14% -> 15% of each run, Pallas kernels for 0% -> 0%
where the time goes in v5:
time: 88.3 us; the launch traced here: 88 us
  waiting for transfers between devices  27.7 us (31%)
  starting transfers between devices  22.5 us (25%)
  Pallas kernels  13.7 us (16%)
  local copies, waits for them, and re-layouts  12 us (14%)
  other arithmetic  7.32 us (8%)
  matrix products  3.97 us (4%)
    ppermute x9, waiting for transfers between devices, passed_along(): lax.ppermute(value, axis, [(i, (i + by) % count) for i in range(count)])  25.4 us
    ppermute x9, starting transfers between devices, passed_along(): lax.ppermute(value, axis, [(i, (i + by) % count) for i in range(count)])  15.3 us
    pallas_call x1, Pallas kernels, adjoints(): pl.pallas_call(adjoint_kernel, in_specs=[smem, smem] + [vmem] * 12, out_s...  13.7 us
    ppermute x4, starting transfers between devices, swapped(): return lax.ppermute(value, 'chan', [(0, 1), (1, 0)])  7.16 us
    dynamic_slice x2, local copies, waits for them, and re-layouts, on_device(): lax.dynamic_slice_in_dim(increments, core * half_m, half_m, axis=1)  5.04 us
    select_n x1, local copies, waits for them, and re-layouts, on_device(): jnp.where(first, jnp.concatenate([mine, other], axis=1), jnp.concatenate(...  4.94 us
    ppermute x4, waiting for transfers between devices, swapped(): return lax.ppermute(value, 'chan', [(0, 1), (1, 0)])  2.29 us
    select_n x1, other arithmetic, on_device(): jnp.where(first, jnp.concatenate([mine, other], axis=1), jnp.concatenate(...  1.81 us
  transfers between devices with their start and end apart: 13, of which 6 were waited for; matrix products, arithmetic and copies ran while one was open for 15% of the time, Pallas kernels for 0%

profile of v5, /device:TPU:1, one launch (start us, length us, event | category | flops | bytes accessed | tf_op | source)
XLA Modules:
  0.0 88.0 jit_solution(13448759962120289684)
XLA Ops:
  0.0 3.2 %collective-permute-start.6 = (bf16[8,308,411]{2,0,1:T(8,128)(2,1)}, bf16[8,308,411]{2,0,1:T(8,128)(2,1)}, u32[]{:S(2)}, u32[]{:S(2)}) collective-permute-start(bf16[8,308,411]{2,0,1:T(8,128)(2,1)} %param.7), channel_id=1, source_target_pairs={{0,1},{1,0},{2,3},{3,2},{4,5},{5,4},{6,7},{7,6},{8,9},{9,8},{10,11... | collective-permute-start | bytes 6076232 | tf_op jit(solution)/shard_map/ppermute | solution.py:20
  3.2 0.9 %convert_reduce_fusion = s32[8]{0:T(128)S(1)} fusion(s32[8]{0:T(128)} %bitcast.27), kind=kLoop, calls=%fused_computation.27 | loop fusion | flops 312 | bytes 64 | tf_op jit(solution)/shard_map/reduce_sum | solution.py:104
  4.1 0.7 multiply_add_fusion.place_ref
  4.8 0.7 select_reduce_fusion
  5.5 0.1 fusion.33
  5.6 1.2 %collective-permute-start.2 = (s32[3]{0:T(128)S(1)}, s32[3]{0:T(128)S(1)}, u32[]{:S(2)}, u32[]{:S(2)}) collective-permute-start(s32[3]{0:T(128)S(1)} %get-tuple-element.15), channel_id=1, source_target_pairs={{0,4},{2,6},{4,8},{6,10},{8,12},{10,14},{12,16},{14,18},{16,20},{1... | collective-permute-start | bytes 44 | tf_op jit(solution)/shard_map/ppermute | solution.py:16
  6.8 0.4 collective-permute-start.1
  7.2 7.1 %collective-permute-start = (s32[3]{0:T(128)S(1)}, s32[3]{0:T(128)S(1)}, u32[]{:S(2)}, u32[]{:S(2)}) collective-permute-start(s32[3]{0:T(128)S(1)} %get-tuple-element.18), channel_id=1, source_target_pairs={{0,254},{2,0},{4,2},{6,4},{8,6},{10,8},{12,10},{14,12},{16,14},{18... | collective-permute-start | bytes 44 | tf_op jit(solution)/shard_map/ppermute | solution.py:16
  14.3 0.4 collective-permute-start.7
  14.6 1.3 %convert_element_type.38.ic_ref = f32[8,308]{1,0:T(8,128)} convert(bf16[8,308]{1,0:T(8,128)(2,1)} %param.9) | non-fusion elementwise | flops 2464 | bytes 14784 | tf_op jit(solution)/shard_map/convert_element_type | solution.py:86
  16.6 1.7 %constant_dynamic-slice_fusion = bf16[16,64,411]{1,0,2:T(8,128)(2,1)} fusion(bf16[16,128,411]{1,0,2:T(8,128)(2,1)S(1)} %copy-done, s32[]{:T(128)S(6)} %select_n.49), kind=kLoop, calls=%fused_computation.49 | loop fusion | bytes 1683460 | tf_op jit(solution)/shard_map/dynamic_slice | solution.py:109
  18.3 3.3 %copy.12 = bf16[16,64,411]{2,0,1:T(8,128)(2,1)S(1)} copy(bf16[16,64,411]{1,0,2:T(8,128)(2,1)} %constant_dynamic-slice_fusion) | data formatting | bytes 1683456 | tf_op jit(solution)/shard_map/dynamic_slice | solution.py:109
  21.7 0.4 fusion.19
  22.0 0.7 copy.25.s1_ref
  22.7 0.0 collective-permute-done.2
  22.8 0.2 collective-permute-start.8
  22.9 0.3 fusion.25
  23.3 2.4 %collective-permute-start.5 = (bf16[3,64,411]{2,1,0:T(8,128)(2,1)S(1)}, bf16[3,64,411]{2,1,0:T(8,128)(2,1)S(1)}, u32[]{:S(2)}, u32[]{:S(2)}) collective-permute-start(bf16[3,64,411]{2,1,0:T(8,128)(2,1)S(1)} %copy.23), channel_id=1, source_target_pairs={{0,252},{2,254},{4,0},{6,2},{8,4},{10,6},{12,8},{14,10},{16,12},{1... | collective-permute-start | bytes 473480 | tf_op jit(solution)/shard_map/ppermute | solution.py:16
  25.7 0.3 fusion.22
  26.1 0.0 collective-permute-done
  26.1 2.4 %collective-permute-start.4 = (bf16[3,64,411]{2,1,0:T(8,128)(2,1)S(1)}, bf16[3,64,411]{2,1,0:T(8,128)(2,1)S(1)}, u32[]{:S(2)}, u32[]{:S(2)}) collective-permute-start(bf16[3,64,411]{2,1,0:T(8,128)(2,1)S(1)} %copy.24), channel_id=1, source_target_pairs={{0,254},{2,0},{4,2},{6,4},{8,6},{10,8},{12,10},{14,12},{16,14},{18... | collective-permute-start | bytes 473480 | tf_op jit(solution)/shard_map/ppermute | solution.py:16
  28.6 0.3 fusion.16
  29.0 0.0 collective-permute-done.7
  29.0 0.3 collective-permute-start.3
  29.3 0.6 convert_element_type.39.io_ref
  29.9 0.0 collective-permute-done.8
  29.9 0.1 broadcast_select_fusion.1
  29.9 1.2 %broadcast_select_fusion.2 = (bf16[308,308]{1,0:T(8,128)(2,1)}, bf16[308,308]{1,0:T(8,128)(2,1)}, bf16[308,308]{1,0:T(8,128)(2,1)}, bf16[308,308]{1,0:T(8,128)(2,1)}) fusion(pred[]{:T(512)S(6)} %eq.44, bf16[308,616]{1,0:T(8,128)(2,1)S(1)} %get-tuple-element.14, bf16[308,616]{1,0:T(8,128)(2,1)S(1)} %get-tuple-element.13), kind=kLoop, calls=%fused_computation.17 | loop fusion | flops 379456 | bytes 1517825 | tf_op jit(solution)/shard_map/jit(_where)/select_n | solution.py:98
  31.1 0.0 collective-permute-done.5.s3_ref
  31.1 2.6 %collective-permute-done.4.s2_ref = bf16[3,64,411]{2,1,0:T(8,128)(2,1)S(1)} collective-permute-done((bf16[3,64,411]{2,1,0:T(8,128)(2,1)S(1)}, bf16[3,64,411]{2,1,0:T(8,128)(2,1)S(1)}, u32[]{:S(2)}, u32[]{:S(2)}) %collective-permute-start.4) | collective-permute-done | bytes 157856 | tf_op jit(solution)/shard_map/ppermute | solution.py:16
  33.7 6.4 %collective-permute-done.3.s0_ref = bf16[3,64,411]{2,1,0:T(8,128)(2,1)S(1)} collective-permute-done((bf16[3,64,411]{2,1,0:T(8,128)(2,1)S(1)}, bf16[3,64,411]{2,1,0:T(8,128)(2,1)S(1)}, u32[]{:S(2)}, u32[]{:S(2)}) %collective-permute-start.3) | collective-permute-done | bytes 157856 | tf_op jit(solution)/shard_map/ppermute | solution.py:16
  40.1 0.0 collective-permute-done.6
  40.1 0.6 copy-done.4
  40.7 13.7 %shard_map.73 = bf16[8,64,411]{2,1,0:T(8,128)(2,1)} custom-call(s32[8]{0:T(128)} %copy-done.5, s32[1]{0:T(128)S(6)} %copy.27.count_ref, bf16[3,64,411]{2,1,0:T(8,128)(2,1)} %copy-done.4, bf16[3,64,411]{2,1,0:T(8,128)(2,1)} %copy.25.s1_ref, bf16[3,64,411]{2,1,0:T(8,128)(2,1)} %copy-done.3, bf16[3,64,411]{2,1,0:T(8,128)(2,1)} %copy-done.2, ...), custom_call_target="tpu_custom_call" | custom-call | tf_op jit(solution)/shard_map/pallas_call | solution.py:65
  54.4 1.6 %convolution_convert_fusion.1 = bf16[12,64,411]{2,0,1:T(8,128)(2,1)S(1)} fusion(bf16[8,64,411]{2,1,0:T(8,128)(2,1)} %shard_map.73, s32[8]{0:T(128)S(1)} %copy-done.6), kind=kOutput, calls=%fused_computation.2 | convolution fusion | flops 5366112 | bytes 1052192 | tf_op jit(solution)/shard_map/af,fmd->amd/dot_general | solution.py:125
  56.1 0.4 fusion.32
  56.5 1.4 %collective-permute-start.9 = (bf16[3,64,411]{2,0,1:T(4,128)(2,1)S(1)}, bf16[3,64,411]{2,0,1:T(4,128)(2,1)S(1)}, u32[]{:S(2)}, u32[]{:S(2)}) collective-permute-start(bf16[3,64,411]{2,0,1:T(4,128)(2,1)S(1)} %get-tuple-element.5), channel_id=1, source_target_pairs={{0,254},{2,0},{4,2},{6,4},{8,6},{10,8},{12,10},{14,12},{16,14},{18... | collective-permute-start | bytes 473480 | tf_op jit(solution)/shard_map/ppermute | solution.py:16
  57.9 0.0 collective-permute-start.11
  57.9 0.1 collective-permute-start.10
  58.0 0.1 pad_add_fusion
  58.1 4.4 %collective-permute-done.9 = bf16[3,64,411]{2,0,1:T(4,128)(2,1)S(1)} collective-permute-done((bf16[3,64,411]{2,0,1:T(4,128)(2,1)S(1)}, bf16[3,64,411]{2,0,1:T(4,128)(2,1)S(1)}, u32[]{:S(2)}, u32[]{:S(2)}) %collective-permute-start.9) | collective-permute-done | bytes 157856 | tf_op jit(solution)/shard_map/ppermute | solution.py:16
  62.5 7.5 %collective-permute-done.11 = bf16[3,64,411]{2,0,1:T(4,128)(2,1)S(1)} collective-permute-done((bf16[3,64,411]{2,0,1:T(4,128)(2,1)S(1)}, bf16[3,64,411]{2,0,1:T(4,128)(2,1)S(1)}, u32[]{:S(2)}, u32[]{:S(2)}) %collective-permute-start.11) | collective-permute-done | bytes 157856 | tf_op jit(solution)/shard_map/ppermute | solution.py:16
  70.0 4.6 %collective-permute-done.10 = bf16[3,64,411]{2,0,1:T(4,128)(2,1)S(1)} collective-permute-done((bf16[3,64,411]{2,0,1:T(4,128)(2,1)S(1)}, bf16[3,64,411]{2,0,1:T(4,128)(2,1)S(1)}, u32[]{:S(2)}, u32[]{:S(2)}) %collective-permute-start.10) | collective-permute-done | bytes 157856 | tf_op jit(solution)/shard_map/ppermute | solution.py:16
  74.6 1.0 %convolution_convert_fusion = bf16[16,64,411]{2,0,1:T(8,128)(2,1)S(1)} fusion(bf16[3,64,411]{2,0,1:T(4,128)(2,1)S(1)} %collective-permute-done.11, bf16[3,64,411]{2,0,1:T(4,128)(2,1)S(1)} %collective-permute-done.10, bf16[3,64,411]{2,0,1:T(4,128)(2,1)S(1)} %get-tuple-element.8, bf16[3,64,411]{2,0,1:T(4,128)(2,1)S(1)} %collective-permute-done.9, ...), kind=kOutput, calls=%fused_computation.1 | convolution fusion | flops 13046976 | bytes 1473072 | tf_op jit(solution)/shard_map/ac,amd->cmd/dot_general | solution.py:135
  75.5 3.4 %collective-permute-start.12 = (bf16[16,64,411]{2,0,1:T(8,128)(2,1)S(1)}, bf16[16,64,411]{2,0,1:T(8,128)(2,1)S(1)}, u32[]{:S(2)}, u32[]{:S(2)}) collective-permute-start(bf16[16,64,411]{2,0,1:T(8,128)(2,1)S(1)} %convolution_convert_fusion), channel_id=1, source_target_pairs={{0,1},{1,0},{2,3},{3,2},{4,5},{5,4},{6,7},{7,6},{8,9},{9,8},{10,11... | collective-permute-start | bytes 2525192 | tf_op jit(solution)/shard_map/ppermute | solution.py:20
  79.0 2.3 %collective-permute-done.12 = bf16[16,64,411]{2,0,1:T(8,128)(2,1)S(1)} collective-permute-done((bf16[16,64,411]{2,0,1:T(8,128)(2,1)S(1)}, bf16[16,64,411]{2,0,1:T(8,128)(2,1)S(1)}, u32[]{:S(2)}, u32[]{:S(2)}) %collective-permute-start.12) | collective-permute-done | bytes 841760 | tf_op jit(solution)/shard_map/ppermute | solution.py:20
  81.3 1.8 %maximum_select_fusion = bf16[16,128,411]{2,0,1:T(8,128)(2,1)} fusion(bf16[16,64,411]{2,0,1:T(8,128)(2,1)S(1)} %collective-permute-done.12, bf16[16,64,411]{2,0,1:T(8,128)(2,1)S(1)} %convolution_convert_fusion, pred[]{:T(512)S(6)} %eq.44), kind=kLoop, calls=%fused_computation | loop fusion | flops 2525184 | bytes 3366913 | tf_op jit(solution)/shard_map/jit(_where)/select_n | solution.py:138
  83.1 4.9 %copy.11 = bf16[16,128,411]{1,0,2:T(8,128)(2,1)} copy(bf16[16,128,411]{2,0,1:T(8,128)(2,1)} %maximum_select_fusion) | data formatting | bytes 3366912 | tf_op jit(solution)/shard_map/jit(_where)/select_n | solution.py:138
  (17 shorter events, 0.2 us)
Async XLA Ops:
  0.0 16.6 %copy-start = (bf16[16,128,411]{1,0,2:T(8,128)(2,1)S(1)}, bf16[16,128,411]{1,0,2:T(8,128)(2,1)}, u32[]{:S(2)}) copy-start(bf16[16,128,411]{1,0,2:T(8,128)(2,1)} %param.10) | copy-start | bytes 5050372
  0.0 40.1 %collective-permute-start.6 = (bf16[8,308,411]{2,0,1:T(8,128)(2,1)}, bf16[8,308,411]{2,0,1:T(8,128)(2,1)}, u32[]{:S(2)}, u32[]{:S(2)}) collective-permute-start(bf16[8,308,411]{2,0,1:T(8,128)(2,1)} %param.7), channel_id=1, source_target_pairs={{0,1},{1,0},{2,3},{3,2},{4,5},{5,4},{6,7},{7,6},{8,9},{9,8},{10,11... | collective-permute-start | bytes 6076232 | tf_op jit(solution)/shard_map/ppermute | solution.py:20
  4.8 16.9 %copy-start.5 = (s32[8]{0:T(128)}, s32[8]{0:T(128)S(1)}, u32[]{:S(2)}) copy-start(s32[8]{0:T(128)S(1)} %multiply_add_fusion.place_ref) | copy-start | bytes 100
  5.6 17.2 %collective-permute-start.2 = (s32[3]{0:T(128)S(1)}, s32[3]{0:T(128)S(1)}, u32[]{:S(2)}, u32[]{:S(2)}) collective-permute-start(s32[3]{0:T(128)S(1)} %get-tuple-element.15), channel_id=1, source_target_pairs={{0,4},{2,6},{4,8},{6,10},{8,12},{10,14},{12,16},{14,18},{16,20},{1... | collective-permute-start | bytes 44 | tf_op jit(solution)/shard_map/ppermute | solution.py:16
  6.8 16.5 %collective-permute-start.1 = (s32[3]{0:T(128)S(1)}, s32[3]{0:T(128)S(1)}, u32[]{:S(2)}, u32[]{:S(2)}) collective-permute-start(s32[3]{0:T(128)S(1)} %get-tuple-element.16), channel_id=1, source_target_pairs={{0,2},{2,4},{4,6},{6,8},{8,10},{10,12},{12,14},{14,16},{16,18},{18... | collective-permute-start | bytes 44 | tf_op jit(solution)/shard_map/ppermute | solution.py:16
  7.2 18.9 %collective-permute-start = (s32[3]{0:T(128)S(1)}, s32[3]{0:T(128)S(1)}, u32[]{:S(2)}, u32[]{:S(2)}) collective-permute-start(s32[3]{0:T(128)S(1)} %get-tuple-element.18), channel_id=1, source_target_pairs={{0,254},{2,0},{4,2},{6,4},{8,6},{10,8},{12,10},{14,12},{16,14},{18... | collective-permute-start | bytes 44 | tf_op jit(solution)/shard_map/ppermute | solution.py:16
  14.3 14.7 %collective-permute-start.7 = (bf16[8,308]{1,0:T(8,128)(2,1)}, bf16[8,308]{1,0:T(8,128)(2,1)S(1)}, u32[]{:S(2)}, u32[]{:S(2)}) collective-permute-start(bf16[8,308]{1,0:T(8,128)(2,1)} %param.9), channel_id=1, source_target_pairs={{0,1},{1,0},{2,3},{3,2},{4,5},{5,4},{6,7},{7,6},{8,9},{9,8},{10,11... | collective-permute-start | bytes 14792 | tf_op jit(solution)/shard_map/ppermute | solution.py:20
  18.3 4.5 %copy-start.1 = (bf16[308,616]{1,0:T(8,128)(2,1)S(1)}, bf16[308,616]{1,0:T(8,128)(2,1)}, u32[]{:S(2)}) copy-start(bf16[308,616]{1,0:T(8,128)(2,1)} %param.8) | copy-start | bytes 1138372
  22.8 7.1 %collective-permute-start.8 = (bf16[308,616]{1,0:T(8,128)(2,1)S(1)}, bf16[308,616]{1,0:T(8,128)(2,1)S(1)}, u32[]{:S(2)}, u32[]{:S(2)}) collective-permute-start(bf16[308,616]{1,0:T(8,128)(2,1)S(1)} %copy-done.1), channel_id=1, source_target_pairs={{0,1},{1,0},{2,3},{3,2},{4,5},{5,4},{6,7},{7,6},{8,9},{9,8},{10,11... | collective-permute-start | bytes 1138376 | tf_op jit(solution)/shard_map/ppermute | solution.py:20
  23.3 7.8 %collective-permute-start.5 = (bf16[3,64,411]{2,1,0:T(8,128)(2,1)S(1)}, bf16[3,64,411]{2,1,0:T(8,128)(2,1)S(1)}, u32[]{:S(2)}, u32[]{:S(2)}) collective-permute-start(bf16[3,64,411]{2,1,0:T(8,128)(2,1)S(1)} %copy.23), channel_id=1, source_target_pairs={{0,252},{2,254},{4,0},{6,2},{8,4},{10,6},{12,8},{14,10},{16,12},{1... | collective-permute-start | bytes 473480 | tf_op jit(solution)/shard_map/ppermute | solution.py:16
  26.1 7.6 %collective-permute-start.4 = (bf16[3,64,411]{2,1,0:T(8,128)(2,1)S(1)}, bf16[3,64,411]{2,1,0:T(8,128)(2,1)S(1)}, u32[]{:S(2)}, u32[]{:S(2)}) collective-permute-start(bf16[3,64,411]{2,1,0:T(8,128)(2,1)S(1)} %copy.24), channel_id=1, source_target_pairs={{0,254},{2,0},{4,2},{6,4},{8,6},{10,8},{12,10},{14,12},{16,14},{18... | collective-permute-start | bytes 473480 | tf_op jit(solution)/shard_map/ppermute | solution.py:16
  29.0 11.1 %collective-permute-start.3 = (bf16[3,64,411]{2,1,0:T(8,128)(2,1)S(1)}, bf16[3,64,411]{2,1,0:T(8,128)(2,1)S(1)}, u32[]{:S(2)}, u32[]{:S(2)}) collective-permute-start(bf16[3,64,411]{2,1,0:T(8,128)(2,1)S(1)} %copy.26), channel_id=1, source_target_pairs={{0,2},{2,4},{4,6},{6,8},{8,10},{10,12},{12,14},{14,16},{16,18},{18... | collective-permute-start | bytes 473480 | tf_op jit(solution)/shard_map/ppermute | solution.py:16
  31.1 9.0 %copy-start.2 = (bf16[3,64,411]{2,1,0:T(8,128)(2,1)}, bf16[3,64,411]{2,1,0:T(8,128)(2,1)S(1)}, u32[]{:S(2)}) copy-start(bf16[3,64,411]{2,1,0:T(8,128)(2,1)S(1)} %collective-permute-done.5.s3_ref) | copy-start | bytes 473476
  33.7 6.4 %copy-start.3 = (bf16[3,64,411]{2,1,0:T(8,128)(2,1)}, bf16[3,64,411]{2,1,0:T(8,128)(2,1)S(1)}, u32[]{:S(2)}) copy-start(bf16[3,64,411]{2,1,0:T(8,128)(2,1)S(1)} %collective-permute-done.4.s2_ref) | copy-start | bytes 473476
  40.1 0.7 copy-start.4
  40.7 13.7 %copy-start.6 = (s32[8]{0:T(128)S(1)}, s32[8]{0:T(128)}, u32[]{:S(2)}) copy-start(s32[8]{0:T(128)} %copy-done.5) | copy-start | bytes 100
  56.5 6.0 %collective-permute-start.9 = (bf16[3,64,411]{2,0,1:T(4,128)(2,1)S(1)}, bf16[3,64,411]{2,0,1:T(4,128)(2,1)S(1)}, u32[]{:S(2)}, u32[]{:S(2)}) collective-permute-start(bf16[3,64,411]{2,0,1:T(4,128)(2,1)S(1)} %get-tuple-element.5), channel_id=1, source_target_pairs={{0,254},{2,0},{4,2},{6,4},{8,6},{10,8},{12,10},{14,12},{16,14},{18... | collective-permute-start | bytes 473480 | tf_op jit(solution)/shard_map/ppermute | solution.py:16
  57.9 12.1 %collective-permute-start.11 = (bf16[3,64,411]{2,0,1:T(4,128)(2,1)S(1)}, bf16[3,64,411]{2,0,1:T(4,128)(2,1)S(1)}, u32[]{:S(2)}, u32[]{:S(2)}) collective-permute-start(bf16[3,64,411]{2,0,1:T(4,128)(2,1)S(1)} %get-tuple-element.6), channel_id=1, source_target_pairs={{0,4},{2,6},{4,8},{6,10},{8,12},{10,14},{12,16},{14,18},{16,20},{1... | collective-permute-start | bytes 473480 | tf_op jit(solution)/shard_map/ppermute | solution.py:16
  57.9 16.7 %collective-permute-start.10 = (bf16[3,64,411]{2,0,1:T(4,128)(2,1)S(1)}, bf16[3,64,411]{2,0,1:T(4,128)(2,1)S(1)}, u32[]{:S(2)}, u32[]{:S(2)}) collective-permute-start(bf16[3,64,411]{2,0,1:T(4,128)(2,1)S(1)} %get-tuple-element.7), channel_id=1, source_target_pairs={{0,2},{2,4},{4,6},{6,8},{8,10},{10,12},{12,14},{14,16},{16,18},{18... | collective-permute-start | bytes 473480 | tf_op jit(solution)/shard_map/ppermute | solution.py:16
  75.5 5.7 %collective-permute-start.12 = (bf16[16,64,411]{2,0,1:T(8,128)(2,1)S(1)}, bf16[16,64,411]{2,0,1:T(8,128)(2,1)S(1)}, u32[]{:S(2)}, u32[]{:S(2)}) collective-permute-start(bf16[16,64,411]{2,0,1:T(8,128)(2,1)S(1)} %convolution_convert_fusion), channel_id=1, source_target_pairs={{0,1},{1,0},{2,3},{3,2},{4,5},{5,4},{6,7},{7,6},{8,9},{9,8},{10,11... | collective-permute-start | bytes 2525192 | tf_op jit(solution)/shard_map/ppermute | solution.py:20

commit v6 on v5

--- a/solution.py
+++ b/solution.py
@@ -82,7 +82,6 @@
     slots_total = SPAN * capacity
 
     jac_c = jnp.transpose(jacobian, (1, 0, 2))
-    jac_o = jnp.transpose(swapped(jacobian), (1, 0, 2))
     innov_c = innovation.astype(jnp.float32)
     innov_o = swapped(innovation).astype(jnp.float32)
     r_o = swapped(r_inverse)
@@ -116,6 +115,8 @@
     for g in range(SPAN):
         wanted = request[g * capacity:(g + 1) * capacity]
         slot_parts.append(wanted if g == 1 else passed_along(wanted, "tile", g - 1))
+    slot_parts, held = lax.optimization_barrier((slot_parts, jacobian))
+    jac_o = jnp.transpose(swapped(held), (1, 0, 2))
     fetched_parts = []
     for g in range(SPAN):
         picked = pick(slot_parts[g])

time: 88.3 us -> 94.6 us (1.071)
  starting transfers between devices: 22.5 us -> 26.6 us
  waiting for transfers between devices: 27.7 us -> 29.9 us
    ppermute x9, starting transfers between devices: 15.3 us -> 21.9 us  [passed_along(): lax.ppermute(value, axis, [(i, (i + by) % count) for i in range(count)])]
    ppermute x4, starting transfers between devices: 7.16 us -> 4.72 us  [swapped(): return lax.ppermute(value, 'chan', [(0, 1), (1, 0)])]
    ppermute x9, waiting for transfers between devices: 25.4 us -> 27.6 us  [passed_along(): lax.ppermute(value, axis, [(i, (i + by) % count) for i in range(count)])]
  transfers between devices with their start and end apart: 13 -> 13, of which waited for: 6 -> 7; matrix products, arithmetic and copies ran while one was open for 15% -> 11% of each run, Pallas kernels for 0% -> 0%
where the time goes in v6:
time: 94.6 us; the launch traced here: 94.3 us
  waiting for transfers between devices  29.9 us (32%)
  starting transfers between devices  26.6 us (28%)
  Pallas kernels  13.7 us (14%)
  local copies, waits for them, and re-layouts  12 us (13%)
  other arithmetic  7.38 us (8%)
  matrix products  3.98 us (4%)
    ppermute x9, waiting for transfers between devices, passed_along(): lax.ppermute(value, axis, [(i, (i + by) % count) for i in range(count)])  27.6 us
    ppermute x9, starting transfers between devices, passed_along(): lax.ppermute(value, axis, [(i, (i + by) % count) for i in range(count)])  21.9 us
    pallas_call x1, Pallas kernels, adjoints(): pl.pallas_call(adjoint_kernel, in_specs=[smem, smem] + [vmem] * 12, out_s...  13.7 us
    dynamic_slice x2, local copies, waits for them, and re-layouts, on_device(): lax.dynamic_slice_in_dim(increments, core * half_m, half_m, axis=1)  4.99 us
    select_n x1, local copies, waits for them, and re-layouts, on_device(): jnp.where(first, jnp.concatenate([mine, other], axis=1), jnp.concatenate(...  4.94 us
    ppermute x4, starting transfers between devices, swapped(): return lax.ppermute(value, 'chan', [(0, 1), (1, 0)])  4.72 us
    ppermute x4, waiting for transfers between devices, swapped(): return lax.ppermute(value, 'chan', [(0, 1), (1, 0)])  2.29 us
  transfers between devices with their start and end apart: 13, of which 7 were waited for; matrix products, arithmetic and copies ran while one was open for 11% of the time, Pallas kernels for 0%

profile of v6, /device:TPU:1, one launch (start us, length us, event | category | flops | bytes accessed | tf_op | source)
XLA Modules:
  0.0 94.3 jit_solution(4906133075359026261)
XLA Ops:
  0.0 1.0 %convert_reduce_fusion = s32[8]{0:T(128)S(1)} fusion(s32[8]{0:T(128)} %bitcast.27), kind=kLoop, calls=%fused_computation.27 | loop fusion | flops 312 | bytes 64 | tf_op jit(solution)/shard_map/reduce_sum | solution.py:103
  1.0 0.7 multiply_add_fusion.place_ref
  1.6 0.7 select_reduce_fusion
  2.4 0.1 fusion.33
  2.5 3.7 %collective-permute-start.2 = (s32[3]{0:T(128)S(1)}, s32[3]{0:T(128)S(1)}, u32[]{:S(2)}, u32[]{:S(2)}) collective-permute-start(s32[3]{0:T(128)S(1)} %get-tuple-element.25), channel_id=1, source_target_pairs={{0,4},{2,6},{4,8},{6,10},{8,12},{10,14},{12,16},{14,18},{16,20},{1... | collective-permute-start | bytes 44 | tf_op jit(solution)/shard_map/ppermute | solution.py:16
  6.2 0.4 collective-permute-start.1
  6.6 7.1 %collective-permute-start = (s32[3]{0:T(128)S(1)}, s32[3]{0:T(128)S(1)}, u32[]{:S(2)}, u32[]{:S(2)}) collective-permute-start(s32[3]{0:T(128)S(1)} %get-tuple-element.28), channel_id=1, source_target_pairs={{0,254},{2,0},{4,2},{6,4},{8,6},{10,8},{12,10},{14,12},{16,14},{18... | collective-permute-start | bytes 44 | tf_op jit(solution)/shard_map/ppermute | solution.py:16
  13.7 1.0 %collective-permute-done.2 = s32[3]{0:T(128)S(1)} collective-permute-done((s32[3]{0:T(128)S(1)}, s32[3]{0:T(128)S(1)}, u32[]{:S(2)}, u32[]{:S(2)}) %collective-permute-start.2) | collective-permute-done | bytes 44 | tf_op jit(solution)/shard_map/ppermute | solution.py:16
  14.6 0.0 collective-permute-done.1
  14.7 0.0 collective-permute-done
  14.7 1.5 %collective-permute-start.6 = (bf16[8,308,411]{2,0,1:T(8,128)(2,1)}, bf16[8,308,411]{2,0,1:T(8,128)(2,1)}, u32[]{:S(2)}, u32[]{:S(2)}) collective-permute-start(bf16[8,308,411]{2,0,1:T(8,128)(2,1)} %param.7), channel_id=1, source_target_pairs={{0,1},{1,0},{2,3},{3,2},{4,5},{5,4},{6,7},{7,6},{8,9},{9,8},{10,11... | collective-permute-start | bytes 6076232 | tf_op jit(solution)/shard_map/ppermute | solution.py:20
  16.2 0.1 collective-permute-start.7
  16.3 0.4 collective-permute-start.8
  16.7 1.3 %convert_element_type.38.ic_ref = f32[8,308]{1,0:T(8,128)} convert(bf16[8,308]{1,0:T(8,128)(2,1)} %param.9) | non-fusion elementwise | flops 2464 | bytes 14784 | tf_op jit(solution)/shard_map/convert_element_type | solution.py:85
  18.7 1.7 %constant_dynamic-slice_fusion = bf16[16,64,411]{1,0,2:T(8,128)(2,1)} fusion(bf16[16,128,411]{1,0,2:T(8,128)(2,1)S(1)} %copy-done, s32[]{:T(128)S(6)} %select_n.49), kind=kLoop, calls=%fused_computation.49 | loop fusion | bytes 1683460 | tf_op jit(solution)/shard_map/dynamic_slice | solution.py:108
  20.4 3.3 %copy.12 = bf16[16,64,411]{2,0,1:T(8,128)(2,1)S(1)} copy(bf16[16,64,411]{1,0,2:T(8,128)(2,1)} %constant_dynamic-slice_fusion) | data formatting | bytes 1683456 | tf_op jit(solution)/shard_map/dynamic_slice | solution.py:108
  23.7 0.4 fusion.25
  24.1 3.3 %collective-permute-start.5 = (bf16[3,64,411]{2,1,0:T(8,128)(2,1)S(1)}, bf16[3,64,411]{2,1,0:T(8,128)(2,1)S(1)}, u32[]{:S(2)}, u32[]{:S(2)}) collective-permute-start(bf16[3,64,411]{2,1,0:T(8,128)(2,1)S(1)} %copy.23), channel_id=1, source_target_pairs={{0,252},{2,254},{4,0},{6,2},{8,4},{10,6},{12,8},{14,10},{16,12},{1... | collective-permute-start | bytes 473480 | tf_op jit(solution)/shard_map/ppermute | solution.py:16
  27.4 0.4 fusion.22
  27.8 0.0 copy-start.1
  27.8 4.0 %collective-permute-start.4 = (bf16[3,64,411]{2,1,0:T(8,128)(2,1)S(1)}, bf16[3,64,411]{2,1,0:T(8,128)(2,1)S(1)}, u32[]{:S(2)}, u32[]{:S(2)}) collective-permute-start(bf16[3,64,411]{2,1,0:T(8,128)(2,1)S(1)} %copy.24), channel_id=1, source_target_pairs={{0,254},{2,0},{4,2},{6,4},{8,6},{10,8},{12,10},{14,12},{16,14},{18... | collective-permute-start | bytes 473480 | tf_op jit(solution)/shard_map/ppermute | solution.py:16
  31.8 0.3 fusion.19
  32.2 0.4 fusion.16
  32.6 0.7 copy.25.s1_ref
  33.3 0.0 collective-permute-done.7
  33.3 0.6 collective-permute-start.3
  33.9 0.6 convert_element_type.39.io_ref
  34.5 0.0 collective-permute-done.8
  34.5 0.1 broadcast_select_fusion.1
  34.6 1.2 %broadcast_select_fusion.2 = (bf16[308,308]{1,0:T(8,128)(2,1)}, bf16[308,308]{1,0:T(8,128)(2,1)}, bf16[308,308]{1,0:T(8,128)(2,1)}, bf16[308,308]{1,0:T(8,128)(2,1)}) fusion(pred[]{:T(512)S(6)} %eq.44, bf16[308,616]{1,0:T(8,128)(2,1)S(1)} %get-tuple-element.24, bf16[308,616]{1,0:T(8,128)(2,1)S(1)} %get-tuple-element.23), kind=kLoop, calls=%fused_computation.17 | loop fusion | flops 379456 | bytes 1517825 | tf_op jit(solution)/shard_map/jit(_where)/select_n | solution.py:97
  35.8 0.0 collective-permute-done.5.s3_ref
  35.8 1.6 %collective-permute-done.4.s2_ref = bf16[3,64,411]{2,1,0:T(8,128)(2,1)S(1)} collective-permute-done((bf16[3,64,411]{2,1,0:T(8,128)(2,1)S(1)}, bf16[3,64,411]{2,1,0:T(8,128)(2,1)S(1)}, u32[]{:S(2)}, u32[]{:S(2)}) %collective-permute-start.4) | collective-permute-done | bytes 157856 | tf_op jit(solution)/shard_map/ppermute | solution.py:16
  37.4 7.6 %collective-permute-done.3.s0_ref = bf16[3,64,411]{2,1,0:T(8,128)(2,1)S(1)} collective-permute-done((bf16[3,64,411]{2,1,0:T(8,128)(2,1)S(1)}, bf16[3,64,411]{2,1,0:T(8,128)(2,1)S(1)}, u32[]{:S(2)}, u32[]{:S(2)}) %collective-permute-start.3) | collective-permute-done | bytes 157856 | tf_op jit(solution)/shard_map/ppermute | solution.py:16
  45.0 0.6 copy-done.4
  45.6 13.7 %shard_map.73 = bf16[8,64,411]{2,1,0:T(8,128)(2,1)} custom-call(s32[8]{0:T(128)} %copy-done.5, s32[1]{0:T(128)S(6)} %copy.27.count_ref, bf16[3,64,411]{2,1,0:T(8,128)(2,1)} %copy-done.4, bf16[3,64,411]{2,1,0:T(8,128)(2,1)} %copy.25.s1_ref, bf16[3,64,411]{2,1,0:T(8,128)(2,1)} %copy-done.3, bf16[3,64,411]{2,1,0:T(8,128)(2,1)} %copy-done.2, ...), custom_call_target="tpu_custom_call" | custom-call | tf_op jit(solution)/shard_map/pallas_call | solution.py:65
  59.3 1.6 %convolution_convert_fusion.1 = bf16[12,64,411]{2,0,1:T(8,128)(2,1)S(1)} fusion(bf16[8,64,411]{2,1,0:T(8,128)(2,1)} %shard_map.73, s32[8]{0:T(128)S(1)} %copy-done.6), kind=kOutput, calls=%fused_computation.2 | convolution fusion | flops 5366112 | bytes 1052192 | tf_op jit(solution)/shard_map/af,fmd->amd/dot_general | solution.py:126
  60.9 0.4 fusion.32
  61.4 2.8 %collective-permute-start.9 = (bf16[3,64,411]{2,0,1:T(4,128)(2,1)S(1)}, bf16[3,64,411]{2,0,1:T(4,128)(2,1)S(1)}, u32[]{:S(2)}, u32[]{:S(2)}) collective-permute-start(bf16[3,64,411]{2,0,1:T(4,128)(2,1)S(1)} %get-tuple-element.15), channel_id=1, source_target_pairs={{0,254},{2,0},{4,2},{6,4},{8,6},{10,8},{12,10},{14,12},{16,14},{18... | collective-permute-start | bytes 473480 | tf_op jit(solution)/shard_map/ppermute | solution.py:16
  64.1 0.0 collective-permute-start.11
  64.1 0.1 pad_add_fusion
  64.2 4.4 %collective-permute-done.9 = bf16[3,64,411]{2,0,1:T(4,128)(2,1)S(1)} collective-permute-done((bf16[3,64,411]{2,0,1:T(4,128)(2,1)S(1)}, bf16[3,64,411]{2,0,1:T(4,128)(2,1)S(1)}, u32[]{:S(2)}, u32[]{:S(2)}) %collective-permute-start.9) | collective-permute-done | bytes 157856 | tf_op jit(solution)/shard_map/ppermute | solution.py:16
  68.6 8.3 %collective-permute-done.11 = bf16[3,64,411]{2,0,1:T(4,128)(2,1)S(1)} collective-permute-done((bf16[3,64,411]{2,0,1:T(4,128)(2,1)S(1)}, bf16[3,64,411]{2,0,1:T(4,128)(2,1)S(1)}, u32[]{:S(2)}, u32[]{:S(2)}) %collective-permute-start.11) | collective-permute-done | bytes 157856 | tf_op jit(solution)/shard_map/ppermute | solution.py:16
  77.0 4.7 %collective-permute-done.10 = bf16[3,64,411]{2,0,1:T(4,128)(2,1)S(1)} collective-permute-done((bf16[3,64,411]{2,0,1:T(4,128)(2,1)S(1)}, bf16[3,64,411]{2,0,1:T(4,128)(2,1)S(1)}, u32[]{:S(2)}, u32[]{:S(2)}) %collective-permute-start.10) | collective-permute-done | bytes 157856 | tf_op jit(solution)/shard_map/ppermute | solution.py:16
  81.6 1.0 %convolution_convert_fusion = bf16[16,64,411]{2,0,1:T(8,128)(2,1)S(1)} fusion(bf16[3,64,411]{2,0,1:T(4,128)(2,1)S(1)} %collective-permute-done.11, bf16[3,64,411]{2,0,1:T(4,128)(2,1)S(1)} %collective-permute-done.10, bf16[3,64,411]{2,0,1:T(4,128)(2,1)S(1)} %get-tuple-element.18, bf16[3,64,411]{2,0,1:T(4,128)(2,1)S(1)} %collective-permute-done.9, ...), kind=kOutput, calls=%fused_computation.1 | convolution fusion | flops 13046976 | bytes 1473072 | tf_op jit(solution)/shard_map/ac,amd->cmd/dot_general | solution.py:136
  82.6 2.7 %collective-permute-start.12 = (bf16[16,64,411]{2,0,1:T(8,128)(2,1)S(1)}, bf16[16,64,411]{2,0,1:T(8,128)(2,1)S(1)}, u32[]{:S(2)}, u32[]{:S(2)}) collective-permute-start(bf16[16,64,411]{2,0,1:T(8,128)(2,1)S(1)} %convolution_convert_fusion), channel_id=1, source_target_pairs={{0,1},{1,0},{2,3},{3,2},{4,5},{5,4},{6,7},{7,6},{8,9},{9,8},{10,11... | collective-permute-start | bytes 2525192 | tf_op jit(solution)/shard_map/ppermute | solution.py:20
  85.2 2.3 %collective-permute-done.12 = bf16[16,64,411]{2,0,1:T(8,128)(2,1)S(1)} collective-permute-done((bf16[16,64,411]{2,0,1:T(8,128)(2,1)S(1)}, bf16[16,64,411]{2,0,1:T(8,128)(2,1)S(1)}, u32[]{:S(2)}, u32[]{:S(2)}) %collective-permute-start.12) | collective-permute-done | bytes 841760 | tf_op jit(solution)/shard_map/ppermute | solution.py:20
  87.5 1.8 %maximum_select_fusion = bf16[16,128,411]{2,0,1:T(8,128)(2,1)} fusion(bf16[16,64,411]{2,0,1:T(8,128)(2,1)S(1)} %collective-permute-done.12, bf16[16,64,411]{2,0,1:T(8,128)(2,1)S(1)} %convolution_convert_fusion, pred[]{:T(512)S(6)} %eq.44), kind=kLoop, calls=%fused_computation | loop fusion | flops 2525184 | bytes 3366913 | tf_op jit(solution)/shard_map/jit(_where)/select_n | solution.py:139
  89.3 4.9 %copy.11 = bf16[16,128,411]{1,0,2:T(8,128)(2,1)} copy(bf16[16,128,411]{2,0,1:T(8,128)(2,1)} %maximum_select_fusion) | data formatting | bytes 3366912 | tf_op jit(solution)/shard_map/jit(_where)/select_n | solution.py:139
  (17 shorter events, 0.2 us)
Async XLA Ops:
  0.0 18.7 %copy-start = (bf16[16,128,411]{1,0,2:T(8,128)(2,1)S(1)}, bf16[16,128,411]{1,0,2:T(8,128)(2,1)}, u32[]{:S(2)}) copy-start(bf16[16,128,411]{1,0,2:T(8,128)(2,1)} %param.10) | copy-start | bytes 5050372
  1.6 22.0 %copy-start.5 = (s32[8]{0:T(128)}, s32[8]{0:T(128)S(1)}, u32[]{:S(2)}) copy-start(s32[8]{0:T(128)S(1)} %multiply_add_fusion.place_ref) | copy-start | bytes 100
  2.5 12.2 %collective-permute-start.2 = (s32[3]{0:T(128)S(1)}, s32[3]{0:T(128)S(1)}, u32[]{:S(2)}, u32[]{:S(2)}) collective-permute-start(s32[3]{0:T(128)S(1)} %get-tuple-element.25), channel_id=1, source_target_pairs={{0,4},{2,6},{4,8},{6,10},{8,12},{10,14},{12,16},{14,18},{16,20},{1... | collective-permute-start | bytes 44 | tf_op jit(solution)/shard_map/ppermute | solution.py:16
  6.2 8.4 %collective-permute-start.1 = (s32[3]{0:T(128)S(1)}, s32[3]{0:T(128)S(1)}, u32[]{:S(2)}, u32[]{:S(2)}) collective-permute-start(s32[3]{0:T(128)S(1)} %get-tuple-element.26), channel_id=1, source_target_pairs={{0,2},{2,4},{4,6},{6,8},{8,10},{10,12},{12,14},{14,16},{16,18},{18... | collective-permute-start | bytes 44 | tf_op jit(solution)/shard_map/ppermute | solution.py:16
  6.6 8.1 %collective-permute-start = (s32[3]{0:T(128)S(1)}, s32[3]{0:T(128)S(1)}, u32[]{:S(2)}, u32[]{:S(2)}) collective-permute-start(s32[3]{0:T(128)S(1)} %get-tuple-element.28), channel_id=1, source_target_pairs={{0,254},{2,0},{4,2},{6,4},{8,6},{10,8},{12,10},{14,12},{16,14},{18... | collective-permute-start | bytes 44 | tf_op jit(solution)/shard_map/ppermute | solution.py:16
  14.7 30.3 %collective-permute-start.6 = (bf16[8,308,411]{2,0,1:T(8,128)(2,1)}, bf16[8,308,411]{2,0,1:T(8,128)(2,1)}, u32[]{:S(2)}, u32[]{:S(2)}) collective-permute-start(bf16[8,308,411]{2,0,1:T(8,128)(2,1)} %param.7), channel_id=1, source_target_pairs={{0,1},{1,0},{2,3},{3,2},{4,5},{5,4},{6,7},{7,6},{8,9},{9,8},{10,11... | collective-permute-start | bytes 6076232 | tf_op jit(solution)/shard_map/ppermute | solution.py:20
  16.2 17.1 %collective-permute-start.7 = (bf16[8,308]{1,0:T(8,128)(2,1)}, bf16[8,308]{1,0:T(8,128)(2,1)S(1)}, u32[]{:S(2)}, u32[]{:S(2)}) collective-permute-start(bf16[8,308]{1,0:T(8,128)(2,1)} %param.9), channel_id=1, source_target_pairs={{0,1},{1,0},{2,3},{3,2},{4,5},{5,4},{6,7},{7,6},{8,9},{9,8},{10,11... | collective-permute-start | bytes 14792 | tf_op jit(solution)/shard_map/ppermute | solution.py:20
  16.3 18.2 %collective-permute-start.8 = (bf16[308,616]{1,0:T(8,128)(2,1)}, bf16[308,616]{1,0:T(8,128)(2,1)S(1)}, u32[]{:S(2)}, u32[]{:S(2)}) collective-permute-start(bf16[308,616]{1,0:T(8,128)(2,1)} %param.8), channel_id=1, source_target_pairs={{0,1},{1,0},{2,3},{3,2},{4,5},{5,4},{6,7},{7,6},{8,9},{9,8},{10,11... | collective-permute-start | bytes 1138376 | tf_op jit(solution)/shard_map/ppermute | solution.py:20
  24.1 11.7 %collective-permute-start.5 = (bf16[3,64,411]{2,1,0:T(8,128)(2,1)S(1)}, bf16[3,64,411]{2,1,0:T(8,128)(2,1)S(1)}, u32[]{:S(2)}, u32[]{:S(2)}) collective-permute-start(bf16[3,64,411]{2,1,0:T(8,128)(2,1)S(1)} %copy.23), channel_id=1, source_target_pairs={{0,252},{2,254},{4,0},{6,2},{8,4},{10,6},{12,8},{14,10},{16,12},{1... | collective-permute-start | bytes 473480 | tf_op jit(solution)/shard_map/ppermute | solution.py:16
  27.8 6.8 %copy-start.1 = (bf16[308,616]{1,0:T(8,128)(2,1)S(1)}, bf16[308,616]{1,0:T(8,128)(2,1)}, u32[]{:S(2)}) copy-start(bf16[308,616]{1,0:T(8,128)(2,1)} %param.8) | copy-start | bytes 1138372
  27.8 9.6 %collective-permute-start.4 = (bf16[3,64,411]{2,1,0:T(8,128)(2,1)S(1)}, bf16[3,64,411]{2,1,0:T(8,128)(2,1)S(1)}, u32[]{:S(2)}, u32[]{:S(2)}) collective-permute-start(bf16[3,64,411]{2,1,0:T(8,128)(2,1)S(1)} %copy.24), channel_id=1, source_target_pairs={{0,254},{2,0},{4,2},{6,4},{8,6},{10,8},{12,10},{14,12},{16,14},{18... | collective-permute-start | bytes 473480 | tf_op jit(solution)/shard_map/ppermute | solution.py:16
  33.3 11.6 %collective-permute-start.3 = (bf16[3,64,411]{2,1,0:T(8,128)(2,1)S(1)}, bf16[3,64,411]{2,1,0:T(8,128)(2,1)S(1)}, u32[]{:S(2)}, u32[]{:S(2)}) collective-permute-start(bf16[3,64,411]{2,1,0:T(8,128)(2,1)S(1)} %copy.26), channel_id=1, source_target_pairs={{0,2},{2,4},{4,6},{6,8},{8,10},{10,12},{12,14},{14,16},{16,18},{18... | collective-permute-start | bytes 473480 | tf_op jit(solution)/shard_map/ppermute | solution.py:16
  35.8 9.2 %copy-start.2 = (bf16[3,64,411]{2,1,0:T(8,128)(2,1)}, bf16[3,64,411]{2,1,0:T(8,128)(2,1)S(1)}, u32[]{:S(2)}) copy-start(bf16[3,64,411]{2,1,0:T(8,128)(2,1)S(1)} %collective-permute-done.5.s3_ref) | copy-start | bytes 473476
  37.4 7.6 %copy-start.3 = (bf16[3,64,411]{2,1,0:T(8,128)(2,1)}, bf16[3,64,411]{2,1,0:T(8,128)(2,1)S(1)}, u32[]{:S(2)}) copy-start(bf16[3,64,411]{2,1,0:T(8,128)(2,1)S(1)} %collective-permute-done.4.s2_ref) | copy-start | bytes 473476
  44.9 0.7 copy-start.4
  45.6 13.7 %copy-start.6 = (s32[8]{0:T(128)S(1)}, s32[8]{0:T(128)}, u32[]{:S(2)}) copy-start(s32[8]{0:T(128)} %copy-done.5) | copy-start | bytes 100
  61.4 7.3 %collective-permute-start.9 = (bf16[3,64,411]{2,0,1:T(4,128)(2,1)S(1)}, bf16[3,64,411]{2,0,1:T(4,128)(2,1)S(1)}, u32[]{:S(2)}, u32[]{:S(2)}) collective-permute-start(bf16[3,64,411]{2,0,1:T(4,128)(2,1)S(1)} %get-tuple-element.15), channel_id=1, source_target_pairs={{0,254},{2,0},{4,2},{6,4},{8,6},{10,8},{12,10},{14,12},{16,14},{18... | collective-permute-start | bytes 473480 | tf_op jit(solution)/shard_map/ppermute | solution.py:16
  64.1 12.8 %collective-permute-start.11 = (bf16[3,64,411]{2,0,1:T(4,128)(2,1)S(1)}, bf16[3,64,411]{2,0,1:T(4,128)(2,1)S(1)}, u32[]{:S(2)}, u32[]{:S(2)}) collective-permute-start(bf16[3,64,411]{2,0,1:T(4,128)(2,1)S(1)} %get-tuple-element.16), channel_id=1, source_target_pairs={{0,4},{2,6},{4,8},{6,10},{8,12},{10,14},{12,16},{14,18},{16,20},{1... | collective-permute-start | bytes 473480 | tf_op jit(solution)/shard_map/ppermute | solution.py:16
  64.1 17.5 %collective-permute-start.10 = (bf16[3,64,411]{2,0,1:T(4,128)(2,1)S(1)}, bf16[3,64,411]{2,0,1:T(4,128)(2,1)S(1)}, u32[]{:S(2)}, u32[]{:S(2)}) collective-permute-start(bf16[3,64,411]{2,0,1:T(4,128)(2,1)S(1)} %get-tuple-element.17), channel_id=1, source_target_pairs={{0,2},{2,4},{4,6},{6,8},{8,10},{10,12},{12,14},{14,16},{16,18},{18... | collective-permute-start | bytes 473480 | tf_op jit(solution)/shard_map/ppermute | solution.py:16
  82.6 4.9 %collective-permute-start.12 = (bf16[16,64,411]{2,0,1:T(8,128)(2,1)S(1)}, bf16[16,64,411]{2,0,1:T(8,128)(2,1)S(1)}, u32[]{:S(2)}, u32[]{:S(2)}) collective-permute-start(bf16[16,64,411]{2,0,1:T(8,128)(2,1)S(1)} %convolution_convert_fusion), channel_id=1, source_target_pairs={{0,1},{1,0},{2,3},{3,2},{4,5},{5,4},{6,7},{7,6},{8,9},{9,8},{10,11... | collective-permute-start | bytes 2525192 | tf_op jit(solution)/shard_map/ppermute | solution.py:20

commit v7 on v5

--- a/solution.py
+++ b/solution.py
@@ -25,9 +25,10 @@
 
 
 def adjoint_kernel(place_ref, count_ref, s0_ref, s1_ref, s2_ref, s3_ref, jc_ref, jo_ref, ic_ref, io_ref,
-                   rcc_ref, rco_ref, roc_ref, roo_ref, out_ref):
+                   rcc_ref, rco_ref, roc_ref, roo_ref, o0_ref, o1_ref, o2_ref, o3_ref):
+    outs = (o0_ref, o1_ref, o2_ref, o3_ref)
     parts = (s0_ref, s1_ref, s2_ref, s3_ref)
-    foot = out_ref.shape[0]
+    foot = jc_ref.shape[1]
     jcs, jos, deps_c, deps_o = [], [], [], []
     for f in range(foot):
         group = place_ref[f] // CAP
@@ -50,11 +51,19 @@
     w_o = (jnp.dot(dep_c, rco_ref[...], preferred_element_type=jnp.float32)
            + jnp.dot(dep_o, roo_ref[...], preferred_element_type=jnp.float32)).astype(jnp.bfloat16)
     rows = deps_c[0].shape[0]
+    for o_ref in outs:
+        o_ref[...] = jnp.zeros(o_ref.shape, o_ref.dtype)
     for f in range(foot):
         adj = (jnp.dot(w_c[f * rows:(f + 1) * rows], jcs[f], preferred_element_type=jnp.float32)
                + jnp.dot(w_o[f * rows:(f + 1) * rows], jos[f], preferred_element_type=jnp.float32))
         live = f < count_ref[0]
-        out_ref[f] = jnp.where(live, adj, 0.0).astype(out_ref.dtype)
+        adj = jnp.where(live, adj, 0.0).astype(jnp.bfloat16)
+        group = place_ref[f] // CAP
+        rank = place_ref[f] % CAP
+        for g in range(SPAN):
+            @pl.when(group == g)
+            def _():
+                outs[g][rank] = adj
 
 
 def adjoints(place, count, fetched, jac_c, jac_o, innov_c, innov_o, r_blocks):
@@ -65,8 +74,8 @@
     return pl.pallas_call(
         adjoint_kernel,
         in_specs=[smem, smem] + [vmem] * 12,
-        out_specs=vmem,
-        out_shape=jax.ShapeDtypeStruct((foot, half_m, state), jnp.bfloat16),
+        out_specs=[vmem] * SPAN,
+        out_shape=[jax.ShapeDtypeStruct((CAP, half_m, state), jnp.bfloat16)] * SPAN,
     )(place, count, *fetched, jac_c, jac_o, innov_c, innov_o, *r_blocks)
 
 
@@ -120,13 +129,10 @@
     for g in range(SPAN):
         picked = pick(slot_parts[g])
         fetched_parts.append(picked if g == 1 else passed_along(picked, "tile", 1 - g))
-    adjoint = adjoints(place, foot_counts, fetched_parts, jac_c, jac_o, innov_c, innov_o, r_blocks)
-
-    packed = jnp.einsum("af,fmd->amd", hit.astype(jnp.bfloat16), adjoint,
-                        preferred_element_type=jnp.float32).astype(jnp.bfloat16)
+    packed = adjoints(place, foot_counts, fetched_parts, jac_c, jac_o, innov_c, innov_o, r_blocks)
     recv_parts = []
     for g in range(SPAN):
-        piece = packed[g * capacity:(g + 1) * capacity]
+        piece = packed[g]
         if g == 1:
             recv_parts.append(piece)
         else:

time: 88.3 us -> 85.1 us (0.964)
  waiting for transfers between devices: 27.7 us -> 23.8 us
  matrix products: 3.97 us -> 1.99 us
  Pallas kernels: 13.7 us -> 14.8 us
  other arithmetic: 7.32 us -> 8.36 us
  starting transfers between devices: 22.5 us -> 23.5 us
    ppermute x9, waiting for transfers between devices: 25.4 us -> 21.5 us  [passed_along(): lax.ppermute(value, axis, [(i, (i + by) % count) for i in range(count)])]
    unnamed x14 -> x13, local copies, waits for them, and re-layouts: 0.67 us -> 4.02 us
    dynamic_slice x2 -> x1, local copies, waits for them, and re-layouts: 5.04 us -> 1.7 us  [on_device(): lax.dynamic_slice_in_dim(increments, core * half_m, half_m, axis=1)]
    dot_general x1 -> x0, matrix products: 1.61 us -> none  [on_device(): jnp.einsum('af,fmd->amd', hit.astype(jnp.bfloat16), adjoint, preferred_el...]
    pallas_call x1, Pallas kernels: 13.7 us -> 14.8 us  [adjoints(): pl.pallas_call(adjoint_kernel, in_specs=[smem, smem] + [vmem] * 12, out_s...]
    ppermute x4, starting transfers between devices: 7.16 us -> 8.22 us  [swapped(): return lax.ppermute(value, 'chan', [(0, 1), (1, 0)])]
    concatenate x0 -> x1, other arithmetic: none -> 1.05 us  [on_device(): jnp.concatenate(recv_parts, axis=0)]
where the time goes in v7:
time: 85.1 us; the launch traced here: 84.8 us
  waiting for transfers between devices  23.8 us (28%)
  starting transfers between devices  23.5 us (28%)
  Pallas kernels  14.8 us (17%)
  local copies, waits for them, and re-layouts  11.6 us (14%)
  other arithmetic  8.36 us (10%)
  matrix products  1.99 us (2%)
    ppermute x9, waiting for transfers between devices, passed_along(): lax.ppermute(value, axis, [(i, (i + by) % count) for i in range(count)])  21.5 us
    ppermute x9, starting transfers between devices, passed_along(): lax.ppermute(value, axis, [(i, (i + by) % count) for i in range(count)])  15.2 us
    pallas_call x1, Pallas kernels, adjoints(): pl.pallas_call(adjoint_kernel, in_specs=[smem, smem] + [vmem] * 12, out_s...  14.8 us
    ppermute x4, starting transfers between devices, swapped(): return lax.ppermute(value, 'chan', [(0, 1), (1, 0)])  8.22 us
    select_n x1, local copies, waits for them, and re-layouts, on_device(): jnp.where(first, jnp.concatenate([mine, other], axis=1), jnp.concatenate(...  4.94 us
    unnamed x13, local copies, waits for them, and re-layouts  4.02 us
    ppermute x4, waiting for transfers between devices, swapped(): return lax.ppermute(value, 'chan', [(0, 1), (1, 0)])  2.29 us
    select_n x1, other arithmetic, on_device(): jnp.where(first, jnp.concatenate([mine, other], axis=1), jnp.concatenate(...  1.82 us
  transfers between devices with their start and end apart: 13, of which 6 were waited for; matrix products, arithmetic and copies ran while one was open for 15% of the time, Pallas kernels for 0%

profile of v7, /device:TPU:1, one launch (start us, length us, event | category | flops | bytes accessed | tf_op | source)
XLA Modules:
  0.0 84.8 jit_solution(15827128998095384260)
XLA Ops:
  0.0 3.2 %collective-permute-start.6 = (bf16[8,308,411]{2,0,1:T(8,128)(2,1)}, bf16[8,308,411]{2,0,1:T(8,128)(2,1)}, u32[]{:S(2)}, u32[]{:S(2)}) collective-permute-start(bf16[8,308,411]{2,0,1:T(8,128)(2,1)} %param.7), channel_id=1, source_target_pairs={{0,1},{1,0},{2,3},{3,2},{4,5},{5,4},{6,7},{7,6},{8,9},{9,8},{10,11... | collective-permute-start | bytes 6076232 | tf_op jit(solution)/shard_map/ppermute | solution.py:20
  3.2 0.9 %convert_reduce_fusion = s32[8]{0:T(128)S(1)} fusion(s32[8]{0:T(128)} %bitcast.24), kind=kLoop, calls=%fused_computation.19 | loop fusion | flops 312 | bytes 64 | tf_op jit(solution)/shard_map/reduce_sum | solution.py:113
  4.1 0.7 multiply_add_fusion.place_ref
  4.8 0.7 select_reduce_fusion
  5.5 0.1 fusion.21
  5.6 1.2 %collective-permute-start.2 = (s32[3]{0:T(128)S(1)}, s32[3]{0:T(128)S(1)}, u32[]{:S(2)}, u32[]{:S(2)}) collective-permute-start(s32[3]{0:T(128)S(1)} %get-tuple-element.19), channel_id=1, source_target_pairs={{0,4},{2,6},{4,8},{6,10},{8,12},{10,14},{12,16},{14,18},{16,20},{1... | collective-permute-start | bytes 44 | tf_op jit(solution)/shard_map/ppermute | solution.py:16
  6.8 0.4 collective-permute-start.1
  7.2 7.1 %collective-permute-start = (s32[3]{0:T(128)S(1)}, s32[3]{0:T(128)S(1)}, u32[]{:S(2)}, u32[]{:S(2)}) collective-permute-start(s32[3]{0:T(128)S(1)} %get-tuple-element.22), channel_id=1, source_target_pairs={{0,254},{2,0},{4,2},{6,4},{8,6},{10,8},{12,10},{14,12},{16,14},{18... | collective-permute-start | bytes 44 | tf_op jit(solution)/shard_map/ppermute | solution.py:16
  14.3 0.4 collective-permute-start.7
  14.6 1.3 %convert_element_type.34.ic_ref = f32[8,308]{1,0:T(8,128)} convert(bf16[8,308]{1,0:T(8,128)(2,1)} %param.9) | non-fusion elementwise | flops 2464 | bytes 14784 | tf_op jit(solution)/shard_map/convert_element_type | solution.py:95
  16.6 1.7 %constant_dynamic-slice_fusion = bf16[16,64,411]{1,0,2:T(8,128)(2,1)} fusion(bf16[16,128,411]{1,0,2:T(8,128)(2,1)S(1)} %copy-done, s32[]{:T(128)S(6)} %select_n.49), kind=kLoop, calls=%fused_computation.40 | loop fusion | bytes 1683460 | tf_op jit(solution)/shard_map/dynamic_slice | solution.py:118
  18.3 3.3 %copy.22 = bf16[16,64,411]{2,0,1:T(8,128)(2,1)S(1)} copy(bf16[16,64,411]{1,0,2:T(8,128)(2,1)} %constant_dynamic-slice_fusion) | data formatting | bytes 1683456
  21.7 0.4 fusion.9
  22.0 0.7 copy.31.s1_ref
  22.7 0.0 collective-permute-done.2
  22.7 0.2 collective-permute-start.8
  22.9 0.4 fusion.15
  23.3 0.0 collective-permute-done.1
  23.3 2.4 %collective-permute-start.5 = (bf16[3,64,411]{2,1,0:T(8,128)(2,1)S(1)}, bf16[3,64,411]{2,1,0:T(8,128)(2,1)S(1)}, u32[]{:S(2)}, u32[]{:S(2)}) collective-permute-start(bf16[3,64,411]{2,1,0:T(8,128)(2,1)S(1)} %copy.29), channel_id=1, source_target_pairs={{0,252},{2,254},{4,0},{6,2},{8,4},{10,6},{12,8},{14,10},{16,12},{1... | collective-permute-start | bytes 473480 | tf_op jit(solution)/shard_map/ppermute | solution.py:16
  25.7 0.3 fusion.12
  26.1 0.0 collective-permute-done
  26.1 2.4 %collective-permute-start.4 = (bf16[3,64,411]{2,1,0:T(8,128)(2,1)S(1)}, bf16[3,64,411]{2,1,0:T(8,128)(2,1)S(1)}, u32[]{:S(2)}, u32[]{:S(2)}) collective-permute-start(bf16[3,64,411]{2,1,0:T(8,128)(2,1)S(1)} %copy.30), channel_id=1, source_target_pairs={{0,254},{2,0},{4,2},{6,4},{8,6},{10,8},{12,10},{14,12},{16,14},{18... | collective-permute-start | bytes 473480 | tf_op jit(solution)/shard_map/ppermute | solution.py:16
  28.6 0.3 fusion.6
  29.0 0.0 collective-permute-done.7
  29.0 0.3 collective-permute-start.3
  29.2 0.6 convert_element_type.35.io_ref
  29.9 0.0 collective-permute-done.8
  29.9 0.1 broadcast_select_fusion.1
  29.9 1.1 %broadcast_select_fusion.2 = (bf16[308,308]{1,0:T(8,128)(2,1)}, bf16[308,308]{1,0:T(8,128)(2,1)}, bf16[308,308]{1,0:T(8,128)(2,1)}, bf16[308,308]{1,0:T(8,128)(2,1)}) fusion(pred[]{:T(512)S(6)} %eq.44, bf16[308,616]{1,0:T(8,128)(2,1)S(1)} %get-tuple-element.18, bf16[308,616]{1,0:T(8,128)(2,1)S(1)} %get-tuple-element.17), kind=kLoop, calls=%fused_computation.10 | loop fusion | flops 379456 | bytes 1517825 | tf_op jit(solution)/shard_map/jit(_where)/select_n | solution.py:107
  31.1 0.0 collective-permute-done.5.s3_ref
  31.1 2.6 %collective-permute-done.4.s2_ref = bf16[3,64,411]{2,1,0:T(8,128)(2,1)S(1)} collective-permute-done((bf16[3,64,411]{2,1,0:T(8,128)(2,1)S(1)}, bf16[3,64,411]{2,1,0:T(8,128)(2,1)S(1)}, u32[]{:S(2)}, u32[]{:S(2)}) %collective-permute-start.4) | collective-permute-done | bytes 157856 | tf_op jit(solution)/shard_map/ppermute | solution.py:16
  33.7 6.4 %collective-permute-done.3.s0_ref = bf16[3,64,411]{2,1,0:T(8,128)(2,1)S(1)} collective-permute-done((bf16[3,64,411]{2,1,0:T(8,128)(2,1)S(1)}, bf16[3,64,411]{2,1,0:T(8,128)(2,1)S(1)}, u32[]{:S(2)}, u32[]{:S(2)}) %collective-permute-start.3) | collective-permute-done | bytes 157856 | tf_op jit(solution)/shard_map/ppermute | solution.py:16
  40.1 0.0 collective-permute-done.6
  40.1 0.7 copy-done.4
  40.7 14.8 %shard_map.73 = (bf16[3,64,411]{2,1,0:T(8,128)(2,1)}, bf16[3,64,411]{2,1,0:T(8,128)(2,1)}, bf16[3,64,411]{2,1,0:T(8,128)(2,1)}, bf16[3,64,411]{2,1,0:T(8,128)(2,1)}) custom-call(s32[8]{0:T(128)} %copy-done.5, s32[1]{0:T(128)S(6)} %copy.33.count_ref, bf16[3,64,411]{2,1,0:T(8,128)(2,1)} %copy-done.4, bf16[3,64,411]{2,1,0:T(8,128)(2,1)} %copy.31.s1_ref, ...), custom_call_target="tpu_custom_call" | custom-call | tf_op jit(solution)/shard_map/pallas_call | solution.py:74
  55.5 1.3 %collective-permute-start.9 = (bf16[3,64,411]{2,1,0:T(8,128)(2,1)}, bf16[3,64,411]{2,1,0:T(8,128)(2,1)S(1)}, u32[]{:S(2)}, u32[]{:S(2)}) collective-permute-start(bf16[3,64,411]{2,1,0:T(8,128)(2,1)} %get-tuple-element.9), channel_id=1, source_target_pairs={{0,254},{2,0},{4,2},{6,4},{8,6},{10,8},{12,10},{14,12},{16,14},{18... | collective-permute-start | bytes 473480 | tf_op jit(solution)/shard_map/ppermute | solution.py:16
  56.8 0.1 collective-permute-start.10
  57.0 0.0 collective-permute-start.11
  57.0 0.1 pad_add_fusion
  57.0 3.2 %collective-permute-done.9 = bf16[3,64,411]{2,1,0:T(8,128)(2,1)S(1)} collective-permute-done((bf16[3,64,411]{2,1,0:T(8,128)(2,1)}, bf16[3,64,411]{2,1,0:T(8,128)(2,1)S(1)}, u32[]{:S(2)}, u32[]{:S(2)}) %collective-permute-start.9) | collective-permute-done | bytes 157856 | tf_op jit(solution)/shard_map/ppermute | solution.py:16
  60.2 8.2 %collective-permute-done.10 = bf16[3,64,411]{2,1,0:T(8,128)(2,1)S(1)} collective-permute-done((bf16[3,64,411]{2,1,0:T(8,128)(2,1)}, bf16[3,64,411]{2,1,0:T(8,128)(2,1)S(1)}, u32[]{:S(2)}, u32[]{:S(2)}) %collective-permute-start.10) | collective-permute-done | bytes 157856 | tf_op jit(solution)/shard_map/ppermute | solution.py:16
  68.5 1.1 %collective-permute-done.11 = bf16[3,64,411]{2,1,0:T(8,128)(2,1)S(1)} collective-permute-done((bf16[3,64,411]{2,1,0:T(8,128)(2,1)}, bf16[3,64,411]{2,1,0:T(8,128)(2,1)S(1)}, u32[]{:S(2)}, u32[]{:S(2)}) %collective-permute-start.11) | collective-permute-done | bytes 157856 | tf_op jit(solution)/shard_map/ppermute | solution.py:16
  69.6 1.0 %pad_maximum_fusion = bf16[12,64,411]{2,1,0:T(8,128)(2,1)S(1)} fusion(bf16[3,64,411]{2,1,0:T(8,128)(2,1)S(1)} %collective-permute-done.11, bf16[3,64,411]{2,1,0:T(8,128)(2,1)S(1)} %collective-permute-done.10, bf16[3,64,411]{2,1,0:T(8,128)(2,1)} %get-tuple-element.10, bf16[3,64,411]{2,1,0:T(8,128)(2,1)S(1)} %collective-permute-done.9), kind=kLoop, calls=%fused_computation.3 | loop fusion | flops 946944 | bytes 1262592 | tf_op jit(solution)/shard_map/concatenate | solution.py:141
  70.6 0.6 convolution_convert_fusion
  71.2 4.5 %collective-permute-start.12 = (bf16[16,64,411]{2,0,1:T(8,128)(2,1)S(1)}, bf16[16,64,411]{2,0,1:T(8,128)(2,1)S(1)}, u32[]{:S(2)}, u32[]{:S(2)}) collective-permute-start(bf16[16,64,411]{2,0,1:T(8,128)(2,1)S(1)} %convolution_convert_fusion), channel_id=1, source_target_pairs={{0,1},{1,0},{2,3},{3,2},{4,5},{5,4},{6,7},{7,6},{8,9},{9,8},{10,11... | collective-permute-start | bytes 2525192 | tf_op jit(solution)/shard_map/ppermute | solution.py:20
  75.7 2.3 %collective-permute-done.12 = bf16[16,64,411]{2,0,1:T(8,128)(2,1)S(1)} collective-permute-done((bf16[16,64,411]{2,0,1:T(8,128)(2,1)S(1)}, bf16[16,64,411]{2,0,1:T(8,128)(2,1)S(1)}, u32[]{:S(2)}, u32[]{:S(2)}) %collective-permute-start.12) | collective-permute-done | bytes 841760 | tf_op jit(solution)/shard_map/ppermute | solution.py:20
  78.0 1.8 %maximum_select_fusion = bf16[16,128,411]{2,0,1:T(8,128)(2,1)} fusion(bf16[16,64,411]{2,0,1:T(8,128)(2,1)S(1)} %collective-permute-done.12, bf16[16,64,411]{2,0,1:T(8,128)(2,1)S(1)} %convolution_convert_fusion, pred[]{:T(512)S(6)} %eq.44), kind=kLoop, calls=%fused_computation | loop fusion | flops 2525184 | bytes 3366913 | tf_op jit(solution)/shard_map/jit(_where)/select_n | solution.py:144
  79.9 4.9 %copy.21 = bf16[16,128,411]{1,0,2:T(8,128)(2,1)} copy(bf16[16,128,411]{2,0,1:T(8,128)(2,1)} %maximum_select_fusion) | data formatting | bytes 3366912 | tf_op jit(solution)/shard_map/jit(_where)/select_n | solution.py:144
  (14 shorter events, 0.2 us)
Async XLA Ops:
  0.0 16.6 %copy-start = (bf16[16,128,411]{1,0,2:T(8,128)(2,1)S(1)}, bf16[16,128,411]{1,0,2:T(8,128)(2,1)}, u32[]{:S(2)}) copy-start(bf16[16,128,411]{1,0,2:T(8,128)(2,1)} %param.10) | copy-start | bytes 5050372
  0.0 40.1 %collective-permute-start.6 = (bf16[8,308,411]{2,0,1:T(8,128)(2,1)}, bf16[8,308,411]{2,0,1:T(8,128)(2,1)}, u32[]{:S(2)}, u32[]{:S(2)}) collective-permute-start(bf16[8,308,411]{2,0,1:T(8,128)(2,1)} %param.7), channel_id=1, source_target_pairs={{0,1},{1,0},{2,3},{3,2},{4,5},{5,4},{6,7},{7,6},{8,9},{9,8},{10,11... | collective-permute-start | bytes 6076232 | tf_op jit(solution)/shard_map/ppermute | solution.py:20
  4.8 16.9 %copy-start.5 = (s32[8]{0:T(128)}, s32[8]{0:T(128)S(1)}, u32[]{:S(2)}) copy-start(s32[8]{0:T(128)S(1)} %multiply_add_fusion.place_ref) | copy-start | bytes 100
  5.6 17.1 %collective-permute-start.2 = (s32[3]{0:T(128)S(1)}, s32[3]{0:T(128)S(1)}, u32[]{:S(2)}, u32[]{:S(2)}) collective-permute-start(s32[3]{0:T(128)S(1)} %get-tuple-element.19), channel_id=1, source_target_pairs={{0,4},{2,6},{4,8},{6,10},{8,12},{10,14},{12,16},{14,18},{16,20},{1... | collective-permute-start | bytes 44 | tf_op jit(solution)/shard_map/ppermute | solution.py:16
  6.8 16.5 %collective-permute-start.1 = (s32[3]{0:T(128)S(1)}, s32[3]{0:T(128)S(1)}, u32[]{:S(2)}, u32[]{:S(2)}) collective-permute-start(s32[3]{0:T(128)S(1)} %get-tuple-element.20), channel_id=1, source_target_pairs={{0,2},{2,4},{4,6},{6,8},{8,10},{10,12},{12,14},{14,16},{16,18},{18... | collective-permute-start | bytes 44 | tf_op jit(solution)/shard_map/ppermute | solution.py:16
  7.2 18.9 %collective-permute-start = (s32[3]{0:T(128)S(1)}, s32[3]{0:T(128)S(1)}, u32[]{:S(2)}, u32[]{:S(2)}) collective-permute-start(s32[3]{0:T(128)S(1)} %get-tuple-element.22), channel_id=1, source_target_pairs={{0,254},{2,0},{4,2},{6,4},{8,6},{10,8},{12,10},{14,12},{16,14},{18... | collective-permute-start | bytes 44 | tf_op jit(solution)/shard_map/ppermute | solution.py:16
  14.3 14.7 %collective-permute-start.7 = (bf16[8,308]{1,0:T(8,128)(2,1)}, bf16[8,308]{1,0:T(8,128)(2,1)S(1)}, u32[]{:S(2)}, u32[]{:S(2)}) collective-permute-start(bf16[8,308]{1,0:T(8,128)(2,1)} %param.9), channel_id=1, source_target_pairs={{0,1},{1,0},{2,3},{3,2},{4,5},{5,4},{6,7},{7,6},{8,9},{9,8},{10,11... | collective-permute-start | bytes 14792 | tf_op jit(solution)/shard_map/ppermute | solution.py:20
  18.3 4.4 %copy-start.1 = (bf16[308,616]{1,0:T(8,128)(2,1)S(1)}, bf16[308,616]{1,0:T(8,128)(2,1)}, u32[]{:S(2)}) copy-start(bf16[308,616]{1,0:T(8,128)(2,1)} %param.8) | copy-start | bytes 1138372
  22.7 7.1 %collective-permute-start.8 = (bf16[308,616]{1,0:T(8,128)(2,1)S(1)}, bf16[308,616]{1,0:T(8,128)(2,1)S(1)}, u32[]{:S(2)}, u32[]{:S(2)}) collective-permute-start(bf16[308,616]{1,0:T(8,128)(2,1)S(1)} %copy-done.1), channel_id=1, source_target_pairs={{0,1},{1,0},{2,3},{3,2},{4,5},{5,4},{6,7},{7,6},{8,9},{9,8},{10,11... | collective-permute-start | bytes 1138376 | tf_op jit(solution)/shard_map/ppermute | solution.py:20
  23.3 7.8 %collective-permute-start.5 = (bf16[3,64,411]{2,1,0:T(8,128)(2,1)S(1)}, bf16[3,64,411]{2,1,0:T(8,128)(2,1)S(1)}, u32[]{:S(2)}, u32[]{:S(2)}) collective-permute-start(bf16[3,64,411]{2,1,0:T(8,128)(2,1)S(1)} %copy.29), channel_id=1, source_target_pairs={{0,252},{2,254},{4,0},{6,2},{8,4},{10,6},{12,8},{14,10},{16,12},{1... | collective-permute-start | bytes 473480 | tf_op jit(solution)/shard_map/ppermute | solution.py:16
  26.1 7.5 %collective-permute-start.4 = (bf16[3,64,411]{2,1,0:T(8,128)(2,1)S(1)}, bf16[3,64,411]{2,1,0:T(8,128)(2,1)S(1)}, u32[]{:S(2)}, u32[]{:S(2)}) collective-permute-start(bf16[3,64,411]{2,1,0:T(8,128)(2,1)S(1)} %copy.30), channel_id=1, source_target_pairs={{0,254},{2,0},{4,2},{6,4},{8,6},{10,8},{12,10},{14,12},{16,14},{18... | collective-permute-start | bytes 473480 | tf_op jit(solution)/shard_map/ppermute | solution.py:16
  29.0 11.1 %collective-permute-start.3 = (bf16[3,64,411]{2,1,0:T(8,128)(2,1)S(1)}, bf16[3,64,411]{2,1,0:T(8,128)(2,1)S(1)}, u32[]{:S(2)}, u32[]{:S(2)}) collective-permute-start(bf16[3,64,411]{2,1,0:T(8,128)(2,1)S(1)} %copy.32), channel_id=1, source_target_pairs={{0,2},{2,4},{4,6},{6,8},{8,10},{10,12},{12,14},{14,16},{16,18},{18... | collective-permute-start | bytes 473480 | tf_op jit(solution)/shard_map/ppermute | solution.py:16
  31.1 9.0 %copy-start.2 = (bf16[3,64,411]{2,1,0:T(8,128)(2,1)}, bf16[3,64,411]{2,1,0:T(8,128)(2,1)S(1)}, u32[]{:S(2)}) copy-start(bf16[3,64,411]{2,1,0:T(8,128)(2,1)S(1)} %collective-permute-done.5.s3_ref) | copy-start | bytes 473476
  33.7 6.4 %copy-start.3 = (bf16[3,64,411]{2,1,0:T(8,128)(2,1)}, bf16[3,64,411]{2,1,0:T(8,128)(2,1)S(1)}, u32[]{:S(2)}) copy-start(bf16[3,64,411]{2,1,0:T(8,128)(2,1)S(1)} %collective-permute-done.4.s2_ref) | copy-start | bytes 473476
  40.1 0.7 copy-start.4
  55.5 4.7 %collective-permute-start.9 = (bf16[3,64,411]{2,1,0:T(8,128)(2,1)}, bf16[3,64,411]{2,1,0:T(8,128)(2,1)S(1)}, u32[]{:S(2)}, u32[]{:S(2)}) collective-permute-start(bf16[3,64,411]{2,1,0:T(8,128)(2,1)} %get-tuple-element.9), channel_id=1, source_target_pairs={{0,254},{2,0},{4,2},{6,4},{8,6},{10,8},{12,10},{14,12},{16,14},{18... | collective-permute-start | bytes 473480 | tf_op jit(solution)/shard_map/ppermute | solution.py:16
  56.8 11.6 %collective-permute-start.10 = (bf16[3,64,411]{2,1,0:T(8,128)(2,1)}, bf16[3,64,411]{2,1,0:T(8,128)(2,1)S(1)}, u32[]{:S(2)}, u32[]{:S(2)}) collective-permute-start(bf16[3,64,411]{2,1,0:T(8,128)(2,1)} %get-tuple-element.11), channel_id=1, source_target_pairs={{0,2},{2,4},{4,6},{6,8},{8,10},{10,12},{12,14},{14,16},{16,18},{18... | collective-permute-start | bytes 473480 | tf_op jit(solution)/shard_map/ppermute | solution.py:16
  57.0 12.6 %collective-permute-start.11 = (bf16[3,64,411]{2,1,0:T(8,128)(2,1)}, bf16[3,64,411]{2,1,0:T(8,128)(2,1)S(1)}, u32[]{:S(2)}, u32[]{:S(2)}) collective-permute-start(bf16[3,64,411]{2,1,0:T(8,128)(2,1)} %get-tuple-element.12), channel_id=1, source_target_pairs={{0,4},{2,6},{4,8},{6,10},{8,12},{10,14},{12,16},{14,18},{16,20},{1... | collective-permute-start | bytes 473480 | tf_op jit(solution)/shard_map/ppermute | solution.py:16
  71.2 6.8 %collective-permute-start.12 = (bf16[16,64,411]{2,0,1:T(8,128)(2,1)S(1)}, bf16[16,64,411]{2,0,1:T(8,128)(2,1)S(1)}, u32[]{:S(2)}, u32[]{:S(2)}) collective-permute-start(bf16[16,64,411]{2,0,1:T(8,128)(2,1)S(1)} %convolution_convert_fusion), channel_id=1, source_target_pairs={{0,1},{1,0},{2,3},{3,2},{4,5},{5,4},{6,7},{7,6},{8,9},{9,8},{10,11... | collective-permute-start | bytes 2525192 | tf_op jit(solution)/shard_map/ppermute | solution.py:20

commit v8 on v4

--- a/solution.py
+++ b/solution.py
@@ -25,41 +25,74 @@
 
 
 def adjoint_kernel(place_ref, count_ref, s0_ref, s1_ref, s2_ref, s3_ref, jc_ref, jo_ref, ic_ref, io_ref,
-                   rcc_ref, rco_ref, roc_ref, roo_ref, out_ref):
+                   rcc_ref, rco_ref, roc_ref, roo_ref, o0_ref, o1_ref, o2_ref, o3_ref,
+                   jc_s, jo_s, dc_s, do_s):
     parts = (s0_ref, s1_ref, s2_ref, s3_ref)
-    foot = out_ref.shape[0]
-    for f in range(foot):
-        group = place_ref[f] // CAP
-        rank = place_ref[f] % CAP
-        s = parts[3][rank]
-        for g in (2, 1, 0):
-            s = jnp.where(group == g, parts[g][rank], s)
-        jc = jc_ref[:, f, :]
-        jo = jo_ref[:, f, :]
-        ev_c = lax.dot_general(s, jc, NT, preferred_element_type=jnp.float32)
-        ev_o = lax.dot_general(s, jo, NT, preferred_element_type=jnp.float32)
-        dep_c = (ev_c - ic_ref[f:f + 1, :]).astype(jnp.bfloat16)
-        dep_o = (ev_o - io_ref[f:f + 1, :]).astype(jnp.bfloat16)
+    outs = (o0_ref, o1_ref, o2_ref, o3_ref)
+    foot = jc_s.shape[0]
+    rows = s0_ref.shape[1]
+    f = pl.program_id(0)
+    group = place_ref[f] // CAP
+    rank = place_ref[f] % CAP
+    s = parts[3][rank]
+    for g in (2, 1, 0):
+        s = jnp.where(group == g, parts[g][rank], s)
+    jc = jc_ref[0]
+    jo = jo_ref[0]
+    jc_s[f] = jc
+    jo_s[f] = jo
+    ev_c = lax.dot_general(s, jc, NT, preferred_element_type=jnp.float32)
+    ev_o = lax.dot_general(s, jo, NT, preferred_element_type=jnp.float32)
+    at = pl.multiple_of(f * rows, rows)
+    dc_s[pl.ds(at, rows), :] = (ev_c - ic_ref[pl.ds(f, 1), :]).astype(jnp.bfloat16)
+    do_s[pl.ds(at, rows), :] = (ev_o - io_ref[pl.ds(f, 1), :]).astype(jnp.bfloat16)
+
+    @pl.when(f == foot - 1)
+    def _():
+        dep_c = dc_s[...]
+        dep_o = do_s[...]
         w_c = (jnp.dot(dep_c, rcc_ref[...], preferred_element_type=jnp.float32)
                + jnp.dot(dep_o, roc_ref[...], preferred_element_type=jnp.float32)).astype(jnp.bfloat16)
         w_o = (jnp.dot(dep_c, rco_ref[...], preferred_element_type=jnp.float32)
                + jnp.dot(dep_o, roo_ref[...], preferred_element_type=jnp.float32)).astype(jnp.bfloat16)
-        adj = (jnp.dot(w_c, jc, preferred_element_type=jnp.float32)
-               + jnp.dot(w_o, jo, preferred_element_type=jnp.float32))
-        live = f < count_ref[0]
-        out_ref[f] = jnp.where(live, adj, 0.0).astype(out_ref.dtype)
+        for o_ref in outs:
+            o_ref[...] = jnp.zeros(o_ref.shape, o_ref.dtype)
+        for h in range(foot):
+            adj = (jnp.dot(w_c[h * rows:(h + 1) * rows], jc_s[h], preferred_element_type=jnp.float32)
+                   + jnp.dot(w_o[h * rows:(h + 1) * rows], jo_s[h], preferred_element_type=jnp.float32))
+            adj = jnp.where(h < count_ref[0], adj, 0.0).astype(jnp.bfloat16)
+            grp = place_ref[h] // CAP
+            rnk = place_ref[h] % CAP
+            for g in range(SPAN):
+                @pl.when(grp == g)
+                def _():
+                    outs[g][rnk] = adj
 
 
 def adjoints(place, count, fetched, jac_c, jac_o, innov_c, innov_o, r_blocks):
-    half_ch, foot, state = jac_c.shape
+    foot, half_ch, state = jac_c.shape
     half_m = fetched[0].shape[1]
-    smem = pl.BlockSpec(memory_space=pltpu.SMEM)
-    vmem = pl.BlockSpec(memory_space=pltpu.VMEM)
+    whole3 = lambda f, p, n: (0, 0, 0)
+    whole2 = lambda f, p, n: (0, 0)
+    part = pl.BlockSpec(fetched[0].shape, whole3)
+    jblock = pl.BlockSpec((1, half_ch, state), lambda f, p, n: (f, 0, 0))
+    grid_spec = pltpu.PrefetchScalarGridSpec(
+        num_scalar_prefetch=2,
+        grid=(foot,),
+        in_specs=[part] * SPAN + [jblock, jblock,
+                                  pl.BlockSpec((foot, half_ch), whole2),
+                                  pl.BlockSpec((foot, half_ch), whole2)]
+                 + [pl.BlockSpec((half_ch, half_ch), whole2)] * 4,
+        out_specs=[pl.BlockSpec((CAP, half_m, state), whole3)] * SPAN,
+        scratch_shapes=[pltpu.VMEM((foot, half_ch, state), jnp.bfloat16),
+                        pltpu.VMEM((foot, half_ch, state), jnp.bfloat16),
+                        pltpu.VMEM((foot * half_m, half_ch), jnp.bfloat16),
+                        pltpu.VMEM((foot * half_m, half_ch), jnp.bfloat16)],
+    )
     return pl.pallas_call(
         adjoint_kernel,
-        in_specs=[smem, smem] + [vmem] * 12,
-        out_specs=vmem,
-        out_shape=jax.ShapeDtypeStruct((foot, half_m, state), jnp.bfloat16),
+        grid_spec=grid_spec,
+        out_shape=[jax.ShapeDtypeStruct((CAP, half_m, state), jnp.bfloat16)] * SPAN,
     )(place, count, *fetched, jac_c, jac_o, innov_c, innov_o, *r_blocks)
 
 
@@ -74,8 +107,8 @@
     capacity = CAP
     slots_total = SPAN * capacity
 
-    jac_c = jnp.transpose(jacobian, (1, 0, 2))
-    jac_o = jnp.transpose(swapped(jacobian), (1, 0, 2))
+    jac_c = jacobian
+    jac_o = swapped(jacobian)
     innov_c = innovation.astype(jnp.float32)
     innov_o = swapped(innovation).astype(jnp.float32)
     r_o = swapped(r_inverse)
@@ -113,13 +146,10 @@
     for g in range(SPAN):
         picked = pick(slot_parts[g])
         fetched_parts.append(picked if g == 1 else passed_along(picked, "tile", 1 - g))
-    adjoint = adjoints(place, foot_counts, fetched_parts, jac_c, jac_o, innov_c, innov_o, r_blocks)
-
-    packed = jnp.einsum("af,fmd->amd", hit.astype(jnp.bfloat16), adjoint,
-                        preferred_element_type=jnp.float32).astype(jnp.bfloat16)
+    packed = adjoints(place, foot_counts, fetched_parts, jac_c, jac_o, innov_c, innov_o, r_blocks)
     recv_parts = []
     for g in range(SPAN):
-        piece = packed[g * capacity:(g + 1) * capacity]
+        piece = packed[g]
         if g == 1:
             recv_parts.append(piece)
         else:

time: 89.8 us -> 86.7 us (0.965)
  waiting for transfers between devices: 27.8 us -> 19.9 us
  local copies, waits for them, and re-layouts: 12 us -> 19.7 us
  Pallas kernels: 15.2 us -> 11.4 us
  matrix products: 3.97 us -> 1.99 us
  starting transfers between devices: 22.5 us -> 24.1 us
  other arithmetic: 7.32 us -> 8.35 us
    ppermute x9, waiting for transfers between devices: 25.5 us -> 17.6 us  [passed_along(): lax.ppermute(value, axis, [(i, (i + by) % count) for i in range(count)])]
    unnamed x14, local copies, waits for them, and re-layouts: 0.67 us -> 8.07 us
    ppermute x0 -> x1, local copies, waits for them, and re-layouts: none -> 4.03 us  [swapped(): return lax.ppermute(value, 'chan', [(0, 1), (1, 0)])]
    pallas_call x1, Pallas kernels: 15.2 us -> 11.4 us  [adjoints(): pl.pallas_call(adjoint_kernel, grid_spec=grid_spec, out_shape=[jax.ShapeD...]
    dynamic_slice x2 -> x1, local copies, waits for them, and re-layouts: 5.04 us -> 1.7 us  [on_device(): lax.dynamic_slice_in_dim(increments, core * half_m, half_m, axis=1)]
    dot_general x1 -> x0, matrix products: 1.61 us -> none  [on_device(): jnp.einsum('af,fmd->amd', hit.astype(jnp.bfloat16), adjoint, preferred_el...]
    ppermute x4, starting transfers between devices: 7.15 us -> 8.25 us  [swapped(): return lax.ppermute(value, 'chan', [(0, 1), (1, 0)])]
    concatenate x0 -> x1, other arithmetic: none -> 1.05 us  [on_device(): jnp.concatenate(recv_parts, axis=0)]
  transfers between devices with their start and end apart: 13 -> 13, of which waited for: 6 -> 5; matrix products, arithmetic and copies ran while one was open for 14% -> 24% of each run, Pallas kernels for 0% -> 0%
where the time goes in v8:
time: 86.7 us; the launch traced here: 86.2 us
  starting transfers between devices  24.1 us (28%)
  waiting for transfers between devices  19.9 us (23%)
  local copies, waits for them, and re-layouts  19.7 us (23%)
  Pallas kernels  11.4 us (13%)
  other arithmetic  8.35 us (10%)
  matrix products  1.99 us (2%)
    ppermute x9, waiting for transfers between devices, passed_along(): lax.ppermute(value, axis, [(i, (i + by) % count) for i in range(count)])  17.6 us
    ppermute x9, starting transfers between devices, passed_along(): lax.ppermute(value, axis, [(i, (i + by) % count) for i in range(count)])  15.9 us
    pallas_call x1, Pallas kernels, adjoints(): pl.pallas_call(adjoint_kernel, grid_spec=grid_spec, out_shape=[jax.ShapeD...  11.4 us
    ppermute x4, starting transfers between devices, swapped(): return lax.ppermute(value, 'chan', [(0, 1), (1, 0)])  8.25 us
    unnamed x14, local copies, waits for them, and re-layouts  8.07 us
    select_n x1, local copies, waits for them, and re-layouts, on_device(): jnp.where(first, jnp.concatenate([mine, other], axis=1), jnp.concatenate(...  4.94 us
    ppermute x1, local copies, waits for them, and re-layouts, swapped(): return lax.ppermute(value, 'chan', [(0, 1), (1, 0)])  4.03 us
    ppermute x4, waiting for transfers between devices, swapped(): return lax.ppermute(value, 'chan', [(0, 1), (1, 0)])  2.29 us
  transfers between devices with their start and end apart: 13, of which 5 were waited for; matrix products, arithmetic and copies ran while one was open for 24% of the time, Pallas kernels for 0%

profile of v8, /device:TPU:1, one launch (start us, length us, event | category | flops | bytes accessed | tf_op | source)
XLA Modules:
  0.0 86.2 jit_solution(2483155937579199218)
XLA Ops:
  0.0 3.2 %collective-permute-start.6 = (bf16[8,308,411]{2,0,1:T(8,128)(2,1)}, bf16[8,308,411]{2,0,1:T(8,128)(2,1)}, u32[]{:S(2)}, u32[]{:S(2)}) collective-permute-start(bf16[8,308,411]{2,0,1:T(8,128)(2,1)} %param.7), channel_id=1, source_target_pairs={{0,1},{1,0},{2,3},{3,2},{4,5},{5,4},{6,7},{7,6},{8,9},{9,8},{10,11... | collective-permute-start | bytes 6076232 | tf_op jit(solution)/shard_map/ppermute | solution.py:20
  3.2 0.9 %convert_reduce_fusion = s32[8]{0:T(128)S(1)} fusion(s32[8]{0:T(128)} %bitcast.21), kind=kLoop, calls=%fused_computation.19 | loop fusion | flops 312 | bytes 64 | tf_op jit(solution)/shard_map/reduce_sum | solution.py:130
  4.1 0.7 multiply_add_fusion.place_ref
  4.8 0.7 select_reduce_fusion
  5.5 0.1 fusion.21
  5.6 1.2 %collective-permute-start.2 = (s32[3]{0:T(128)S(1)}, s32[3]{0:T(128)S(1)}, u32[]{:S(2)}, u32[]{:S(2)}) collective-permute-start(s32[3]{0:T(128)S(1)} %get-tuple-element.19), channel_id=1, source_target_pairs={{0,4},{2,6},{4,8},{6,10},{8,12},{10,14},{12,16},{14,18},{16,20},{1... | collective-permute-start | bytes 44 | tf_op jit(solution)/shard_map/ppermute | solution.py:16
  6.8 0.4 collective-permute-start.1
  7.2 7.1 %collective-permute-start = (s32[3]{0:T(128)S(1)}, s32[3]{0:T(128)S(1)}, u32[]{:S(2)}, u32[]{:S(2)}) collective-permute-start(s32[3]{0:T(128)S(1)} %get-tuple-element.22), channel_id=1, source_target_pairs={{0,254},{2,0},{4,2},{6,4},{8,6},{10,8},{12,10},{14,12},{16,14},{18... | collective-permute-start | bytes 44 | tf_op jit(solution)/shard_map/ppermute | solution.py:16
  14.3 0.4 collective-permute-start.7
  14.6 1.3 %convert_element_type.34.ic_ref = f32[8,308]{1,0:T(8,128)} convert(bf16[8,308]{1,0:T(8,128)(2,1)} %param.9) | non-fusion elementwise | flops 2464 | bytes 14784 | tf_op jit(solution)/shard_map/convert_element_type | solution.py:112
  15.9 4.0 %copy.31.jc_ref = bf16[8,308,411]{2,1,0:T(8,128)(2,1)} copy(bf16[8,308,411]{2,0,1:T(8,128)(2,1)} %param.7) | data formatting | bytes 4050816 | tf_op args[0]
  20.6 1.7 %constant_dynamic-slice_fusion = bf16[16,64,411]{1,0,2:T(8,128)(2,1)} fusion(bf16[16,128,411]{1,0,2:T(8,128)(2,1)S(1)} %copy-done, s32[]{:T(128)S(6)} %select_n.49), kind=kLoop, calls=%fused_computation.40 | loop fusion | bytes 1683460 | tf_op jit(solution)/shard_map/dynamic_slice | solution.py:135
  22.3 3.3 %copy.35 = bf16[16,64,411]{2,0,1:T(8,128)(2,1)S(1)} copy(bf16[16,64,411]{1,0,2:T(8,128)(2,1)} %constant_dynamic-slice_fusion) | data formatting | bytes 1683456
  25.7 0.4 fusion.9
  26.0 0.7 copy.44.s1_ref
  26.8 0.0 collective-permute-done.2
  26.8 0.2 collective-permute-start.8
  26.9 0.3 fusion.15
  27.3 0.0 collective-permute-done.1
  27.4 2.4 %collective-permute-start.5 = (bf16[3,64,411]{2,1,0:T(8,128)(2,1)S(1)}, bf16[3,64,411]{2,1,0:T(8,128)(2,1)S(1)}, u32[]{:S(2)}, u32[]{:S(2)}) collective-permute-start(bf16[3,64,411]{2,1,0:T(8,128)(2,1)S(1)} %copy.42), channel_id=1, source_target_pairs={{0,252},{2,254},{4,0},{6,2},{8,4},{10,6},{12,8},{14,10},{16,12},{1... | collective-permute-start | bytes 473480 | tf_op jit(solution)/shard_map/ppermute | solution.py:16
  29.7 0.3 fusion.12
  30.2 0.0 collective-permute-done
  30.2 2.4 %collective-permute-start.4 = (bf16[3,64,411]{2,1,0:T(8,128)(2,1)S(1)}, bf16[3,64,411]{2,1,0:T(8,128)(2,1)S(1)}, u32[]{:S(2)}, u32[]{:S(2)}) collective-permute-start(bf16[3,64,411]{2,1,0:T(8,128)(2,1)S(1)} %copy.43), channel_id=1, source_target_pairs={{0,254},{2,0},{4,2},{6,4},{8,6},{10,8},{12,10},{14,12},{16,14},{18... | collective-permute-start | bytes 473480 | tf_op jit(solution)/shard_map/ppermute | solution.py:16
  32.6 0.3 fusion.6
  33.0 0.0 collective-permute-done.7
  33.0 0.3 collective-permute-start.3
  33.3 0.6 convert_element_type.35.io_ref
  33.9 0.0 collective-permute-done.8
  33.9 0.1 broadcast_select_fusion.1
  34.0 1.1 %broadcast_select_fusion.2 = (bf16[308,308]{1,0:T(8,128)(2,1)}, bf16[308,308]{1,0:T(8,128)(2,1)}, bf16[308,308]{1,0:T(8,128)(2,1)}, bf16[308,308]{1,0:T(8,128)(2,1)}) fusion(pred[]{:T(512)S(6)} %eq.44, bf16[308,616]{1,0:T(8,128)(2,1)S(1)} %get-tuple-element.18, bf16[308,616]{1,0:T(8,128)(2,1)S(1)} %get-tuple-element.17), kind=kLoop, calls=%fused_computation.10 | loop fusion | flops 379456 | bytes 1517825 | tf_op jit(solution)/shard_map/jit(_where)/select_n | solution.py:124
  35.1 0.0 collective-permute-done.6
  35.1 4.0 %copy.32.jo_ref = bf16[8,308,411]{2,1,0:T(8,128)(2,1)} copy(bf16[8,308,411]{2,0,1:T(8,128)(2,1)} %collective-permute-done.6) | data formatting | bytes 4050816 | tf_op jit(solution)/shard_map/ppermute | solution.py:20
  39.2 4.9 %collective-permute-done.3.s0_ref = bf16[3,64,411]{2,1,0:T(8,128)(2,1)S(1)} collective-permute-done((bf16[3,64,411]{2,1,0:T(8,128)(2,1)S(1)}, bf16[3,64,411]{2,1,0:T(8,128)(2,1)S(1)}, u32[]{:S(2)}, u32[]{:S(2)}) %collective-permute-start.3) | collective-permute-done | bytes 157856 | tf_op jit(solution)/shard_map/ppermute | solution.py:16
  44.1 0.7 copy-done.4
  44.8 11.4 %shard_map.73 = (bf16[3,64,411]{2,1,0:T(8,128)(2,1)}, bf16[3,64,411]{2,1,0:T(8,128)(2,1)}, bf16[3,64,411]{2,1,0:T(8,128)(2,1)}, bf16[3,64,411]{2,1,0:T(8,128)(2,1)}) custom-call(s32[8]{0:T(128)} %copy-done.5, s32[1]{0:T(128)S(6)} %copy.46.count_ref, bf16[3,64,411]{2,1,0:T(8,128)(2,1)} %copy-done.4, bf16[3,64,411]{2,1,0:T(8,128)(2,1)} %copy.44.s1_ref, ...), custom_call_target="tpu_custom_call" | custom-call | tf_op jit(solution)/shard_map/pallas_call | solution.py:92
  56.2 2.1 %collective-permute-start.9 = (bf16[3,64,411]{2,1,0:T(8,128)(2,1)}, bf16[3,64,411]{2,1,0:T(8,128)(2,1)S(1)}, u32[]{:S(2)}, u32[]{:S(2)}) collective-permute-start(bf16[3,64,411]{2,1,0:T(8,128)(2,1)} %get-tuple-element.9), channel_id=1, source_target_pairs={{0,254},{2,0},{4,2},{6,4},{8,6},{10,8},{12,10},{14,12},{16,14},{18... | collective-permute-start | bytes 473480 | tf_op jit(solution)/shard_map/ppermute | solution.py:16
  58.3 0.0 collective-permute-start.10
  58.3 0.0 collective-permute-start.11
  58.3 0.1 pad_add_fusion
  58.4 3.2 %collective-permute-done.9 = bf16[3,64,411]{2,1,0:T(8,128)(2,1)S(1)} collective-permute-done((bf16[3,64,411]{2,1,0:T(8,128)(2,1)}, bf16[3,64,411]{2,1,0:T(8,128)(2,1)S(1)}, u32[]{:S(2)}, u32[]{:S(2)}) %collective-permute-start.9) | collective-permute-done | bytes 157856 | tf_op jit(solution)/shard_map/ppermute | solution.py:16
  61.5 8.5 %collective-permute-done.10 = bf16[3,64,411]{2,1,0:T(8,128)(2,1)S(1)} collective-permute-done((bf16[3,64,411]{2,1,0:T(8,128)(2,1)}, bf16[3,64,411]{2,1,0:T(8,128)(2,1)S(1)}, u32[]{:S(2)}, u32[]{:S(2)}) %collective-permute-start.10) | collective-permute-done | bytes 157856 | tf_op jit(solution)/shard_map/ppermute | solution.py:16
  70.0 1.0 %collective-permute-done.11 = bf16[3,64,411]{2,1,0:T(8,128)(2,1)S(1)} collective-permute-done((bf16[3,64,411]{2,1,0:T(8,128)(2,1)}, bf16[3,64,411]{2,1,0:T(8,128)(2,1)S(1)}, u32[]{:S(2)}, u32[]{:S(2)}) %collective-permute-start.11) | collective-permute-done | bytes 157856 | tf_op jit(solution)/shard_map/ppermute | solution.py:16
  71.0 1.0 %pad_maximum_fusion = bf16[12,64,411]{2,1,0:T(8,128)(2,1)S(1)} fusion(bf16[3,64,411]{2,1,0:T(8,128)(2,1)S(1)} %collective-permute-done.11, bf16[3,64,411]{2,1,0:T(8,128)(2,1)S(1)} %collective-permute-done.10, bf16[3,64,411]{2,1,0:T(8,128)(2,1)} %get-tuple-element.10, bf16[3,64,411]{2,1,0:T(8,128)(2,1)S(1)} %collective-permute-done.9), kind=kLoop, calls=%fused_computation.3 | loop fusion | flops 946944 | bytes 1262592 | tf_op jit(solution)/shard_map/concatenate | solution.py:158
  72.1 0.6 convolution_convert_fusion
  72.7 4.5 %collective-permute-start.12 = (bf16[16,64,411]{2,0,1:T(8,128)(2,1)S(1)}, bf16[16,64,411]{2,0,1:T(8,128)(2,1)S(1)}, u32[]{:S(2)}, u32[]{:S(2)}) collective-permute-start(bf16[16,64,411]{2,0,1:T(8,128)(2,1)S(1)} %convolution_convert_fusion), channel_id=1, source_target_pairs={{0,1},{1,0},{2,3},{3,2},{4,5},{5,4},{6,7},{7,6},{8,9},{9,8},{10,11... | collective-permute-start | bytes 2525192 | tf_op jit(solution)/shard_map/ppermute | solution.py:20
  77.2 2.3 %collective-permute-done.12 = bf16[16,64,411]{2,0,1:T(8,128)(2,1)S(1)} collective-permute-done((bf16[16,64,411]{2,0,1:T(8,128)(2,1)S(1)}, bf16[16,64,411]{2,0,1:T(8,128)(2,1)S(1)}, u32[]{:S(2)}, u32[]{:S(2)}) %collective-permute-start.12) | collective-permute-done | bytes 841760 | tf_op jit(solution)/shard_map/ppermute | solution.py:20
  79.5 1.8 %maximum_select_fusion = bf16[16,128,411]{2,0,1:T(8,128)(2,1)} fusion(bf16[16,64,411]{2,0,1:T(8,128)(2,1)S(1)} %collective-permute-done.12, bf16[16,64,411]{2,0,1:T(8,128)(2,1)S(1)} %convolution_convert_fusion, pred[]{:T(512)S(6)} %eq.44), kind=kLoop, calls=%fused_computation | loop fusion | flops 2525184 | bytes 3366913 | tf_op jit(solution)/shard_map/jit(_where)/select_n | solution.py:161
  81.3 4.9 %copy.34 = bf16[16,128,411]{1,0,2:T(8,128)(2,1)} copy(bf16[16,128,411]{2,0,1:T(8,128)(2,1)} %maximum_select_fusion) | data formatting | bytes 3366912 | tf_op jit(solution)/shard_map/jit(_where)/select_n | solution.py:161
  (16 shorter events, 0.2 us)
Async XLA Ops:
  0.0 20.6 %copy-start = (bf16[16,128,411]{1,0,2:T(8,128)(2,1)S(1)}, bf16[16,128,411]{1,0,2:T(8,128)(2,1)}, u32[]{:S(2)}) copy-start(bf16[16,128,411]{1,0,2:T(8,128)(2,1)} %param.10) | copy-start | bytes 5050372
  0.0 35.1 %collective-permute-start.6 = (bf16[8,308,411]{2,0,1:T(8,128)(2,1)}, bf16[8,308,411]{2,0,1:T(8,128)(2,1)}, u32[]{:S(2)}, u32[]{:S(2)}) collective-permute-start(bf16[8,308,411]{2,0,1:T(8,128)(2,1)} %param.7), channel_id=1, source_target_pairs={{0,1},{1,0},{2,3},{3,2},{4,5},{5,4},{6,7},{7,6},{8,9},{9,8},{10,11... | collective-permute-start | bytes 6076232 | tf_op jit(solution)/shard_map/ppermute | solution.py:20
  4.8 15.2 %copy-start.5 = (s32[8]{0:T(128)}, s32[8]{0:T(128)S(1)}, u32[]{:S(2)}) copy-start(s32[8]{0:T(128)S(1)} %multiply_add_fusion.place_ref) | copy-start | bytes 100
  5.6 21.2 %collective-permute-start.2 = (s32[3]{0:T(128)S(1)}, s32[3]{0:T(128)S(1)}, u32[]{:S(2)}, u32[]{:S(2)}) collective-permute-start(s32[3]{0:T(128)S(1)} %get-tuple-element.19), channel_id=1, source_target_pairs={{0,4},{2,6},{4,8},{6,10},{8,12},{10,14},{12,16},{14,18},{16,20},{1... | collective-permute-start | bytes 44 | tf_op jit(solution)/shard_map/ppermute | solution.py:16
  6.8 20.5 %collective-permute-start.1 = (s32[3]{0:T(128)S(1)}, s32[3]{0:T(128)S(1)}, u32[]{:S(2)}, u32[]{:S(2)}) collective-permute-start(s32[3]{0:T(128)S(1)} %get-tuple-element.20), channel_id=1, source_target_pairs={{0,2},{2,4},{4,6},{6,8},{8,10},{10,12},{12,14},{14,16},{16,18},{18... | collective-permute-start | bytes 44 | tf_op jit(solution)/shard_map/ppermute | solution.py:16
  7.2 23.0 %collective-permute-start = (s32[3]{0:T(128)S(1)}, s32[3]{0:T(128)S(1)}, u32[]{:S(2)}, u32[]{:S(2)}) collective-permute-start(s32[3]{0:T(128)S(1)} %get-tuple-element.22), channel_id=1, source_target_pairs={{0,254},{2,0},{4,2},{6,4},{8,6},{10,8},{12,10},{14,12},{16,14},{18... | collective-permute-start | bytes 44 | tf_op jit(solution)/shard_map/ppermute | solution.py:16
  14.3 18.7 %collective-permute-start.7 = (bf16[8,308]{1,0:T(8,128)(2,1)}, bf16[8,308]{1,0:T(8,128)(2,1)S(1)}, u32[]{:S(2)}, u32[]{:S(2)}) collective-permute-start(bf16[8,308]{1,0:T(8,128)(2,1)} %param.9), channel_id=1, source_target_pairs={{0,1},{1,0},{2,3},{3,2},{4,5},{5,4},{6,7},{7,6},{8,9},{9,8},{10,11... | collective-permute-start | bytes 14792 | tf_op jit(solution)/shard_map/ppermute | solution.py:20
  22.3 4.4 %copy-start.1 = (bf16[308,616]{1,0:T(8,128)(2,1)S(1)}, bf16[308,616]{1,0:T(8,128)(2,1)}, u32[]{:S(2)}) copy-start(bf16[308,616]{1,0:T(8,128)(2,1)} %param.8) | copy-start | bytes 1138372
  26.8 7.1 %collective-permute-start.8 = (bf16[308,616]{1,0:T(8,128)(2,1)S(1)}, bf16[308,616]{1,0:T(8,128)(2,1)S(1)}, u32[]{:S(2)}, u32[]{:S(2)}) collective-permute-start(bf16[308,616]{1,0:T(8,128)(2,1)S(1)} %copy-done.1), channel_id=1, source_target_pairs={{0,1},{1,0},{2,3},{3,2},{4,5},{5,4},{6,7},{7,6},{8,9},{9,8},{10,11... | collective-permute-start | bytes 1138376 | tf_op jit(solution)/shard_map/ppermute | solution.py:20
  27.4 11.8 %collective-permute-start.5 = (bf16[3,64,411]{2,1,0:T(8,128)(2,1)S(1)}, bf16[3,64,411]{2,1,0:T(8,128)(2,1)S(1)}, u32[]{:S(2)}, u32[]{:S(2)}) collective-permute-start(bf16[3,64,411]{2,1,0:T(8,128)(2,1)S(1)} %copy.42), channel_id=1, source_target_pairs={{0,252},{2,254},{4,0},{6,2},{8,4},{10,6},{12,8},{14,10},{16,12},{1... | collective-permute-start | bytes 473480 | tf_op jit(solution)/shard_map/ppermute | solution.py:16
  30.2 9.0 %collective-permute-start.4 = (bf16[3,64,411]{2,1,0:T(8,128)(2,1)S(1)}, bf16[3,64,411]{2,1,0:T(8,128)(2,1)S(1)}, u32[]{:S(2)}, u32[]{:S(2)}) collective-permute-start(bf16[3,64,411]{2,1,0:T(8,128)(2,1)S(1)} %copy.43), channel_id=1, source_target_pairs={{0,254},{2,0},{4,2},{6,4},{8,6},{10,8},{12,10},{14,12},{16,14},{18... | collective-permute-start | bytes 473480 | tf_op jit(solution)/shard_map/ppermute | solution.py:16
  33.0 11.1 %collective-permute-start.3 = (bf16[3,64,411]{2,1,0:T(8,128)(2,1)S(1)}, bf16[3,64,411]{2,1,0:T(8,128)(2,1)S(1)}, u32[]{:S(2)}, u32[]{:S(2)}) collective-permute-start(bf16[3,64,411]{2,1,0:T(8,128)(2,1)S(1)} %copy.45), channel_id=1, source_target_pairs={{0,2},{2,4},{4,6},{6,8},{8,10},{10,12},{12,14},{14,16},{16,18},{18... | collective-permute-start | bytes 473480 | tf_op jit(solution)/shard_map/ppermute | solution.py:16
  39.1 5.0 %copy-start.2 = (bf16[3,64,411]{2,1,0:T(8,128)(2,1)}, bf16[3,64,411]{2,1,0:T(8,128)(2,1)S(1)}, u32[]{:S(2)}) copy-start(bf16[3,64,411]{2,1,0:T(8,128)(2,1)S(1)} %collective-permute-done.5.s3_ref) | copy-start | bytes 473476
  39.2 5.0 %copy-start.3 = (bf16[3,64,411]{2,1,0:T(8,128)(2,1)}, bf16[3,64,411]{2,1,0:T(8,128)(2,1)S(1)}, u32[]{:S(2)}) copy-start(bf16[3,64,411]{2,1,0:T(8,128)(2,1)S(1)} %collective-permute-done.4.s2_ref) | copy-start | bytes 473476
  44.1 0.7 copy-start.4
  56.2 5.3 %collective-permute-start.9 = (bf16[3,64,411]{2,1,0:T(8,128)(2,1)}, bf16[3,64,411]{2,1,0:T(8,128)(2,1)S(1)}, u32[]{:S(2)}, u32[]{:S(2)}) collective-permute-start(bf16[3,64,411]{2,1,0:T(8,128)(2,1)} %get-tuple-element.9), channel_id=1, source_target_pairs={{0,254},{2,0},{4,2},{6,4},{8,6},{10,8},{12,10},{14,12},{16,14},{18... | collective-permute-start | bytes 473480 | tf_op jit(solution)/shard_map/ppermute | solution.py:16
  58.3 11.7 %collective-permute-start.10 = (bf16[3,64,411]{2,1,0:T(8,128)(2,1)}, bf16[3,64,411]{2,1,0:T(8,128)(2,1)S(1)}, u32[]{:S(2)}, u32[]{:S(2)}) collective-permute-start(bf16[3,64,411]{2,1,0:T(8,128)(2,1)} %get-tuple-element.11), channel_id=1, source_target_pairs={{0,2},{2,4},{4,6},{6,8},{8,10},{10,12},{12,14},{14,16},{16,18},{18... | collective-permute-start | bytes 473480 | tf_op jit(solution)/shard_map/ppermute | solution.py:16
  58.3 12.7 %collective-permute-start.11 = (bf16[3,64,411]{2,1,0:T(8,128)(2,1)}, bf16[3,64,411]{2,1,0:T(8,128)(2,1)S(1)}, u32[]{:S(2)}, u32[]{:S(2)}) collective-permute-start(bf16[3,64,411]{2,1,0:T(8,128)(2,1)} %get-tuple-element.12), channel_id=1, source_target_pairs={{0,4},{2,6},{4,8},{6,10},{8,12},{10,14},{12,16},{14,18},{16,20},{1... | collective-permute-start | bytes 473480 | tf_op jit(solution)/shard_map/ppermute | solution.py:16
  72.7 6.8 %collective-permute-start.12 = (bf16[16,64,411]{2,0,1:T(8,128)(2,1)S(1)}, bf16[16,64,411]{2,0,1:T(8,128)(2,1)S(1)}, u32[]{:S(2)}, u32[]{:S(2)}) collective-permute-start(bf16[16,64,411]{2,0,1:T(8,128)(2,1)S(1)} %convolution_convert_fusion), channel_id=1, source_target_pairs={{0,1},{1,0},{2,3},{3,2},{4,5},{5,4},{6,7},{7,6},{8,9},{9,8},{10,11... | collective-permute-start | bytes 2525192 | tf_op jit(solution)/shard_map/ppermute | solution.py:20

commit v9 on v8

--- a/solution.py
+++ b/solution.py
@@ -142,10 +142,9 @@
     for g in range(SPAN):
         wanted = request[g * capacity:(g + 1) * capacity]
         slot_parts.append(wanted if g == 1 else passed_along(wanted, "tile", g - 1))
-    fetched_parts = []
-    for g in range(SPAN):
-        picked = pick(slot_parts[g])
-        fetched_parts.append(picked if g == 1 else passed_along(picked, "tile", 1 - g))
+    picked = [pick(slot_parts[g]) for g in range(SPAN)]
+    picked, jac_c = lax.optimization_barrier((picked, jac_c))
+    fetched_parts = [p if g == 1 else passed_along(p, "tile", 1 - g) for g, p in enumerate(picked)]
     packed = adjoints(place, foot_counts, fetched_parts, jac_c, jac_o, innov_c, innov_o, r_blocks)
     recv_parts = []
     for g in range(SPAN):

time: 86.7 us -> 86.8 us (level)
  starting transfers between devices: 24.1 us -> 30 us
  waiting for transfers between devices: 19.9 us -> 15.8 us
  local copies, waits for them, and re-layouts: 19.7 us -> 18 us
    ppermute x9, starting transfers between devices: 15.9 us -> 21.5 us  [passed_along(): lax.ppermute(value, axis, [(i, (i + by) % count) for i in range(count)])]
    ppermute x9, waiting for transfers between devices: 17.6 us -> 13.5 us  [passed_along(): lax.ppermute(value, axis, [(i, (i + by) % count) for i in range(count)])]
    unnamed x14 -> x15, local copies, waits for them, and re-layouts: 8.07 us -> 4.06 us
    optimization_barrier x0 -> x1, local copies, waits for them, and re-layouts: none -> 2.32 us  [on_device(): picked, jac_c = lax.optimization_barrier((picked, jac_c))]
  transfers between devices with their start and end apart: 13 -> 13, of which waited for: 5 -> 5; matrix products, arithmetic and copies ran while one was open for 24% -> 22% of each run, Pallas kernels for 0% -> 0%
where the time goes in v9:
time: 86.8 us; the launch traced here: 86.4 us
  starting transfers between devices  30 us (35%)
  local copies, waits for them, and re-layouts  18 us (21%)
  waiting for transfers between devices  15.8 us (18%)
  Pallas kernels  11.4 us (13%)
  other arithmetic  8.42 us (10%)
  matrix products  2 us (2%)
    ppermute x9, starting transfers between devices, passed_along(): lax.ppermute(value, axis, [(i, (i + by) % count) for i in range(count)])  21.5 us
    ppermute x9, waiting for transfers between devices, passed_along(): lax.ppermute(value, axis, [(i, (i + by) % count) for i in range(count)])  13.5 us
    pallas_call x1, Pallas kernels, adjoints(): pl.pallas_call(adjoint_kernel, grid_spec=grid_spec, out_shape=[jax.ShapeD...  11.4 us
    ppermute x4, starting transfers between devices, swapped(): return lax.ppermute(value, 'chan', [(0, 1), (1, 0)])  8.48 us
    select_n x1, local copies, waits for them, and re-layouts, on_device(): jnp.where(first, jnp.concatenate([mine, other], axis=1), jnp.concatenate(...  4.94 us
    unnamed x15, local copies, waits for them, and re-layouts  4.06 us
    ppermute x1, local copies, waits for them, and re-layouts, swapped(): return lax.ppermute(value, 'chan', [(0, 1), (1, 0)])  4.04 us
    optimization_barrier x1, local copies, waits for them, and re-layouts, on_device(): picked, jac_c = lax.optimization_barrier((picked, jac_c))  2.32 us
  transfers between devices with their start and end apart: 13, of which 5 were waited for; matrix products, arithmetic and copies ran while one was open for 22% of the time, Pallas kernels for 0%

profile of v9, /device:TPU:1, one launch (start us, length us, event | category | flops | bytes accessed | tf_op | source)
XLA Modules:
  0.0 86.4 jit_solution(15017799304948597216)
XLA Ops:
  0.0 3.2 %collective-permute-start.6 = (bf16[8,308,411]{2,0,1:T(8,128)(2,1)}, bf16[8,308,411]{2,0,1:T(8,128)(2,1)}, u32[]{:S(2)}, u32[]{:S(2)}) collective-permute-start(bf16[8,308,411]{2,0,1:T(8,128)(2,1)} %param.7), channel_id=1, source_target_pairs={{0,1},{1,0},{2,3},{3,2},{4,5},{5,4},{6,7},{7,6},{8,9},{9,8},{10,11... | collective-permute-start | bytes 6076232 | tf_op jit(solution)/shard_map/ppermute | solution.py:20
  3.2 0.9 %convert_reduce_fusion = s32[8]{0:T(128)S(1)} fusion(s32[8]{0:T(128)} %bitcast.21), kind=kLoop, calls=%fused_computation.19 | loop fusion | flops 312 | bytes 64 | tf_op jit(solution)/shard_map/reduce_sum | solution.py:130
  4.1 0.7 multiply_add_fusion.place_ref
  4.8 0.7 select_reduce_fusion
  5.5 0.1 fusion.21
  5.6 1.2 %collective-permute-start.2 = (s32[3]{0:T(128)S(1)}, s32[3]{0:T(128)S(1)}, u32[]{:S(2)}, u32[]{:S(2)}) collective-permute-start(s32[3]{0:T(128)S(1)} %get-tuple-element.29), channel_id=1, source_target_pairs={{0,4},{2,6},{4,8},{6,10},{8,12},{10,14},{12,16},{14,18},{16,20},{1... | collective-permute-start | bytes 44 | tf_op jit(solution)/shard_map/ppermute | solution.py:16
  6.8 0.4 collective-permute-start.1
  7.2 7.1 %collective-permute-start = (s32[3]{0:T(128)S(1)}, s32[3]{0:T(128)S(1)}, u32[]{:S(2)}, u32[]{:S(2)}) collective-permute-start(s32[3]{0:T(128)S(1)} %get-tuple-element.32), channel_id=1, source_target_pairs={{0,254},{2,0},{4,2},{6,4},{8,6},{10,8},{12,10},{14,12},{16,14},{18... | collective-permute-start | bytes 44 | tf_op jit(solution)/shard_map/ppermute | solution.py:16
  14.3 0.4 collective-permute-start.7
  14.6 1.3 %convert_element_type.34.ic_ref = f32[8,308]{1,0:T(8,128)} convert(bf16[8,308]{1,0:T(8,128)(2,1)} %param.9) | non-fusion elementwise | flops 2464 | bytes 14784 | tf_op jit(solution)/shard_map/convert_element_type | solution.py:112
  16.6 1.7 %constant_dynamic-slice_fusion = bf16[16,64,411]{1,0,2:T(8,128)(2,1)} fusion(bf16[16,128,411]{1,0,2:T(8,128)(2,1)S(1)} %copy-done, s32[]{:T(128)S(6)} %select_n.49), kind=kLoop, calls=%fused_computation.40 | loop fusion | bytes 1683460 | tf_op jit(solution)/shard_map/dynamic_slice | solution.py:135
  18.3 3.3 %copy.35 = bf16[16,64,411]{2,0,1:T(8,128)(2,1)S(1)} copy(bf16[16,64,411]{1,0,2:T(8,128)(2,1)} %constant_dynamic-slice_fusion) | data formatting | bytes 1683456
  21.7 0.4 fusion.9
  22.0 0.7 copy.44.s1_ref
  22.7 0.0 collective-permute-done.2
  22.7 0.2 collective-permute-start.8
  22.9 0.3 fusion.15
  23.2 0.0 copy-start.1
  23.3 0.0 collective-permute-done.1
  23.3 0.4 fusion.12
  23.6 0.0 collective-permute-done
  23.6 0.4 fusion.6
  24.2 0.1 collective-permute-start.3
  24.3 6.9 %collective-permute-start.4 = (bf16[3,64,411]{2,1,0:T(8,128)(2,1)S(1)}, bf16[3,64,411]{2,1,0:T(8,128)(2,1)S(1)}, u32[]{:S(2)}, u32[]{:S(2)}) collective-permute-start(bf16[3,64,411]{2,1,0:T(8,128)(2,1)S(1)} %copy.43), channel_id=1, source_target_pairs={{0,254},{2,0},{4,2},{6,4},{8,6},{10,8},{12,10},{14,12},{16,14},{18... | collective-permute-start | bytes 473480 | tf_op jit(solution)/shard_map/ppermute | solution.py:16
  31.1 2.3 %copy.31.jc_ref = bf16[8,308,411]{2,1,0:T(8,128)(2,1)} copy(bf16[8,308,411]{2,0,1:T(8,128)(2,1)S(1)} %copy-done.1) | data formatting | bytes 4050816 | tf_op jit(solution)/shard_map/optimization_barrier | solution.py:146
  33.5 0.0 collective-permute-start.5
  33.5 0.6 convert_element_type.35.io_ref
  34.1 0.0 collective-permute-done.8
  34.1 0.1 broadcast_select_fusion.1
  34.2 1.2 %broadcast_select_fusion.2 = (bf16[308,308]{1,0:T(8,128)(2,1)}, bf16[308,308]{1,0:T(8,128)(2,1)}, bf16[308,308]{1,0:T(8,128)(2,1)}, bf16[308,308]{1,0:T(8,128)(2,1)}) fusion(pred[]{:T(512)S(6)} %eq.44, bf16[308,616]{1,0:T(8,128)(2,1)S(1)} %get-tuple-element.28, bf16[308,616]{1,0:T(8,128)(2,1)S(1)} %get-tuple-element.27), kind=kLoop, calls=%fused_computation.10 | loop fusion | flops 379456 | bytes 1517825 | tf_op jit(solution)/shard_map/jit(_where)/select_n | solution.py:124
  35.4 4.0 %copy.32.jo_ref = bf16[8,308,411]{2,1,0:T(8,128)(2,1)} copy(bf16[8,308,411]{2,0,1:T(8,128)(2,1)} %collective-permute-done.6) | data formatting | bytes 4050816 | tf_op jit(solution)/shard_map/ppermute | solution.py:20
  39.4 0.0 collective-permute-done.4.s2_ref
  39.4 1.1 %collective-permute-done.5.s3_ref = bf16[3,64,411]{2,1,0:T(8,128)(2,1)S(1)} collective-permute-done((bf16[3,64,411]{2,1,0:T(8,128)(2,1)S(1)}, bf16[3,64,411]{2,1,0:T(8,128)(2,1)S(1)}, u32[]{:S(2)}, u32[]{:S(2)}) %collective-permute-start.5) | collective-permute-done | bytes 157856 | tf_op jit(solution)/shard_map/ppermute | solution.py:16
  40.5 0.7 copy-done.5
  41.2 11.4 %shard_map.73 = (bf16[3,64,411]{2,1,0:T(8,128)(2,1)}, bf16[3,64,411]{2,1,0:T(8,128)(2,1)}, bf16[3,64,411]{2,1,0:T(8,128)(2,1)}, bf16[3,64,411]{2,1,0:T(8,128)(2,1)}) custom-call(s32[8]{0:T(128)} %copy-done.6, s32[1]{0:T(128)S(6)} %copy.46.count_ref, bf16[3,64,411]{2,1,0:T(8,128)(2,1)} %copy-done.3, bf16[3,64,411]{2,1,0:T(8,128)(2,1)} %copy.44.s1_ref, ...), custom_call_target="tpu_custom_call" | custom-call | tf_op jit(solution)/shard_map/pallas_call | solution.py:92
  52.6 5.8 %collective-permute-start.9 = (bf16[3,64,411]{2,1,0:T(8,128)(2,1)}, bf16[3,64,411]{2,1,0:T(8,128)(2,1)S(1)}, u32[]{:S(2)}, u32[]{:S(2)}) collective-permute-start(bf16[3,64,411]{2,1,0:T(8,128)(2,1)} %get-tuple-element.19), channel_id=1, source_target_pairs={{0,254},{2,0},{4,2},{6,4},{8,6},{10,8},{12,10},{14,12},{16,14},{18... | collective-permute-start | bytes 473480 | tf_op jit(solution)/shard_map/ppermute | solution.py:16
  58.4 0.0 collective-permute-start.10
  58.4 0.0 collective-permute-start.11
  58.4 0.1 pad_add_fusion
  58.5 2.8 %collective-permute-done.9 = bf16[3,64,411]{2,1,0:T(8,128)(2,1)S(1)} collective-permute-done((bf16[3,64,411]{2,1,0:T(8,128)(2,1)}, bf16[3,64,411]{2,1,0:T(8,128)(2,1)S(1)}, u32[]{:S(2)}, u32[]{:S(2)}) %collective-permute-start.9) | collective-permute-done | bytes 157856 | tf_op jit(solution)/shard_map/ppermute | solution.py:16
  61.4 8.8 %collective-permute-done.10 = bf16[3,64,411]{2,1,0:T(8,128)(2,1)S(1)} collective-permute-done((bf16[3,64,411]{2,1,0:T(8,128)(2,1)}, bf16[3,64,411]{2,1,0:T(8,128)(2,1)S(1)}, u32[]{:S(2)}, u32[]{:S(2)}) %collective-permute-start.10) | collective-permute-done | bytes 157856 | tf_op jit(solution)/shard_map/ppermute | solution.py:16
  70.1 0.8 collective-permute-done.11
  70.9 1.0 %pad_maximum_fusion = bf16[12,64,411]{2,1,0:T(8,128)(2,1)S(1)} fusion(bf16[3,64,411]{2,1,0:T(8,128)(2,1)S(1)} %collective-permute-done.11, bf16[3,64,411]{2,1,0:T(8,128)(2,1)S(1)} %collective-permute-done.10, bf16[3,64,411]{2,1,0:T(8,128)(2,1)} %get-tuple-element.20, bf16[3,64,411]{2,1,0:T(8,128)(2,1)S(1)} %collective-permute-done.9), kind=kLoop, calls=%fused_computation.3 | loop fusion | flops 946944 | bytes 1262592 | tf_op jit(solution)/shard_map/concatenate | solution.py:157
  72.0 0.6 convolution_convert_fusion
  72.6 4.8 %collective-permute-start.12 = (bf16[16,64,411]{2,0,1:T(8,128)(2,1)S(1)}, bf16[16,64,411]{2,0,1:T(8,128)(2,1)S(1)}, u32[]{:S(2)}, u32[]{:S(2)}) collective-permute-start(bf16[16,64,411]{2,0,1:T(8,128)(2,1)S(1)} %convolution_convert_fusion), channel_id=1, source_target_pairs={{0,1},{1,0},{2,3},{3,2},{4,5},{5,4},{6,7},{7,6},{8,9},{9,8},{10,11... | collective-permute-start | bytes 2525192 | tf_op jit(solution)/shard_map/ppermute | solution.py:20
  77.3 2.3 %collective-permute-done.12 = bf16[16,64,411]{2,0,1:T(8,128)(2,1)S(1)} collective-permute-done((bf16[16,64,411]{2,0,1:T(8,128)(2,1)S(1)}, bf16[16,64,411]{2,0,1:T(8,128)(2,1)S(1)}, u32[]{:S(2)}, u32[]{:S(2)}) %collective-permute-start.12) | collective-permute-done | bytes 841760 | tf_op jit(solution)/shard_map/ppermute | solution.py:20
  79.6 1.8 %maximum_select_fusion = bf16[16,128,411]{2,0,1:T(8,128)(2,1)} fusion(bf16[16,64,411]{2,0,1:T(8,128)(2,1)S(1)} %collective-permute-done.12, bf16[16,64,411]{2,0,1:T(8,128)(2,1)S(1)} %convolution_convert_fusion, pred[]{:T(512)S(6)} %eq.44), kind=kLoop, calls=%fused_computation | loop fusion | flops 2525184 | bytes 3366913 | tf_op jit(solution)/shard_map/jit(_where)/select_n | solution.py:160
  81.4 4.9 %copy.34 = bf16[16,128,411]{1,0,2:T(8,128)(2,1)} copy(bf16[16,128,411]{2,0,1:T(8,128)(2,1)} %maximum_select_fusion) | data formatting | bytes 3366912 | tf_op jit(solution)/shard_map/jit(_where)/select_n | solution.py:160
  (18 shorter events, 0.2 us)
Async XLA Ops:
  0.0 16.6 %copy-start = (bf16[16,128,411]{1,0,2:T(8,128)(2,1)S(1)}, bf16[16,128,411]{1,0,2:T(8,128)(2,1)}, u32[]{:S(2)}) copy-start(bf16[16,128,411]{1,0,2:T(8,128)(2,1)} %param.10) | copy-start | bytes 5050372
  0.0 35.4 %collective-permute-start.6 = (bf16[8,308,411]{2,0,1:T(8,128)(2,1)}, bf16[8,308,411]{2,0,1:T(8,128)(2,1)}, u32[]{:S(2)}, u32[]{:S(2)}) collective-permute-start(bf16[8,308,411]{2,0,1:T(8,128)(2,1)} %param.7), channel_id=1, source_target_pairs={{0,1},{1,0},{2,3},{3,2},{4,5},{5,4},{6,7},{7,6},{8,9},{9,8},{10,11... | collective-permute-start | bytes 6076232 | tf_op jit(solution)/shard_map/ppermute | solution.py:20
  4.8 16.9 %copy-start.6 = (s32[8]{0:T(128)}, s32[8]{0:T(128)S(1)}, u32[]{:S(2)}) copy-start(s32[8]{0:T(128)S(1)} %multiply_add_fusion.place_ref) | copy-start | bytes 100
  5.6 17.1 %collective-permute-start.2 = (s32[3]{0:T(128)S(1)}, s32[3]{0:T(128)S(1)}, u32[]{:S(2)}, u32[]{:S(2)}) collective-permute-start(s32[3]{0:T(128)S(1)} %get-tuple-element.29), channel_id=1, source_target_pairs={{0,4},{2,6},{4,8},{6,10},{8,12},{10,14},{12,16},{14,18},{16,20},{1... | collective-permute-start | bytes 44 | tf_op jit(solution)/shard_map/ppermute | solution.py:16
  6.8 16.5 %collective-permute-start.1 = (s32[3]{0:T(128)S(1)}, s32[3]{0:T(128)S(1)}, u32[]{:S(2)}, u32[]{:S(2)}) collective-permute-start(s32[3]{0:T(128)S(1)} %get-tuple-element.30), channel_id=1, source_target_pairs={{0,2},{2,4},{4,6},{6,8},{8,10},{10,12},{12,14},{14,16},{16,18},{18... | collective-permute-start | bytes 44 | tf_op jit(solution)/shard_map/ppermute | solution.py:16
  7.2 16.4 %collective-permute-start = (s32[3]{0:T(128)S(1)}, s32[3]{0:T(128)S(1)}, u32[]{:S(2)}, u32[]{:S(2)}) collective-permute-start(s32[3]{0:T(128)S(1)} %get-tuple-element.32), channel_id=1, source_target_pairs={{0,254},{2,0},{4,2},{6,4},{8,6},{10,8},{12,10},{14,12},{16,14},{18... | collective-permute-start | bytes 44 | tf_op jit(solution)/shard_map/ppermute | solution.py:16
  14.3 19.2 %collective-permute-start.7 = (bf16[8,308]{1,0:T(8,128)(2,1)}, bf16[8,308]{1,0:T(8,128)(2,1)S(1)}, u32[]{:S(2)}, u32[]{:S(2)}) collective-permute-start(bf16[8,308]{1,0:T(8,128)(2,1)} %param.9), channel_id=1, source_target_pairs={{0,1},{1,0},{2,3},{3,2},{4,5},{5,4},{6,7},{7,6},{8,9},{9,8},{10,11... | collective-permute-start | bytes 14792 | tf_op jit(solution)/shard_map/ppermute | solution.py:20
  18.3 4.4 %copy-start.2 = (bf16[308,616]{1,0:T(8,128)(2,1)S(1)}, bf16[308,616]{1,0:T(8,128)(2,1)}, u32[]{:S(2)}) copy-start(bf16[308,616]{1,0:T(8,128)(2,1)} %param.8) | copy-start | bytes 1138372
  22.7 11.3 %collective-permute-start.8 = (bf16[308,616]{1,0:T(8,128)(2,1)S(1)}, bf16[308,616]{1,0:T(8,128)(2,1)S(1)}, u32[]{:S(2)}, u32[]{:S(2)}) collective-permute-start(bf16[308,616]{1,0:T(8,128)(2,1)S(1)} %copy-done.2), channel_id=1, source_target_pairs={{0,1},{1,0},{2,3},{3,2},{4,5},{5,4},{6,7},{7,6},{8,9},{9,8},{10,11... | collective-permute-start | bytes 1138376 | tf_op jit(solution)/shard_map/ppermute | solution.py:20
  23.2 7.9 %copy-start.1 = (bf16[8,308,411]{2,0,1:T(8,128)(2,1)S(1)}, bf16[8,308,411]{2,0,1:T(8,128)(2,1)}, u32[]{:S(2)}) copy-start(bf16[8,308,411]{2,0,1:T(8,128)(2,1)} %param.7) | copy-start | bytes 6076228
  24.2 15.2 %collective-permute-start.3 = (bf16[3,64,411]{2,1,0:T(8,128)(2,1)S(1)}, bf16[3,64,411]{2,1,0:T(8,128)(2,1)S(1)}, u32[]{:S(2)}, u32[]{:S(2)}) collective-permute-start(bf16[3,64,411]{2,1,0:T(8,128)(2,1)S(1)} %copy.45), channel_id=1, source_target_pairs={{0,2},{2,4},{4,6},{6,8},{8,10},{10,12},{12,14},{14,16},{16,18},{18... | collective-permute-start | bytes 473480 | tf_op jit(solution)/shard_map/ppermute | solution.py:16
  24.3 15.2 %collective-permute-start.4 = (bf16[3,64,411]{2,1,0:T(8,128)(2,1)S(1)}, bf16[3,64,411]{2,1,0:T(8,128)(2,1)S(1)}, u32[]{:S(2)}, u32[]{:S(2)}) collective-permute-start(bf16[3,64,411]{2,1,0:T(8,128)(2,1)S(1)} %copy.43), channel_id=1, source_target_pairs={{0,254},{2,0},{4,2},{6,4},{8,6},{10,8},{12,10},{14,12},{16,14},{18... | collective-permute-start | bytes 473480 | tf_op jit(solution)/shard_map/ppermute | solution.py:16
  33.5 7.0 %collective-permute-start.5 = (bf16[3,64,411]{2,1,0:T(8,128)(2,1)S(1)}, bf16[3,64,411]{2,1,0:T(8,128)(2,1)S(1)}, u32[]{:S(2)}, u32[]{:S(2)}) collective-permute-start(bf16[3,64,411]{2,1,0:T(8,128)(2,1)S(1)} %copy.42), channel_id=1, source_target_pairs={{0,252},{2,254},{4,0},{6,2},{8,4},{10,6},{12,8},{14,10},{16,12},{1... | collective-permute-start | bytes 473480 | tf_op jit(solution)/shard_map/ppermute | solution.py:16
  39.4 1.1 %copy-start.3 = (bf16[3,64,411]{2,1,0:T(8,128)(2,1)}, bf16[3,64,411]{2,1,0:T(8,128)(2,1)S(1)}, u32[]{:S(2)}) copy-start(bf16[3,64,411]{2,1,0:T(8,128)(2,1)S(1)} %collective-permute-done.3.s0_ref) | copy-start | bytes 473476
  39.4 1.1 %copy-start.4 = (bf16[3,64,411]{2,1,0:T(8,128)(2,1)}, bf16[3,64,411]{2,1,0:T(8,128)(2,1)S(1)}, u32[]{:S(2)}) copy-start(bf16[3,64,411]{2,1,0:T(8,128)(2,1)S(1)} %collective-permute-done.4.s2_ref) | copy-start | bytes 473476
  40.5 0.7 copy-start.5
  52.6 8.7 %collective-permute-start.9 = (bf16[3,64,411]{2,1,0:T(8,128)(2,1)}, bf16[3,64,411]{2,1,0:T(8,128)(2,1)S(1)}, u32[]{:S(2)}, u32[]{:S(2)}) collective-permute-start(bf16[3,64,411]{2,1,0:T(8,128)(2,1)} %get-tuple-element.19), channel_id=1, source_target_pairs={{0,254},{2,0},{4,2},{6,4},{8,6},{10,8},{12,10},{14,12},{16,14},{18... | collective-permute-start | bytes 473480 | tf_op jit(solution)/shard_map/ppermute | solution.py:16
  58.4 11.7 %collective-permute-start.10 = (bf16[3,64,411]{2,1,0:T(8,128)(2,1)}, bf16[3,64,411]{2,1,0:T(8,128)(2,1)S(1)}, u32[]{:S(2)}, u32[]{:S(2)}) collective-permute-start(bf16[3,64,411]{2,1,0:T(8,128)(2,1)} %get-tuple-element.21), channel_id=1, source_target_pairs={{0,2},{2,4},{4,6},{6,8},{8,10},{10,12},{12,14},{14,16},{16,18},{18... | collective-permute-start | bytes 473480 | tf_op jit(solution)/shard_map/ppermute | solution.py:16
  58.4 12.5 %collective-permute-start.11 = (bf16[3,64,411]{2,1,0:T(8,128)(2,1)}, bf16[3,64,411]{2,1,0:T(8,128)(2,1)S(1)}, u32[]{:S(2)}, u32[]{:S(2)}) collective-permute-start(bf16[3,64,411]{2,1,0:T(8,128)(2,1)} %get-tuple-element.22), channel_id=1, source_target_pairs={{0,4},{2,6},{4,8},{6,10},{8,12},{10,14},{12,16},{14,18},{16,20},{1... | collective-permute-start | bytes 473480 | tf_op jit(solution)/shard_map/ppermute | solution.py:16
  72.6 7.1 %collective-permute-start.12 = (bf16[16,64,411]{2,0,1:T(8,128)(2,1)S(1)}, bf16[16,64,411]{2,0,1:T(8,128)(2,1)S(1)}, u32[]{:S(2)}, u32[]{:S(2)}) collective-permute-start(bf16[16,64,411]{2,0,1:T(8,128)(2,1)S(1)} %convolution_convert_fusion), channel_id=1, source_target_pairs={{0,1},{1,0},{2,3},{3,2},{4,5},{5,4},{6,7},{7,6},{8,9},{9,8},{10,11... | collective-permute-start | bytes 2525192 | tf_op jit(solution)/shard_map/ppermute | solution.py:20

commit v10 on v8

--- a/solution.py
+++ b/solution.py
@@ -37,9 +37,13 @@
     s = parts[3][rank]
     for g in (2, 1, 0):
         s = jnp.where(group == g, parts[g][rank], s)
-    jc = jc_ref[0]
+    @pl.when(f == 0)
+    def _():
+        for h in range(foot):
+            jc_s[h] = jc_ref[:, h, :]
+
+    jc = jc_s[f]
     jo = jo_ref[0]
-    jc_s[f] = jc
     jo_s[f] = jo
     ev_c = lax.dot_general(s, jc, NT, preferred_element_type=jnp.float32)
     ev_o = lax.dot_general(s, jo, NT, preferred_element_type=jnp.float32)
@@ -70,7 +74,7 @@
 
 
 def adjoints(place, count, fetched, jac_c, jac_o, innov_c, innov_o, r_blocks):
-    foot, half_ch, state = jac_c.shape
+    half_ch, foot, state = jac_c.shape
     half_m = fetched[0].shape[1]
     whole3 = lambda f, p, n: (0, 0, 0)
     whole2 = lambda f, p, n: (0, 0)
@@ -79,7 +83,7 @@
     grid_spec = pltpu.PrefetchScalarGridSpec(
         num_scalar_prefetch=2,
         grid=(foot,),
-        in_specs=[part] * SPAN + [jblock, jblock,
+        in_specs=[part] * SPAN + [pl.BlockSpec((half_ch, foot, state), whole3), jblock,
                                   pl.BlockSpec((foot, half_ch), whole2),
                                   pl.BlockSpec((foot, half_ch), whole2)]
                  + [pl.BlockSpec((half_ch, half_ch), whole2)] * 4,
@@ -107,7 +111,7 @@
     capacity = CAP
     slots_total = SPAN * capacity
 
-    jac_c = jacobian
+    jac_c = jnp.transpose(jacobian, (1, 0, 2))
     jac_o = swapped(jacobian)
     innov_c = innovation.astype(jnp.float32)
     innov_o = swapped(innovation).astype(jnp.float32)

time: 86.7 us -> 84.9 us (0.979)
  waiting for transfers between devices: 19.9 us -> 9.98 us
  starting transfers between devices: 24.1 us -> 32.1 us
  Pallas kernels: 11.4 us -> 15.4 us
  local copies, waits for them, and re-layouts: 19.7 us -> 15.8 us
    ppermute x9, starting transfers between devices: 15.9 us -> 25.8 us  [passed_along(): lax.ppermute(value, axis, [(i, (i + by) % count) for i in range(count)])]
    ppermute x9, waiting for transfers between devices: 17.6 us -> 7.68 us  [passed_along(): lax.ppermute(value, axis, [(i, (i + by) % count) for i in range(count)])]
    pallas_call x1, Pallas kernels: 11.4 us -> 15.4 us  [adjoints(): pl.pallas_call(adjoint_kernel, grid_spec=grid_spec, out_shape=[jax.ShapeD...]
    unnamed x14 -> x13, local copies, waits for them, and re-layouts: 8.07 us -> 4.14 us
    ppermute x4, starting transfers between devices: 8.25 us -> 6.3 us  [swapped(): return lax.ppermute(value, 'chan', [(0, 1), (1, 0)])]
  transfers between devices with their start and end apart: 13 -> 13, of which waited for: 5 -> 3; matrix products, arithmetic and copies ran while one was open for 24% -> 20% of each run, Pallas kernels for 0% -> 0%
where the time goes in v10:
time: 84.9 us; the launch traced here: 84.5 us
  starting transfers between devices  32.1 us (38%)
  local copies, waits for them, and re-layouts  15.8 us (19%)
  Pallas kernels  15.4 us (18%)
  waiting for transfers between devices  9.98 us (12%)
  other arithmetic  8.35 us (10%)
  matrix products  1.99 us (2%)
    ppermute x9, starting transfers between devices, passed_along(): lax.ppermute(value, axis, [(i, (i + by) % count) for i in range(count)])  25.8 us
    pallas_call x1, Pallas kernels, adjoints(): pl.pallas_call(adjoint_kernel, grid_spec=grid_spec, out_shape=[jax.ShapeD...  15.4 us
    ppermute x9, waiting for transfers between devices, passed_along(): lax.ppermute(value, axis, [(i, (i + by) % count) for i in range(count)])  7.68 us
    ppermute x4, starting transfers between devices, swapped(): return lax.ppermute(value, 'chan', [(0, 1), (1, 0)])  6.3 us
    select_n x1, local copies, waits for them, and re-layouts, on_device(): jnp.where(first, jnp.concatenate([mine, other], axis=1), jnp.concatenate(...  4.94 us
    unnamed x13, local copies, waits for them, and re-layouts  4.14 us
    ppermute x1, local copies, waits for them, and re-layouts, swapped(): return lax.ppermute(value, 'chan', [(0, 1), (1, 0)])  4.04 us
    ppermute x4, waiting for transfers between devices, swapped(): return lax.ppermute(value, 'chan', [(0, 1), (1, 0)])  2.29 us
  transfers between devices with their start and end apart: 13, of which 3 were waited for; matrix products, arithmetic and copies ran while one was open for 20% of the time, Pallas kernels for 0%

profile of v10, /device:TPU:1, one launch (start us, length us, event | category | flops | bytes accessed | tf_op | source)
XLA Modules:
  0.0 84.5 jit_solution(14060646647111137870)
XLA Ops:
  0.0 3.2 %collective-permute-start.6 = (bf16[8,308,411]{2,0,1:T(8,128)(2,1)}, bf16[8,308,411]{2,0,1:T(8,128)(2,1)}, u32[]{:S(2)}, u32[]{:S(2)}) collective-permute-start(bf16[8,308,411]{2,0,1:T(8,128)(2,1)} %param.7), channel_id=1, source_target_pairs={{0,1},{1,0},{2,3},{3,2},{4,5},{5,4},{6,7},{7,6},{8,9},{9,8},{10,11... | collective-permute-start | bytes 6076232 | tf_op jit(solution)/shard_map/ppermute | solution.py:20
  3.2 0.9 %convert_reduce_fusion = s32[8]{0:T(128)S(1)} fusion(s32[8]{0:T(128)} %bitcast.23), kind=kLoop, calls=%fused_computation.19 | loop fusion | flops 312 | bytes 64 | tf_op jit(solution)/shard_map/reduce_sum | solution.py:134
  4.1 0.7 multiply_add_fusion.place_ref
  4.8 0.7 select_reduce_fusion
  5.5 0.1 fusion.21
  5.6 8.5 %collective-permute-start = (s32[3]{0:T(128)S(1)}, s32[3]{0:T(128)S(1)}, u32[]{:S(2)}, u32[]{:S(2)}) collective-permute-start(s32[3]{0:T(128)S(1)} %get-tuple-element.22), channel_id=1, source_target_pairs={{0,254},{2,0},{4,2},{6,4},{8,6},{10,8},{12,10},{14,12},{16,14},{18... | collective-permute-start | bytes 44 | tf_op jit(solution)/shard_map/ppermute | solution.py:16
  14.1 0.0 collective-permute-start.1
  14.1 0.0 collective-permute-start.2
  14.1 0.4 collective-permute-start.7
  14.5 1.3 %convert_element_type.34.ic_ref = f32[8,308]{1,0:T(8,128)} convert(bf16[8,308]{1,0:T(8,128)(2,1)} %param.9) | non-fusion elementwise | flops 2464 | bytes 14784 | tf_op jit(solution)/shard_map/convert_element_type | solution.py:116
  16.4 1.7 %constant_dynamic-slice_fusion = bf16[16,64,411]{1,0,2:T(8,128)(2,1)} fusion(bf16[16,128,411]{1,0,2:T(8,128)(2,1)S(1)} %copy-done, s32[]{:T(128)S(6)} %select_n.49), kind=kLoop, calls=%fused_computation.40 | loop fusion | bytes 1683460 | tf_op jit(solution)/shard_map/dynamic_slice | solution.py:139
  18.1 3.3 %copy.32 = bf16[16,64,411]{2,0,1:T(8,128)(2,1)S(1)} copy(bf16[16,64,411]{1,0,2:T(8,128)(2,1)} %constant_dynamic-slice_fusion) | data formatting | bytes 1683456
  21.5 0.4 fusion.9
  21.9 0.7 copy.41.s1_ref
  22.6 0.0 collective-permute-done
  22.6 0.2 collective-permute-start.8
  22.8 0.3 fusion.6
  23.2 0.0 collective-permute-done.1
  23.2 0.1 collective-permute-start.3
  23.3 0.4 fusion.12
  23.7 0.0 collective-permute-done.2
  23.7 7.1 %collective-permute-start.4 = (bf16[3,64,411]{2,1,0:T(8,128)(2,1)S(1)}, bf16[3,64,411]{2,1,0:T(8,128)(2,1)S(1)}, u32[]{:S(2)}, u32[]{:S(2)}) collective-permute-start(bf16[3,64,411]{2,1,0:T(8,128)(2,1)S(1)} %copy.40), channel_id=1, source_target_pairs={{0,254},{2,0},{4,2},{6,4},{8,6},{10,8},{12,10},{14,12},{16,14},{18... | collective-permute-start | bytes 473480 | tf_op jit(solution)/shard_map/ppermute | solution.py:16
  30.8 0.3 fusion.15
  31.2 2.9 %collective-permute-start.5 = (bf16[3,64,411]{2,1,0:T(8,128)(2,1)S(1)}, bf16[3,64,411]{2,1,0:T(8,128)(2,1)S(1)}, u32[]{:S(2)}, u32[]{:S(2)}) collective-permute-start(bf16[3,64,411]{2,1,0:T(8,128)(2,1)S(1)} %copy.39), channel_id=1, source_target_pairs={{0,252},{2,254},{4,0},{6,2},{8,4},{10,6},{12,8},{14,10},{16,12},{1... | collective-permute-start | bytes 473480 | tf_op jit(solution)/shard_map/ppermute | solution.py:16
  34.1 0.6 convert_element_type.35.io_ref
  34.7 0.0 collective-permute-done.8
  34.7 0.1 broadcast_select_fusion.1
  34.8 1.1 %broadcast_select_fusion.2 = (bf16[308,308]{1,0:T(8,128)(2,1)}, bf16[308,308]{1,0:T(8,128)(2,1)}, bf16[308,308]{1,0:T(8,128)(2,1)}, bf16[308,308]{1,0:T(8,128)(2,1)}) fusion(pred[]{:T(512)S(6)} %eq.44, bf16[308,616]{1,0:T(8,128)(2,1)S(1)} %get-tuple-element.18, bf16[308,616]{1,0:T(8,128)(2,1)S(1)} %get-tuple-element.17), kind=kLoop, calls=%fused_computation.10 | loop fusion | flops 379456 | bytes 1517825 | tf_op jit(solution)/shard_map/jit(_where)/select_n | solution.py:128
  35.9 4.0 %copy.29.jo_ref = bf16[8,308,411]{2,1,0:T(8,128)(2,1)} copy(bf16[8,308,411]{2,0,1:T(8,128)(2,1)} %collective-permute-done.6) | data formatting | bytes 4050816 | tf_op jit(solution)/shard_map/ppermute | solution.py:20
  40.0 0.0 collective-permute-done.3.s0_ref
  40.0 0.0 collective-permute-done.5.s3_ref
  40.0 0.6 copy-done.2
  40.6 0.1 copy-done.3
  40.7 0.1 copy-done.4
  40.8 15.4 %shard_map.73 = (bf16[3,64,411]{2,1,0:T(8,128)(2,1)}, bf16[3,64,411]{2,1,0:T(8,128)(2,1)}, bf16[3,64,411]{2,1,0:T(8,128)(2,1)}, bf16[3,64,411]{2,1,0:T(8,128)(2,1)}) custom-call(s32[8]{0:T(128)} %copy-done.5, s32[1]{0:T(128)S(6)} %copy.43.count_ref, bf16[3,64,411]{2,1,0:T(8,128)(2,1)} %copy-done.2, bf16[3,64,411]{2,1,0:T(8,128)(2,1)} %copy.41.s1_ref, ...), custom_call_target="tpu_custom_call" | custom-call | tf_op jit(solution)/shard_map/pallas_call | solution.py:96
  56.2 0.3 collective-permute-start.11
  56.5 0.0 collective-permute-start.10
  56.5 6.9 %collective-permute-start.9 = (bf16[3,64,411]{2,1,0:T(8,128)(2,1)}, bf16[3,64,411]{2,1,0:T(8,128)(2,1)S(1)}, u32[]{:S(2)}, u32[]{:S(2)}) collective-permute-start(bf16[3,64,411]{2,1,0:T(8,128)(2,1)} %get-tuple-element.9), channel_id=1, source_target_pairs={{0,254},{2,0},{4,2},{6,4},{8,6},{10,8},{12,10},{14,12},{16,14},{18... | collective-permute-start | bytes 473480 | tf_op jit(solution)/shard_map/ppermute | solution.py:16
  63.4 0.1 pad_add_fusion
  63.5 4.5 %collective-permute-done.11 = bf16[3,64,411]{2,1,0:T(8,128)(2,1)S(1)} collective-permute-done((bf16[3,64,411]{2,1,0:T(8,128)(2,1)}, bf16[3,64,411]{2,1,0:T(8,128)(2,1)S(1)}, u32[]{:S(2)}, u32[]{:S(2)}) %collective-permute-start.11) | collective-permute-done | bytes 157856 | tf_op jit(solution)/shard_map/ppermute | solution.py:16
  68.0 3.1 %collective-permute-done.10 = bf16[3,64,411]{2,1,0:T(8,128)(2,1)S(1)} collective-permute-done((bf16[3,64,411]{2,1,0:T(8,128)(2,1)}, bf16[3,64,411]{2,1,0:T(8,128)(2,1)S(1)}, u32[]{:S(2)}, u32[]{:S(2)}) %collective-permute-start.10) | collective-permute-done | bytes 157856 | tf_op jit(solution)/shard_map/ppermute | solution.py:16
  71.2 0.0 collective-permute-done.9
  71.2 1.0 %pad_maximum_fusion = bf16[12,64,411]{2,1,0:T(8,128)(2,1)S(1)} fusion(bf16[3,64,411]{2,1,0:T(8,128)(2,1)S(1)} %collective-permute-done.11, bf16[3,64,411]{2,1,0:T(8,128)(2,1)S(1)} %collective-permute-done.10, bf16[3,64,411]{2,1,0:T(8,128)(2,1)} %get-tuple-element.10, bf16[3,64,411]{2,1,0:T(8,128)(2,1)S(1)} %collective-permute-done.9), kind=kLoop, calls=%fused_computation.3 | loop fusion | flops 946944 | bytes 1262592 | tf_op jit(solution)/shard_map/concatenate | solution.py:162
  72.2 0.6 convolution_convert_fusion
  72.8 2.6 %collective-permute-start.12 = (bf16[16,64,411]{2,0,1:T(8,128)(2,1)S(1)}, bf16[16,64,411]{2,0,1:T(8,128)(2,1)S(1)}, u32[]{:S(2)}, u32[]{:S(2)}) collective-permute-start(bf16[16,64,411]{2,0,1:T(8,128)(2,1)S(1)} %convolution_convert_fusion), channel_id=1, source_target_pairs={{0,1},{1,0},{2,3},{3,2},{4,5},{5,4},{6,7},{7,6},{8,9},{9,8},{10,11... | collective-permute-start | bytes 2525192 | tf_op jit(solution)/shard_map/ppermute | solution.py:20
  75.4 2.3 %collective-permute-done.12 = bf16[16,64,411]{2,0,1:T(8,128)(2,1)S(1)} collective-permute-done((bf16[16,64,411]{2,0,1:T(8,128)(2,1)S(1)}, bf16[16,64,411]{2,0,1:T(8,128)(2,1)S(1)}, u32[]{:S(2)}, u32[]{:S(2)}) %collective-permute-start.12) | collective-permute-done | bytes 841760 | tf_op jit(solution)/shard_map/ppermute | solution.py:20
  77.7 1.8 %maximum_select_fusion = bf16[16,128,411]{2,0,1:T(8,128)(2,1)} fusion(bf16[16,64,411]{2,0,1:T(8,128)(2,1)S(1)} %collective-permute-done.12, bf16[16,64,411]{2,0,1:T(8,128)(2,1)S(1)} %convolution_convert_fusion, pred[]{:T(512)S(6)} %eq.44), kind=kLoop, calls=%fused_computation | loop fusion | flops 2525184 | bytes 3366913 | tf_op jit(solution)/shard_map/jit(_where)/select_n | solution.py:165
  79.5 4.9 %copy.31 = bf16[16,128,411]{1,0,2:T(8,128)(2,1)} copy(bf16[16,128,411]{2,0,1:T(8,128)(2,1)} %maximum_select_fusion) | data formatting | bytes 3366912 | tf_op jit(solution)/shard_map/jit(_where)/select_n | solution.py:165
  (15 shorter events, 0.2 us)
Async XLA Ops:
  0.0 16.4 %copy-start = (bf16[16,128,411]{1,0,2:T(8,128)(2,1)S(1)}, bf16[16,128,411]{1,0,2:T(8,128)(2,1)}, u32[]{:S(2)}) copy-start(bf16[16,128,411]{1,0,2:T(8,128)(2,1)} %param.10) | copy-start | bytes 5050372
  0.0 35.9 %collective-permute-start.6 = (bf16[8,308,411]{2,0,1:T(8,128)(2,1)}, bf16[8,308,411]{2,0,1:T(8,128)(2,1)}, u32[]{:S(2)}, u32[]{:S(2)}) collective-permute-start(bf16[8,308,411]{2,0,1:T(8,128)(2,1)} %param.7), channel_id=1, source_target_pairs={{0,1},{1,0},{2,3},{3,2},{4,5},{5,4},{6,7},{7,6},{8,9},{9,8},{10,11... | collective-permute-start | bytes 6076232 | tf_op jit(solution)/shard_map/ppermute | solution.py:20
  4.8 16.7 %copy-start.5 = (s32[8]{0:T(128)}, s32[8]{0:T(128)S(1)}, u32[]{:S(2)}) copy-start(s32[8]{0:T(128)S(1)} %multiply_add_fusion.place_ref) | copy-start | bytes 100
  5.6 17.0 %collective-permute-start = (s32[3]{0:T(128)S(1)}, s32[3]{0:T(128)S(1)}, u32[]{:S(2)}, u32[]{:S(2)}) collective-permute-start(s32[3]{0:T(128)S(1)} %get-tuple-element.22), channel_id=1, source_target_pairs={{0,254},{2,0},{4,2},{6,4},{8,6},{10,8},{12,10},{14,12},{16,14},{18... | collective-permute-start | bytes 44 | tf_op jit(solution)/shard_map/ppermute | solution.py:16
  14.1 9.0 %collective-permute-start.1 = (s32[3]{0:T(128)S(1)}, s32[3]{0:T(128)S(1)}, u32[]{:S(2)}, u32[]{:S(2)}) collective-permute-start(s32[3]{0:T(128)S(1)} %get-tuple-element.20), channel_id=1, source_target_pairs={{0,2},{2,4},{4,6},{6,8},{8,10},{10,12},{12,14},{14,16},{16,18},{18... | collective-permute-start | bytes 44 | tf_op jit(solution)/shard_map/ppermute | solution.py:16
  14.1 9.6 %collective-permute-start.2 = (s32[3]{0:T(128)S(1)}, s32[3]{0:T(128)S(1)}, u32[]{:S(2)}, u32[]{:S(2)}) collective-permute-start(s32[3]{0:T(128)S(1)} %get-tuple-element.19), channel_id=1, source_target_pairs={{0,4},{2,6},{4,8},{6,10},{8,12},{10,14},{12,16},{14,18},{16,20},{1... | collective-permute-start | bytes 44 | tf_op jit(solution)/shard_map/ppermute | solution.py:16
  14.1 17.1 %collective-permute-start.7 = (bf16[8,308]{1,0:T(8,128)(2,1)}, bf16[8,308]{1,0:T(8,128)(2,1)S(1)}, u32[]{:S(2)}, u32[]{:S(2)}) collective-permute-start(bf16[8,308]{1,0:T(8,128)(2,1)} %param.9), channel_id=1, source_target_pairs={{0,1},{1,0},{2,3},{3,2},{4,5},{5,4},{6,7},{7,6},{8,9},{9,8},{10,11... | collective-permute-start | bytes 14792 | tf_op jit(solution)/shard_map/ppermute | solution.py:20
  18.1 4.5 %copy-start.1 = (bf16[308,616]{1,0:T(8,128)(2,1)S(1)}, bf16[308,616]{1,0:T(8,128)(2,1)}, u32[]{:S(2)}) copy-start(bf16[308,616]{1,0:T(8,128)(2,1)} %param.8) | copy-start | bytes 1138372
  22.6 12.1 %collective-permute-start.8 = (bf16[308,616]{1,0:T(8,128)(2,1)S(1)}, bf16[308,616]{1,0:T(8,128)(2,1)S(1)}, u32[]{:S(2)}, u32[]{:S(2)}) collective-permute-start(bf16[308,616]{1,0:T(8,128)(2,1)S(1)} %copy-done.1), channel_id=1, source_target_pairs={{0,1},{1,0},{2,3},{3,2},{4,5},{5,4},{6,7},{7,6},{8,9},{9,8},{10,11... | collective-permute-start | bytes 1138376 | tf_op jit(solution)/shard_map/ppermute | solution.py:20
  23.2 16.8 %collective-permute-start.3 = (bf16[3,64,411]{2,1,0:T(8,128)(2,1)S(1)}, bf16[3,64,411]{2,1,0:T(8,128)(2,1)S(1)}, u32[]{:S(2)}, u32[]{:S(2)}) collective-permute-start(bf16[3,64,411]{2,1,0:T(8,128)(2,1)S(1)} %copy.42), channel_id=1, source_target_pairs={{0,2},{2,4},{4,6},{6,8},{8,10},{10,12},{12,14},{14,16},{16,18},{18... | collective-permute-start | bytes 473480 | tf_op jit(solution)/shard_map/ppermute | solution.py:16
  23.7 16.3 %collective-permute-start.4 = (bf16[3,64,411]{2,1,0:T(8,128)(2,1)S(1)}, bf16[3,64,411]{2,1,0:T(8,128)(2,1)S(1)}, u32[]{:S(2)}, u32[]{:S(2)}) collective-permute-start(bf16[3,64,411]{2,1,0:T(8,128)(2,1)S(1)} %copy.40), channel_id=1, source_target_pairs={{0,254},{2,0},{4,2},{6,4},{8,6},{10,8},{12,10},{14,12},{16,14},{18... | collective-permute-start | bytes 473480 | tf_op jit(solution)/shard_map/ppermute | solution.py:16
  31.2 8.8 %collective-permute-start.5 = (bf16[3,64,411]{2,1,0:T(8,128)(2,1)S(1)}, bf16[3,64,411]{2,1,0:T(8,128)(2,1)S(1)}, u32[]{:S(2)}, u32[]{:S(2)}) collective-permute-start(bf16[3,64,411]{2,1,0:T(8,128)(2,1)S(1)} %copy.39), channel_id=1, source_target_pairs={{0,252},{2,254},{4,0},{6,2},{8,4},{10,6},{12,8},{14,10},{16,12},{1... | collective-permute-start | bytes 473480 | tf_op jit(solution)/shard_map/ppermute | solution.py:16
  40.0 0.7 copy-start.2
  40.0 0.8 copy-start.3
  40.0 0.8 copy-start.4
  56.2 11.8 %collective-permute-start.11 = (bf16[3,64,411]{2,1,0:T(8,128)(2,1)}, bf16[3,64,411]{2,1,0:T(8,128)(2,1)S(1)}, u32[]{:S(2)}, u32[]{:S(2)}) collective-permute-start(bf16[3,64,411]{2,1,0:T(8,128)(2,1)} %get-tuple-element.12), channel_id=1, source_target_pairs={{0,4},{2,6},{4,8},{6,10},{8,12},{10,14},{12,16},{14,18},{16,20},{1... | collective-permute-start | bytes 473480 | tf_op jit(solution)/shard_map/ppermute | solution.py:16
  56.5 14.6 %collective-permute-start.10 = (bf16[3,64,411]{2,1,0:T(8,128)(2,1)}, bf16[3,64,411]{2,1,0:T(8,128)(2,1)S(1)}, u32[]{:S(2)}, u32[]{:S(2)}) collective-permute-start(bf16[3,64,411]{2,1,0:T(8,128)(2,1)} %get-tuple-element.11), channel_id=1, source_target_pairs={{0,2},{2,4},{4,6},{6,8},{8,10},{10,12},{12,14},{14,16},{16,18},{18... | collective-permute-start | bytes 473480 | tf_op jit(solution)/shard_map/ppermute | solution.py:16
  56.5 14.6 %collective-permute-start.9 = (bf16[3,64,411]{2,1,0:T(8,128)(2,1)}, bf16[3,64,411]{2,1,0:T(8,128)(2,1)S(1)}, u32[]{:S(2)}, u32[]{:S(2)}) collective-permute-start(bf16[3,64,411]{2,1,0:T(8,128)(2,1)} %get-tuple-element.9), channel_id=1, source_target_pairs={{0,254},{2,0},{4,2},{6,4},{8,6},{10,8},{12,10},{14,12},{16,14},{18... | collective-permute-start | bytes 473480 | tf_op jit(solution)/shard_map/ppermute | solution.py:16
  72.8 4.9 %collective-permute-start.12 = (bf16[16,64,411]{2,0,1:T(8,128)(2,1)S(1)}, bf16[16,64,411]{2,0,1:T(8,128)(2,1)S(1)}, u32[]{:S(2)}, u32[]{:S(2)}) collective-permute-start(bf16[16,64,411]{2,0,1:T(8,128)(2,1)S(1)} %convolution_convert_fusion), channel_id=1, source_target_pairs={{0,1},{1,0},{2,3},{3,2},{4,5},{5,4},{6,7},{7,6},{8,9},{9,8},{10,11... | collective-permute-start | bytes 2525192 | tf_op jit(solution)/shard_map/ppermute | solution.py:20

commit v11 on v10

--- a/solution.py
+++ b/solution.py
@@ -37,9 +37,9 @@
     s = parts[3][rank]
     for g in (2, 1, 0):
         s = jnp.where(group == g, parts[g][rank], s)
-    @pl.when(f == 0)
-    def _():
-        for h in range(foot):
+    for h in range(foot):
+        @pl.when(f == h)
+        def _():
             jc_s[h] = jc_ref[:, h, :]
 
     jc = jc_s[f]

time: 84.9 us -> 83.7 us (0.986)
  Pallas kernels: 15.4 us -> 14.2 us
    pallas_call x1, Pallas kernels: 15.4 us -> 14.2 us  [adjoints(): pl.pallas_call(adjoint_kernel, grid_spec=grid_spec, out_shape=[jax.ShapeD...]
where the time goes in v11:
time: 83.7 us; the launch traced here: 83.2 us
  starting transfers between devices  32.1 us (38%)
  local copies, waits for them, and re-layouts  15.8 us (19%)
  Pallas kernels  14.2 us (17%)
  waiting for transfers between devices  9.98 us (12%)
  other arithmetic  8.35 us (10%)
  matrix products  1.99 us (2%)
    ppermute x9, starting transfers between devices, passed_along(): lax.ppermute(value, axis, [(i, (i + by) % count) for i in range(count)])  25.8 us
    pallas_call x1, Pallas kernels, adjoints(): pl.pallas_call(adjoint_kernel, grid_spec=grid_spec, out_shape=[jax.ShapeD...  14.2 us
    ppermute x9, waiting for transfers between devices, passed_along(): lax.ppermute(value, axis, [(i, (i + by) % count) for i in range(count)])  7.68 us
    ppermute x4, starting transfers between devices, swapped(): return lax.ppermute(value, 'chan', [(0, 1), (1, 0)])  6.3 us
    select_n x1, local copies, waits for them, and re-layouts, on_device(): jnp.where(first, jnp.concatenate([mine, other], axis=1), jnp.concatenate(...  4.94 us
    unnamed x13, local copies, waits for them, and re-layouts  4.14 us
    ppermute x1, local copies, waits for them, and re-layouts, swapped(): return lax.ppermute(value, 'chan', [(0, 1), (1, 0)])  4.04 us
    ppermute x4, waiting for transfers between devices, swapped(): return lax.ppermute(value, 'chan', [(0, 1), (1, 0)])  2.29 us
  transfers between devices with their start and end apart: 13, of which 3 were waited for; matrix products, arithmetic and copies ran while one was open for 20% of the time, Pallas kernels for 0%

profile of v11, /device:TPU:1, one launch (start us, length us, event | category | flops | bytes accessed | tf_op | source)
XLA Modules:
  0.0 83.2 jit_solution(15601885998259650700)
XLA Ops:
  0.0 3.2 %collective-permute-start.6 = (bf16[8,308,411]{2,0,1:T(8,128)(2,1)}, bf16[8,308,411]{2,0,1:T(8,128)(2,1)}, u32[]{:S(2)}, u32[]{:S(2)}) collective-permute-start(bf16[8,308,411]{2,0,1:T(8,128)(2,1)} %param.7), channel_id=1, source_target_pairs={{0,1},{1,0},{2,3},{3,2},{4,5},{5,4},{6,7},{7,6},{8,9},{9,8},{10,11... | collective-permute-start | bytes 6076232 | tf_op jit(solution)/shard_map/ppermute | solution.py:20
  3.2 0.9 %convert_reduce_fusion = s32[8]{0:T(128)S(1)} fusion(s32[8]{0:T(128)} %bitcast.23), kind=kLoop, calls=%fused_computation.19 | loop fusion | flops 312 | bytes 64 | tf_op jit(solution)/shard_map/reduce_sum | solution.py:134
  4.1 0.7 multiply_add_fusion.place_ref
  4.8 0.7 select_reduce_fusion
  5.5 0.1 fusion.21
  5.6 8.5 %collective-permute-start = (s32[3]{0:T(128)S(1)}, s32[3]{0:T(128)S(1)}, u32[]{:S(2)}, u32[]{:S(2)}) collective-permute-start(s32[3]{0:T(128)S(1)} %get-tuple-element.22), channel_id=1, source_target_pairs={{0,254},{2,0},{4,2},{6,4},{8,6},{10,8},{12,10},{14,12},{16,14},{18... | collective-permute-start | bytes 44 | tf_op jit(solution)/shard_map/ppermute | solution.py:16
  14.1 0.0 collective-permute-start.1
  14.1 0.0 collective-permute-start.2
  14.1 0.4 collective-permute-start.7
  14.5 1.3 %convert_element_type.34.ic_ref = f32[8,308]{1,0:T(8,128)} convert(bf16[8,308]{1,0:T(8,128)(2,1)} %param.9) | non-fusion elementwise | flops 2464 | bytes 14784 | tf_op jit(solution)/shard_map/convert_element_type | solution.py:116
  16.4 1.7 %constant_dynamic-slice_fusion = bf16[16,64,411]{1,0,2:T(8,128)(2,1)} fusion(bf16[16,128,411]{1,0,2:T(8,128)(2,1)S(1)} %copy-done, s32[]{:T(128)S(6)} %select_n.49), kind=kLoop, calls=%fused_computation.40 | loop fusion | bytes 1683460 | tf_op jit(solution)/shard_map/dynamic_slice | solution.py:139
  18.1 3.3 %copy.32 = bf16[16,64,411]{2,0,1:T(8,128)(2,1)S(1)} copy(bf16[16,64,411]{1,0,2:T(8,128)(2,1)} %constant_dynamic-slice_fusion) | data formatting | bytes 1683456
  21.5 0.4 fusion.9
  21.9 0.7 copy.41.s1_ref
  22.6 0.0 collective-permute-done
  22.6 0.2 collective-permute-start.8
  22.8 0.3 fusion.6
  23.2 0.0 collective-permute-done.1
  23.2 0.1 collective-permute-start.3
  23.3 0.4 fusion.12
  23.7 0.0 collective-permute-done.2
  23.7 7.1 %collective-permute-start.4 = (bf16[3,64,411]{2,1,0:T(8,128)(2,1)S(1)}, bf16[3,64,411]{2,1,0:T(8,128)(2,1)S(1)}, u32[]{:S(2)}, u32[]{:S(2)}) collective-permute-start(bf16[3,64,411]{2,1,0:T(8,128)(2,1)S(1)} %copy.40), channel_id=1, source_target_pairs={{0,254},{2,0},{4,2},{6,4},{8,6},{10,8},{12,10},{14,12},{16,14},{18... | collective-permute-start | bytes 473480 | tf_op jit(solution)/shard_map/ppermute | solution.py:16
  30.8 0.3 fusion.15
  31.2 0.0 collective-permute-done.7
  31.2 2.9 %collective-permute-start.5 = (bf16[3,64,411]{2,1,0:T(8,128)(2,1)S(1)}, bf16[3,64,411]{2,1,0:T(8,128)(2,1)S(1)}, u32[]{:S(2)}, u32[]{:S(2)}) collective-permute-start(bf16[3,64,411]{2,1,0:T(8,128)(2,1)S(1)} %copy.39), channel_id=1, source_target_pairs={{0,252},{2,254},{4,0},{6,2},{8,4},{10,6},{12,8},{14,10},{16,12},{1... | collective-permute-start | bytes 473480 | tf_op jit(solution)/shard_map/ppermute | solution.py:16
  34.1 0.6 convert_element_type.35.io_ref
  34.7 0.0 collective-permute-done.8
  34.7 0.1 broadcast_select_fusion.1
  34.8 1.1 %broadcast_select_fusion.2 = (bf16[308,308]{1,0:T(8,128)(2,1)}, bf16[308,308]{1,0:T(8,128)(2,1)}, bf16[308,308]{1,0:T(8,128)(2,1)}, bf16[308,308]{1,0:T(8,128)(2,1)}) fusion(pred[]{:T(512)S(6)} %eq.44, bf16[308,616]{1,0:T(8,128)(2,1)S(1)} %get-tuple-element.18, bf16[308,616]{1,0:T(8,128)(2,1)S(1)} %get-tuple-element.17), kind=kLoop, calls=%fused_computation.10 | loop fusion | flops 379456 | bytes 1517825 | tf_op jit(solution)/shard_map/jit(_where)/select_n | solution.py:128
  35.9 0.0 collective-permute-done.6
  35.9 4.0 %copy.29.jo_ref = bf16[8,308,411]{2,1,0:T(8,128)(2,1)} copy(bf16[8,308,411]{2,0,1:T(8,128)(2,1)} %collective-permute-done.6) | data formatting | bytes 4050816 | tf_op jit(solution)/shard_map/ppermute | solution.py:20
  40.0 0.0 collective-permute-done.3.s0_ref
  40.0 0.0 collective-permute-done.5.s3_ref
  40.0 0.6 copy-done.2
  40.6 0.1 copy-done.3
  40.7 0.1 copy-done.4
  40.8 14.2 %shard_map.73 = (bf16[3,64,411]{2,1,0:T(8,128)(2,1)}, bf16[3,64,411]{2,1,0:T(8,128)(2,1)}, bf16[3,64,411]{2,1,0:T(8,128)(2,1)}, bf16[3,64,411]{2,1,0:T(8,128)(2,1)}) custom-call(s32[8]{0:T(128)} %copy-done.5, s32[1]{0:T(128)S(6)} %copy.43.count_ref, bf16[3,64,411]{2,1,0:T(8,128)(2,1)} %copy-done.2, bf16[3,64,411]{2,1,0:T(8,128)(2,1)} %copy.41.s1_ref, ...), custom_call_target="tpu_custom_call" | custom-call | tf_op jit(solution)/shard_map/pallas_call | solution.py:96
  55.0 0.3 collective-permute-start.11
  55.3 6.9 %collective-permute-start.9 = (bf16[3,64,411]{2,1,0:T(8,128)(2,1)}, bf16[3,64,411]{2,1,0:T(8,128)(2,1)S(1)}, u32[]{:S(2)}, u32[]{:S(2)}) collective-permute-start(bf16[3,64,411]{2,1,0:T(8,128)(2,1)} %get-tuple-element.9), channel_id=1, source_target_pairs={{0,254},{2,0},{4,2},{6,4},{8,6},{10,8},{12,10},{14,12},{16,14},{18... | collective-permute-start | bytes 473480 | tf_op jit(solution)/shard_map/ppermute | solution.py:16
  62.2 0.1 pad_add_fusion
  62.3 4.5 %collective-permute-done.11 = bf16[3,64,411]{2,1,0:T(8,128)(2,1)S(1)} collective-permute-done((bf16[3,64,411]{2,1,0:T(8,128)(2,1)}, bf16[3,64,411]{2,1,0:T(8,128)(2,1)S(1)}, u32[]{:S(2)}, u32[]{:S(2)}) %collective-permute-start.11) | collective-permute-done | bytes 157856 | tf_op jit(solution)/shard_map/ppermute | solution.py:16
  66.8 3.1 %collective-permute-done.10 = bf16[3,64,411]{2,1,0:T(8,128)(2,1)S(1)} collective-permute-done((bf16[3,64,411]{2,1,0:T(8,128)(2,1)}, bf16[3,64,411]{2,1,0:T(8,128)(2,1)S(1)}, u32[]{:S(2)}, u32[]{:S(2)}) %collective-permute-start.10) | collective-permute-done | bytes 157856 | tf_op jit(solution)/shard_map/ppermute | solution.py:16
  69.9 1.0 %pad_maximum_fusion = bf16[12,64,411]{2,1,0:T(8,128)(2,1)S(1)} fusion(bf16[3,64,411]{2,1,0:T(8,128)(2,1)S(1)} %collective-permute-done.11, bf16[3,64,411]{2,1,0:T(8,128)(2,1)S(1)} %collective-permute-done.10, bf16[3,64,411]{2,1,0:T(8,128)(2,1)} %get-tuple-element.10, bf16[3,64,411]{2,1,0:T(8,128)(2,1)S(1)} %collective-permute-done.9), kind=kLoop, calls=%fused_computation.3 | loop fusion | flops 946944 | bytes 1262592 | tf_op jit(solution)/shard_map/concatenate | solution.py:162
  71.0 0.6 convolution_convert_fusion
  71.6 2.6 %collective-permute-start.12 = (bf16[16,64,411]{2,0,1:T(8,128)(2,1)S(1)}, bf16[16,64,411]{2,0,1:T(8,128)(2,1)S(1)}, u32[]{:S(2)}, u32[]{:S(2)}) collective-permute-start(bf16[16,64,411]{2,0,1:T(8,128)(2,1)S(1)} %convolution_convert_fusion), channel_id=1, source_target_pairs={{0,1},{1,0},{2,3},{3,2},{4,5},{5,4},{6,7},{7,6},{8,9},{9,8},{10,11... | collective-permute-start | bytes 2525192 | tf_op jit(solution)/shard_map/ppermute | solution.py:20
  74.2 2.3 %collective-permute-done.12 = bf16[16,64,411]{2,0,1:T(8,128)(2,1)S(1)} collective-permute-done((bf16[16,64,411]{2,0,1:T(8,128)(2,1)S(1)}, bf16[16,64,411]{2,0,1:T(8,128)(2,1)S(1)}, u32[]{:S(2)}, u32[]{:S(2)}) %collective-permute-start.12) | collective-permute-done | bytes 841760 | tf_op jit(solution)/shard_map/ppermute | solution.py:20
  76.5 1.8 %maximum_select_fusion = bf16[16,128,411]{2,0,1:T(8,128)(2,1)} fusion(bf16[16,64,411]{2,0,1:T(8,128)(2,1)S(1)} %collective-permute-done.12, bf16[16,64,411]{2,0,1:T(8,128)(2,1)S(1)} %convolution_convert_fusion, pred[]{:T(512)S(6)} %eq.44), kind=kLoop, calls=%fused_computation | loop fusion | flops 2525184 | bytes 3366913 | tf_op jit(solution)/shard_map/jit(_where)/select_n | solution.py:165
  78.3 4.9 %copy.31 = bf16[16,128,411]{1,0,2:T(8,128)(2,1)} copy(bf16[16,128,411]{2,0,1:T(8,128)(2,1)} %maximum_select_fusion) | data formatting | bytes 3366912 | tf_op jit(solution)/shard_map/jit(_where)/select_n | solution.py:165
  (15 shorter events, 0.2 us)
Async XLA Ops:
  0.0 16.4 %copy-start = (bf16[16,128,411]{1,0,2:T(8,128)(2,1)S(1)}, bf16[16,128,411]{1,0,2:T(8,128)(2,1)}, u32[]{:S(2)}) copy-start(bf16[16,128,411]{1,0,2:T(8,128)(2,1)} %param.10) | copy-start | bytes 5050372
  0.0 35.9 %collective-permute-start.6 = (bf16[8,308,411]{2,0,1:T(8,128)(2,1)}, bf16[8,308,411]{2,0,1:T(8,128)(2,1)}, u32[]{:S(2)}, u32[]{:S(2)}) collective-permute-start(bf16[8,308,411]{2,0,1:T(8,128)(2,1)} %param.7), channel_id=1, source_target_pairs={{0,1},{1,0},{2,3},{3,2},{4,5},{5,4},{6,7},{7,6},{8,9},{9,8},{10,11... | collective-permute-start | bytes 6076232 | tf_op jit(solution)/shard_map/ppermute | solution.py:20
  4.8 16.7 %copy-start.5 = (s32[8]{0:T(128)}, s32[8]{0:T(128)S(1)}, u32[]{:S(2)}) copy-start(s32[8]{0:T(128)S(1)} %multiply_add_fusion.place_ref) | copy-start | bytes 100
  5.6 17.0 %collective-permute-start = (s32[3]{0:T(128)S(1)}, s32[3]{0:T(128)S(1)}, u32[]{:S(2)}, u32[]{:S(2)}) collective-permute-start(s32[3]{0:T(128)S(1)} %get-tuple-element.22), channel_id=1, source_target_pairs={{0,254},{2,0},{4,2},{6,4},{8,6},{10,8},{12,10},{14,12},{16,14},{18... | collective-permute-start | bytes 44 | tf_op jit(solution)/shard_map/ppermute | solution.py:16
  14.1 9.0 %collective-permute-start.1 = (s32[3]{0:T(128)S(1)}, s32[3]{0:T(128)S(1)}, u32[]{:S(2)}, u32[]{:S(2)}) collective-permute-start(s32[3]{0:T(128)S(1)} %get-tuple-element.20), channel_id=1, source_target_pairs={{0,2},{2,4},{4,6},{6,8},{8,10},{10,12},{12,14},{14,16},{16,18},{18... | collective-permute-start | bytes 44 | tf_op jit(solution)/shard_map/ppermute | solution.py:16
  14.1 9.6 %collective-permute-start.2 = (s32[3]{0:T(128)S(1)}, s32[3]{0:T(128)S(1)}, u32[]{:S(2)}, u32[]{:S(2)}) collective-permute-start(s32[3]{0:T(128)S(1)} %get-tuple-element.19), channel_id=1, source_target_pairs={{0,4},{2,6},{4,8},{6,10},{8,12},{10,14},{12,16},{14,18},{16,20},{1... | collective-permute-start | bytes 44 | tf_op jit(solution)/shard_map/ppermute | solution.py:16
  14.1 17.1 %collective-permute-start.7 = (bf16[8,308]{1,0:T(8,128)(2,1)}, bf16[8,308]{1,0:T(8,128)(2,1)S(1)}, u32[]{:S(2)}, u32[]{:S(2)}) collective-permute-start(bf16[8,308]{1,0:T(8,128)(2,1)} %param.9), channel_id=1, source_target_pairs={{0,1},{1,0},{2,3},{3,2},{4,5},{5,4},{6,7},{7,6},{8,9},{9,8},{10,11... | collective-permute-start | bytes 14792 | tf_op jit(solution)/shard_map/ppermute | solution.py:20
  18.1 4.5 %copy-start.1 = (bf16[308,616]{1,0:T(8,128)(2,1)S(1)}, bf16[308,616]{1,0:T(8,128)(2,1)}, u32[]{:S(2)}) copy-start(bf16[308,616]{1,0:T(8,128)(2,1)} %param.8) | copy-start | bytes 1138372
  22.6 12.1 %collective-permute-start.8 = (bf16[308,616]{1,0:T(8,128)(2,1)S(1)}, bf16[308,616]{1,0:T(8,128)(2,1)S(1)}, u32[]{:S(2)}, u32[]{:S(2)}) collective-permute-start(bf16[308,616]{1,0:T(8,128)(2,1)S(1)} %copy-done.1), channel_id=1, source_target_pairs={{0,1},{1,0},{2,3},{3,2},{4,5},{5,4},{6,7},{7,6},{8,9},{9,8},{10,11... | collective-permute-start | bytes 1138376 | tf_op jit(solution)/shard_map/ppermute | solution.py:20
  23.2 16.8 %collective-permute-start.3 = (bf16[3,64,411]{2,1,0:T(8,128)(2,1)S(1)}, bf16[3,64,411]{2,1,0:T(8,128)(2,1)S(1)}, u32[]{:S(2)}, u32[]{:S(2)}) collective-permute-start(bf16[3,64,411]{2,1,0:T(8,128)(2,1)S(1)} %copy.42), channel_id=1, source_target_pairs={{0,2},{2,4},{4,6},{6,8},{8,10},{10,12},{12,14},{14,16},{16,18},{18... | collective-permute-start | bytes 473480 | tf_op jit(solution)/shard_map/ppermute | solution.py:16
  23.7 16.3 %collective-permute-start.4 = (bf16[3,64,411]{2,1,0:T(8,128)(2,1)S(1)}, bf16[3,64,411]{2,1,0:T(8,128)(2,1)S(1)}, u32[]{:S(2)}, u32[]{:S(2)}) collective-permute-start(bf16[3,64,411]{2,1,0:T(8,128)(2,1)S(1)} %copy.40), channel_id=1, source_target_pairs={{0,254},{2,0},{4,2},{6,4},{8,6},{10,8},{12,10},{14,12},{16,14},{18... | collective-permute-start | bytes 473480 | tf_op jit(solution)/shard_map/ppermute | solution.py:16
  31.2 8.8 %collective-permute-start.5 = (bf16[3,64,411]{2,1,0:T(8,128)(2,1)S(1)}, bf16[3,64,411]{2,1,0:T(8,128)(2,1)S(1)}, u32[]{:S(2)}, u32[]{:S(2)}) collective-permute-start(bf16[3,64,411]{2,1,0:T(8,128)(2,1)S(1)} %copy.39), channel_id=1, source_target_pairs={{0,252},{2,254},{4,0},{6,2},{8,4},{10,6},{12,8},{14,10},{16,12},{1... | collective-permute-start | bytes 473480 | tf_op jit(solution)/shard_map/ppermute | solution.py:16
  40.0 0.7 copy-start.2
  40.0 0.8 copy-start.3
  40.0 0.8 copy-start.4
  55.0 11.8 %collective-permute-start.11 = (bf16[3,64,411]{2,1,0:T(8,128)(2,1)}, bf16[3,64,411]{2,1,0:T(8,128)(2,1)S(1)}, u32[]{:S(2)}, u32[]{:S(2)}) collective-permute-start(bf16[3,64,411]{2,1,0:T(8,128)(2,1)} %get-tuple-element.12), channel_id=1, source_target_pairs={{0,4},{2,6},{4,8},{6,10},{8,12},{10,14},{12,16},{14,18},{16,20},{1... | collective-permute-start | bytes 473480 | tf_op jit(solution)/shard_map/ppermute | solution.py:16
  55.3 14.6 %collective-permute-start.10 = (bf16[3,64,411]{2,1,0:T(8,128)(2,1)}, bf16[3,64,411]{2,1,0:T(8,128)(2,1)S(1)}, u32[]{:S(2)}, u32[]{:S(2)}) collective-permute-start(bf16[3,64,411]{2,1,0:T(8,128)(2,1)} %get-tuple-element.11), channel_id=1, source_target_pairs={{0,2},{2,4},{4,6},{6,8},{8,10},{10,12},{12,14},{14,16},{16,18},{18... | collective-permute-start | bytes 473480 | tf_op jit(solution)/shard_map/ppermute | solution.py:16
  55.3 14.6 %collective-permute-start.9 = (bf16[3,64,411]{2,1,0:T(8,128)(2,1)}, bf16[3,64,411]{2,1,0:T(8,128)(2,1)S(1)}, u32[]{:S(2)}, u32[]{:S(2)}) collective-permute-start(bf16[3,64,411]{2,1,0:T(8,128)(2,1)} %get-tuple-element.9), channel_id=1, source_target_pairs={{0,254},{2,0},{4,2},{6,4},{8,6},{10,8},{12,10},{14,12},{16,14},{18... | collective-permute-start | bytes 473480 | tf_op jit(solution)/shard_map/ppermute | solution.py:16
  71.6 4.9 %collective-permute-start.12 = (bf16[16,64,411]{2,0,1:T(8,128)(2,1)S(1)}, bf16[16,64,411]{2,0,1:T(8,128)(2,1)S(1)}, u32[]{:S(2)}, u32[]{:S(2)}) collective-permute-start(bf16[16,64,411]{2,0,1:T(8,128)(2,1)S(1)} %convolution_convert_fusion), channel_id=1, source_target_pairs={{0,1},{1,0},{2,3},{3,2},{4,5},{5,4},{6,7},{7,6},{8,9},{9,8},{10,11... | collective-permute-start | bytes 2525192 | tf_op jit(solution)/shard_map/ppermute | solution.py:20

commit v12 on v11

--- a/solution.py
+++ b/solution.py
@@ -4,6 +4,7 @@
 from jax.experimental import pallas as pl
 from jax.experimental.pallas import tpu as pltpu
 from jax.sharding import PartitionSpec as P
+from jax.experimental.layout import Layout, with_layout_constraint
 
 SPAN = 4
 CAP = 3
@@ -162,6 +163,9 @@
     mine = jnp.einsum("ac,amd->cmd", one_hot(got_slots, columns), jnp.concatenate(recv_parts, axis=0),
                       preferred_element_type=jnp.float32).astype(jnp.bfloat16)
     other = swapped(mine)
+    out_order = Layout((2, 0, 1))
+    mine = with_layout_constraint(mine, out_order)
+    other = with_layout_constraint(other, out_order)
     return jnp.where(first, jnp.concatenate([mine, other], axis=1),
                      jnp.concatenate([other, mine], axis=1))
 

time: 83.7 us -> 86.9 us (1.038)
  other arithmetic: 8.35 us -> 11.6 us
  local copies, waits for them, and re-layouts: 15.8 us -> 18.1 us
  waiting for transfers between devices: 9.98 us -> 7.77 us
    select_n x1 -> x0, local copies, waits for them, and re-layouts: 4.94 us -> none  [on_device(): jnp.where(first, jnp.concatenate([mine, other], axis=1), jnp.concatenate(...]
    select_n x1, other arithmetic: 1.82 us -> 5.06 us  [on_device(): jnp.where(first, jnp.concatenate([mine, other], axis=1), jnp.concatenate(...]
    ppermute x1 -> x2, local copies, waits for them, and re-layouts: 4.04 us -> 7.24 us  [swapped(): return lax.ppermute(value, 'chan', [(0, 1), (1, 0)])]
    convert_element_type x0 -> x1, local copies, waits for them, and re-layouts: none -> 2.53 us  [on_device(): mine = jnp.einsum('ac,amd->cmd', one_hot(got_slots, columns), jnp.concate...]
    ppermute x4, waiting for transfers between devices: 2.29 us -> 0.09 us  [swapped(): return lax.ppermute(value, 'chan', [(0, 1), (1, 0)])]
    dot_general x0 -> x1, local copies, waits for them, and re-layouts: none -> 1.55 us  [on_device(): jnp.einsum('ac,amd->cmd', one_hot(got_slots, columns), jnp.concatenate(re...]
  transfers between devices with their start and end apart: 13 -> 13, of which waited for: 3 -> 3; matrix products, arithmetic and copies ran while one was open for 20% -> 22% of each run, Pallas kernels for 0% -> 0%
where the time goes in v12:
time: 86.9 us; the launch traced here: 86.5 us
  starting transfers between devices  32 us (37%)
  local copies, waits for them, and re-layouts  18.1 us (21%)
  Pallas kernels  14.2 us (16%)
  other arithmetic  11.6 us (13%)
  waiting for transfers between devices  7.77 us (9%)
  matrix products  1.99 us (2%)
    ppermute x9, starting transfers between devices, passed_along(): lax.ppermute(value, axis, [(i, (i + by) % count) for i in range(count)])  25.8 us
    pallas_call x1, Pallas kernels, adjoints(): pl.pallas_call(adjoint_kernel, grid_spec=grid_spec, out_shape=[jax.ShapeD...  14.2 us
    ppermute x9, waiting for transfers between devices, passed_along(): lax.ppermute(value, axis, [(i, (i + by) % count) for i in range(count)])  7.67 us
    ppermute x2, local copies, waits for them, and re-layouts, swapped(): return lax.ppermute(value, 'chan', [(0, 1), (1, 0)])  7.24 us
    ppermute x4, starting transfers between devices, swapped(): return lax.ppermute(value, 'chan', [(0, 1), (1, 0)])  6.21 us
    select_n x1, other arithmetic, on_device(): jnp.where(first, jnp.concatenate([mine, other], axis=1), jnp.concatenate(...  5.06 us
    unnamed x13, local copies, waits for them, and re-layouts  4.14 us
    convert_element_type x1, local copies, waits for them, and re-layouts, on_device(): mine = jnp.einsum('ac,amd->cmd', one_hot(got_slots, columns), jnp.concate...  2.53 us
  transfers between devices with their start and end apart: 13, of which 3 were waited for; matrix products, arithmetic and copies ran while one was open for 22% of the time, Pallas kernels for 0%

profile of v12, /device:TPU:1, one launch (start us, length us, event | category | flops | bytes accessed | tf_op | source)
XLA Modules:
  0.0 86.5 jit_solution(3316056534521023266)
XLA Ops:
  0.0 3.2 %collective-permute-start.6 = (bf16[8,308,411]{2,0,1:T(8,128)(2,1)}, bf16[8,308,411]{2,0,1:T(8,128)(2,1)}, u32[]{:S(2)}, u32[]{:S(2)}) collective-permute-start(bf16[8,308,411]{2,0,1:T(8,128)(2,1)} %param.7), channel_id=1, source_target_pairs={{0,1},{1,0},{2,3},{3,2},{4,5},{5,4},{6,7},{7,6},{8,9},{9,8},{10,11... | collective-permute-start | bytes 6076232 | tf_op jit(solution)/shard_map/ppermute | solution.py:21
  3.2 0.9 %convert_reduce_fusion = s32[8]{0:T(128)S(1)} fusion(s32[8]{0:T(128)} %bitcast.23), kind=kLoop, calls=%fused_computation.20 | loop fusion | flops 312 | bytes 64 | tf_op jit(solution)/shard_map/reduce_sum | solution.py:135
  4.1 0.7 multiply_add_fusion.place_ref
  4.8 0.7 select_reduce_fusion
  5.5 0.1 fusion.22
  5.6 8.5 %collective-permute-start = (s32[3]{0:T(128)S(1)}, s32[3]{0:T(128)S(1)}, u32[]{:S(2)}, u32[]{:S(2)}) collective-permute-start(s32[3]{0:T(128)S(1)} %get-tuple-element.22), channel_id=1, source_target_pairs={{0,254},{2,0},{4,2},{6,4},{8,6},{10,8},{12,10},{14,12},{16,14},{18... | collective-permute-start | bytes 44 | tf_op jit(solution)/shard_map/ppermute | solution.py:17
  14.1 0.0 collective-permute-start.2
  14.1 0.4 collective-permute-start.7
  14.5 1.3 %convert_element_type.34.ic_ref = f32[8,308]{1,0:T(8,128)} convert(bf16[8,308]{1,0:T(8,128)(2,1)} %param.9) | non-fusion elementwise | flops 2464 | bytes 14784 | tf_op jit(solution)/shard_map/convert_element_type | solution.py:117
  16.4 1.7 %constant_dynamic-slice_fusion = bf16[16,64,411]{1,0,2:T(8,128)(2,1)} fusion(bf16[16,128,411]{1,0,2:T(8,128)(2,1)S(1)} %copy-done, s32[]{:T(128)S(6)} %select_n.49), kind=kLoop, calls=%fused_computation.41 | loop fusion | bytes 1683460 | tf_op jit(solution)/shard_map/dynamic_slice | solution.py:140
  18.1 3.3 %copy.46 = bf16[16,64,411]{2,0,1:T(8,128)(2,1)S(1)} copy(bf16[16,64,411]{1,0,2:T(8,128)(2,1)} %constant_dynamic-slice_fusion) | data formatting | bytes 1683456
  21.5 0.4 fusion.10
  21.8 0.7 copy.57.s1_ref
  22.6 0.0 collective-permute-done
  22.6 0.2 collective-permute-start.8
  22.7 0.3 fusion.7
  23.2 0.1 collective-permute-start.3
  23.3 0.4 fusion.13
  23.7 0.0 collective-permute-done.2
  23.7 7.1 %collective-permute-start.4 = (bf16[3,64,411]{2,1,0:T(8,128)(2,1)S(1)}, bf16[3,64,411]{2,1,0:T(8,128)(2,1)S(1)}, u32[]{:S(2)}, u32[]{:S(2)}) collective-permute-start(bf16[3,64,411]{2,1,0:T(8,128)(2,1)S(1)} %copy.56), channel_id=1, source_target_pairs={{0,254},{2,0},{4,2},{6,4},{8,6},{10,8},{12,10},{14,12},{16,14},{18... | collective-permute-start | bytes 473480 | tf_op jit(solution)/shard_map/ppermute | solution.py:17
  30.8 0.3 fusion.16
  31.2 0.0 collective-permute-done.7
  31.2 2.9 %collective-permute-start.5 = (bf16[3,64,411]{2,1,0:T(8,128)(2,1)S(1)}, bf16[3,64,411]{2,1,0:T(8,128)(2,1)S(1)}, u32[]{:S(2)}, u32[]{:S(2)}) collective-permute-start(bf16[3,64,411]{2,1,0:T(8,128)(2,1)S(1)} %copy.55), channel_id=1, source_target_pairs={{0,252},{2,254},{4,0},{6,2},{8,4},{10,6},{12,8},{14,10},{16,12},{1... | collective-permute-start | bytes 473480 | tf_op jit(solution)/shard_map/ppermute | solution.py:17
  34.1 0.6 convert_element_type.35.io_ref
  34.7 0.1 broadcast_select_fusion.1
  34.8 1.1 %broadcast_select_fusion.2 = (bf16[308,308]{1,0:T(8,128)(2,1)}, bf16[308,308]{1,0:T(8,128)(2,1)}, bf16[308,308]{1,0:T(8,128)(2,1)}, bf16[308,308]{1,0:T(8,128)(2,1)}) fusion(pred[]{:T(512)S(6)} %eq.44, bf16[308,616]{1,0:T(8,128)(2,1)S(1)} %get-tuple-element.18, bf16[308,616]{1,0:T(8,128)(2,1)S(1)} %get-tuple-element.17), kind=kLoop, calls=%fused_computation.11 | loop fusion | flops 379456 | bytes 1517825 | tf_op jit(solution)/shard_map/jit(_where)/select_n | solution.py:129
  35.9 0.0 collective-permute-done.6
  35.9 4.0 %copy.41.jo_ref = bf16[8,308,411]{2,1,0:T(8,128)(2,1)} copy(bf16[8,308,411]{2,0,1:T(8,128)(2,1)} %collective-permute-done.6) | data formatting | bytes 4050816 | tf_op jit(solution)/shard_map/ppermute | solution.py:21
  40.0 0.0 collective-permute-done.3.s0_ref
  40.0 0.0 collective-permute-done.4.s2_ref
  40.0 0.6 copy-done.2
  40.6 0.1 copy-done.3
  40.7 0.1 copy-done.4
  40.8 14.2 %shard_map.73 = (bf16[3,64,411]{2,1,0:T(8,128)(2,1)}, bf16[3,64,411]{2,1,0:T(8,128)(2,1)}, bf16[3,64,411]{2,1,0:T(8,128)(2,1)}, bf16[3,64,411]{2,1,0:T(8,128)(2,1)}) custom-call(s32[8]{0:T(128)} %copy-done.5, s32[1]{0:T(128)S(6)} %copy.59.count_ref, bf16[3,64,411]{2,1,0:T(8,128)(2,1)} %copy-done.2, bf16[3,64,411]{2,1,0:T(8,128)(2,1)} %copy.57.s1_ref, ...), custom_call_target="tpu_custom_call" | custom-call | tf_op jit(solution)/shard_map/pallas_call | solution.py:97
  54.9 0.3 collective-permute-start.11
  55.3 6.9 %collective-permute-start.9 = (bf16[3,64,411]{2,1,0:T(8,128)(2,1)}, bf16[3,64,411]{2,1,0:T(8,128)(2,1)S(1)}, u32[]{:S(2)}, u32[]{:S(2)}) collective-permute-start(bf16[3,64,411]{2,1,0:T(8,128)(2,1)} %get-tuple-element.9), channel_id=1, source_target_pairs={{0,254},{2,0},{4,2},{6,4},{8,6},{10,8},{12,10},{14,12},{16,14},{18... | collective-permute-start | bytes 473480 | tf_op jit(solution)/shard_map/ppermute | solution.py:17
  62.2 0.1 pad_add_fusion
  62.3 4.5 %collective-permute-done.11 = bf16[3,64,411]{2,1,0:T(8,128)(2,1)S(1)} collective-permute-done((bf16[3,64,411]{2,1,0:T(8,128)(2,1)}, bf16[3,64,411]{2,1,0:T(8,128)(2,1)S(1)}, u32[]{:S(2)}, u32[]{:S(2)}) %collective-permute-start.11) | collective-permute-done | bytes 157856 | tf_op jit(solution)/shard_map/ppermute | solution.py:17
  66.8 3.2 %collective-permute-done.10 = bf16[3,64,411]{2,1,0:T(8,128)(2,1)S(1)} collective-permute-done((bf16[3,64,411]{2,1,0:T(8,128)(2,1)}, bf16[3,64,411]{2,1,0:T(8,128)(2,1)S(1)}, u32[]{:S(2)}, u32[]{:S(2)}) %collective-permute-start.10) | collective-permute-done | bytes 157856 | tf_op jit(solution)/shard_map/ppermute | solution.py:17
  69.9 0.0 collective-permute-done.9
  69.9 1.0 %pad_maximum_fusion = bf16[12,64,411]{2,1,0:T(8,128)(2,1)S(1)} fusion(bf16[3,64,411]{2,1,0:T(8,128)(2,1)S(1)} %collective-permute-done.11, bf16[3,64,411]{2,1,0:T(8,128)(2,1)S(1)} %collective-permute-done.10, bf16[3,64,411]{2,1,0:T(8,128)(2,1)} %get-tuple-element.10, bf16[3,64,411]{2,1,0:T(8,128)(2,1)S(1)} %collective-permute-done.9), kind=kLoop, calls=%fused_computation.4 | loop fusion | flops 946944 | bytes 1262592 | tf_op jit(solution)/shard_map/concatenate | solution.py:163
  71.0 0.6 fusion
  71.6 1.5 %copy.54 = bf16[16,64,411]{2,1,0:T(8,128)(2,1)} copy(bf16[16,64,411]{2,0,1:T(8,128)(2,1)S(1)} %fusion) | data formatting | bytes 1683456 | tf_op jit(solution)/shard_map/ac,amd->cmd/dot_general | solution.py:163
  73.1 2.5 %collective-permute-start.12 = (bf16[16,64,411]{2,1,0:T(8,128)(2,1)}, bf16[16,64,411]{2,1,0:T(8,128)(2,1)}, u32[]{:S(2)}, u32[]{:S(2)}) collective-permute-start(bf16[16,64,411]{2,1,0:T(8,128)(2,1)} %copy.54), channel_id=1, source_target_pairs={{0,1},{1,0},{2,3},{3,2},{4,5},{5,4},{6,7},{7,6},{8,9},{9,8},{10,11... | collective-permute-start | bytes 2525192 | tf_op jit(solution)/shard_map/ppermute | solution.py:21
  75.6 2.5 %copy.44 = bf16[16,64,411]{1,0,2:T(8,128)(2,1)S(1)} copy(bf16[16,64,411]{2,1,0:T(8,128)(2,1)} %copy.54) | data formatting | bytes 1683456 | tf_op jit(solution)/shard_map/convert_element_type | solution.py:164
  78.2 0.1 collective-permute-done.12
  78.2 3.2 %copy.45 = bf16[16,64,411]{1,0,2:T(8,128)(2,1)} copy(bf16[16,64,411]{2,1,0:T(8,128)(2,1)} %collective-permute-done.12) | data formatting | bytes 1683456 | tf_op jit(solution)/shard_map/ppermute | solution.py:21
  81.4 5.1 %maximum_select_fusion = bf16[16,128,411]{1,0,2:T(8,128)(2,1)} fusion(bf16[16,64,411]{1,0,2:T(8,128)(2,1)} %copy.45, bf16[16,64,411]{1,0,2:T(8,128)(2,1)S(1)} %copy.44, pred[]{:T(512)S(6)} %eq.44), kind=kLoop, calls=%fused_computation.1 | loop fusion | flops 7575552 | bytes 3366913 | tf_op jit(solution)/shard_map/jit(_where)/select_n | solution.py:169
  (17 shorter events, 0.2 us)
Async XLA Ops:
  0.0 16.4 %copy-start = (bf16[16,128,411]{1,0,2:T(8,128)(2,1)S(1)}, bf16[16,128,411]{1,0,2:T(8,128)(2,1)}, u32[]{:S(2)}) copy-start(bf16[16,128,411]{1,0,2:T(8,128)(2,1)} %param.10) | copy-start | bytes 5050372
  0.0 35.9 %collective-permute-start.6 = (bf16[8,308,411]{2,0,1:T(8,128)(2,1)}, bf16[8,308,411]{2,0,1:T(8,128)(2,1)}, u32[]{:S(2)}, u32[]{:S(2)}) collective-permute-start(bf16[8,308,411]{2,0,1:T(8,128)(2,1)} %param.7), channel_id=1, source_target_pairs={{0,1},{1,0},{2,3},{3,2},{4,5},{5,4},{6,7},{7,6},{8,9},{9,8},{10,11... | collective-permute-start | bytes 6076232 | tf_op jit(solution)/shard_map/ppermute | solution.py:21
  4.8 13.4 %copy-start.5 = (s32[8]{0:T(128)}, s32[8]{0:T(128)S(1)}, u32[]{:S(2)}) copy-start(s32[8]{0:T(128)S(1)} %multiply_add_fusion.place_ref) | copy-start | bytes 100
  5.6 17.0 %collective-permute-start = (s32[3]{0:T(128)S(1)}, s32[3]{0:T(128)S(1)}, u32[]{:S(2)}, u32[]{:S(2)}) collective-permute-start(s32[3]{0:T(128)S(1)} %get-tuple-element.22), channel_id=1, source_target_pairs={{0,254},{2,0},{4,2},{6,4},{8,6},{10,8},{12,10},{14,12},{16,14},{18... | collective-permute-start | bytes 44 | tf_op jit(solution)/shard_map/ppermute | solution.py:17
  14.1 9.0 %collective-permute-start.1 = (s32[3]{0:T(128)S(1)}, s32[3]{0:T(128)S(1)}, u32[]{:S(2)}, u32[]{:S(2)}) collective-permute-start(s32[3]{0:T(128)S(1)} %get-tuple-element.20), channel_id=1, source_target_pairs={{0,2},{2,4},{4,6},{6,8},{8,10},{10,12},{12,14},{14,16},{16,18},{18... | collective-permute-start | bytes 44 | tf_op jit(solution)/shard_map/ppermute | solution.py:17
  14.1 9.6 %collective-permute-start.2 = (s32[3]{0:T(128)S(1)}, s32[3]{0:T(128)S(1)}, u32[]{:S(2)}, u32[]{:S(2)}) collective-permute-start(s32[3]{0:T(128)S(1)} %get-tuple-element.19), channel_id=1, source_target_pairs={{0,4},{2,6},{4,8},{6,10},{8,12},{10,14},{12,16},{14,18},{16,20},{1... | collective-permute-start | bytes 44 | tf_op jit(solution)/shard_map/ppermute | solution.py:17
  14.1 17.1 %collective-permute-start.7 = (bf16[8,308]{1,0:T(8,128)(2,1)}, bf16[8,308]{1,0:T(8,128)(2,1)S(1)}, u32[]{:S(2)}, u32[]{:S(2)}) collective-permute-start(bf16[8,308]{1,0:T(8,128)(2,1)} %param.9), channel_id=1, source_target_pairs={{0,1},{1,0},{2,3},{3,2},{4,5},{5,4},{6,7},{7,6},{8,9},{9,8},{10,11... | collective-permute-start | bytes 14792 | tf_op jit(solution)/shard_map/ppermute | solution.py:21
  18.1 4.5 %copy-start.1 = (bf16[308,616]{1,0:T(8,128)(2,1)S(1)}, bf16[308,616]{1,0:T(8,128)(2,1)}, u32[]{:S(2)}) copy-start(bf16[308,616]{1,0:T(8,128)(2,1)} %param.8) | copy-start | bytes 1138372
  22.6 12.1 %collective-permute-start.8 = (bf16[308,616]{1,0:T(8,128)(2,1)S(1)}, bf16[308,616]{1,0:T(8,128)(2,1)S(1)}, u32[]{:S(2)}, u32[]{:S(2)}) collective-permute-start(bf16[308,616]{1,0:T(8,128)(2,1)S(1)} %copy-done.1), channel_id=1, source_target_pairs={{0,1},{1,0},{2,3},{3,2},{4,5},{5,4},{6,7},{7,6},{8,9},{9,8},{10,11... | collective-permute-start | bytes 1138376 | tf_op jit(solution)/shard_map/ppermute | solution.py:21
  23.2 16.8 %collective-permute-start.3 = (bf16[3,64,411]{2,1,0:T(8,128)(2,1)S(1)}, bf16[3,64,411]{2,1,0:T(8,128)(2,1)S(1)}, u32[]{:S(2)}, u32[]{:S(2)}) collective-permute-start(bf16[3,64,411]{2,1,0:T(8,128)(2,1)S(1)} %copy.58), channel_id=1, source_target_pairs={{0,2},{2,4},{4,6},{6,8},{8,10},{10,12},{12,14},{14,16},{16,18},{18... | collective-permute-start | bytes 473480 | tf_op jit(solution)/shard_map/ppermute | solution.py:17
  23.7 16.3 %collective-permute-start.4 = (bf16[3,64,411]{2,1,0:T(8,128)(2,1)S(1)}, bf16[3,64,411]{2,1,0:T(8,128)(2,1)S(1)}, u32[]{:S(2)}, u32[]{:S(2)}) collective-permute-start(bf16[3,64,411]{2,1,0:T(8,128)(2,1)S(1)} %copy.56), channel_id=1, source_target_pairs={{0,254},{2,0},{4,2},{6,4},{8,6},{10,8},{12,10},{14,12},{16,14},{18... | collective-permute-start | bytes 473480 | tf_op jit(solution)/shard_map/ppermute | solution.py:17
  31.2 8.8 %collective-permute-start.5 = (bf16[3,64,411]{2,1,0:T(8,128)(2,1)S(1)}, bf16[3,64,411]{2,1,0:T(8,128)(2,1)S(1)}, u32[]{:S(2)}, u32[]{:S(2)}) collective-permute-start(bf16[3,64,411]{2,1,0:T(8,128)(2,1)S(1)} %copy.55), channel_id=1, source_target_pairs={{0,252},{2,254},{4,0},{6,2},{8,4},{10,6},{12,8},{14,10},{16,12},{1... | collective-permute-start | bytes 473480 | tf_op jit(solution)/shard_map/ppermute | solution.py:17
  40.0 0.7 copy-start.2
  40.0 0.8 copy-start.3
  40.0 0.8 copy-start.4
  54.9 11.8 %collective-permute-start.11 = (bf16[3,64,411]{2,1,0:T(8,128)(2,1)}, bf16[3,64,411]{2,1,0:T(8,128)(2,1)S(1)}, u32[]{:S(2)}, u32[]{:S(2)}) collective-permute-start(bf16[3,64,411]{2,1,0:T(8,128)(2,1)} %get-tuple-element.12), channel_id=1, source_target_pairs={{0,4},{2,6},{4,8},{6,10},{8,12},{10,14},{12,16},{14,18},{16,20},{1... | collective-permute-start | bytes 473480 | tf_op jit(solution)/shard_map/ppermute | solution.py:17
  55.3 14.6 %collective-permute-start.10 = (bf16[3,64,411]{2,1,0:T(8,128)(2,1)}, bf16[3,64,411]{2,1,0:T(8,128)(2,1)S(1)}, u32[]{:S(2)}, u32[]{:S(2)}) collective-permute-start(bf16[3,64,411]{2,1,0:T(8,128)(2,1)} %get-tuple-element.11), channel_id=1, source_target_pairs={{0,2},{2,4},{4,6},{6,8},{8,10},{10,12},{12,14},{14,16},{16,18},{18... | collective-permute-start | bytes 473480 | tf_op jit(solution)/shard_map/ppermute | solution.py:17
  55.3 14.6 %collective-permute-start.9 = (bf16[3,64,411]{2,1,0:T(8,128)(2,1)}, bf16[3,64,411]{2,1,0:T(8,128)(2,1)S(1)}, u32[]{:S(2)}, u32[]{:S(2)}) collective-permute-start(bf16[3,64,411]{2,1,0:T(8,128)(2,1)} %get-tuple-element.9), channel_id=1, source_target_pairs={{0,254},{2,0},{4,2},{6,4},{8,6},{10,8},{12,10},{14,12},{16,14},{18... | collective-permute-start | bytes 473480 | tf_op jit(solution)/shard_map/ppermute | solution.py:17
  73.1 5.1 %collective-permute-start.12 = (bf16[16,64,411]{2,1,0:T(8,128)(2,1)}, bf16[16,64,411]{2,1,0:T(8,128)(2,1)}, u32[]{:S(2)}, u32[]{:S(2)}) collective-permute-start(bf16[16,64,411]{2,1,0:T(8,128)(2,1)} %copy.54), channel_id=1, source_target_pairs={{0,1},{1,0},{2,3},{3,2},{4,5},{5,4},{6,7},{7,6},{8,9},{9,8},{10,11... | collective-permute-start | bytes 2525192 | tf_op jit(solution)/shard_map/ppermute | solution.py:21

commit v13 on v11

--- a/solution.py
+++ b/solution.py
@@ -162,8 +162,9 @@
     mine = jnp.einsum("ac,amd->cmd", one_hot(got_slots, columns), jnp.concatenate(recv_parts, axis=0),
                       preferred_element_type=jnp.float32).astype(jnp.bfloat16)
     other = swapped(mine)
-    return jnp.where(first, jnp.concatenate([mine, other], axis=1),
-                     jnp.concatenate([other, mine], axis=1))
+    full = jnp.zeros((columns, members, mine.shape[2]), mine.dtype)
+    full = lax.dynamic_update_slice_in_dim(full, mine, core * half_m, axis=1)
+    return lax.dynamic_update_slice_in_dim(full, other, (1 - core) * half_m, axis=1)
 
 
 def solution(mesh):

time: 83.7 us -> 174 us (2.08)
  local copies, waits for them, and re-layouts: 15.8 us -> 109 us
  waiting for transfers between devices: 9.98 us -> 6.24 us
  other arithmetic: 8.35 us -> 6.53 us
    dynamic_update_slice x0 -> x2, local copies, waits for them, and re-layouts: none -> 90.5 us  [the longest x1 70.8 us: on_device(): full = lax.dynamic_update_slice_in_dim(full, mine, core * half_m, axis=1)]
    select_n x1 -> x0, local copies, waits for them, and re-layouts: 4.94 us -> none  [on_device(): jnp.where(first, jnp.concatenate([mine, other], axis=1), jnp.concatenate(...]
    ppermute x1 -> x2, local copies, waits for them, and re-layouts: 4.04 us -> 7.34 us  [swapped(): return lax.ppermute(value, 'chan', [(0, 1), (1, 0)])]
    convert_element_type x0 -> x1, local copies, waits for them, and re-layouts: none -> 3.29 us  [on_device(): mine = jnp.einsum('ac,amd->cmd', one_hot(got_slots, columns), jnp.concate...]
    ppermute x4, waiting for transfers between devices: 2.29 us -> 0.01 us  [swapped(): return lax.ppermute(value, 'chan', [(0, 1), (1, 0)])]
    select_n x1 -> x0, other arithmetic: 1.82 us -> none  [on_device(): jnp.where(first, jnp.concatenate([mine, other], axis=1), jnp.concatenate(...]
  transfers between devices with their start and end apart: 13 -> 13, of which waited for: 3 -> 2; matrix products, arithmetic and copies ran while one was open for 20% -> 53% of each run, Pallas kernels for 0% -> 0%
where the time goes in v13:
time: 174 us; the launch traced here: 173 us
  local copies, waits for them, and re-layouts  109 us (63%)
  starting transfers between devices  33.3 us (19%)
  Pallas kernels  14.2 us (8%)
  other arithmetic  6.53 us (4%)
  waiting for transfers between devices  6.24 us (4%)
  matrix products  2.98 us (2%)
    dynamic_update_slice x1, local copies, waits for them, and re-layouts, on_device(): full = lax.dynamic_update_slice_in_dim(full, mine, core * half_m, axis=1)  70.8 us
    ppermute x9, starting transfers between devices, passed_along(): lax.ppermute(value, axis, [(i, (i + by) % count) for i in range(count)])  25.5 us
    dynamic_update_slice x1, local copies, waits for them, and re-layouts, on_device(): lax.dynamic_update_slice_in_dim(full, other, (1 - core) * half_m, axis=1)  19.6 us
    pallas_call x1, Pallas kernels, adjoints(): pl.pallas_call(adjoint_kernel, grid_spec=grid_spec, out_shape=[jax.ShapeD...  14.2 us
    ppermute x4, starting transfers between devices, swapped(): return lax.ppermute(value, 'chan', [(0, 1), (1, 0)])  7.78 us
    ppermute x2, local copies, waits for them, and re-layouts, swapped(): return lax.ppermute(value, 'chan', [(0, 1), (1, 0)])  7.34 us
    ppermute x9, waiting for transfers between devices, passed_along(): lax.ppermute(value, axis, [(i, (i + by) % count) for i in range(count)])  6.23 us
    unnamed x13, local copies, waits for them, and re-layouts  4.14 us
  transfers between devices with their start and end apart: 13, of which 2 were waited for; matrix products, arithmetic and copies ran while one was open for 53% of the time, Pallas kernels for 0%

profile of v13, /device:TPU:1, one launch (start us, length us, event | category | flops | bytes accessed | tf_op | source)
XLA Modules:
  0.0 173.4 jit_solution(14871830750268667273)
XLA Ops:
  0.0 3.2 %collective-permute-start.6 = (bf16[8,308,411]{2,0,1:T(8,128)(2,1)}, bf16[8,308,411]{2,0,1:T(8,128)(2,1)}, u32[]{:S(2)}, u32[]{:S(2)}) collective-permute-start(bf16[8,308,411]{2,0,1:T(8,128)(2,1)} %param.7), channel_id=1, source_target_pairs={{0,1},{1,0},{2,3},{3,2},{4,5},{5,4},{6,7},{7,6},{8,9},{9,8},{10,11... | collective-permute-start | bytes 6076232 | tf_op jit(solution)/shard_map/ppermute | solution.py:20
  3.2 0.9 convert_reduce_fusion
  4.1 0.7 multiply_add_fusion.place_ref
  4.8 0.7 select_reduce_fusion
  5.5 0.1 fusion.21
  5.6 8.5 %collective-permute-start = (s32[3]{0:T(128)S(1)}, s32[3]{0:T(128)S(1)}, u32[]{:S(2)}, u32[]{:S(2)}) collective-permute-start(s32[3]{0:T(128)S(1)} %get-tuple-element.22), channel_id=1, source_target_pairs={{0,254},{2,0},{4,2},{6,4},{8,6},{10,8},{12,10},{14,12},{16,14},{18... | collective-permute-start | bytes 44 | tf_op jit(solution)/shard_map/ppermute | solution.py:16
  14.1 0.0 collective-permute-start.1
  14.1 0.0 collective-permute-start.2
  14.1 0.4 collective-permute-start.7
  14.5 1.3 convert_element_type.34.ic_ref
  15.8 1.7 constant_dynamic-slice_fusion
  17.5 3.3 %copy.35 = bf16[16,64,411]{2,0,1:T(8,128)(2,1)S(1)} copy(bf16[16,64,411]{1,0,2:T(8,128)(2,1)} %constant_dynamic-slice_fusion) | data formatting | bytes 1683456
  20.8 0.4 fusion.9
  21.2 0.7 copy.44.s1_ref
  22.6 0.2 collective-permute-start.8
  22.8 0.3 fusion.6
  23.2 0.1 collective-permute-start.3
  23.3 0.4 fusion.12
  23.8 7.1 %collective-permute-start.4 = (bf16[3,64,411]{2,1,0:T(8,128)(2,1)S(1)}, bf16[3,64,411]{2,1,0:T(8,128)(2,1)S(1)}, u32[]{:S(2)}, u32[]{:S(2)}) collective-permute-start(bf16[3,64,411]{2,1,0:T(8,128)(2,1)S(1)} %copy.43), channel_id=1, source_target_pairs={{0,254},{2,0},{4,2},{6,4},{8,6},{10,8},{12,10},{14,12},{16,14},{18... | collective-permute-start | bytes 473480 | tf_op jit(solution)/shard_map/ppermute | solution.py:16
  30.9 0.3 fusion.15
  31.3 0.0 collective-permute-done.7
  31.3 2.9 %collective-permute-start.5 = (bf16[3,64,411]{2,1,0:T(8,128)(2,1)S(1)}, bf16[3,64,411]{2,1,0:T(8,128)(2,1)S(1)}, u32[]{:S(2)}, u32[]{:S(2)}) collective-permute-start(bf16[3,64,411]{2,1,0:T(8,128)(2,1)S(1)} %copy.42), channel_id=1, source_target_pairs={{0,252},{2,254},{4,0},{6,2},{8,4},{10,6},{12,8},{14,10},{16,12},{1... | collective-permute-start | bytes 473480 | tf_op jit(solution)/shard_map/ppermute | solution.py:16
  34.2 0.6 convert_element_type.35.io_ref
  34.8 0.0 collective-permute-done.8
  34.8 0.1 broadcast_select_fusion.1
  34.9 1.1 broadcast_select_fusion.2
  36.0 4.0 %copy.31.jo_ref = bf16[8,308,411]{2,1,0:T(8,128)(2,1)} copy(bf16[8,308,411]{2,0,1:T(8,128)(2,1)} %collective-permute-done.6) | data formatting | bytes 4050816 | tf_op jit(solution)/shard_map/ppermute | solution.py:20
  40.0 0.0 collective-permute-done.3.s0_ref
  40.1 0.0 collective-permute-done.5.s3_ref
  40.1 0.6 copy-done.2
  40.7 0.1 copy-done.3
  40.8 0.1 copy-done.4
  40.9 14.2 %shard_map.73 = (bf16[3,64,411]{2,1,0:T(8,128)(2,1)}, bf16[3,64,411]{2,1,0:T(8,128)(2,1)}, bf16[3,64,411]{2,1,0:T(8,128)(2,1)}, bf16[3,64,411]{2,1,0:T(8,128)(2,1)}) custom-call(s32[8]{0:T(128)} %copy-done.5, s32[1]{0:T(128)S(6)} %copy.48.count_ref, bf16[3,64,411]{2,1,0:T(8,128)(2,1)} %copy-done.2, bf16[3,64,411]{2,1,0:T(8,128)(2,1)} %copy.44.s1_ref, ...), custom_call_target="tpu_custom_call" | custom-call | tf_op jit(solution)/shard_map/pallas_call | solution.py:96
  55.0 0.0 collective-permute-start.10
  55.0 0.4 collective-permute-start.11
  55.5 6.5 %collective-permute-start.9 = (bf16[3,64,411]{2,1,0:T(8,128)(2,1)}, bf16[3,64,411]{2,1,0:T(8,128)(2,1)S(1)}, u32[]{:S(2)}, u32[]{:S(2)}) collective-permute-start(bf16[3,64,411]{2,1,0:T(8,128)(2,1)} %get-tuple-element.9), channel_id=1, source_target_pairs={{0,254},{2,0},{4,2},{6,4},{8,6},{10,8},{12,10},{14,12},{16,14},{18... | collective-permute-start | bytes 473480 | tf_op jit(solution)/shard_map/ppermute | solution.py:16
  61.9 0.1 pad_add_fusion
  62.0 5.7 %collective-permute-done.10 = bf16[3,64,411]{2,1,0:T(8,128)(2,1)S(1)} collective-permute-done((bf16[3,64,411]{2,1,0:T(8,128)(2,1)}, bf16[3,64,411]{2,1,0:T(8,128)(2,1)S(1)}, u32[]{:S(2)}, u32[]{:S(2)}) %collective-permute-start.10) | collective-permute-done | bytes 157856 | tf_op jit(solution)/shard_map/ppermute | solution.py:16
  67.7 0.5 collective-permute-done.11
  68.2 1.0 pad_maximum_fusion
  69.3 1.6 convolution_convert_fusion
  70.9 4.0 %collective-permute-start.12 = (bf16[16,64,411]{2,0,1:T(8,128)(2,1)}, bf16[16,64,411]{2,0,1:T(8,128)(2,1)}, u32[]{:S(2)}, u32[]{:S(2)}) collective-permute-start(bf16[16,64,411]{2,0,1:T(8,128)(2,1)} %convolution_convert_fusion), channel_id=1, source_target_pairs={{0,1},{1,0},{2,3},{3,2},{4,5},{5,4},{6,7},{7,6},{8,9},{9,8},{10,11... | collective-permute-start | bytes 2525192 | tf_op jit(solution)/shard_map/ppermute | solution.py:20
  74.8 3.3 %copy.33 = bf16[16,64,411]{1,0,2:T(8,128)(2,1)S(1)} copy(bf16[16,64,411]{2,0,1:T(8,128)(2,1)} %convolution_convert_fusion) | data formatting | bytes 1683456 | tf_op jit(solution)/shard_map/convert_element_type | solution.py:163
  78.1 1.4 broadcast_in_dim.14
  79.5 70.8 %dynamic_update_slice.6 = bf16[16,128,411]{1,0,2:T(8,128)(2,1)} dynamic-update-slice(bf16[16,128,411]{1,0,2:T(8,128)(2,1)} %broadcast_in_dim.14, bf16[16,64,411]{1,0,2:T(8,128)(2,1)S(1)} %copy.33, s32[]{:T(128)} %constant.2.clone.1, s32[]{:T(128)S(6)} %select_n.44, s32[]{:T(128)} %constant.2.clone.1) | dynamic-update-slice | bytes 1683460 | tf_op jit(solution)/shard_map/dynamic_update_slice | solution.py:166
  150.4 0.0 collective-permute-done.12
  150.4 3.3 %copy.34 = bf16[16,64,411]{1,0,2:T(8,128)(2,1)S(1)} copy(bf16[16,64,411]{2,0,1:T(8,128)(2,1)} %collective-permute-done.12) | data formatting | bytes 1683456 | tf_op jit(solution)/shard_map/ppermute | solution.py:20
  153.7 19.6 %dynamic_update_slice.7 = bf16[16,128,411]{1,0,2:T(8,128)(2,1)} dynamic-update-slice(bf16[16,128,411]{1,0,2:T(8,128)(2,1)} %dynamic_update_slice.6, bf16[16,64,411]{1,0,2:T(8,128)(2,1)S(1)} %copy.34, s32[]{:T(128)} %constant.2.clone.1, s32[]{:T(128)S(6)} %select_n.53, s32[]{:T(128)} %constant.2.clone.1) | dynamic-update-slice | bytes 1683460 | tf_op jit(solution)/shard_map/dynamic_update_slice | solution.py:167
  (18 shorter events, 0.2 us)
Async XLA Ops:
  0.0 15.8 %copy-start = (bf16[16,128,411]{1,0,2:T(8,128)(2,1)S(1)}, bf16[16,128,411]{1,0,2:T(8,128)(2,1)}, u32[]{:S(2)}) copy-start(bf16[16,128,411]{1,0,2:T(8,128)(2,1)} %param.10) | copy-start | bytes 5050372
  0.0 36.0 %collective-permute-start.6 = (bf16[8,308,411]{2,0,1:T(8,128)(2,1)}, bf16[8,308,411]{2,0,1:T(8,128)(2,1)}, u32[]{:S(2)}, u32[]{:S(2)}) collective-permute-start(bf16[8,308,411]{2,0,1:T(8,128)(2,1)} %param.7), channel_id=1, source_target_pairs={{0,1},{1,0},{2,3},{3,2},{4,5},{5,4},{6,7},{7,6},{8,9},{9,8},{10,11... | collective-permute-start | bytes 6076232 | tf_op jit(solution)/shard_map/ppermute | solution.py:20
  4.8 12.7 %copy-start.5 = (s32[8]{0:T(128)}, s32[8]{0:T(128)S(1)}, u32[]{:S(2)}) copy-start(s32[8]{0:T(128)S(1)} %multiply_add_fusion.place_ref) | copy-start | bytes 100
  5.6 17.0 %collective-permute-start = (s32[3]{0:T(128)S(1)}, s32[3]{0:T(128)S(1)}, u32[]{:S(2)}, u32[]{:S(2)}) collective-permute-start(s32[3]{0:T(128)S(1)} %get-tuple-element.22), channel_id=1, source_target_pairs={{0,254},{2,0},{4,2},{6,4},{8,6},{10,8},{12,10},{14,12},{16,14},{18... | collective-permute-start | bytes 44 | tf_op jit(solution)/shard_map/ppermute | solution.py:16
  14.1 9.1 %collective-permute-start.1 = (s32[3]{0:T(128)S(1)}, s32[3]{0:T(128)S(1)}, u32[]{:S(2)}, u32[]{:S(2)}) collective-permute-start(s32[3]{0:T(128)S(1)} %get-tuple-element.20), channel_id=1, source_target_pairs={{0,2},{2,4},{4,6},{6,8},{8,10},{10,12},{12,14},{14,16},{16,18},{18... | collective-permute-start | bytes 44 | tf_op jit(solution)/shard_map/ppermute | solution.py:16
  14.1 9.6 %collective-permute-start.2 = (s32[3]{0:T(128)S(1)}, s32[3]{0:T(128)S(1)}, u32[]{:S(2)}, u32[]{:S(2)}) collective-permute-start(s32[3]{0:T(128)S(1)} %get-tuple-element.19), channel_id=1, source_target_pairs={{0,4},{2,6},{4,8},{6,10},{8,12},{10,14},{12,16},{14,18},{16,20},{1... | collective-permute-start | bytes 44 | tf_op jit(solution)/shard_map/ppermute | solution.py:16
  14.1 17.2 %collective-permute-start.7 = (bf16[8,308]{1,0:T(8,128)(2,1)}, bf16[8,308]{1,0:T(8,128)(2,1)S(1)}, u32[]{:S(2)}, u32[]{:S(2)}) collective-permute-start(bf16[8,308]{1,0:T(8,128)(2,1)} %param.9), channel_id=1, source_target_pairs={{0,1},{1,0},{2,3},{3,2},{4,5},{5,4},{6,7},{7,6},{8,9},{9,8},{10,11... | collective-permute-start | bytes 14792 | tf_op jit(solution)/shard_map/ppermute | solution.py:20
  17.5 5.1 %copy-start.1 = (bf16[308,616]{1,0:T(8,128)(2,1)S(1)}, bf16[308,616]{1,0:T(8,128)(2,1)}, u32[]{:S(2)}) copy-start(bf16[308,616]{1,0:T(8,128)(2,1)} %param.8) | copy-start | bytes 1138372
  22.6 12.2 %collective-permute-start.8 = (bf16[308,616]{1,0:T(8,128)(2,1)S(1)}, bf16[308,616]{1,0:T(8,128)(2,1)S(1)}, u32[]{:S(2)}, u32[]{:S(2)}) collective-permute-start(bf16[308,616]{1,0:T(8,128)(2,1)S(1)} %copy-done.1), channel_id=1, source_target_pairs={{0,1},{1,0},{2,3},{3,2},{4,5},{5,4},{6,7},{7,6},{8,9},{9,8},{10,11... | collective-permute-start | bytes 1138376 | tf_op jit(solution)/shard_map/ppermute | solution.py:20
  23.2 16.8 %collective-permute-start.3 = (bf16[3,64,411]{2,1,0:T(8,128)(2,1)S(1)}, bf16[3,64,411]{2,1,0:T(8,128)(2,1)S(1)}, u32[]{:S(2)}, u32[]{:S(2)}) collective-permute-start(bf16[3,64,411]{2,1,0:T(8,128)(2,1)S(1)} %copy.45), channel_id=1, source_target_pairs={{0,2},{2,4},{4,6},{6,8},{8,10},{10,12},{12,14},{14,16},{16,18},{18... | collective-permute-start | bytes 473480 | tf_op jit(solution)/shard_map/ppermute | solution.py:16
  23.8 16.3 %collective-permute-start.4 = (bf16[3,64,411]{2,1,0:T(8,128)(2,1)S(1)}, bf16[3,64,411]{2,1,0:T(8,128)(2,1)S(1)}, u32[]{:S(2)}, u32[]{:S(2)}) collective-permute-start(bf16[3,64,411]{2,1,0:T(8,128)(2,1)S(1)} %copy.43), channel_id=1, source_target_pairs={{0,254},{2,0},{4,2},{6,4},{8,6},{10,8},{12,10},{14,12},{16,14},{18... | collective-permute-start | bytes 473480 | tf_op jit(solution)/shard_map/ppermute | solution.py:16
  31.3 8.8 %collective-permute-start.5 = (bf16[3,64,411]{2,1,0:T(8,128)(2,1)S(1)}, bf16[3,64,411]{2,1,0:T(8,128)(2,1)S(1)}, u32[]{:S(2)}, u32[]{:S(2)}) collective-permute-start(bf16[3,64,411]{2,1,0:T(8,128)(2,1)S(1)} %copy.42), channel_id=1, source_target_pairs={{0,252},{2,254},{4,0},{6,2},{8,4},{10,6},{12,8},{14,10},{16,12},{1... | collective-permute-start | bytes 473480 | tf_op jit(solution)/shard_map/ppermute | solution.py:16
  40.0 0.7 copy-start.2
  40.1 0.8 copy-start.3
  40.1 0.8 copy-start.4
  55.0 12.6 %collective-permute-start.10 = (bf16[3,64,411]{2,1,0:T(8,128)(2,1)}, bf16[3,64,411]{2,1,0:T(8,128)(2,1)S(1)}, u32[]{:S(2)}, u32[]{:S(2)}) collective-permute-start(bf16[3,64,411]{2,1,0:T(8,128)(2,1)} %get-tuple-element.11), channel_id=1, source_target_pairs={{0,2},{2,4},{4,6},{6,8},{8,10},{10,12},{12,14},{14,16},{16,18},{18... | collective-permute-start | bytes 473480 | tf_op jit(solution)/shard_map/ppermute | solution.py:16
  55.0 13.2 %collective-permute-start.11 = (bf16[3,64,411]{2,1,0:T(8,128)(2,1)}, bf16[3,64,411]{2,1,0:T(8,128)(2,1)S(1)}, u32[]{:S(2)}, u32[]{:S(2)}) collective-permute-start(bf16[3,64,411]{2,1,0:T(8,128)(2,1)} %get-tuple-element.12), channel_id=1, source_target_pairs={{0,4},{2,6},{4,8},{6,10},{8,12},{10,14},{12,16},{14,18},{16,20},{1... | collective-permute-start | bytes 473480 | tf_op jit(solution)/shard_map/ppermute | solution.py:16
  55.5 12.8 %collective-permute-start.9 = (bf16[3,64,411]{2,1,0:T(8,128)(2,1)}, bf16[3,64,411]{2,1,0:T(8,128)(2,1)S(1)}, u32[]{:S(2)}, u32[]{:S(2)}) collective-permute-start(bf16[3,64,411]{2,1,0:T(8,128)(2,1)} %get-tuple-element.9), channel_id=1, source_target_pairs={{0,254},{2,0},{4,2},{6,4},{8,6},{10,8},{12,10},{14,12},{16,14},{18... | collective-permute-start | bytes 473480 | tf_op jit(solution)/shard_map/ppermute | solution.py:16
  70.9 79.5 %collective-permute-start.12 = (bf16[16,64,411]{2,0,1:T(8,128)(2,1)}, bf16[16,64,411]{2,0,1:T(8,128)(2,1)}, u32[]{:S(2)}, u32[]{:S(2)}) collective-permute-start(bf16[16,64,411]{2,0,1:T(8,128)(2,1)} %convolution_convert_fusion), channel_id=1, source_target_pairs={{0,1},{1,0},{2,3},{3,2},{4,5},{5,4},{6,7},{7,6},{8,9},{9,8},{10,11... | collective-permute-start | bytes 2525192 | tf_op jit(solution)/shard_map/ppermute | solution.py:20

commit v14 on v11

--- a/solution.py
+++ b/solution.py
@@ -142,14 +142,15 @@
         return jnp.einsum("ac,cms->ams", one_hot(index, columns), own_inc,
                           preferred_element_type=jnp.float32).astype(jnp.bfloat16)
 
-    slot_parts = []
-    for g in range(SPAN):
+    issue = (3, 2, 0, 1)
+    slot_parts = [None] * SPAN
+    for g in issue:
         wanted = request[g * capacity:(g + 1) * capacity]
-        slot_parts.append(wanted if g == 1 else passed_along(wanted, "tile", g - 1))
-    fetched_parts = []
-    for g in range(SPAN):
+        slot_parts[g] = wanted if g == 1 else passed_along(wanted, "tile", g - 1)
+    fetched_parts = [None] * SPAN
+    for g in issue:
         picked = pick(slot_parts[g])
-        fetched_parts.append(picked if g == 1 else passed_along(picked, "tile", 1 - g))
+        fetched_parts[g] = picked if g == 1 else passed_along(picked, "tile", 1 - g)
     packed = adjoints(place, foot_counts, fetched_parts, jac_c, jac_o, innov_c, innov_o, r_blocks)
     recv_parts = []
     for g in range(SPAN):

time: 83.7 us -> 83.7 us (level)
  no operation moved by 1% of the time
where the time goes in v14:
time: 83.7 us; the launch traced here: 83.2 us
  starting transfers between devices  32.1 us (38%)
  local copies, waits for them, and re-layouts  15.8 us (19%)
  Pallas kernels  14.2 us (17%)
  waiting for transfers between devices  9.97 us (12%)
  other arithmetic  8.35 us (10%)
  matrix products  1.99 us (2%)
    ppermute x9, starting transfers between devices, passed_along(): lax.ppermute(value, axis, [(i, (i + by) % count) for i in range(count)])  25.8 us
    pallas_call x1, Pallas kernels, adjoints(): pl.pallas_call(adjoint_kernel, grid_spec=grid_spec, out_shape=[jax.ShapeD...  14.2 us
    ppermute x9, waiting for transfers between devices, passed_along(): lax.ppermute(value, axis, [(i, (i + by) % count) for i in range(count)])  7.68 us
    ppermute x4, starting transfers between devices, swapped(): return lax.ppermute(value, 'chan', [(0, 1), (1, 0)])  6.3 us
    select_n x1, local copies, waits for them, and re-layouts, on_device(): jnp.where(first, jnp.concatenate([mine, other], axis=1), jnp.concatenate(...  4.94 us
    unnamed x13, local copies, waits for them, and re-layouts  4.14 us
    ppermute x1, local copies, waits for them, and re-layouts, swapped(): return lax.ppermute(value, 'chan', [(0, 1), (1, 0)])  4.04 us
    ppermute x4, waiting for transfers between devices, swapped(): return lax.ppermute(value, 'chan', [(0, 1), (1, 0)])  2.29 us
  transfers between devices with their start and end apart: 13, of which 3 were waited for; matrix products, arithmetic and copies ran while one was open for 20% of the time, Pallas kernels for 0%

profile of v14, /device:TPU:1, one launch (start us, length us, event | category | flops | bytes accessed | tf_op | source)
XLA Modules:
  0.0 83.2 jit_solution(15601885998259650700)
XLA Ops:
  0.0 3.2 %collective-permute-start.6 = (bf16[8,308,411]{2,0,1:T(8,128)(2,1)}, bf16[8,308,411]{2,0,1:T(8,128)(2,1)}, u32[]{:S(2)}, u32[]{:S(2)}) collective-permute-start(bf16[8,308,411]{2,0,1:T(8,128)(2,1)} %param.7), channel_id=1, source_target_pairs={{0,1},{1,0},{2,3},{3,2},{4,5},{5,4},{6,7},{7,6},{8,9},{9,8},{10,11... | collective-permute-start | bytes 6076232 | tf_op jit(solution)/shard_map/ppermute | solution.py:20
  3.2 0.9 %convert_reduce_fusion = s32[8]{0:T(128)S(1)} fusion(s32[8]{0:T(128)} %bitcast.23), kind=kLoop, calls=%fused_computation.19 | loop fusion | flops 312 | bytes 64 | tf_op jit(solution)/shard_map/reduce_sum | solution.py:134
  4.1 0.7 multiply_add_fusion.place_ref
  4.8 0.7 select_reduce_fusion
  5.5 0.1 fusion.21
  5.6 8.5 %collective-permute-start = (s32[3]{0:T(128)S(1)}, s32[3]{0:T(128)S(1)}, u32[]{:S(2)}, u32[]{:S(2)}) collective-permute-start(s32[3]{0:T(128)S(1)} %get-tuple-element.22), channel_id=1, source_target_pairs={{0,254},{2,0},{4,2},{6,4},{8,6},{10,8},{12,10},{14,12},{16,14},{18... | collective-permute-start | bytes 44 | tf_op jit(solution)/shard_map/ppermute | solution.py:16
  14.1 0.0 collective-permute-start.1
  14.1 0.0 collective-permute-start.2
  14.1 0.4 collective-permute-start.7
  14.5 1.3 %convert_element_type.34.ic_ref = f32[8,308]{1,0:T(8,128)} convert(bf16[8,308]{1,0:T(8,128)(2,1)} %param.9) | non-fusion elementwise | flops 2464 | bytes 14784 | tf_op jit(solution)/shard_map/convert_element_type | solution.py:116
  16.4 1.7 %constant_dynamic-slice_fusion = bf16[16,64,411]{1,0,2:T(8,128)(2,1)} fusion(bf16[16,128,411]{1,0,2:T(8,128)(2,1)S(1)} %copy-done, s32[]{:T(128)S(6)} %select_n.49), kind=kLoop, calls=%fused_computation.40 | loop fusion | bytes 1683460 | tf_op jit(solution)/shard_map/dynamic_slice | solution.py:139
  18.1 3.3 %copy.32 = bf16[16,64,411]{2,0,1:T(8,128)(2,1)S(1)} copy(bf16[16,64,411]{1,0,2:T(8,128)(2,1)} %constant_dynamic-slice_fusion) | data formatting | bytes 1683456
  21.5 0.4 fusion.9
  21.9 0.7 copy.41.s1_ref
  22.6 0.0 collective-permute-done
  22.6 0.2 collective-permute-start.8
  22.8 0.3 fusion.6
  23.2 0.0 collective-permute-done.1
  23.2 0.1 collective-permute-start.3
  23.3 0.4 fusion.12
  23.7 0.0 collective-permute-done.2
  23.7 7.1 %collective-permute-start.4 = (bf16[3,64,411]{2,1,0:T(8,128)(2,1)S(1)}, bf16[3,64,411]{2,1,0:T(8,128)(2,1)S(1)}, u32[]{:S(2)}, u32[]{:S(2)}) collective-permute-start(bf16[3,64,411]{2,1,0:T(8,128)(2,1)S(1)} %copy.40), channel_id=1, source_target_pairs={{0,254},{2,0},{4,2},{6,4},{8,6},{10,8},{12,10},{14,12},{16,14},{18... | collective-permute-start | bytes 473480 | tf_op jit(solution)/shard_map/ppermute | solution.py:16
  30.8 0.3 fusion.15
  31.2 2.9 %collective-permute-start.5 = (bf16[3,64,411]{2,1,0:T(8,128)(2,1)S(1)}, bf16[3,64,411]{2,1,0:T(8,128)(2,1)S(1)}, u32[]{:S(2)}, u32[]{:S(2)}) collective-permute-start(bf16[3,64,411]{2,1,0:T(8,128)(2,1)S(1)} %copy.39), channel_id=1, source_target_pairs={{0,252},{2,254},{4,0},{6,2},{8,4},{10,6},{12,8},{14,10},{16,12},{1... | collective-permute-start | bytes 473480 | tf_op jit(solution)/shard_map/ppermute | solution.py:16
  34.1 0.6 convert_element_type.35.io_ref
  34.7 0.0 collective-permute-done.8
  34.7 0.1 broadcast_select_fusion.1
  34.8 1.1 %broadcast_select_fusion.2 = (bf16[308,308]{1,0:T(8,128)(2,1)}, bf16[308,308]{1,0:T(8,128)(2,1)}, bf16[308,308]{1,0:T(8,128)(2,1)}, bf16[308,308]{1,0:T(8,128)(2,1)}) fusion(pred[]{:T(512)S(6)} %eq.44, bf16[308,616]{1,0:T(8,128)(2,1)S(1)} %get-tuple-element.18, bf16[308,616]{1,0:T(8,128)(2,1)S(1)} %get-tuple-element.17), kind=kLoop, calls=%fused_computation.10 | loop fusion | flops 379456 | bytes 1517825 | tf_op jit(solution)/shard_map/jit(_where)/select_n | solution.py:128
  35.9 4.0 %copy.29.jo_ref = bf16[8,308,411]{2,1,0:T(8,128)(2,1)} copy(bf16[8,308,411]{2,0,1:T(8,128)(2,1)} %collective-permute-done.6) | data formatting | bytes 4050816 | tf_op jit(solution)/shard_map/ppermute | solution.py:20
  40.0 0.0 collective-permute-done.3.s0_ref
  40.0 0.0 collective-permute-done.5.s3_ref
  40.0 0.6 copy-done.2
  40.6 0.1 copy-done.3
  40.7 0.1 copy-done.4
  40.8 14.2 %shard_map.73 = (bf16[3,64,411]{2,1,0:T(8,128)(2,1)}, bf16[3,64,411]{2,1,0:T(8,128)(2,1)}, bf16[3,64,411]{2,1,0:T(8,128)(2,1)}, bf16[3,64,411]{2,1,0:T(8,128)(2,1)}) custom-call(s32[8]{0:T(128)} %copy-done.5, s32[1]{0:T(128)S(6)} %copy.43.count_ref, bf16[3,64,411]{2,1,0:T(8,128)(2,1)} %copy-done.2, bf16[3,64,411]{2,1,0:T(8,128)(2,1)} %copy.41.s1_ref, ...), custom_call_target="tpu_custom_call" | custom-call | tf_op jit(solution)/shard_map/pallas_call | solution.py:96
  55.0 0.3 collective-permute-start.11
  55.3 0.0 collective-permute-start.10
  55.3 6.9 %collective-permute-start.9 = (bf16[3,64,411]{2,1,0:T(8,128)(2,1)}, bf16[3,64,411]{2,1,0:T(8,128)(2,1)S(1)}, u32[]{:S(2)}, u32[]{:S(2)}) collective-permute-start(bf16[3,64,411]{2,1,0:T(8,128)(2,1)} %get-tuple-element.9), channel_id=1, source_target_pairs={{0,254},{2,0},{4,2},{6,4},{8,6},{10,8},{12,10},{14,12},{16,14},{18... | collective-permute-start | bytes 473480 | tf_op jit(solution)/shard_map/ppermute | solution.py:16
  62.2 0.1 pad_add_fusion
  62.3 4.5 %collective-permute-done.11 = bf16[3,64,411]{2,1,0:T(8,128)(2,1)S(1)} collective-permute-done((bf16[3,64,411]{2,1,0:T(8,128)(2,1)}, bf16[3,64,411]{2,1,0:T(8,128)(2,1)S(1)}, u32[]{:S(2)}, u32[]{:S(2)}) %collective-permute-start.11) | collective-permute-done | bytes 157856 | tf_op jit(solution)/shard_map/ppermute | solution.py:16
  66.8 3.1 %collective-permute-done.10 = bf16[3,64,411]{2,1,0:T(8,128)(2,1)S(1)} collective-permute-done((bf16[3,64,411]{2,1,0:T(8,128)(2,1)}, bf16[3,64,411]{2,1,0:T(8,128)(2,1)S(1)}, u32[]{:S(2)}, u32[]{:S(2)}) %collective-permute-start.10) | collective-permute-done | bytes 157856 | tf_op jit(solution)/shard_map/ppermute | solution.py:16
  69.9 0.0 collective-permute-done.9
  69.9 1.0 %pad_maximum_fusion = bf16[12,64,411]{2,1,0:T(8,128)(2,1)S(1)} fusion(bf16[3,64,411]{2,1,0:T(8,128)(2,1)S(1)} %collective-permute-done.11, bf16[3,64,411]{2,1,0:T(8,128)(2,1)S(1)} %collective-permute-done.10, bf16[3,64,411]{2,1,0:T(8,128)(2,1)} %get-tuple-element.10, bf16[3,64,411]{2,1,0:T(8,128)(2,1)S(1)} %collective-permute-done.9), kind=kLoop, calls=%fused_computation.3 | loop fusion | flops 946944 | bytes 1262592 | tf_op jit(solution)/shard_map/concatenate | solution.py:163
  71.0 0.6 convolution_convert_fusion
  71.6 2.6 %collective-permute-start.12 = (bf16[16,64,411]{2,0,1:T(8,128)(2,1)S(1)}, bf16[16,64,411]{2,0,1:T(8,128)(2,1)S(1)}, u32[]{:S(2)}, u32[]{:S(2)}) collective-permute-start(bf16[16,64,411]{2,0,1:T(8,128)(2,1)S(1)} %convolution_convert_fusion), channel_id=1, source_target_pairs={{0,1},{1,0},{2,3},{3,2},{4,5},{5,4},{6,7},{7,6},{8,9},{9,8},{10,11... | collective-permute-start | bytes 2525192 | tf_op jit(solution)/shard_map/ppermute | solution.py:20
  74.2 2.3 %collective-permute-done.12 = bf16[16,64,411]{2,0,1:T(8,128)(2,1)S(1)} collective-permute-done((bf16[16,64,411]{2,0,1:T(8,128)(2,1)S(1)}, bf16[16,64,411]{2,0,1:T(8,128)(2,1)S(1)}, u32[]{:S(2)}, u32[]{:S(2)}) %collective-permute-start.12) | collective-permute-done | bytes 841760 | tf_op jit(solution)/shard_map/ppermute | solution.py:20
  76.5 1.8 %maximum_select_fusion = bf16[16,128,411]{2,0,1:T(8,128)(2,1)} fusion(bf16[16,64,411]{2,0,1:T(8,128)(2,1)S(1)} %collective-permute-done.12, bf16[16,64,411]{2,0,1:T(8,128)(2,1)S(1)} %convolution_convert_fusion, pred[]{:T(512)S(6)} %eq.44), kind=kLoop, calls=%fused_computation | loop fusion | flops 2525184 | bytes 3366913 | tf_op jit(solution)/shard_map/jit(_where)/select_n | solution.py:166
  78.3 4.9 %copy.31 = bf16[16,128,411]{1,0,2:T(8,128)(2,1)} copy(bf16[16,128,411]{2,0,1:T(8,128)(2,1)} %maximum_select_fusion) | data formatting | bytes 3366912 | tf_op jit(solution)/shard_map/jit(_where)/select_n | solution.py:166
  (15 shorter events, 0.2 us)
Async XLA Ops:
  0.0 16.4 %copy-start = (bf16[16,128,411]{1,0,2:T(8,128)(2,1)S(1)}, bf16[16,128,411]{1,0,2:T(8,128)(2,1)}, u32[]{:S(2)}) copy-start(bf16[16,128,411]{1,0,2:T(8,128)(2,1)} %param.10) | copy-start | bytes 5050372
  0.0 35.9 %collective-permute-start.6 = (bf16[8,308,411]{2,0,1:T(8,128)(2,1)}, bf16[8,308,411]{2,0,1:T(8,128)(2,1)}, u32[]{:S(2)}, u32[]{:S(2)}) collective-permute-start(bf16[8,308,411]{2,0,1:T(8,128)(2,1)} %param.7), channel_id=1, source_target_pairs={{0,1},{1,0},{2,3},{3,2},{4,5},{5,4},{6,7},{7,6},{8,9},{9,8},{10,11... | collective-permute-start | bytes 6076232 | tf_op jit(solution)/shard_map/ppermute | solution.py:20
  4.8 16.7 %copy-start.5 = (s32[8]{0:T(128)}, s32[8]{0:T(128)S(1)}, u32[]{:S(2)}) copy-start(s32[8]{0:T(128)S(1)} %multiply_add_fusion.place_ref) | copy-start | bytes 100
  5.6 17.0 %collective-permute-start = (s32[3]{0:T(128)S(1)}, s32[3]{0:T(128)S(1)}, u32[]{:S(2)}, u32[]{:S(2)}) collective-permute-start(s32[3]{0:T(128)S(1)} %get-tuple-element.22), channel_id=1, source_target_pairs={{0,254},{2,0},{4,2},{6,4},{8,6},{10,8},{12,10},{14,12},{16,14},{18... | collective-permute-start | bytes 44 | tf_op jit(solution)/shard_map/ppermute | solution.py:16
  14.1 9.0 %collective-permute-start.1 = (s32[3]{0:T(128)S(1)}, s32[3]{0:T(128)S(1)}, u32[]{:S(2)}, u32[]{:S(2)}) collective-permute-start(s32[3]{0:T(128)S(1)} %get-tuple-element.20), channel_id=1, source_target_pairs={{0,2},{2,4},{4,6},{6,8},{8,10},{10,12},{12,14},{14,16},{16,18},{18... | collective-permute-start | bytes 44 | tf_op jit(solution)/shard_map/ppermute | solution.py:16
  14.1 9.6 %collective-permute-start.2 = (s32[3]{0:T(128)S(1)}, s32[3]{0:T(128)S(1)}, u32[]{:S(2)}, u32[]{:S(2)}) collective-permute-start(s32[3]{0:T(128)S(1)} %get-tuple-element.19), channel_id=1, source_target_pairs={{0,4},{2,6},{4,8},{6,10},{8,12},{10,14},{12,16},{14,18},{16,20},{1... | collective-permute-start | bytes 44 | tf_op jit(solution)/shard_map/ppermute | solution.py:16
  14.1 17.1 %collective-permute-start.7 = (bf16[8,308]{1,0:T(8,128)(2,1)}, bf16[8,308]{1,0:T(8,128)(2,1)S(1)}, u32[]{:S(2)}, u32[]{:S(2)}) collective-permute-start(bf16[8,308]{1,0:T(8,128)(2,1)} %param.9), channel_id=1, source_target_pairs={{0,1},{1,0},{2,3},{3,2},{4,5},{5,4},{6,7},{7,6},{8,9},{9,8},{10,11... | collective-permute-start | bytes 14792 | tf_op jit(solution)/shard_map/ppermute | solution.py:20
  18.1 4.5 %copy-start.1 = (bf16[308,616]{1,0:T(8,128)(2,1)S(1)}, bf16[308,616]{1,0:T(8,128)(2,1)}, u32[]{:S(2)}) copy-start(bf16[308,616]{1,0:T(8,128)(2,1)} %param.8) | copy-start | bytes 1138372
  22.6 12.1 %collective-permute-start.8 = (bf16[308,616]{1,0:T(8,128)(2,1)S(1)}, bf16[308,616]{1,0:T(8,128)(2,1)S(1)}, u32[]{:S(2)}, u32[]{:S(2)}) collective-permute-start(bf16[308,616]{1,0:T(8,128)(2,1)S(1)} %copy-done.1), channel_id=1, source_target_pairs={{0,1},{1,0},{2,3},{3,2},{4,5},{5,4},{6,7},{7,6},{8,9},{9,8},{10,11... | collective-permute-start | bytes 1138376 | tf_op jit(solution)/shard_map/ppermute | solution.py:20
  23.2 16.8 %collective-permute-start.3 = (bf16[3,64,411]{2,1,0:T(8,128)(2,1)S(1)}, bf16[3,64,411]{2,1,0:T(8,128)(2,1)S(1)}, u32[]{:S(2)}, u32[]{:S(2)}) collective-permute-start(bf16[3,64,411]{2,1,0:T(8,128)(2,1)S(1)} %copy.42), channel_id=1, source_target_pairs={{0,2},{2,4},{4,6},{6,8},{8,10},{10,12},{12,14},{14,16},{16,18},{18... | collective-permute-start | bytes 473480 | tf_op jit(solution)/shard_map/ppermute | solution.py:16
  23.7 16.3 %collective-permute-start.4 = (bf16[3,64,411]{2,1,0:T(8,128)(2,1)S(1)}, bf16[3,64,411]{2,1,0:T(8,128)(2,1)S(1)}, u32[]{:S(2)}, u32[]{:S(2)}) collective-permute-start(bf16[3,64,411]{2,1,0:T(8,128)(2,1)S(1)} %copy.40), channel_id=1, source_target_pairs={{0,254},{2,0},{4,2},{6,4},{8,6},{10,8},{12,10},{14,12},{16,14},{18... | collective-permute-start | bytes 473480 | tf_op jit(solution)/shard_map/ppermute | solution.py:16
  31.2 8.8 %collective-permute-start.5 = (bf16[3,64,411]{2,1,0:T(8,128)(2,1)S(1)}, bf16[3,64,411]{2,1,0:T(8,128)(2,1)S(1)}, u32[]{:S(2)}, u32[]{:S(2)}) collective-permute-start(bf16[3,64,411]{2,1,0:T(8,128)(2,1)S(1)} %copy.39), channel_id=1, source_target_pairs={{0,252},{2,254},{4,0},{6,2},{8,4},{10,6},{12,8},{14,10},{16,12},{1... | collective-permute-start | bytes 473480 | tf_op jit(solution)/shard_map/ppermute | solution.py:16
  40.0 0.7 copy-start.2
  40.0 0.8 copy-start.3
  40.0 0.8 copy-start.4
  55.0 11.8 %collective-permute-start.11 = (bf16[3,64,411]{2,1,0:T(8,128)(2,1)}, bf16[3,64,411]{2,1,0:T(8,128)(2,1)S(1)}, u32[]{:S(2)}, u32[]{:S(2)}) collective-permute-start(bf16[3,64,411]{2,1,0:T(8,128)(2,1)} %get-tuple-element.12), channel_id=1, source_target_pairs={{0,4},{2,6},{4,8},{6,10},{8,12},{10,14},{12,16},{14,18},{16,20},{1... | collective-permute-start | bytes 473480 | tf_op jit(solution)/shard_map/ppermute | solution.py:16
  55.3 14.6 %collective-permute-start.10 = (bf16[3,64,411]{2,1,0:T(8,128)(2,1)}, bf16[3,64,411]{2,1,0:T(8,128)(2,1)S(1)}, u32[]{:S(2)}, u32[]{:S(2)}) collective-permute-start(bf16[3,64,411]{2,1,0:T(8,128)(2,1)} %get-tuple-element.11), channel_id=1, source_target_pairs={{0,2},{2,4},{4,6},{6,8},{8,10},{10,12},{12,14},{14,16},{16,18},{18... | collective-permute-start | bytes 473480 | tf_op jit(solution)/shard_map/ppermute | solution.py:16
  55.3 14.6 %collective-permute-start.9 = (bf16[3,64,411]{2,1,0:T(8,128)(2,1)}, bf16[3,64,411]{2,1,0:T(8,128)(2,1)S(1)}, u32[]{:S(2)}, u32[]{:S(2)}) collective-permute-start(bf16[3,64,411]{2,1,0:T(8,128)(2,1)} %get-tuple-element.9), channel_id=1, source_target_pairs={{0,254},{2,0},{4,2},{6,4},{8,6},{10,8},{12,10},{14,12},{16,14},{18... | collective-permute-start | bytes 473480 | tf_op jit(solution)/shard_map/ppermute | solution.py:16
  71.6 4.9 %collective-permute-start.12 = (bf16[16,64,411]{2,0,1:T(8,128)(2,1)S(1)}, bf16[16,64,411]{2,0,1:T(8,128)(2,1)S(1)}, u32[]{:S(2)}, u32[]{:S(2)}) collective-permute-start(bf16[16,64,411]{2,0,1:T(8,128)(2,1)S(1)} %convolution_convert_fusion), channel_id=1, source_target_pairs={{0,1},{1,0},{2,3},{3,2},{4,5},{5,4},{6,7},{7,6},{8,9},{9,8},{10,11... | collective-permute-start | bytes 2525192 | tf_op jit(solution)/shard_map/ppermute | solution.py:20

commit v15 on v11

--- a/solution.py
+++ b/solution.py
@@ -48,8 +48,11 @@
     ev_c = lax.dot_general(s, jc, NT, preferred_element_type=jnp.float32)
     ev_o = lax.dot_general(s, jo, NT, preferred_element_type=jnp.float32)
     at = pl.multiple_of(f * rows, rows)
-    dc_s[pl.ds(at, rows), :] = (ev_c - ic_ref[pl.ds(f, 1), :]).astype(jnp.bfloat16)
-    do_s[pl.ds(at, rows), :] = (ev_o - io_ref[pl.ds(f, 1), :]).astype(jnp.bfloat16)
+    which = lax.broadcasted_iota(jnp.int32, ic_ref.shape, 0) == f
+    innov_row_c = jnp.sum(jnp.where(which, ic_ref[...].astype(jnp.float32), 0.0), axis=0, keepdims=True)
+    innov_row_o = jnp.sum(jnp.where(which, io_ref[...].astype(jnp.float32), 0.0), axis=0, keepdims=True)
+    dc_s[pl.ds(at, rows), :] = (ev_c - innov_row_c).astype(jnp.bfloat16)
+    do_s[pl.ds(at, rows), :] = (ev_o - innov_row_o).astype(jnp.bfloat16)
 
     @pl.when(f == foot - 1)
     def _():
@@ -113,8 +116,8 @@
 
     jac_c = jnp.transpose(jacobian, (1, 0, 2))
     jac_o = swapped(jacobian)
-    innov_c = innovation.astype(jnp.float32)
-    innov_o = swapped(innovation).astype(jnp.float32)
+    innov_c = innovation
+    innov_o = swapped(innovation)
     r_o = swapped(r_inverse)
     first = core == 0
     rows_lo = jnp.where(first, r_inverse, r_o)

time: 83.7 us -> 81.8 us (0.977)
  other arithmetic: 8.35 us -> 6.45 us
    convert_element_type x2 -> x0, other arithmetic: 1.89 us -> none  [the longest x1 1.29 us: on_device(): innov_c = innovation.astype(jnp.float32)]
    unnamed x13 -> x15, local copies, waits for them, and re-layouts: 4.14 us -> 4.13 us
  transfers between devices with their start and end apart: 13 -> 13, of which waited for: 3 -> 4; matrix products, arithmetic and copies ran while one was open for 20% -> 18% of each run, Pallas kernels for 0% -> 0%
where the time goes in v15:
time: 81.8 us; the launch traced here: 81.4 us
  starting transfers between devices  32.4 us (40%)
  local copies, waits for them, and re-layouts  15.7 us (19%)
  Pallas kernels  14.2 us (17%)
  waiting for transfers between devices  9.75 us (12%)
  other arithmetic  6.45 us (8%)
  matrix products  1.99 us (2%)
  between operations  0.83 us (1%)
    ppermute x9, starting transfers between devices, passed_along(): lax.ppermute(value, axis, [(i, (i + by) % count) for i in range(count)])  25.7 us
    pallas_call x1, Pallas kernels, adjoints(): pl.pallas_call(adjoint_kernel, grid_spec=grid_spec, out_shape=[jax.ShapeD...  14.2 us
    ppermute x9, waiting for transfers between devices, passed_along(): lax.ppermute(value, axis, [(i, (i + by) % count) for i in range(count)])  7.46 us
    ppermute x4, starting transfers between devices, swapped(): return lax.ppermute(value, 'chan', [(0, 1), (1, 0)])  6.68 us
    select_n x1, local copies, waits for them, and re-layouts, on_device(): jnp.where(first, jnp.concatenate([mine, other], axis=1), jnp.concatenate(...  4.94 us
    unnamed x15, local copies, waits for them, and re-layouts  4.13 us
    ppermute x1, local copies, waits for them, and re-layouts, swapped(): return lax.ppermute(value, 'chan', [(0, 1), (1, 0)])  4.03 us
    ppermute x4, waiting for transfers between devices, swapped(): return lax.ppermute(value, 'chan', [(0, 1), (1, 0)])  2.29 us
  transfers between devices with their start and end apart: 13, of which 4 were waited for; matrix products, arithmetic and copies ran while one was open for 18% of the time, Pallas kernels for 0%

profile of v15, /device:TPU:1, one launch (start us, length us, event | category | flops | bytes accessed | tf_op | source)
XLA Modules:
  0.0 81.4 jit_solution(1866133218846614261)
XLA Ops:
  0.0 3.2 %collective-permute-start.6 = (bf16[8,308,411]{2,0,1:T(8,128)(2,1)}, bf16[8,308,411]{2,0,1:T(8,128)(2,1)}, u32[]{:S(2)}, u32[]{:S(2)}) collective-permute-start(bf16[8,308,411]{2,0,1:T(8,128)(2,1)} %param.7), channel_id=1, source_target_pairs={{0,1},{1,0},{2,3},{3,2},{4,5},{5,4},{6,7},{7,6},{8,9},{9,8},{10,11... | collective-permute-start | bytes 6076232 | tf_op jit(solution)/shard_map/ppermute | solution.py:20
  3.2 0.9 %convert_reduce_fusion = s32[8]{0:T(128)S(1)} fusion(s32[8]{0:T(128)} %bitcast.23), kind=kLoop, calls=%fused_computation.19 | loop fusion | flops 312 | bytes 64 | tf_op jit(solution)/shard_map/reduce_sum | solution.py:137
  4.1 0.7 multiply_add_fusion.place_ref
  4.8 0.7 select_reduce_fusion
  5.5 0.1 fusion.21
  5.6 8.5 %collective-permute-start = (s32[3]{0:T(128)S(1)}, s32[3]{0:T(128)S(1)}, u32[]{:S(2)}, u32[]{:S(2)}) collective-permute-start(s32[3]{0:T(128)S(1)} %get-tuple-element.22), channel_id=1, source_target_pairs={{0,254},{2,0},{4,2},{6,4},{8,6},{10,8},{12,10},{14,12},{16,14},{18... | collective-permute-start | bytes 44 | tf_op jit(solution)/shard_map/ppermute | solution.py:16
  14.1 0.0 collective-permute-start.1
  14.1 0.0 collective-permute-start.2
  14.1 0.4 collective-permute-start.7
  15.1 1.7 %constant_dynamic-slice_fusion = bf16[16,64,411]{1,0,2:T(8,128)(2,1)} fusion(bf16[16,128,411]{1,0,2:T(8,128)(2,1)S(1)} %copy-done, s32[]{:T(128)S(6)} %select_n.49), kind=kLoop, calls=%fused_computation.40 | loop fusion | bytes 1683460 | tf_op jit(solution)/shard_map/dynamic_slice | solution.py:142
  16.8 3.3 %copy.32 = bf16[16,64,411]{2,0,1:T(8,128)(2,1)S(1)} copy(bf16[16,64,411]{1,0,2:T(8,128)(2,1)} %constant_dynamic-slice_fusion) | data formatting | bytes 1683456
  20.2 0.4 fusion.9
  20.6 0.7 copy.41.s1_ref
  21.3 0.0 collective-permute-done
  21.3 0.2 collective-permute-start.8
  21.4 0.3 fusion.6
  21.8 0.1 collective-permute-done.1
  22.0 0.0 collective-permute-start.3
  22.0 0.4 fusion.12
  22.4 0.0 collective-permute-done.2
  22.4 7.1 %collective-permute-start.4 = (bf16[3,64,411]{2,1,0:T(8,128)(2,1)S(1)}, bf16[3,64,411]{2,1,0:T(8,128)(2,1)S(1)}, u32[]{:S(2)}, u32[]{:S(2)}) collective-permute-start(bf16[3,64,411]{2,1,0:T(8,128)(2,1)S(1)} %copy.40), channel_id=1, source_target_pairs={{0,254},{2,0},{4,2},{6,4},{8,6},{10,8},{12,10},{14,12},{16,14},{18... | collective-permute-start | bytes 473480 | tf_op jit(solution)/shard_map/ppermute | solution.py:16
  29.5 0.3 fusion.15
  29.9 0.0 collective-permute-done.8
  29.9 2.9 %collective-permute-start.5 = (bf16[3,64,411]{2,1,0:T(8,128)(2,1)S(1)}, bf16[3,64,411]{2,1,0:T(8,128)(2,1)S(1)}, u32[]{:S(2)}, u32[]{:S(2)}) collective-permute-start(bf16[3,64,411]{2,1,0:T(8,128)(2,1)S(1)} %copy.39), channel_id=1, source_target_pairs={{0,252},{2,254},{4,0},{6,2},{8,4},{10,6},{12,8},{14,10},{16,12},{1... | collective-permute-start | bytes 473480 | tf_op jit(solution)/shard_map/ppermute | solution.py:16
  32.8 0.1 broadcast_select_fusion.1
  32.9 1.1 %broadcast_select_fusion.2 = (bf16[308,308]{1,0:T(8,128)(2,1)}, bf16[308,308]{1,0:T(8,128)(2,1)}, bf16[308,308]{1,0:T(8,128)(2,1)}, bf16[308,308]{1,0:T(8,128)(2,1)}) fusion(pred[]{:T(512)S(6)} %eq.44, bf16[308,616]{1,0:T(8,128)(2,1)S(1)} %get-tuple-element.18, bf16[308,616]{1,0:T(8,128)(2,1)S(1)} %get-tuple-element.17), kind=kLoop, calls=%fused_computation.10 | loop fusion | flops 379456 | bytes 1517825 | tf_op jit(solution)/shard_map/jit(_where)/select_n | solution.py:131
  34.0 0.0 collective-permute-done.6
  34.0 4.0 %copy.29.jo_ref = bf16[8,308,411]{2,1,0:T(8,128)(2,1)} copy(bf16[8,308,411]{2,0,1:T(8,128)(2,1)} %collective-permute-done.6) | data formatting | bytes 4050816 | tf_op jit(solution)/shard_map/ppermute | solution.py:20
  38.0 0.0 collective-permute-done.7.io_ref
  38.0 0.0 collective-permute-done.3.s0_ref
  38.1 0.0 collective-permute-done.5.s3_ref
  38.1 0.5 copy-done.5
  38.6 0.1 copy-done.2
  38.7 0.1 copy-done.3
  38.8 0.0 copy-done.4
  38.9 14.2 %shard_map.73 = (bf16[3,64,411]{2,1,0:T(8,128)(2,1)}, bf16[3,64,411]{2,1,0:T(8,128)(2,1)}, bf16[3,64,411]{2,1,0:T(8,128)(2,1)}, bf16[3,64,411]{2,1,0:T(8,128)(2,1)}) custom-call(s32[8]{0:T(128)} %copy-done.6, s32[1]{0:T(128)S(6)} %copy.43.count_ref, bf16[3,64,411]{2,1,0:T(8,128)(2,1)} %copy-done.2, bf16[3,64,411]{2,1,0:T(8,128)(2,1)} %copy.41.s1_ref, ...), custom_call_target="tpu_custom_call" | custom-call | tf_op jit(solution)/shard_map/pallas_call | solution.py:99
  53.1 0.3 collective-permute-start.11
  53.4 0.0 collective-permute-start.10
  53.4 6.9 %collective-permute-start.9 = (bf16[3,64,411]{2,1,0:T(8,128)(2,1)}, bf16[3,64,411]{2,1,0:T(8,128)(2,1)S(1)}, u32[]{:S(2)}, u32[]{:S(2)}) collective-permute-start(bf16[3,64,411]{2,1,0:T(8,128)(2,1)} %get-tuple-element.9), channel_id=1, source_target_pairs={{0,254},{2,0},{4,2},{6,4},{8,6},{10,8},{12,10},{14,12},{16,14},{18... | collective-permute-start | bytes 473480 | tf_op jit(solution)/shard_map/ppermute | solution.py:16
  60.3 0.1 pad_add_fusion
  60.4 5.0 %collective-permute-done.11 = bf16[3,64,411]{2,1,0:T(8,128)(2,1)S(1)} collective-permute-done((bf16[3,64,411]{2,1,0:T(8,128)(2,1)}, bf16[3,64,411]{2,1,0:T(8,128)(2,1)S(1)}, u32[]{:S(2)}, u32[]{:S(2)}) %collective-permute-start.11) | collective-permute-done | bytes 157856 | tf_op jit(solution)/shard_map/ppermute | solution.py:16
  65.4 2.4 %collective-permute-done.10 = bf16[3,64,411]{2,1,0:T(8,128)(2,1)S(1)} collective-permute-done((bf16[3,64,411]{2,1,0:T(8,128)(2,1)}, bf16[3,64,411]{2,1,0:T(8,128)(2,1)S(1)}, u32[]{:S(2)}, u32[]{:S(2)}) %collective-permute-start.10) | collective-permute-done | bytes 157856 | tf_op jit(solution)/shard_map/ppermute | solution.py:16
  67.7 1.0 %pad_maximum_fusion = bf16[12,64,411]{2,1,0:T(8,128)(2,1)S(1)} fusion(bf16[3,64,411]{2,1,0:T(8,128)(2,1)S(1)} %collective-permute-done.11, bf16[3,64,411]{2,1,0:T(8,128)(2,1)S(1)} %collective-permute-done.10, bf16[3,64,411]{2,1,0:T(8,128)(2,1)} %get-tuple-element.10, bf16[3,64,411]{2,1,0:T(8,128)(2,1)S(1)} %collective-permute-done.9), kind=kLoop, calls=%fused_computation.3 | loop fusion | flops 946944 | bytes 1262592 | tf_op jit(solution)/shard_map/concatenate | solution.py:165
  68.8 0.6 convolution_convert_fusion
  69.4 3.0 %collective-permute-start.12 = (bf16[16,64,411]{2,0,1:T(8,128)(2,1)S(1)}, bf16[16,64,411]{2,0,1:T(8,128)(2,1)S(1)}, u32[]{:S(2)}, u32[]{:S(2)}) collective-permute-start(bf16[16,64,411]{2,0,1:T(8,128)(2,1)S(1)} %convolution_convert_fusion), channel_id=1, source_target_pairs={{0,1},{1,0},{2,3},{3,2},{4,5},{5,4},{6,7},{7,6},{8,9},{9,8},{10,11... | collective-permute-start | bytes 2525192 | tf_op jit(solution)/shard_map/ppermute | solution.py:20
  72.3 2.3 %collective-permute-done.12 = bf16[16,64,411]{2,0,1:T(8,128)(2,1)S(1)} collective-permute-done((bf16[16,64,411]{2,0,1:T(8,128)(2,1)S(1)}, bf16[16,64,411]{2,0,1:T(8,128)(2,1)S(1)}, u32[]{:S(2)}, u32[]{:S(2)}) %collective-permute-start.12) | collective-permute-done | bytes 841760 | tf_op jit(solution)/shard_map/ppermute | solution.py:20
  74.6 1.8 %maximum_select_fusion = bf16[16,128,411]{2,0,1:T(8,128)(2,1)} fusion(bf16[16,64,411]{2,0,1:T(8,128)(2,1)S(1)} %collective-permute-done.12, bf16[16,64,411]{2,0,1:T(8,128)(2,1)S(1)} %convolution_convert_fusion, pred[]{:T(512)S(6)} %eq.44), kind=kLoop, calls=%fused_computation | loop fusion | flops 2525184 | bytes 3366913 | tf_op jit(solution)/shard_map/jit(_where)/select_n | solution.py:168
  76.4 4.9 %copy.31 = bf16[16,128,411]{1,0,2:T(8,128)(2,1)} copy(bf16[16,128,411]{2,0,1:T(8,128)(2,1)} %maximum_select_fusion) | data formatting | bytes 3366912 | tf_op jit(solution)/shard_map/jit(_where)/select_n | solution.py:168
  (15 shorter events, 0.2 us)
Async XLA Ops:
  0.0 15.1 %copy-start = (bf16[16,128,411]{1,0,2:T(8,128)(2,1)S(1)}, bf16[16,128,411]{1,0,2:T(8,128)(2,1)}, u32[]{:S(2)}) copy-start(bf16[16,128,411]{1,0,2:T(8,128)(2,1)} %param.10) | copy-start | bytes 5050372
  0.0 34.0 %collective-permute-start.6 = (bf16[8,308,411]{2,0,1:T(8,128)(2,1)}, bf16[8,308,411]{2,0,1:T(8,128)(2,1)}, u32[]{:S(2)}, u32[]{:S(2)}) collective-permute-start(bf16[8,308,411]{2,0,1:T(8,128)(2,1)} %param.7), channel_id=1, source_target_pairs={{0,1},{1,0},{2,3},{3,2},{4,5},{5,4},{6,7},{7,6},{8,9},{9,8},{10,11... | collective-permute-start | bytes 6076232 | tf_op jit(solution)/shard_map/ppermute | solution.py:20
  4.8 15.4 %copy-start.6 = (s32[8]{0:T(128)}, s32[8]{0:T(128)S(1)}, u32[]{:S(2)}) copy-start(s32[8]{0:T(128)S(1)} %multiply_add_fusion.place_ref) | copy-start | bytes 100
  5.6 15.7 %collective-permute-start = (s32[3]{0:T(128)S(1)}, s32[3]{0:T(128)S(1)}, u32[]{:S(2)}, u32[]{:S(2)}) collective-permute-start(s32[3]{0:T(128)S(1)} %get-tuple-element.22), channel_id=1, source_target_pairs={{0,254},{2,0},{4,2},{6,4},{8,6},{10,8},{12,10},{14,12},{16,14},{18... | collective-permute-start | bytes 44 | tf_op jit(solution)/shard_map/ppermute | solution.py:16
  14.1 7.8 %collective-permute-start.1 = (s32[3]{0:T(128)S(1)}, s32[3]{0:T(128)S(1)}, u32[]{:S(2)}, u32[]{:S(2)}) collective-permute-start(s32[3]{0:T(128)S(1)} %get-tuple-element.20), channel_id=1, source_target_pairs={{0,2},{2,4},{4,6},{6,8},{8,10},{10,12},{12,14},{14,16},{16,18},{18... | collective-permute-start | bytes 44 | tf_op jit(solution)/shard_map/ppermute | solution.py:16
  14.1 8.3 %collective-permute-start.2 = (s32[3]{0:T(128)S(1)}, s32[3]{0:T(128)S(1)}, u32[]{:S(2)}, u32[]{:S(2)}) collective-permute-start(s32[3]{0:T(128)S(1)} %get-tuple-element.19), channel_id=1, source_target_pairs={{0,4},{2,6},{4,8},{6,10},{8,12},{10,14},{12,16},{14,18},{16,20},{1... | collective-permute-start | bytes 44 | tf_op jit(solution)/shard_map/ppermute | solution.py:16
  14.1 23.9 %collective-permute-start.7 = (bf16[8,308]{1,0:T(8,128)(2,1)}, bf16[8,308]{1,0:T(8,128)(2,1)S(1)}, u32[]{:S(2)}, u32[]{:S(2)}) collective-permute-start(bf16[8,308]{1,0:T(8,128)(2,1)} %ic_ref.1), channel_id=1, source_target_pairs={{0,1},{1,0},{2,3},{3,2},{4,5},{5,4},{6,7},{7,6},{8,9},{9,8},{10,11... | collective-permute-start | bytes 14792 | tf_op jit(solution)/shard_map/ppermute | solution.py:20
  16.8 4.4 %copy-start.1 = (bf16[308,616]{1,0:T(8,128)(2,1)S(1)}, bf16[308,616]{1,0:T(8,128)(2,1)}, u32[]{:S(2)}) copy-start(bf16[308,616]{1,0:T(8,128)(2,1)} %param.8) | copy-start | bytes 1138372
  21.3 8.6 %collective-permute-start.8 = (bf16[308,616]{1,0:T(8,128)(2,1)S(1)}, bf16[308,616]{1,0:T(8,128)(2,1)S(1)}, u32[]{:S(2)}, u32[]{:S(2)}) collective-permute-start(bf16[308,616]{1,0:T(8,128)(2,1)S(1)} %copy-done.1), channel_id=1, source_target_pairs={{0,1},{1,0},{2,3},{3,2},{4,5},{5,4},{6,7},{7,6},{8,9},{9,8},{10,11... | collective-permute-start | bytes 1138376 | tf_op jit(solution)/shard_map/ppermute | solution.py:20
  22.0 16.1 %collective-permute-start.3 = (bf16[3,64,411]{2,1,0:T(8,128)(2,1)S(1)}, bf16[3,64,411]{2,1,0:T(8,128)(2,1)S(1)}, u32[]{:S(2)}, u32[]{:S(2)}) collective-permute-start(bf16[3,64,411]{2,1,0:T(8,128)(2,1)S(1)} %copy.42), channel_id=1, source_target_pairs={{0,2},{2,4},{4,6},{6,8},{8,10},{10,12},{12,14},{14,16},{16,18},{18... | collective-permute-start | bytes 473480 | tf_op jit(solution)/shard_map/ppermute | solution.py:16
  22.4 15.7 %collective-permute-start.4 = (bf16[3,64,411]{2,1,0:T(8,128)(2,1)S(1)}, bf16[3,64,411]{2,1,0:T(8,128)(2,1)S(1)}, u32[]{:S(2)}, u32[]{:S(2)}) collective-permute-start(bf16[3,64,411]{2,1,0:T(8,128)(2,1)S(1)} %copy.40), channel_id=1, source_target_pairs={{0,254},{2,0},{4,2},{6,4},{8,6},{10,8},{12,10},{14,12},{16,14},{18... | collective-permute-start | bytes 473480 | tf_op jit(solution)/shard_map/ppermute | solution.py:16
  29.9 8.2 %collective-permute-start.5 = (bf16[3,64,411]{2,1,0:T(8,128)(2,1)S(1)}, bf16[3,64,411]{2,1,0:T(8,128)(2,1)S(1)}, u32[]{:S(2)}, u32[]{:S(2)}) collective-permute-start(bf16[3,64,411]{2,1,0:T(8,128)(2,1)S(1)} %copy.39), channel_id=1, source_target_pairs={{0,252},{2,254},{4,0},{6,2},{8,4},{10,6},{12,8},{14,10},{16,12},{1... | collective-permute-start | bytes 473480 | tf_op jit(solution)/shard_map/ppermute | solution.py:16
  38.0 0.6 copy-start.5
  38.0 0.7 copy-start.2
  38.1 0.8 copy-start.3
  38.1 0.8 copy-start.4
  53.1 12.3 %collective-permute-start.11 = (bf16[3,64,411]{2,1,0:T(8,128)(2,1)}, bf16[3,64,411]{2,1,0:T(8,128)(2,1)S(1)}, u32[]{:S(2)}, u32[]{:S(2)}) collective-permute-start(bf16[3,64,411]{2,1,0:T(8,128)(2,1)} %get-tuple-element.12), channel_id=1, source_target_pairs={{0,4},{2,6},{4,8},{6,10},{8,12},{10,14},{12,16},{14,18},{16,20},{1... | collective-permute-start | bytes 473480 | tf_op jit(solution)/shard_map/ppermute | solution.py:16
  53.4 14.3 %collective-permute-start.10 = (bf16[3,64,411]{2,1,0:T(8,128)(2,1)}, bf16[3,64,411]{2,1,0:T(8,128)(2,1)S(1)}, u32[]{:S(2)}, u32[]{:S(2)}) collective-permute-start(bf16[3,64,411]{2,1,0:T(8,128)(2,1)} %get-tuple-element.11), channel_id=1, source_target_pairs={{0,2},{2,4},{4,6},{6,8},{8,10},{10,12},{12,14},{14,16},{16,18},{18... | collective-permute-start | bytes 473480 | tf_op jit(solution)/shard_map/ppermute | solution.py:16
  53.4 14.3 %collective-permute-start.9 = (bf16[3,64,411]{2,1,0:T(8,128)(2,1)}, bf16[3,64,411]{2,1,0:T(8,128)(2,1)S(1)}, u32[]{:S(2)}, u32[]{:S(2)}) collective-permute-start(bf16[3,64,411]{2,1,0:T(8,128)(2,1)} %get-tuple-element.9), channel_id=1, source_target_pairs={{0,254},{2,0},{4,2},{6,4},{8,6},{10,8},{12,10},{14,12},{16,14},{18... | collective-permute-start | bytes 473480 | tf_op jit(solution)/shard_map/ppermute | solution.py:16
  69.4 5.3 %collective-permute-start.12 = (bf16[16,64,411]{2,0,1:T(8,128)(2,1)S(1)}, bf16[16,64,411]{2,0,1:T(8,128)(2,1)S(1)}, u32[]{:S(2)}, u32[]{:S(2)}) collective-permute-start(bf16[16,64,411]{2,0,1:T(8,128)(2,1)S(1)} %convolution_convert_fusion), channel_id=1, source_target_pairs={{0,1},{1,0},{2,3},{3,2},{4,5},{5,4},{6,7},{7,6},{8,9},{9,8},{10,11... | collective-permute-start | bytes 2525192 | tf_op jit(solution)/shard_map/ppermute | solution.py:20
